TPU v7x, 256 devices: a whole 4x4x8 slice. The times are simulated.
256 devices in a mesh: seq: 32 (over y, z_lo, x), tp: 8 (over z_hi, core).
Axes of the slice: x: 4, y: 4, z: 8 (z_hi: 4, z_lo: 2; z = z_hi * 2 + z_lo), core: 2. Of those that a mesh axis runs over, the one named last changes fastest.
Arguments:
- hidden_in: bfloat16 [8192, 2048], P('seq')
- token_order: int32 [8192], P('seq'), may hold values from 0 to 8191, as said below
- span_lengths: int32 [8], replicated, may hold values from 1 to 4096, 8192 in all
- placement: int32 [64], replicated, may hold values from 0 to 63, as said below
- norm_in: float32 [2048], replicated, may hold values from 0.1 to 1.9
- q_weight: bfloat16 [2048, 2048], P(None, 'tp')
- k_weight: bfloat16 [2048, 1024], P(None, 'tp')
- v_weight: bfloat16 [2048, 1024], P(None, 'tp'), may hold values from -0.125 to 0.125
- q_gain: float32 [128], replicated
- k_gain: float32 [128], replicated
- o_weight: bfloat16 [2048, 2048], P('tp'), may hold values from -0.125 to 0.125
- norm_mid: float32 [2048], replicated, may hold values from 0.1 to 1.9
- gate_weight: bfloat16 [2048, 3072], P(None, 'tp'), may hold values from -0.125 to 0.125
- up_weight: bfloat16 [2048, 3072], P(None, 'tp'), may hold values from -0.125 to 0.125
- down_weight: bfloat16 [3072, 2048], P('tp'), may hold values from -0.109375 to 0.109375
Outputs:
- hidden_out: bfloat16 [8192, 2048], P('seq', 'tp')
- kv_cache: bfloat16 [64, 128, 2048], P('seq', None, 'tp')
Inputs may be any that keep to these rules, and one draw needn't show every extreme that they name: `token_order`: a permutation of all tokens; for each block b of 128 consecutive tokens and each seq index d, rows d * 256 + placement[b] * 4 + j, j < 4, hold tokens of block b. `placement`: a permutation of the blocks. `span_lengths`: sum to 8192.
All inputs are finite; a program needn't handle non-finite values.
Results may differ from a plain program's by a relative error of at most 0.022.
The roundings to bfloat16 on the way count: a program that leaves them out, or rounds other values in their place, can miss the bound.
Values may be sent and summed in bfloat16 or wider, within the bound.
No kernel may reach another device: no remote copies, remote signals or barrier semaphores. Data moves between devices by JAX's collectives and lax.ppermute only.
A program may use at most 128 MiB of HBM per device.

v0:
```python
import jax
import jax.numpy as jnp
from jax import lax
from jax.sharding import PartitionSpec as P

HD = 128
BLK = 128


EPS = 1e-06
THETA = 1000000.0


def rms(values, gain):
    return values * lax.rsqrt(jnp.mean(values * values, axis=-1, keepdims=True) + EPS) * gain


def rotary(values, pos):
    half = values.shape[-1] // 2
    freq = THETA ** (-jnp.arange(half, dtype=jnp.float32) * 2.0 / values.shape[-1])
    angle = pos.astype(jnp.float32)[:, None] * freq[None, :]
    cosine = jnp.cos(angle)[:, None, :]
    sine = jnp.sin(angle)[:, None, :]
    first = values[..., :half]
    second = values[..., half:]
    return jnp.concatenate(
        [first * cosine - second * sine, second * cosine + first * sine], axis=-1
    )


def request_start(order, lengths):
    ends = jnp.cumsum(lengths)
    begins = ends - lengths
    return jnp.max(jnp.where(begins[None, :] <= order[:, None], begins[None, :], 0), axis=1)


def relay_cache(stacked, token_order, rows, seq_count):
    arrived, anchor = (
        lax.all_to_all(stacked, "seq", split_axis=0, concat_axis=0, tiled=True),
        lax.all_to_all(token_order, "seq", split_axis=0, concat_axis=0, tiled=True),
    )
    group_rows = rows // seq_count
    share = BLK // seq_count
    local_slot = jnp.arange(rows, dtype=jnp.int32) % group_rows // share
    target = local_slot * BLK + anchor % BLK
    cache = jnp.zeros(stacked.shape, jnp.bfloat16).at[target].set(arrived)
    return cache.reshape(rows // BLK, BLK, stacked.shape[1])


def body(
    hidden_in,
    token_order,
    span_lengths,
    placement,
    norm_in,
    q_weight,
    k_weight,
    v_weight,
    q_gain,
    k_gain,
    o_weight,
    norm_mid,
    gate_weight,
    up_weight,
    down_weight,
):
    rows, width = hidden_in.shape
    seq_count = lax.axis_size("seq")
    tp_count = lax.axis_size("tp")
    part = width // tp_count
    kv_heads = k_weight.shape[1] // HD
    q_heads = q_weight.shape[1] // HD
    group = q_heads // kv_heads
    xfull = hidden_in.astype(jnp.float32)
    normed = rms(xfull, norm_in).astype(jnp.bfloat16)
    begin = request_start(token_order, span_lengths)
    pos = token_order - begin
    query = jnp.dot(normed, q_weight, preferred_element_type=jnp.float32).reshape(rows, q_heads, HD)
    keys = jnp.dot(normed, k_weight, preferred_element_type=jnp.float32).reshape(rows, kv_heads, HD)
    values = (
        jnp.dot(normed, v_weight, preferred_element_type=jnp.float32)
        .reshape(rows, kv_heads, HD)
        .astype(jnp.bfloat16)
    )
    qnorm = rotary(rms(query, q_gain), pos).astype(jnp.bfloat16).reshape(rows, kv_heads, group, HD)
    knorm = rotary(rms(keys, k_gain), pos).astype(jnp.bfloat16)
    stacked = jnp.stack([knorm, values], axis=2).reshape(rows, kv_heads * 2 * HD)
    scale = 1.0 / HD**0.5
    start_best = jnp.full((rows, kv_heads, group), -1e30, jnp.float32)
    best = start_best
    piece_keys = lax.all_gather(knorm, "seq", axis=0, tiled=True)
    piece_values = lax.all_gather(values, "seq", axis=0, tiled=True)
    piece_order = lax.all_gather(token_order, "seq", axis=0, tiled=True)
    score = (
        jnp.einsum("qkge,nke->qkgn", qnorm, piece_keys, preferred_element_type=jnp.float32) * scale
    )
    mask = (piece_order[None, :] >= begin[:, None]) & (piece_order[None, :] <= token_order[:, None])
    mask = mask[:, None, None, :]
    score = jnp.where(mask, score, -1e30)
    new_best = jnp.maximum(best, jnp.max(score, axis=-1))
    weights = jnp.where(mask, jnp.exp(score - new_best[..., None]), 0.0)
    total = jnp.sum(weights, axis=-1)
    accum = jnp.einsum(
        "qkgn,nke->qkge",
        weights.astype(jnp.bfloat16),
        piece_values,
        preferred_element_type=jnp.float32,
    )
    best, total, accum = (new_best, total, accum)
    attn = (accum / total[..., None]).astype(jnp.bfloat16).reshape(rows, q_heads * HD)
    terms = jnp.dot(attn, o_weight, preferred_element_type=jnp.float32)
    column = lax.axis_index("tp") * part
    own_input = lax.dynamic_slice_in_dim(xfull, column, part, 1)
    mid = (
        own_input
        + lax.psum_scatter(
            terms.astype(jnp.bfloat16), "tp", scatter_dimension=1, tiled=True
        ).astype(jnp.float32)
    ).astype(jnp.bfloat16)
    mid_full = lax.all_gather(mid, "tp", axis=1, tiled=True)
    normed_mid = rms(mid_full.astype(jnp.float32), norm_mid).astype(jnp.bfloat16)
    gate = jnp.dot(normed_mid, gate_weight, preferred_element_type=jnp.float32)
    upper = jnp.dot(normed_mid, up_weight, preferred_element_type=jnp.float32)
    act = (jax.nn.silu(gate) * upper).astype(jnp.bfloat16)
    feed = lax.psum_scatter(
        jnp.dot(act, down_weight, preferred_element_type=jnp.float32).astype(jnp.bfloat16),
        "tp",
        scatter_dimension=1,
        tiled=True,
    ).astype(jnp.float32)
    out = (mid.astype(jnp.float32) + feed).astype(jnp.bfloat16)
    blocks_dev = rows // BLK
    share = BLK // seq_count
    slots = placement.reshape(seq_count, blocks_dev)
    send_rows = (
        slots[:, :, None] * share + jnp.arange(share, dtype=jnp.int32)[None, None, :]
    ).reshape(rows)
    arrived, anchor = (
        lax.all_to_all(out[send_rows], "seq", split_axis=0, concat_axis=0, tiled=True),
        lax.all_to_all(token_order[send_rows], "seq", split_axis=0, concat_axis=0, tiled=True),
    )
    local_row = anchor - lax.axis_index("seq") * rows
    hidden_out = jnp.zeros_like(out).at[local_row].set(arrived)
    kv_cache = relay_cache(stacked, token_order, rows, seq_count)
    return (hidden_out, kv_cache)


def solution(mesh):
    in_specs = (
        P("seq", None),
        P("seq"),
        P(),
        P(),
        P(),
        P(None, "tp"),
        P(None, "tp"),
        P(None, "tp"),
        P(),
        P(),
        P("tp", None),
        P(),
        P(None, "tp"),
        P(None, "tp"),
        P("tp", None),
    )
    out_specs = (P("seq", "tp"), P("seq", None, "tp"))
    return jax.shard_map(body, mesh=mesh, in_specs=in_specs, out_specs=out_specs, check_vma=False)
```

profile of v0, /device:TPU:1, one launch (start us, length us, event | category | flops | bytes accessed | tf_op | source)
XLA Modules:
  0.0 481.9 jit_solution(16180101352515753356)
XLA Ops:
  7.2 0.0 all-gather.6.cloned.1.call-start
  7.3 1.7 multiply_reduce_fusion
  9.0 2.0 multiply_reduce_fusion.2
  10.9 0.1 copy.34
  11.0 0.2 reduce-window.9
  11.2 0.1 select_reduce_fusion
  11.3 0.1 multiply_bitcast_fusion
  11.4 0.6 fusion.44
  12.0 0.7 pad_maximum_fusion.1
  12.8 0.0 all-gather.6.cloned.1.call-update
  12.8 0.0 all-gather.10.cloned.1.call-start
  12.8 2.2 convolution_convert_fusion.2
  15.0 0.0 all-gather.10.cloned.1.call-update
  15.1 0.0 reduce-scatter.3.cloned.1.call-start
  15.1 0.5 multiply_cosine_fusion
  15.6 1.9 multiply_reduce_fusion.1
  17.6 0.1 copy.35
  17.7 69.2 %all-gather.1 = s32[32,1,256]{2,1,0:T(1,128)S(1)} all-gather(s32[1,1,256]{2,1,0:T(1,128)S(1)} %bitcast.90), channel_id=1, replica_groups=mesh['seq'=32,'tp'=8] {'seq'}, dimensions={0}, use_global_device_ids=true | all-gather | bytes 33792 | tf_op jit(solution)/shard_map/all_gather | solution.py:93
  86.9 0.8 multiply_multiply_fusion
  87.7 0.2 subtract_convert_fusion
  87.8 4.7 compare_and_fusion
  92.5 59.4 %all-gather.6.cloned.1.call-done = bf16[8192,1,128]{2,0,1:T(8,128)(2,1)} async-done(((bf16[256,1,128]{2,0,1:T(8,128)(2,1)}), bf16[8192,1,128]{2,0,1:T(8,128)(2,1)}) %all-gather.6.cloned.1.call-update) | async-done | bytes 2097168 | tf_op jit(solution)/shard_map/all_gather | solution.py:91
  151.9 4.9 %fusion = (f32[256,2]{0,1:T(2,128)S(1)}, f32[8192,256,2]{1,0,2:T(8,128)S(1)}) fusion(pred[256,8192]{0,1:T(8,128)(4,1)} %compare_and_fusion, bf16[256,2,64]{2,0,1:T(8,128)(2,1)S(1)} %get-tuple-element.3, bf16[256,2,64]{2,0,1:T(8,128)(2,1)S(1)} %get-tuple-element.2, bf16[8192,1,128]{2,0,1:T(8,128)(2,1)} %all-gather.6.cloned.1.call-done), kind=kOutput, calls=%fused_computation.6 | convolution fusion | flops 1086586368 | bytes 21104640 | tf_op jit(solution)/shard_map/qkge,nke->qkgn/dot_general | solution.py:95
  156.8 5.7 %copy-done.2 = f32[8192,256,2]{1,0,2:T(8,128)} copy-done((f32[8192,256,2]{1,0,2:T(8,128)}, f32[8192,256,2]{1,0,2:T(8,128)S(1)}, u32[]{:S(2)}) %copy-start.2) | copy-done | bytes 16777240
  162.5 4.4 fusion.1
  167.0 142.3 %all-gather.10.cloned.1.call-done = bf16[8192,128]{1,0:T(8,128)(2,1)} async-done(((bf16[256,128]{1,0:T(8,128)(2,1)}), bf16[8192,128]{1,0:T(8,128)(2,1)}) %all-gather.10.cloned.1.call-update) | async-done | bytes 2097168 | tf_op jit(solution)/shard_map/all_gather | solution.py:92
  309.3 9.2 %fusion.24 = bf16[1,128,256,2]{2,1,3,0:T(8,128)(2,1)S(1)} fusion(f32[8192,256,2]{1,0,2:T(8,128)} %copy-done.2, f32[256,2]{0,1:T(2,128)S(1)} %broadcast_maximum_fusion, pred[256,8192]{0,1:T(8,128)(4,1)} %compare_and_fusion, bf16[8192,128]{1,0:T(8,128)(2,1)} %all-gather.10.cloned.1.call-done, f32[256,2]{0,1:T(2,128)S(1)} %fusion.1), kind=kOutput, calls=%fused_computation.30 | convolution fusion | flops 1094844416 | bytes 21106688 | tf_op jit(solution)/shard_map/qkgn,nke->qkge/dot_general | solution.py:103
  318.5 1.5 convolution_convert_fusion.1
  320.0 0.0 all-gather.8.cloned.1.call-start
  320.1 1.6 convert_element_type.74
  321.7 55.9 %reduce-scatter.3.cloned.1.call-done = bf16[256,256]{1,0:T(8,128)(2,1)} async-done(((bf16[256,2048]{1,0:T(8,128)(2,1)}), bf16[256,256]{1,0:T(8,128)(2,1)}) %reduce-scatter.3.cloned.1.call-update) | async-done | bytes 131088 | tf_op jit(solution)/shard_map/reduce_scatter | solution.py:116
  377.5 1.7 add_convert_fusion.1
  379.3 0.2 reduce-scatter.5.cloned.1.call-start
  379.5 32.3 %all-gather.8.cloned.1.call-done = bf16[256,2048]{1,0:T(8,128)(2,1)} async-done(((bf16[256,256]{1,0:T(8,128)(2,1)}), bf16[256,2048]{1,0:T(8,128)(2,1)}) %all-gather.8.cloned.1.call-update) | async-done | bytes 1048592 | tf_op jit(solution)/shard_map/all_gather | solution.py:120
  411.8 1.5 fusion.7
  413.3 2.6 fusion.36
  415.9 3.8 convolution_convert_fusion
  419.8 0.1 mul.217
  419.9 0.1 iota_add_fusion
  420.0 0.1 add.159
  420.1 1.9 gather_fusion
  422.1 0.7 all_to_all.30
  422.8 6.6 %all-to-all-start = ((s32[32,8,1]{1,2,0:T(1,128)}), s32[32,8,1]{1,2,0:T(1,128)S(1)}, u32[]{:S(2)}, u32[]{:S(2)}) async-start(s32[32,8,1]{1,2,0:T(1,128)} %bitcast.1), calls=%async_computation | async-start | bytes 32768 | tf_op jit(solution)/shard_map/all_to_all | solution.py:140
  429.4 0.7 all_to_all.35
  430.1 6.5 %all-to-all-done = s32[32,8,1]{1,2,0:T(1,128)S(1)} async-done(((s32[32,8,1]{1,2,0:T(1,128)}), s32[32,8,1]{1,2,0:T(1,128)S(1)}, u32[]{:S(2)}, u32[]{:S(2)}) %all-to-all-start) | async-done | bytes 1056 | tf_op jit(solution)/shard_map/all_to_all | solution.py:140
  436.5 3.8 all-to-all-start.2
  440.3 0.1 pad_maximum_fusion
  440.4 0.1 copy.39
  440.6 0.7 all_to_all.38
  441.3 6.2 %all-to-all-done.2 = s32[32,8,1]{1,2,0:T(1,128)S(1)} async-done(((s32[32,8,1]{1,2,0:T(1,128)}), s32[32,8,1]{1,2,0:T(1,128)S(1)}, u32[]{:S(2)}, u32[]{:S(2)}) %all-to-all-start.2) | async-done | bytes 1056 | tf_op jit(solution)/shard_map/all_to_all | solution.py:40
  447.5 3.9 all-to-all-start.3
  451.3 0.1 subtract_reduce_fusion
  451.4 0.1 sub.44
  451.5 4.0 reduce-scatter.5.cloned.1.call-done
  455.5 0.9 add_convert_fusion
  456.5 1.8 gather_fusion.1
  458.3 1.1 all-to-all-done.3
  459.4 6.3 %all-to-all-start.1 = ((bf16[32,8,256]{2,1,0:T(8,128)(2,1)}), bf16[32,8,256]{2,1,0:T(8,128)(2,1)S(1)}, u32[]{:S(2)}, u32[]{:S(2)}) async-start(bf16[32,8,256]{2,1,0:T(8,128)(2,1)} %bitcast.18), calls=%async_computation.3 | async-start | bytes 262144 | tf_op jit(solution)/shard_map/all_to_all | solution.py:139
  465.7 0.5 broadcast.413
  466.2 0.7 reduce.11
  466.9 0.1 all_to_all.37
  467.1 2.1 scatter_custom_fusion.1
  469.1 4.1 all-to-all-done.1
  473.3 2.1 scatter_custom_fusion
  (43 shorter events, 0.2 us)
Async XLA Ops:
  7.2 408.7 %copy-start = (bf16[384,2048]{1,0:T(8,128)(2,1)S(1)}, bf16[384,2048]{1,0:T(8,128)(2,1)}, u32[]{:S(2)}) copy-start(bf16[384,2048]{1,0:T(8,128)(2,1)} %param.29) | copy-start | bytes 4718596
  7.2 3.9 copy-start.12
  7.2 4.1 copy-start.1
  7.2 4.1 copy-start.9
  7.2 144.7 %all-gather.6.cloned.1.call-start = ((), (), s32[]{:S(2)}) async-start(), calls=%async_computation.6 | async-start | bytes 2162688 | tf_op jit(solution)/shard_map/all_gather | solution.py:91
  7.3 5.6 %copy-start.4 = (bf16[256,2048]{1,0:T(8,128)(2,1)S(1)}, bf16[256,2048]{1,0:T(8,128)(2,1)}, u32[]{:S(2)}) copy-start(bf16[256,2048]{1,0:T(8,128)(2,1)} %param.15) | copy-start | bytes 3145732
  7.3 5.6 %copy-start.10 = (f32[2048]{0:T(1024)S(1)}, f32[2048]{0:T(1024)}, u32[]{:S(2)}) copy-start(f32[2048]{0:T(1024)} %param.19) | copy-start | bytes 24580
  12.8 296.5 %all-gather.10.cloned.1.call-start = ((), (), s32[]{:S(2)}) async-start(), calls=%async_computation.10 | async-start | bytes 2162688 | tf_op jit(solution)/shard_map/all_gather | solution.py:92
  15.1 362.5 %reduce-scatter.3.cloned.1.call-start = ((), (), s32[]{:S(2)}) async-start(), calls=%async_computation.7 | async-start | bytes 1179648 | tf_op jit(solution)/shard_map/reduce_scatter | solution.py:116
  151.9 10.6 %copy-start.3 = (pred[256,8192]{0,1:T(8,128)(4,1)S(1)}, pred[256,8192]{0,1:T(8,128)(4,1)}, u32[]{:S(2)}) copy-start(pred[256,8192]{0,1:T(8,128)(4,1)} %compare_and_fusion) | copy-start | bytes 6291460
  156.8 5.7 %copy-start.2 = (f32[8192,256,2]{1,0,2:T(8,128)}, f32[8192,256,2]{1,0,2:T(8,128)S(1)}, u32[]{:S(2)}) copy-start(f32[8192,256,2]{1,0,2:T(8,128)S(1)} %get-tuple-element.13) | copy-start | bytes 50331652
  309.3 9.3 %copy-start.7 = (bf16[256,2048]{1,0:T(8,128)(2,1)S(1)}, bf16[256,2048]{1,0:T(8,128)(2,1)}, u32[]{:S(2)}) copy-start(bf16[256,2048]{1,0:T(8,128)(2,1)} %param.25) | copy-start | bytes 3145732
  320.0 91.8 %all-gather.8.cloned.1.call-start = ((), (), s32[]{:S(2)}) async-start(), calls=%async_computation.8 | async-start | bytes 1179648 | tf_op jit(solution)/shard_map/all_gather | solution.py:120
  320.1 93.2 %copy-start.11 = (f32[2048]{0:T(1024)S(1)}, f32[2048]{0:T(1024)}, u32[]{:S(2)}) copy-start(f32[2048]{0:T(1024)} %param.26) | copy-start | bytes 24580
  379.3 76.3 %reduce-scatter.5.cloned.1.call-start = ((), (), s32[]{:S(2)}) async-start(), calls=%async_computation.9 | async-start | bytes 1179648 | tf_op jit(solution)/shard_map/reduce_scatter | solution.py:125
  413.3 2.6 copy-start.6
  415.9 3.9 copy-start.13
  419.7 20.6 %copy-start.8 = (bf16[256,128]{1,0:T(8,128)(2,1)S(1)}, bf16[256,128]{1,0:T(8,128)(2,1)}, u32[]{:S(2)}) copy-start(bf16[256,128]{1,0:T(8,128)(2,1)} %convolution_convert_fusion.2) | copy-start | bytes 196612
  419.7 35.8 %copy-start.5 = (bf16[256,256]{1,0:T(8,128)(2,1)S(1)}, bf16[256,256]{1,0:T(8,128)(2,1)}, u32[]{:S(2)}) copy-start(bf16[256,256]{1,0:T(8,128)(2,1)} %add_convert_fusion.1) | copy-start | bytes 393220
  422.8 13.8 %all-to-all-start = ((s32[32,8,1]{1,2,0:T(1,128)}), s32[32,8,1]{1,2,0:T(1,128)S(1)}, u32[]{:S(2)}, u32[]{:S(2)}) async-start(s32[32,8,1]{1,2,0:T(1,128)} %bitcast.1), calls=%async_computation | async-start | bytes 32768 | tf_op jit(solution)/shard_map/all_to_all | solution.py:140
  436.5 10.9 %all-to-all-start.2 = ((s32[32,8,1]{1,2,0:T(1,128)}), s32[32,8,1]{1,2,0:T(1,128)S(1)}, u32[]{:S(2)}, u32[]{:S(2)}) async-start(s32[32,8,1]{1,2,0:T(1,128)} %bitcast.20), calls=%async_computation.4 | async-start | bytes 32768 | tf_op jit(solution)/shard_map/all_to_all | solution.py:40
  447.5 11.9 %all-to-all-start.3 = ((bf16[32,8,256]{2,1,0:T(8,128)(2,1)}), bf16[32,8,256]{2,1,0:T(8,128)(2,1)S(1)}, u32[]{:S(2)}, u32[]{:S(2)}) async-start(bf16[32,8,256]{2,1,0:T(8,128)(2,1)} %all_to_all.38), calls=%async_computation.5 | async-start | bytes 262144 | tf_op jit(solution)/shard_map/all_to_all | solution.py:39
  459.4 13.9 %all-to-all-start.1 = ((bf16[32,8,256]{2,1,0:T(8,128)(2,1)}), bf16[32,8,256]{2,1,0:T(8,128)(2,1)S(1)}, u32[]{:S(2)}, u32[]{:S(2)}) async-start(bf16[32,8,256]{2,1,0:T(8,128)(2,1)} %bitcast.18), calls=%async_computation.3 | async-start | bytes 262144 | tf_op jit(solution)/shard_map/all_to_all | solution.py:139
Sparse Core Ops, SparseCore 0:
  12.9 138.9 all-gather.5
  154.3 154.9 all-gather.9
  320.1 57.3 reduce-scatter.2
  379.8 31.9 all-gather.7
  419.9 35.6 reduce-scatter.4
where the time goes:
time: 484 us; the launch traced here: 482 us
  waiting for transfers between devices  312 us (64%)
  blocking collectives  69.2 us (14%)
  matrix products  28 us (6%)
  starting transfers between devices  21 us (4%)
  other arithmetic  20.7 us (4%)
  local copies, waits for them, and re-layouts  17 us (4%)
  between operations  14.2 us (3%)
    all_gather x1, waiting for transfers between devices, body(): piece_values = lax.all_gather(values, 'seq', axis=0, tiled=True)  142 us
    all_gather x1, blocking collectives, body(): piece_order = lax.all_gather(token_order, 'seq', axis=0, tiled=True)  69.2 us
    all_gather x1, waiting for transfers between devices, body(): piece_keys = lax.all_gather(knorm, 'seq', axis=0, tiled=True)  59.4 us
    reduce_scatter x1, waiting for transfers between devices, body(): lax.psum_scatter(terms.astype(jnp.bfloat16), 'tp', scatter_dimension=1, t...  55.9 us
    all_gather x1, waiting for transfers between devices, body(): mid_full = lax.all_gather(mid, 'tp', axis=1, tiled=True)  32.3 us
  transfers between devices with their start and end apart: 9, of which 9 were waited for; matrix products, arithmetic and copies ran while one was open for 6% of the time, Pallas kernels for 0%

commit v1 on v0

--- a/solution.py
+++ b/solution.py
@@ -34,17 +34,21 @@
     return jnp.max(jnp.where(begins[None, :] <= order[:, None], begins[None, :], 0), axis=1)
 
 
-def relay_cache(stacked, token_order, rows, seq_count):
-    arrived, anchor = (
-        lax.all_to_all(stacked, "seq", split_axis=0, concat_axis=0, tiled=True),
-        lax.all_to_all(token_order, "seq", split_axis=0, concat_axis=0, tiled=True),
-    )
+def gather_seq(block, seq_count):
+    copies = jnp.broadcast_to(block[None], (seq_count,) + block.shape)
+    return lax.all_to_all(copies, "seq", split_axis=0, concat_axis=0, tiled=True)
+
+
+def build_cache(pieces, piece_tokens, rows, seq_count):
     group_rows = rows // seq_count
     share = BLK // seq_count
+    start = lax.axis_index("seq") * group_rows
+    arrived = lax.dynamic_slice_in_dim(pieces, start, group_rows, axis=1).reshape(rows, pieces.shape[-1])
+    anchor = lax.dynamic_slice_in_dim(piece_tokens, start, group_rows, axis=1).reshape(rows)
     local_slot = jnp.arange(rows, dtype=jnp.int32) % group_rows // share
     target = local_slot * BLK + anchor % BLK
-    cache = jnp.zeros(stacked.shape, jnp.bfloat16).at[target].set(arrived)
-    return cache.reshape(rows // BLK, BLK, stacked.shape[1])
+    cache = jnp.zeros(arrived.shape, jnp.bfloat16).at[target].set(arrived)
+    return cache.reshape(rows // BLK, BLK, arrived.shape[1])
 
 
 def body(
@@ -88,9 +92,12 @@
     scale = 1.0 / HD**0.5
     start_best = jnp.full((rows, kv_heads, group), -1e30, jnp.float32)
     best = start_best
-    piece_keys = lax.all_gather(knorm, "seq", axis=0, tiled=True)
-    piece_values = lax.all_gather(values, "seq", axis=0, tiled=True)
-    piece_order = lax.all_gather(token_order, "seq", axis=0, tiled=True)
+    pieces = gather_seq(stacked, seq_count)
+    piece_tokens = gather_seq(token_order, seq_count)
+    gathered = pieces.reshape(seq_count * rows, kv_heads, 2, HD)
+    piece_keys = gathered[:, :, 0]
+    piece_values = gathered[:, :, 1]
+    piece_order = piece_tokens.reshape(seq_count * rows)
     score = (
         jnp.einsum("qkge,nke->qkgn", qnorm, piece_keys, preferred_element_type=jnp.float32) * scale
     )
@@ -141,7 +148,7 @@
     )
     local_row = anchor - lax.axis_index("seq") * rows
     hidden_out = jnp.zeros_like(out).at[local_row].set(arrived)
-    kv_cache = relay_cache(stacked, token_order, rows, seq_count)
+    kv_cache = build_cache(pieces, piece_tokens, rows, seq_count)
     return (hidden_out, kv_cache)
 
 

time: 484 us -> 280 us (0.58)
  waiting for transfers between devices: 312 us -> 149 us
  blocking collectives: 69.2 us -> 0 us
  local copies, waits for them, and re-layouts: 17 us -> 39.7 us
  starting transfers between devices: 21 us -> 31.6 us
  matrix products: 28 us -> 22 us
    all_gather x2 -> x0, waiting for transfers between devices: 202 us -> none  [the longest x1 142 us: body(): piece_values = lax.all_gather(values, 'seq', axis=0, tiled=True)]
    all_gather x1 -> x0, blocking collectives: 69.2 us -> none  [body(): piece_order = lax.all_gather(token_order, 'seq', axis=0, tiled=True)]
    all_to_all x2, waiting for transfers between devices: 7.26 us -> 44.1 us  [gather_seq(): lax.all_to_all(copies, 'seq', split_axis=0, concat_axis=0, tiled=True)]
    reduce_scatter x1, waiting for transfers between devices: 4.04 us -> 18.8 us  [body(): lax.psum_scatter(jnp.dot(act, down_weight, preferred_element_type=jnp.flo...]
    reduce_scatter x1, waiting for transfers between devices: 55.9 us -> 41.6 us  [body(): lax.psum_scatter(terms.astype(jnp.bfloat16), 'tp', scatter_dimension=1, t...]
    slice x0 -> x1, local copies, waits for them, and re-layouts: none -> 9.85 us  [body(): piece_values = gathered[:, :, 1]]
    all_to_all x2, starting transfers between devices: 7.66 us -> 17.1 us  [gather_seq(): lax.all_to_all(copies, 'seq', split_axis=0, concat_axis=0, tiled=True)]
    reshape x0 -> x2, local copies, waits for them, and re-layouts: none -> 7 us  [the longest x1 6.91 us: body(): gathered = pieces.reshape(seq_count * rows, kv_heads, 2, HD)]
  transfers between devices with their start and end apart: 9 -> 7, of which waited for: 9 -> 6; matrix products, arithmetic and copies ran while one was open for 6% -> 8% of each run, Pallas kernels for 0% -> 0%
where the time goes in v1:
time: 280 us; the launch traced here: 278 us
  waiting for transfers between devices  149 us (53%)
  local copies, waits for them, and re-layouts  39.7 us (14%)
  starting transfers between devices  31.6 us (11%)
  matrix products  22 us (8%)
  other arithmetic  20.8 us (7%)
  between operations  14.2 us (5%)
    all_to_all x2, waiting for transfers between devices, gather_seq(): lax.all_to_all(copies, 'seq', split_axis=0, concat_axis=0, tiled=True)  44.1 us
    reduce_scatter x1, waiting for transfers between devices, body(): lax.psum_scatter(terms.astype(jnp.bfloat16), 'tp', scatter_dimension=1, t...  41.6 us
    all_gather x1, waiting for transfers between devices, body(): mid_full = lax.all_gather(mid, 'tp', axis=1, tiled=True)  32.8 us
    reduce_scatter x1, waiting for transfers between devices, body(): lax.psum_scatter(jnp.dot(act, down_weight, preferred_element_type=jnp.flo...  18.8 us
    all_to_all x2, starting transfers between devices, gather_seq(): lax.all_to_all(copies, 'seq', split_axis=0, concat_axis=0, tiled=True)  17.1 us
    slice x1, local copies, waits for them, and re-layouts, body(): piece_values = gathered[:, :, 1]  9.85 us
    unnamed x29, local copies, waits for them, and re-layouts  9.31 us
    all_to_all x1, starting transfers between devices, body(): lax.all_to_all(out[send_rows], 'seq', split_axis=0, concat_axis=0, tiled=...  7.57 us
  transfers between devices with their start and end apart: 7, of which 6 were waited for; matrix products, arithmetic and copies ran while one was open for 8% of the time, Pallas kernels for 0%

profile of v1, /device:TPU:1, one launch (start us, length us, event | category | flops | bytes accessed | tf_op | source)
XLA Modules:
  0.0 277.6 jit_solution(209837615477706278)
XLA Ops:
  7.2 0.0 copy-start
  7.2 0.0 copy-start.3
  7.2 0.0 copy-start.11
  7.2 1.5 broadcast_in_dim.35
  8.7 9.2 %all-to-all-start.2 = ((s32[32,1,256]{2,1,0:T(1,128)}), s32[32,1,256]{2,1,0:T(1,128)S(1)}, u32[]{:S(2)}, u32[]{:S(2)}) async-start(s32[32,1,256]{2,1,0:T(1,128)} %broadcast_in_dim.35), calls=%async_computation.2 | async-start | bytes 65536 | tf_op jit(solution)/shard_map/all_to_all | solution.py:39
  17.9 0.8 reduce-window.9
  18.7 0.7 bitcast_subtract_fusion
  19.5 0.8 select_reduce_fusion
  20.2 0.7 subtract_convert_fusion.1
  20.9 1.5 multiply_reduce_fusion
  22.4 0.0 copy-start.8
  22.4 2.0 fusion.18
  24.4 0.6 multiply_reduce_fusion.2
  25.0 0.1 multiply_bitcast_fusion
  25.1 0.3 fusion.58
  25.5 0.1 copy.36
  25.6 2.4 broadcast_in_dim.34
  28.0 7.9 %all-to-all-start.1 = ((bf16[32,256,256]{2,1,0:T(8,128)(2,1)}), bf16[32,256,256]{2,1,0:T(8,128)(2,1)}, u32[]{:S(2)}, u32[]{:S(2)}) async-start(bf16[32,256,256]{2,1,0:T(8,128)(2,1)} %broadcast_in_dim.34), calls=%async_computation.1 | async-start | bytes 8388608 | tf_op jit(solution)/shard_map/all_to_all | solution.py:39
  35.9 0.0 copy-start.9
  35.9 0.0 reduce-scatter.3.cloned.1.call-start
  36.0 1.9 multiply_reduce_fusion.1
  37.9 0.1 copy.39
  38.0 0.5 multiply_cosine_fusion
  38.6 0.1 multiply_multiply_fusion
  38.7 0.2 subtract_convert_fusion
  38.9 4.7 %compare_and_fusion = pred[256,8192]{0,1:T(8,128)(4,1)} fusion(s32[256]{0:T(256)S(1)} %copy-done.1, s32[256]{0:T(256)S(1)} %select_reduce_fusion, s32[8192]{0:T(1024)S(1)} %bitcast.96), kind=kLoop, calls=%fused_computation.12 | loop fusion | flops 6291456 | bytes 2131968 | tf_op jit(solution)/shard_map/and | solution.py:104
  43.6 44.1 %all-to-all-done.1 = bf16[32,256,256]{2,1,0:T(8,128)(2,1)} async-done(((bf16[32,256,256]{2,1,0:T(8,128)(2,1)}), bf16[32,256,256]{2,1,0:T(8,128)(2,1)}, u32[]{:S(2)}, u32[]{:S(2)}) %all-to-all-start.1) | async-done | bytes 4194336 | tf_op jit(solution)/shard_map/all_to_all | solution.py:39
  87.7 6.9 %reshape.579 = bf16[8192,1,2,128]{3,2,0,1:T(2,128)(2,1)} reshape(bf16[32,256,256]{2,1,0:T(8,128)(2,1)} %all-to-all-done.1) | data formatting | bytes 8388608 | tf_op jit(solution)/shard_map/reshape | solution.py:97
  94.6 9.8 %fusion.68 = (bf16[8192,1,1,128]{3,2,0,1:T(2,128)(2,1)}, bf16[8192,1,1,128]{3,2,0,1:T(2,128)(2,1)}) fusion(bf16[8192,1,2,128]{3,2,0,1:T(2,128)(2,1)} %reshape.579), kind=kLoop, calls=%fused_computation.106 | loop fusion | bytes 8388608 | tf_op jit(solution)/shard_map/slice | solution.py:99
  104.4 9.2 %copy.44 = bf16[8192,1,1,128]{0,3,2,1:T(8,128)(2,1)} copy(bf16[8192,1,1,128]{3,2,0,1:T(2,128)(2,1)} %get-tuple-element.2) | data formatting | bytes 4194304
  113.7 5.5 %fusion = (f32[256,2]{0,1:T(2,128)S(1)}, f32[8192,256,2]{1,0,2:T(8,128)S(1)}) fusion(pred[256,8192]{0,1:T(8,128)(4,1)} %compare_and_fusion, bf16[256,2,64]{2,0,1:T(8,128)(2,1)S(1)} %get-tuple-element.5, bf16[256,2,64]{2,0,1:T(8,128)(2,1)S(1)} %get-tuple-element.4, bf16[8192,1,1,128]{3,2,0,1:T(2,128)(2,1)} %get-tuple-element.3), kind=kOutput, calls=%fused_computation.6 | convolution fusion | flops 1086586368 | bytes 21104640 | tf_op jit(solution)/shard_map/qkge,nke->qkgn/dot_general | solution.py:102
  119.2 4.5 %fusion.1 = f32[256,2]{0,1:T(2,128)S(1)} fusion(f32[8192,256,2]{1,0,2:T(8,128)S(1)} %get-tuple-element.15, f32[256,2]{0,1:T(2,128)S(1)} %broadcast_maximum_fusion, pred[256,8192]{0,1:T(8,128)(4,1)S(1)} %copy-done.2), kind=kLoop, calls=%fused_computation.7 | loop fusion | flops 20971008 | bytes 18878464 | tf_op jit(solution)/shard_map/reduce_sum | solution.py:109
  123.7 0.0 copy-start.7
  123.7 4.2 %fusion.24 = bf16[1,128,256,2]{2,1,3,0:T(8,128)(2,1)S(1)} fusion(f32[8192,256,2]{1,0,2:T(8,128)S(1)} %get-tuple-element.15, f32[256,2]{0,1:T(2,128)S(1)} %broadcast_maximum_fusion, pred[256,8192]{0,1:T(8,128)(4,1)S(1)} %copy-done.2, bf16[8192,1,1,128]{0,3,2,1:T(8,128)(2,1)S(1)} %copy-done.4, f32[256,2]{0,1:T(2,128)S(1)} %fusion.1), kind=kOutput, calls=%fused_computation.31 | convolution fusion | flops 1094844416 | bytes 21106688 | tf_op jit(solution)/shard_map/qkgn,nke->qkge/dot_general | solution.py:110
  127.9 1.5 convolution_convert_fusion.1
  129.4 0.0 reduce-scatter.3.cloned.1.call-update
  129.4 0.2 all-gather.2.cloned.1.call-start
  129.6 1.6 convert_element_type.66
  131.2 41.6 %reduce-scatter.3.cloned.1.call-done = bf16[256,256]{1,0:T(8,128)(2,1)} async-done(((bf16[256,2048]{1,0:T(8,128)(2,1)}), bf16[256,256]{1,0:T(8,128)(2,1)}) %reduce-scatter.3.cloned.1.call-update) | async-done | bytes 131088 | tf_op jit(solution)/shard_map/reduce_scatter | solution.py:123
  172.8 1.7 add_convert_fusion.1
  174.5 0.0 all-gather.2.cloned.1.call-update
  174.6 0.0 reduce-scatter.5.cloned.1.call-start
  174.6 32.8 %all-gather.2.cloned.1.call-done = bf16[256,2048]{1,0:T(8,128)(2,1)} async-done(((bf16[256,256]{1,0:T(8,128)(2,1)}), bf16[256,2048]{1,0:T(8,128)(2,1)}) %all-gather.2.cloned.1.call-update) | async-done | bytes 1048592 | tf_op jit(solution)/shard_map/all_gather | solution.py:127
  207.4 1.5 fusion.7
  209.0 2.6 fusion.36
  211.6 3.8 %convolution_convert_fusion = bf16[256,2048]{1,0:T(8,128)(2,1)} fusion(bf16[384,2048]{1,0:T(8,128)(2,1)S(1)} %copy-done, bf16[2048,384]{1,0:T(8,128)(2,1)} %param.28, f32[256,384]{1,0:T(8,128)S(1)} %fusion.36, bf16[256,2048]{1,0:T(8,128)(2,1)S(1)} %copy-done.6, f32[2048]{0:T(1024)S(1)} %copy-done.12, f32[256]{0:T(256)S(1)} %add_rsqrt_fusion.1), kind=kOutput, calls=%fused_computation.15 | convolution fusion | flops 808517632 | bytes 5645312 | tf_op jit(solution)/shard_map/dot_general | solution.py:133
  215.4 0.0 reduce-scatter.5.cloned.1.call-update
  215.5 0.1 mul.220
  215.6 0.1 iota_add_fusion
  215.7 0.1 add.163
  215.8 1.9 gather_fusion
  217.8 0.7 all_to_all.21
  218.5 6.6 %all-to-all-start = ((s32[32,8,1]{1,2,0:T(1,128)}), s32[32,8,1]{1,2,0:T(1,128)S(1)}, u32[]{:S(2)}, u32[]{:S(2)}) async-start(s32[32,8,1]{1,2,0:T(1,128)} %bitcast.1), calls=%async_computation | async-start | bytes 32768 | tf_op jit(solution)/shard_map/all_to_all | solution.py:147
  225.1 7.1 %all-to-all-done = s32[32,8,1]{1,2,0:T(1,128)S(1)} async-done(((s32[32,8,1]{1,2,0:T(1,128)}), s32[32,8,1]{1,2,0:T(1,128)S(1)}, u32[]{:S(2)}, u32[]{:S(2)}) %all-to-all-start) | async-done | bytes 1056 | tf_op jit(solution)/shard_map/all_to_all | solution.py:147
  232.2 0.1 sub.44
  232.3 18.8 %reduce-scatter.5.cloned.1.call-done = bf16[256,256]{1,0:T(8,128)(2,1)} async-done(((bf16[256,2048]{1,0:T(8,128)(2,1)}), bf16[256,256]{1,0:T(8,128)(2,1)}) %reduce-scatter.5.cloned.1.call-update) | async-done | bytes 131088 | tf_op jit(solution)/shard_map/reduce_scatter | solution.py:132
  251.1 0.9 add_convert_fusion
  252.0 1.8 gather_fusion.1
  253.8 7.6 %all-to-all-start.3 = ((bf16[32,8,256]{2,1,0:T(8,128)(2,1)}), bf16[32,8,256]{2,1,0:T(8,128)(2,1)S(1)}, u32[]{:S(2)}, u32[]{:S(2)}) async-start(bf16[32,8,256]{2,1,0:T(8,128)(2,1)} %bitcast.22), calls=%async_computation.5 | async-start | bytes 262144 | tf_op jit(solution)/shard_map/all_to_all | solution.py:146
  261.4 0.1 dynamic-slice_reduce_fusion
  261.6 0.1 reshape.542
  261.7 2.4 scatter_custom_fusion.1
  264.1 4.9 %all-to-all-done.3 = bf16[32,8,256]{2,1,0:T(8,128)(2,1)S(1)} async-done(((bf16[32,8,256]{2,1,0:T(8,128)(2,1)}), bf16[32,8,256]{2,1,0:T(8,128)(2,1)S(1)}, u32[]{:S(2)}, u32[]{:S(2)}) %all-to-all-start.3) | async-done | bytes 131104 | tf_op jit(solution)/shard_map/all_to_all | solution.py:146
  269.0 2.1 scatter_custom_fusion
  (36 shorter events, 0.2 us)
Async XLA Ops:
  7.2 204.4 %copy-start = (bf16[384,2048]{1,0:T(8,128)(2,1)S(1)}, bf16[384,2048]{1,0:T(8,128)(2,1)}, u32[]{:S(2)}) copy-start(bf16[384,2048]{1,0:T(8,128)(2,1)} %param.29) | copy-start | bytes 4718596
  7.2 17.2 %copy-start.3 = (bf16[256,2048]{1,0:T(8,128)(2,1)S(1)}, bf16[256,2048]{1,0:T(8,128)(2,1)}, u32[]{:S(2)}) copy-start(bf16[256,2048]{1,0:T(8,128)(2,1)} %param.15) | copy-start | bytes 3145732
  7.2 17.2 %copy-start.11 = (f32[2048]{0:T(1024)S(1)}, f32[2048]{0:T(1024)}, u32[]{:S(2)}) copy-start(f32[2048]{0:T(1024)} %param.19) | copy-start | bytes 24580
  8.7 16.9 %all-to-all-start.2 = ((s32[32,1,256]{2,1,0:T(1,128)}), s32[32,1,256]{2,1,0:T(1,128)S(1)}, u32[]{:S(2)}, u32[]{:S(2)}) async-start(s32[32,1,256]{2,1,0:T(1,128)} %broadcast_in_dim.35), calls=%async_computation.2 | async-start | bytes 65536 | tf_op jit(solution)/shard_map/all_to_all | solution.py:39
  18.7 5.7 %copy-start.10 = (bf16[2048,128]{1,0:T(8,128)(2,1)S(1)}, bf16[2048,128]{1,0:T(8,128)(2,1)}, u32[]{:S(2)}) copy-start(bf16[2048,128]{1,0:T(8,128)(2,1)} %param.21) | copy-start | bytes 1572868
  22.4 2.6 copy-start.8
  28.0 59.6 %all-to-all-start.1 = ((bf16[32,256,256]{2,1,0:T(8,128)(2,1)}), bf16[32,256,256]{2,1,0:T(8,128)(2,1)}, u32[]{:S(2)}, u32[]{:S(2)}) async-start(bf16[32,256,256]{2,1,0:T(8,128)(2,1)} %broadcast_in_dim.34), calls=%async_computation.1 | async-start | bytes 8388608 | tf_op jit(solution)/shard_map/all_to_all | solution.py:39
  35.9 2.7 copy-start.9
  35.9 3.0 %copy-start.1 = (s32[256]{0:T(256)S(1)}, s32[256]{0:T(256)}, u32[]{:S(2)}) copy-start(s32[256]{0:T(256)} %param.16) | copy-start | bytes 3076
  35.9 136.9 %reduce-scatter.3.cloned.1.call-start = ((), (), s32[]{:S(2)}) async-start(), calls=%async_computation.6 | async-start | bytes 1179648 | tf_op jit(solution)/shard_map/reduce_scatter | solution.py:123
  113.7 5.5 %copy-start.2 = (pred[256,8192]{0,1:T(8,128)(4,1)S(1)}, pred[256,8192]{0,1:T(8,128)(4,1)}, u32[]{:S(2)}) copy-start(pred[256,8192]{0,1:T(8,128)(4,1)} %compare_and_fusion) | copy-start | bytes 6291460
  119.2 4.5 %copy-start.4 = (bf16[8192,1,1,128]{0,3,2,1:T(8,128)(2,1)S(1)}, bf16[8192,1,1,128]{0,3,2,1:T(8,128)(2,1)}, u32[]{:S(2)}) copy-start(bf16[8192,1,1,128]{0,3,2,1:T(8,128)(2,1)} %copy.44) | copy-start | bytes 6291460
  123.7 4.2 %copy-start.7 = (bf16[256,2048]{1,0:T(8,128)(2,1)S(1)}, bf16[256,2048]{1,0:T(8,128)(2,1)}, u32[]{:S(2)}) copy-start(bf16[256,2048]{1,0:T(8,128)(2,1)} %param.25) | copy-start | bytes 3145732
  129.4 78.0 %all-gather.2.cloned.1.call-start = ((), (), s32[]{:S(2)}) async-start(), calls=%async_computation.7 | async-start | bytes 1179648 | tf_op jit(solution)/shard_map/all_gather | solution.py:127
  129.6 79.3 %copy-start.12 = (f32[2048]{0:T(1024)S(1)}, f32[2048]{0:T(1024)}, u32[]{:S(2)}) copy-start(f32[2048]{0:T(1024)} %param.26) | copy-start | bytes 24580
  174.6 76.5 %reduce-scatter.5.cloned.1.call-start = ((), (), s32[]{:S(2)}) async-start(), calls=%async_computation.8 | async-start | bytes 1179648 | tf_op jit(solution)/shard_map/reduce_scatter | solution.py:132
  208.9 2.6 copy-start.6
  211.6 3.9 %copy-start.13 = (s32[64]{0:T(128)S(1)}, s32[64]{0:T(128)}, u32[]{:S(2)}) copy-start(s32[64]{0:T(128)} %param.18) | copy-start | bytes 772
  215.4 35.7 %copy-start.5 = (bf16[256,256]{1,0:T(8,128)(2,1)S(1)}, bf16[256,256]{1,0:T(8,128)(2,1)}, u32[]{:S(2)}) copy-start(bf16[256,256]{1,0:T(8,128)(2,1)} %add_convert_fusion.1) | copy-start | bytes 393220
  218.5 13.7 %all-to-all-start = ((s32[32,8,1]{1,2,0:T(1,128)}), s32[32,8,1]{1,2,0:T(1,128)S(1)}, u32[]{:S(2)}, u32[]{:S(2)}) async-start(s32[32,8,1]{1,2,0:T(1,128)} %bitcast.1), calls=%async_computation | async-start | bytes 32768 | tf_op jit(solution)/shard_map/all_to_all | solution.py:147
  253.8 15.1 %all-to-all-start.3 = ((bf16[32,8,256]{2,1,0:T(8,128)(2,1)}), bf16[32,8,256]{2,1,0:T(8,128)(2,1)S(1)}, u32[]{:S(2)}, u32[]{:S(2)}) async-start(bf16[32,8,256]{2,1,0:T(8,128)(2,1)} %bitcast.22), calls=%async_computation.5 | async-start | bytes 262144 | tf_op jit(solution)/shard_map/all_to_all | solution.py:146
Sparse Core Ops, SparseCore 0:
  129.5 43.2 reduce-scatter.2
  175.2 32.1 all-gather.1
  215.6 35.4 reduce-scatter.4

commit v2 on v1

--- a/solution.py
+++ b/solution.py
@@ -90,31 +90,31 @@
     knorm = rotary(rms(keys, k_gain), pos).astype(jnp.bfloat16)
     stacked = jnp.stack([knorm, values], axis=2).reshape(rows, kv_heads * 2 * HD)
     scale = 1.0 / HD**0.5
-    start_best = jnp.full((rows, kv_heads, group), -1e30, jnp.float32)
-    best = start_best
     pieces = gather_seq(stacked, seq_count)
     piece_tokens = gather_seq(token_order, seq_count)
-    gathered = pieces.reshape(seq_count * rows, kv_heads, 2, HD)
-    piece_keys = gathered[:, :, 0]
-    piece_values = gathered[:, :, 1]
+    flat = pieces.reshape(seq_count * rows, kv_heads * 2 * HD)
     piece_order = piece_tokens.reshape(seq_count * rows)
-    score = (
-        jnp.einsum("qkge,nke->qkgn", qnorm, piece_keys, preferred_element_type=jnp.float32) * scale
-    )
     mask = (piece_order[None, :] >= begin[:, None]) & (piece_order[None, :] <= token_order[:, None])
-    mask = mask[:, None, None, :]
-    score = jnp.where(mask, score, -1e30)
-    new_best = jnp.maximum(best, jnp.max(score, axis=-1))
-    weights = jnp.where(mask, jnp.exp(score - new_best[..., None]), 0.0)
-    total = jnp.sum(weights, axis=-1)
-    accum = jnp.einsum(
-        "qkgn,nke->qkge",
-        weights.astype(jnp.bfloat16),
-        piece_values,
-        preferred_element_type=jnp.float32,
-    )
-    best, total, accum = (new_best, total, accum)
-    attn = (accum / total[..., None]).astype(jnp.bfloat16).reshape(rows, q_heads * HD)
+    mask = mask[:, None, :]
+    heads_out = []
+    for head in range(kv_heads):
+        piece_keys = flat[:, (2 * head) * HD : (2 * head + 1) * HD]
+        piece_values = flat[:, (2 * head + 1) * HD : (2 * head + 2) * HD]
+        qhead = qnorm[:, head].reshape(rows * group, HD)
+        score = lax.dot_general(
+            qhead, piece_keys, (((1,), (1,)), ((), ())), preferred_element_type=jnp.float32
+        ).reshape(rows, group, seq_count * rows) * scale
+        score = jnp.where(mask, score, -1e30)
+        best = jnp.maximum(jnp.max(score, axis=-1), -1e30)
+        weights = jnp.where(mask, jnp.exp(score - best[..., None]), 0.0)
+        total = jnp.sum(weights, axis=-1)
+        accum = jnp.dot(
+            weights.astype(jnp.bfloat16).reshape(rows * group, seq_count * rows),
+            piece_values,
+            preferred_element_type=jnp.float32,
+        ).reshape(rows, group, HD)
+        heads_out.append((accum / total[..., None]).astype(jnp.bfloat16))
+    attn = jnp.stack(heads_out, axis=1).reshape(rows, q_heads * HD)
     terms = jnp.dot(attn, o_weight, preferred_element_type=jnp.float32)
     column = lax.axis_index("tp") * part
     own_input = lax.dynamic_slice_in_dim(xfull, column, part, 1)
@@ -142,10 +142,10 @@
     send_rows = (
         slots[:, :, None] * share + jnp.arange(share, dtype=jnp.int32)[None, None, :]
     ).reshape(rows)
-    arrived, anchor = (
-        lax.all_to_all(out[send_rows], "seq", split_axis=0, concat_axis=0, tiled=True),
-        lax.all_to_all(token_order[send_rows], "seq", split_axis=0, concat_axis=0, tiled=True),
-    )
+    arrived = lax.all_to_all(out[send_rows], "seq", split_axis=0, concat_axis=0, tiled=True)
+    group_rows = rows // seq_count
+    mine = lax.dynamic_slice_in_dim(send_rows, lax.axis_index("seq") * group_rows, group_rows)
+    anchor = piece_tokens[:, mine].reshape(rows)
     local_row = anchor - lax.axis_index("seq") * rows
     hidden_out = jnp.zeros_like(out).at[local_row].set(arrived)
     kv_cache = build_cache(pieces, piece_tokens, rows, seq_count)

time: 280 us -> 264 us (0.943)
  local copies, waits for them, and re-layouts: 39.7 us -> 17.5 us
  waiting for transfers between devices: 149 us -> 160 us
  starting transfers between devices: 31.6 us -> 23.9 us
  matrix products: 22 us -> 29.1 us
  other arithmetic: 20.8 us -> 17.2 us
    reduce_scatter x1, waiting for transfers between devices: 18.8 us -> 34.2 us  [body(): lax.psum_scatter(jnp.dot(act, down_weight, preferred_element_type=jnp.flo...]
    slice x1 -> x0, local copies, waits for them, and re-layouts: 9.85 us -> none  [body(): piece_values = gathered[:, :, 1]]
    all_to_all x1 -> x0, waiting for transfers between devices: 7.07 us -> none  [body(): lax.all_to_all(token_order[send_rows], 'seq', split_axis=0, concat_axis=0...]
    reshape x1 -> x0, local copies, waits for them, and re-layouts: 6.91 us -> none  [body(): gathered = pieces.reshape(seq_count * rows, kv_heads, 2, HD)]
    all_to_all x1 -> x0, starting transfers between devices: 6.59 us -> none  [body(): lax.all_to_all(token_order[send_rows], 'seq', split_axis=0, concat_axis=0...]
    dot_general x2, matrix products: 9.7 us -> 15.8 us  [the longest x1 10.1 us: body(): jnp.dot(weights.astype(jnp.bfloat16).reshape(rows * group, seq_count * ro...]
    unnamed x29 -> x28, local copies, waits for them, and re-layouts: 9.31 us -> 5.77 us
    all_to_all x2, waiting for transfers between devices: 44.1 us -> 46.9 us  [gather_seq(): lax.all_to_all(copies, 'seq', split_axis=0, concat_axis=0, tiled=True)]
  transfers between devices with their start and end apart: 7 -> 6, of which waited for: 6 -> 6; matrix products, arithmetic and copies ran while one was open for 8% -> 7% of each run, Pallas kernels for 0% -> 0%
where the time goes in v2:
time: 264 us; the launch traced here: 262 us
  waiting for transfers between devices  160 us (61%)
  matrix products  29.1 us (11%)
  starting transfers between devices  23.9 us (9%)
  local copies, waits for them, and re-layouts  17.5 us (7%)
  other arithmetic  17.2 us (7%)
  between operations  14.2 us (5%)
    all_to_all x2, waiting for transfers between devices, gather_seq(): lax.all_to_all(copies, 'seq', split_axis=0, concat_axis=0, tiled=True)  46.9 us
    reduce_scatter x1, waiting for transfers between devices, body(): lax.psum_scatter(terms.astype(jnp.bfloat16), 'tp', scatter_dimension=1, t...  41.8 us
    reduce_scatter x1, waiting for transfers between devices, body(): lax.psum_scatter(jnp.dot(act, down_weight, preferred_element_type=jnp.flo...  34.2 us
    all_gather x1, waiting for transfers between devices, body(): mid_full = lax.all_gather(mid, 'tp', axis=1, tiled=True)  32.5 us
    all_to_all x2, starting transfers between devices, gather_seq(): lax.all_to_all(copies, 'seq', split_axis=0, concat_axis=0, tiled=True)  15.9 us
    dot_general x1, matrix products, body(): jnp.dot(weights.astype(jnp.bfloat16).reshape(rows * group, seq_count * ro...  10.1 us
    all_to_all x1, starting transfers between devices, body(): lax.all_to_all(out[send_rows], 'seq', split_axis=0, concat_axis=0, tiled=...  7.46 us
    unnamed x28, local copies, waits for them, and re-layouts  5.77 us
  transfers between devices with their start and end apart: 6, of which 6 were waited for; matrix products, arithmetic and copies ran while one was open for 7% of the time, Pallas kernels for 0%

profile of v2, /device:TPU:1, one launch (start us, length us, event | category | flops | bytes accessed | tf_op | source)
XLA Modules:
  0.0 262.3 jit_solution(8664013726430051842)
XLA Ops:
  7.2 0.0 copy-start
  7.2 0.0 copy-start.3
  7.2 0.0 copy-start.10
  7.2 1.5 broadcast_in_dim.32
  8.7 9.2 %all-to-all-start = ((s32[32,1,256]{2,1,0:T(1,128)}), s32[32,1,256]{2,1,0:T(1,128)S(1)}, u32[]{:S(2)}, u32[]{:S(2)}) async-start(s32[32,1,256]{2,1,0:T(1,128)} %broadcast_in_dim.32), calls=%async_computation | async-start | bytes 65536 | tf_op jit(solution)/shard_map/all_to_all | solution.py:39
  17.9 1.5 multiply_reduce_fusion
  19.5 0.0 copy-start.8
  19.5 2.0 multiply_reduce_fusion.2
  21.5 0.2 reduce-window.9
  21.7 0.1 select_reduce_fusion
  21.8 1.6 fusion.11
  23.4 0.1 multiply_bitcast_fusion
  23.5 0.3 fusion.47
  23.8 0.1 copy.34
  23.9 1.2 all-to-all-done
  25.1 2.4 broadcast_in_dim.37
  27.5 6.7 %all-to-all-start.1 = ((bf16[32,256,256]{2,1,0:T(8,128)(2,1)}), bf16[32,256,256]{2,1,0:T(8,128)(2,1)}, u32[]{:S(2)}, u32[]{:S(2)}) async-start(bf16[32,256,256]{2,1,0:T(8,128)(2,1)} %broadcast_in_dim.37), calls=%async_computation.1 | async-start | bytes 8388608 | tf_op jit(solution)/shard_map/all_to_all | solution.py:39
  34.2 0.0 copy-start.9
  34.2 0.2 reduce-scatter.3.cloned.1.call-start
  34.5 1.9 multiply_reduce_fusion.1
  36.4 0.1 copy.33
  36.5 0.5 multiply_cosine_fusion
  37.0 0.1 multiply_multiply_fusion
  37.2 0.2 subtract_convert_fusion
  37.3 2.9 %compare_and_fusion = pred[256,8192]{1,0:T(8,128)(4,1)} fusion(s32[8192]{0:T(1024)S(1)} %bitcast.53, s32[256]{0:T(256)S(1)} %copy-done.7, s32[256]{0:T(256)S(1)} %select_reduce_fusion), kind=kLoop, calls=%fused_computation.11 | loop fusion | flops 6291456 | bytes 2131968 | tf_op jit(solution)/shard_map/and | solution.py:97
  40.2 45.7 %all-to-all-done.1 = bf16[32,256,256]{2,1,0:T(8,128)(2,1)} async-done(((bf16[32,256,256]{2,1,0:T(8,128)(2,1)}), bf16[32,256,256]{2,1,0:T(8,128)(2,1)}, u32[]{:S(2)}, u32[]{:S(2)}) %all-to-all-start.1) | async-done | bytes 4194336 | tf_op jit(solution)/shard_map/all_to_all | solution.py:39
  86.0 5.7 %fusion = (f32[256,2]{0,1:T(2,128)S(1)}, f32[256,2,8192]{2,0,1:T(8,128)S(1)}) fusion(pred[256,8192]{1,0:T(8,128)(4,1)} %compare_and_fusion, bf16[8192,256]{1,0:T(8,128)(2,1)} %bitcast.12, bf16[256,2,64]{2,0,1:T(8,128)(2,1)S(1)} %get-tuple-element.3, bf16[256,2,64]{2,0,1:T(8,128)(2,1)S(1)} %get-tuple-element.2), kind=kOutput, calls=%fused_computation.6 | convolution fusion | flops 1086586368 | bytes 21104640 | tf_op jit(solution)/shard_map/dot_general | solution.py:104
  91.7 5.7 %copy-done.1 = f32[256,2,8192]{2,0,1:T(8,128)} copy-done((f32[256,2,8192]{2,0,1:T(8,128)}, f32[256,2,8192]{2,0,1:T(8,128)S(1)}, u32[]{:S(2)}) %copy-start.1) | copy-done | bytes 16777240
  97.4 5.3 %fusion.1 = f32[256,2]{0,1:T(2,128)S(1)} fusion(f32[256,2,8192]{2,0,1:T(8,128)S(1)} %get-tuple-element.13, f32[256,2]{0,1:T(2,128)S(1)} %broadcast_maximum_fusion, pred[256,8192]{1,0:T(8,128)(4,1)S(1)} %copy-done.2), kind=kLoop, calls=%fused_computation.7 | loop fusion | flops 20971008 | bytes 18878464 | tf_op jit(solution)/shard_map/reduce_sum | solution.py:110
  102.7 10.1 %fusion.15 = bf16[256,2,128]{0,2,1:T(8,128)(2,1)S(1)} fusion(bf16[8192,256]{1,0:T(8,128)(2,1)} %bitcast.12, f32[256,2,8192]{2,0,1:T(8,128)} %copy-done.1, f32[256,2]{0,1:T(2,128)S(1)} %broadcast_maximum_fusion, pred[256,8192]{1,0:T(8,128)(4,1)S(1)} %copy-done.2, f32[256,2]{0,1:T(2,128)S(1)} %fusion.1), kind=kOutput, calls=%fused_computation.29 | convolution fusion | flops 1094844416 | bytes 21106688 | tf_op jit(solution)/shard_map/dot_general | solution.py:111
  112.8 1.4 convolution_convert_fusion.1
  114.2 0.0 reduce-scatter.3.cloned.1.call-update
  114.3 0.0 all-gather.2.cloned.1.call-start
  114.3 0.0 copy-start.11
  114.3 1.6 convert_element_type.63
  115.9 41.8 %reduce-scatter.3.cloned.1.call-done = bf16[256,256]{1,0:T(8,128)(2,1)} async-done(((bf16[256,2048]{1,0:T(8,128)(2,1)}), bf16[256,256]{1,0:T(8,128)(2,1)}) %reduce-scatter.3.cloned.1.call-update) | async-done | bytes 131088 | tf_op jit(solution)/shard_map/reduce_scatter | solution.py:123
  157.7 1.7 add_convert_fusion.1
  159.4 0.0 all-gather.2.cloned.1.call-update
  159.4 0.3 reduce-scatter.5.cloned.1.call-start
  159.7 32.5 %all-gather.2.cloned.1.call-done = bf16[256,2048]{1,0:T(8,128)(2,1)} async-done(((bf16[256,256]{1,0:T(8,128)(2,1)}), bf16[256,2048]{1,0:T(8,128)(2,1)}) %all-gather.2.cloned.1.call-update) | async-done | bytes 1048592 | tf_op jit(solution)/shard_map/all_gather | solution.py:127
  192.3 1.5 fusion.6
  193.8 2.6 fusion.25
  196.4 0.0 copy-start.13
  196.4 0.0 copy-start.4
  196.4 3.9 %convolution_convert_fusion = bf16[256,2048]{1,0:T(8,128)(2,1)} fusion(bf16[384,2048]{1,0:T(8,128)(2,1)S(1)} %copy-done, bf16[2048,384]{1,0:T(8,128)(2,1)} %param.28, f32[256,384]{1,0:T(8,128)S(1)} %fusion.25, bf16[256,2048]{1,0:T(8,128)(2,1)S(1)} %copy-done.5, f32[2048]{0:T(1024)S(1)} %copy-done.11, f32[256]{0:T(256)S(1)} %add_rsqrt_fusion.1), kind=kOutput, calls=%fused_computation.14 | convolution fusion | flops 808517632 | bytes 5645312 | tf_op jit(solution)/shard_map/dot_general | solution.py:133
  200.3 0.0 reduce-scatter.5.cloned.1.call-update
  200.3 0.1 mul.215
  200.4 0.1 iota_add_fusion
  200.5 0.1 add.184
  200.7 0.1 add.169
  200.8 0.1 compare_select_fusion.5
  200.9 0.1 copy.31
  201.0 0.6 gather_fusion
  201.6 0.1 copy.32
  201.6 0.1 sub.44
  201.7 34.2 %reduce-scatter.5.cloned.1.call-done = bf16[256,256]{1,0:T(8,128)(2,1)} async-done(((bf16[256,2048]{1,0:T(8,128)(2,1)}), bf16[256,256]{1,0:T(8,128)(2,1)}) %reduce-scatter.5.cloned.1.call-update) | async-done | bytes 131088 | tf_op jit(solution)/shard_map/reduce_scatter | solution.py:132
  236.0 0.9 add_convert_fusion
  236.9 1.8 gather_fusion.1
  238.7 7.5 %all-to-all-start.2 = ((bf16[32,8,256]{2,1,0:T(8,128)(2,1)}), bf16[32,8,256]{2,1,0:T(8,128)(2,1)S(1)}, u32[]{:S(2)}, u32[]{:S(2)}) async-start(bf16[32,8,256]{2,1,0:T(8,128)(2,1)} %bitcast.17), calls=%async_computation.4 | async-start | bytes 262144 | tf_op jit(solution)/shard_map/all_to_all | solution.py:145
  246.2 0.1 dynamic-slice_reduce_fusion
  246.3 0.1 reshape.512
  246.4 2.4 scatter_custom_fusion.1
  248.9 4.9 %all-to-all-done.2 = bf16[32,8,256]{2,1,0:T(8,128)(2,1)S(1)} async-done(((bf16[32,8,256]{2,1,0:T(8,128)(2,1)}), bf16[32,8,256]{2,1,0:T(8,128)(2,1)S(1)}, u32[]{:S(2)}, u32[]{:S(2)}) %all-to-all-start.2) | async-done | bytes 131104 | tf_op jit(solution)/shard_map/all_to_all | solution.py:145
  253.7 2.1 scatter_custom_fusion
  (35 shorter events, 0.2 us)
Async XLA Ops:
  7.2 189.2 %copy-start = (bf16[384,2048]{1,0:T(8,128)(2,1)S(1)}, bf16[384,2048]{1,0:T(8,128)(2,1)}, u32[]{:S(2)}) copy-start(bf16[384,2048]{1,0:T(8,128)(2,1)} %param.29) | copy-start | bytes 4718596
  7.2 14.5 %copy-start.7 = (s32[256]{0:T(256)S(1)}, s32[256]{0:T(256)}, u32[]{:S(2)}) copy-start(s32[256]{0:T(256)} %param.16) | copy-start | bytes 3076
  7.2 14.6 %copy-start.3 = (bf16[256,2048]{1,0:T(8,128)(2,1)S(1)}, bf16[256,2048]{1,0:T(8,128)(2,1)}, u32[]{:S(2)}) copy-start(bf16[256,2048]{1,0:T(8,128)(2,1)} %param.15) | copy-start | bytes 3145732
  7.2 14.6 %copy-start.10 = (f32[2048]{0:T(1024)S(1)}, f32[2048]{0:T(1024)}, u32[]{:S(2)}) copy-start(f32[2048]{0:T(1024)} %param.19) | copy-start | bytes 24580
  7.2 14.2 %copy-start.12 = (s32[8]{0:T(128)S(1)}, s32[8]{0:T(128)}, u32[]{:S(2)}) copy-start(s32[8]{0:T(128)} %param.17) | copy-start | bytes 100
  8.7 16.4 %all-to-all-start = ((s32[32,1,256]{2,1,0:T(1,128)}), s32[32,1,256]{2,1,0:T(1,128)S(1)}, u32[]{:S(2)}, u32[]{:S(2)}) async-start(s32[32,1,256]{2,1,0:T(1,128)} %broadcast_in_dim.32), calls=%async_computation | async-start | bytes 65536 | tf_op jit(solution)/shard_map/all_to_all | solution.py:39
  19.5 3.9 %copy-start.8 = (f32[128]{0:T(128)S(1)}, f32[128]{0:T(128)}, u32[]{:S(2)}) copy-start(f32[128]{0:T(128)} %param.24) | copy-start | bytes 1540
  27.5 58.4 %all-to-all-start.1 = ((bf16[32,256,256]{2,1,0:T(8,128)(2,1)}), bf16[32,256,256]{2,1,0:T(8,128)(2,1)}, u32[]{:S(2)}, u32[]{:S(2)}) async-start(bf16[32,256,256]{2,1,0:T(8,128)(2,1)} %broadcast_in_dim.37), calls=%async_computation.1 | async-start | bytes 8388608 | tf_op jit(solution)/shard_map/all_to_all | solution.py:39
  34.2 2.8 %copy-start.9 = (f32[128]{0:T(128)S(1)}, f32[128]{0:T(128)}, u32[]{:S(2)}) copy-start(f32[128]{0:T(128)} %param.23) | copy-start | bytes 1540
  34.2 123.5 %reduce-scatter.3.cloned.1.call-start = ((), (), s32[]{:S(2)}) async-start(), calls=%async_computation.5 | async-start | bytes 1179648 | tf_op jit(solution)/shard_map/reduce_scatter | solution.py:123
  86.0 11.4 %copy-start.2 = (pred[256,8192]{1,0:T(8,128)(4,1)S(1)}, pred[256,8192]{1,0:T(8,128)(4,1)}, u32[]{:S(2)}) copy-start(pred[256,8192]{1,0:T(8,128)(4,1)} %compare_and_fusion) | copy-start | bytes 6291460
  91.7 5.7 %copy-start.1 = (f32[256,2,8192]{2,0,1:T(8,128)}, f32[256,2,8192]{2,0,1:T(8,128)S(1)}, u32[]{:S(2)}) copy-start(f32[256,2,8192]{2,0,1:T(8,128)S(1)} %get-tuple-element.13) | copy-start | bytes 50331652
  102.7 10.1 %copy-start.6 = (bf16[256,2048]{1,0:T(8,128)(2,1)S(1)}, bf16[256,2048]{1,0:T(8,128)(2,1)}, u32[]{:S(2)}) copy-start(bf16[256,2048]{1,0:T(8,128)(2,1)} %param.25) | copy-start | bytes 3145732
  114.3 78.0 %all-gather.2.cloned.1.call-start = ((), (), s32[]{:S(2)}) async-start(), calls=%async_computation.6 | async-start | bytes 1179648 | tf_op jit(solution)/shard_map/all_gather | solution.py:127
  114.3 79.5 %copy-start.11 = (f32[2048]{0:T(1024)S(1)}, f32[2048]{0:T(1024)}, u32[]{:S(2)}) copy-start(f32[2048]{0:T(1024)} %param.26) | copy-start | bytes 24580
  159.4 76.5 %reduce-scatter.5.cloned.1.call-start = ((), (), s32[]{:S(2)}) async-start(), calls=%async_computation.7 | async-start | bytes 1179648 | tf_op jit(solution)/shard_map/reduce_scatter | solution.py:132
  193.8 2.6 copy-start.5
  196.4 3.9 %copy-start.13 = (s32[64]{0:T(128)S(1)}, s32[64]{0:T(128)}, u32[]{:S(2)}) copy-start(s32[64]{0:T(128)} %param.18) | copy-start | bytes 772
  196.4 39.5 %copy-start.4 = (bf16[256,256]{1,0:T(8,128)(2,1)S(1)}, bf16[256,256]{1,0:T(8,128)(2,1)}, u32[]{:S(2)}) copy-start(bf16[256,256]{1,0:T(8,128)(2,1)} %add_convert_fusion.1) | copy-start | bytes 393220
  238.7 15.0 %all-to-all-start.2 = ((bf16[32,8,256]{2,1,0:T(8,128)(2,1)}), bf16[32,8,256]{2,1,0:T(8,128)(2,1)S(1)}, u32[]{:S(2)}, u32[]{:S(2)}) async-start(bf16[32,8,256]{2,1,0:T(8,128)(2,1)} %bitcast.17), calls=%async_computation.4 | async-start | bytes 262144 | tf_op jit(solution)/shard_map/all_to_all | solution.py:145
Sparse Core Ops, SparseCore 0:
  114.4 43.3 reduce-scatter.2
  160.1 32.0 all-gather.1
  200.4 35.4 reduce-scatter.4

commit v3 on v2

--- a/solution.py
+++ b/solution.py
@@ -37,6 +37,20 @@
 def gather_seq(block, seq_count):
     copies = jnp.broadcast_to(block[None], (seq_count,) + block.shape)
     return lax.all_to_all(copies, "seq", split_axis=0, concat_axis=0, tiled=True)
+
+
+def scatter_sum_tp(terms, tp_count):
+    rows, width = terms.shape
+    split = terms.astype(jnp.bfloat16).reshape(rows, tp_count, width // tp_count).transpose(1, 0, 2)
+    arrived = lax.all_to_all(split, "tp", split_axis=0, concat_axis=0, tiled=True)
+    return jnp.sum(arrived.astype(jnp.float32), axis=0)
+
+
+def gather_tp(block, tp_count):
+    rows, part = block.shape
+    copies = jnp.broadcast_to(block[None], (tp_count,) + block.shape)
+    arrived = lax.all_to_all(copies, "tp", split_axis=0, concat_axis=0, tiled=True)
+    return arrived.transpose(1, 0, 2).reshape(rows, tp_count * part)
 
 
 def build_cache(pieces, piece_tokens, rows, seq_count):
@@ -118,23 +132,13 @@
     terms = jnp.dot(attn, o_weight, preferred_element_type=jnp.float32)
     column = lax.axis_index("tp") * part
     own_input = lax.dynamic_slice_in_dim(xfull, column, part, 1)
-    mid = (
-        own_input
-        + lax.psum_scatter(
-            terms.astype(jnp.bfloat16), "tp", scatter_dimension=1, tiled=True
-        ).astype(jnp.float32)
-    ).astype(jnp.bfloat16)
-    mid_full = lax.all_gather(mid, "tp", axis=1, tiled=True)
+    mid = (own_input + scatter_sum_tp(terms, tp_count)).astype(jnp.bfloat16)
+    mid_full = gather_tp(mid, tp_count)
     normed_mid = rms(mid_full.astype(jnp.float32), norm_mid).astype(jnp.bfloat16)
     gate = jnp.dot(normed_mid, gate_weight, preferred_element_type=jnp.float32)
     upper = jnp.dot(normed_mid, up_weight, preferred_element_type=jnp.float32)
     act = (jax.nn.silu(gate) * upper).astype(jnp.bfloat16)
-    feed = lax.psum_scatter(
-        jnp.dot(act, down_weight, preferred_element_type=jnp.float32).astype(jnp.bfloat16),
-        "tp",
-        scatter_dimension=1,
-        tiled=True,
-    ).astype(jnp.float32)
+    feed = scatter_sum_tp(jnp.dot(act, down_weight, preferred_element_type=jnp.float32), tp_count)
     out = (mid.astype(jnp.float32) + feed).astype(jnp.bfloat16)
     blocks_dev = rows // BLK
     share = BLK // seq_count

time: 264 us -> 243 us (0.920)
  waiting for transfers between devices: 160 us -> 102 us
  blocking collectives: 0 us -> 28.2 us
  starting transfers between devices: 23.9 us -> 47.4 us
  between operations: 14.2 us -> 1.03 us
  local copies, waits for them, and re-layouts: 17.5 us -> 21.8 us
  matrix products: 29.1 us -> 26.2 us
    reduce_scatter x2 -> x0, waiting for transfers between devices: 76 us -> none  [the longest x1 41.8 us: body(): lax.psum_scatter(terms.astype(jnp.bfloat16), 'tp', scatter_dimension=1, t...]
    all_to_all x0 -> x2, waiting for transfers between devices: none -> 49.8 us  [scatter_sum_tp(): lax.all_to_all(split, 'tp', split_axis=0, concat_axis=0, tiled=True)]
    all_gather x1 -> x0, waiting for transfers between devices: 32.5 us -> none  [body(): mid_full = lax.all_gather(mid, 'tp', axis=1, tiled=True)]
    all_to_all x0 -> x1, blocking collectives: none -> 28.2 us  [gather_tp(): lax.all_to_all(copies, 'tp', split_axis=0, concat_axis=0, tiled=True)]
    all_to_all x0 -> x2, starting transfers between devices: none -> 19.7 us  [scatter_sum_tp(): lax.all_to_all(split, 'tp', split_axis=0, concat_axis=0, tiled=True)]
    all_to_all x1, starting transfers between devices: 7.46 us -> 11.6 us  [body(): lax.all_to_all(out[send_rows], 'seq', split_axis=0, concat_axis=0, tiled=...]
    reshape x0 -> x2, local copies, waits for them, and re-layouts: none -> 3.39 us  [scatter_sum_tp(): terms.astype(jnp.bfloat16).reshape(rows, tp_count, width // tp_count)]
    unnamed x28 -> x26, local copies, waits for them, and re-layouts: 5.77 us -> 6.5 us
  transfers between devices with their start and end apart: 6 -> 5, of which waited for: 6 -> 5; matrix products, arithmetic and copies ran while one was open for 7% -> 7% of each run, Pallas kernels for 0% -> 0%
where the time goes in v3:
time: 243 us
  waiting for transfers between devices  102 us (42%)
  starting transfers between devices  47.4 us (20%)
  blocking collectives  28.2 us (12%)
  matrix products  26.2 us (11%)
  local copies, waits for them, and re-layouts  21.8 us (9%)
  other arithmetic  16.3 us (7%)
    all_to_all x2, waiting for transfers between devices, scatter_sum_tp(): lax.all_to_all(split, 'tp', split_axis=0, concat_axis=0, tiled=True)  49.8 us
    all_to_all x2, waiting for transfers between devices, gather_seq(): lax.all_to_all(copies, 'seq', split_axis=0, concat_axis=0, tiled=True)  47 us
    all_to_all x1, blocking collectives, gather_tp(): lax.all_to_all(copies, 'tp', split_axis=0, concat_axis=0, tiled=True)  28.2 us
    all_to_all x2, starting transfers between devices, scatter_sum_tp(): lax.all_to_all(split, 'tp', split_axis=0, concat_axis=0, tiled=True)  19.7 us
    all_to_all x2, starting transfers between devices, gather_seq(): lax.all_to_all(copies, 'seq', split_axis=0, concat_axis=0, tiled=True)  16.1 us
    all_to_all x1, starting transfers between devices, body(): lax.all_to_all(out[send_rows], 'seq', split_axis=0, concat_axis=0, tiled=...  11.6 us
    dot_general x1, matrix products, body(): jnp.dot(weights.astype(jnp.bfloat16).reshape(rows * group, seq_count * ro...  10.1 us
    unnamed x26, local copies, waits for them, and re-layouts  6.5 us
  transfers between devices with their start and end apart: 5, of which 5 were waited for; matrix products, arithmetic and copies ran while one was open for 7% of the time, Pallas kernels for 0%

profile of v3, /device:TPU:1, one launch (start us, length us, event | category | flops | bytes accessed | tf_op | source)
XLA Modules:
  0.0 242.7 jit_solution(17201778118562601483)
XLA Ops:
  0.6 0.0 copy-start
  0.7 0.0 copy-start.3
  0.7 0.0 copy-start.10
  0.7 1.5 broadcast_in_dim.34
  2.2 9.2 %all-to-all-start = ((s32[32,1,256]{2,1,0:T(1,128)}), s32[32,1,256]{2,1,0:T(1,128)S(1)}, u32[]{:S(2)}, u32[]{:S(2)}) async-start(s32[32,1,256]{2,1,0:T(1,128)} %broadcast_in_dim.34), calls=%async_computation | async-start | bytes 65536 | tf_op jit(solution)/shard_map/all_to_all | solution.py:39
  11.4 1.5 multiply_reduce_fusion.1
  12.9 2.0 multiply_reduce_fusion.3
  14.9 0.2 reduce-window.9
  15.1 0.1 select_reduce_fusion
  15.2 1.6 fusion.10
  16.9 0.1 multiply_bitcast_fusion
  17.0 0.3 fusion.42
  17.3 0.1 copy.38
  17.4 1.2 all-to-all-done
  18.6 2.4 broadcast_in_dim.43
  21.0 6.9 %all-to-all-start.1 = ((bf16[32,256,256]{2,1,0:T(8,128)(2,1)}), bf16[32,256,256]{2,1,0:T(8,128)(2,1)}, u32[]{:S(2)}, u32[]{:S(2)}) async-start(bf16[32,256,256]{2,1,0:T(8,128)(2,1)} %broadcast_in_dim.43), calls=%async_computation.1 | async-start | bytes 8388608 | tf_op jit(solution)/shard_map/all_to_all | solution.py:39
  27.9 0.0 copy-start.9
  27.9 1.9 multiply_reduce_fusion.2
  29.8 0.1 copy.37
  29.9 0.5 multiply_cosine_fusion
  30.5 0.1 multiply_multiply_fusion
  30.6 0.2 subtract_convert_fusion
  30.8 2.9 %compare_and_fusion = pred[256,8192]{1,0:T(8,128)(4,1)} fusion(s32[8192]{0:T(1024)S(1)} %bitcast.81, s32[256]{0:T(256)S(1)} %copy-done.6, s32[256]{0:T(256)S(1)} %select_reduce_fusion), kind=kLoop, calls=%fused_computation.11 | loop fusion | flops 6291456 | bytes 2131968 | tf_op jit(solution)/shard_map/and | solution.py:111
  33.6 45.8 %all-to-all-done.1 = bf16[32,256,256]{2,1,0:T(8,128)(2,1)} async-done(((bf16[32,256,256]{2,1,0:T(8,128)(2,1)}), bf16[32,256,256]{2,1,0:T(8,128)(2,1)}, u32[]{:S(2)}, u32[]{:S(2)}) %all-to-all-start.1) | async-done | bytes 4194336 | tf_op jit(solution)/shard_map/all_to_all | solution.py:39
  79.4 5.7 %fusion = (f32[256,2]{0,1:T(2,128)S(1)}, f32[256,2,8192]{2,0,1:T(8,128)S(1)}) fusion(pred[256,8192]{1,0:T(8,128)(4,1)} %compare_and_fusion, bf16[8192,256]{1,0:T(8,128)(2,1)} %bitcast.12, bf16[256,2,64]{2,0,1:T(8,128)(2,1)S(1)} %get-tuple-element.3, bf16[256,2,64]{2,0,1:T(8,128)(2,1)S(1)} %get-tuple-element.2), kind=kOutput, calls=%fused_computation.6 | convolution fusion | flops 1086586368 | bytes 21104640 | tf_op jit(solution)/shard_map/dot_general | solution.py:118
  85.2 5.7 %copy-done.1 = f32[256,2,8192]{2,0,1:T(8,128)} copy-done((f32[256,2,8192]{2,0,1:T(8,128)}, f32[256,2,8192]{2,0,1:T(8,128)S(1)}, u32[]{:S(2)}) %copy-start.1) | copy-done | bytes 16777240
  90.9 5.3 %fusion.1 = f32[256,2]{0,1:T(2,128)S(1)} fusion(f32[256,2,8192]{2,0,1:T(8,128)S(1)} %get-tuple-element.13, f32[256,2]{0,1:T(2,128)S(1)} %broadcast_maximum_fusion, pred[256,8192]{1,0:T(8,128)(4,1)S(1)} %copy-done.2), kind=kLoop, calls=%fused_computation.7 | loop fusion | flops 20971008 | bytes 18878464 | tf_op jit(solution)/shard_map/reduce_sum | solution.py:124
  96.2 10.1 %fusion.14 = bf16[256,2,128]{0,2,1:T(8,128)(2,1)S(1)} fusion(bf16[8192,256]{1,0:T(8,128)(2,1)} %bitcast.12, f32[256,2,8192]{2,0,1:T(8,128)} %copy-done.1, f32[256,2]{0,1:T(2,128)S(1)} %broadcast_maximum_fusion, pred[256,8192]{1,0:T(8,128)(4,1)S(1)} %copy-done.2, f32[256,2]{0,1:T(2,128)S(1)} %fusion.1), kind=kOutput, calls=%fused_computation.30 | convolution fusion | flops 1094844416 | bytes 21106688 | tf_op jit(solution)/shard_map/dot_general | solution.py:125
  106.2 0.5 convolution_convert_fusion.1
  106.7 1.1 copy.50
  107.8 10.3 %all-to-all-start.2 = ((bf16[8,256,256]{2,1,0:T(8,128)(2,1)}), bf16[8,256,256]{2,1,0:T(8,128)(2,1)}, u32[]{:S(2)}, u32[]{:S(2)}) async-start(bf16[8,256,256]{2,1,0:T(8,128)(2,1)} %bitcast.76), calls=%async_computation.2 | async-start | bytes 2097152 | tf_op jit(solution)/shard_map/all_to_all | solution.py:45
  118.0 1.6 convert_element_type.73
  119.6 24.9 %all-to-all-done.2 = bf16[8,256,256]{2,1,0:T(8,128)(2,1)} async-done(((bf16[8,256,256]{2,1,0:T(8,128)(2,1)}), bf16[8,256,256]{2,1,0:T(8,128)(2,1)}, u32[]{:S(2)}, u32[]{:S(2)}) %all-to-all-start.2) | async-done | bytes 1048608 | tf_op jit(solution)/shard_map/all_to_all | solution.py:45
  144.5 1.4 convert_reduce_fusion.1
  145.8 1.0 add_convert_fusion.1
  146.8 0.1 copy.41
  146.9 0.0 copy-start.7
  147.0 0.1 broadcast_in_dim.46
  147.0 28.2 %all_to_all.41 = bf16[8,256,256]{1,2,0:T(8,128)(2,1)S(1)} all-to-all(bf16[8,256,256]{1,2,0:T(8,128)(2,1)S(1)} %broadcast_in_dim.46), channel_id=1, replica_groups=mesh['seq'=32,'tp'=8] {'tp'}, dimensions={0} | all-to-all | bytes 2097152 | tf_op jit(solution)/shard_map/all_to_all | solution.py:52
  175.3 0.3 multiply_reduce_fusion
  175.6 0.3 fusion.8
  175.9 0.7 copy-done.4
  176.7 0.7 fusion.52
  177.4 3.8 %convolution_convert_fusion = bf16[256,2048]{1,0:T(8,128)(2,1)} fusion(bf16[384,2048]{1,0:T(8,128)(2,1)S(1)} %copy-done, bf16[256,2048]{0,1:T(8,128)(2,1)S(1)} %fusion.8, bf16[2048,384]{1,0:T(8,128)(2,1)} %param.28, f32[256,384]{1,0:T(8,128)S(1)} %fusion.52), kind=kOutput, calls=%fused_computation.12 | convolution fusion | flops 806420480 | bytes 5636096 | tf_op jit(solution)/shard_map/dot_general | solution.py:141
  181.2 2.3 copy.49
  183.6 9.5 %all-to-all-start.4 = ((bf16[8,256,256]{2,1,0:T(8,128)(2,1)}), bf16[8,256,256]{2,1,0:T(8,128)(2,1)S(1)}, u32[]{:S(2)}, u32[]{:S(2)}) async-start(bf16[8,256,256]{2,1,0:T(8,128)(2,1)} %bitcast.75), calls=%async_computation.4 | async-start | bytes 2097152 | tf_op jit(solution)/shard_map/all_to_all | solution.py:45
  193.0 0.1 mul.217
  193.1 0.1 iota_add_fusion
  193.2 0.1 add.180
  193.4 0.1 add.165
  193.5 0.1 compare_select_fusion.5
  193.6 0.1 copy.35
  193.7 0.6 gather_fusion
  194.3 0.1 copy.36
  194.3 0.1 sub.44
  194.4 25.0 %all-to-all-done.4 = bf16[8,256,256]{2,1,0:T(8,128)(2,1)S(1)} async-done(((bf16[8,256,256]{2,1,0:T(8,128)(2,1)}), bf16[8,256,256]{2,1,0:T(8,128)(2,1)S(1)}, u32[]{:S(2)}, u32[]{:S(2)}) %all-to-all-start.4) | async-done | bytes 1048608 | tf_op jit(solution)/shard_map/all_to_all | solution.py:45
  219.4 0.1 convert_reduce_fusion
  219.6 1.8 gather_fusion.1
  221.4 11.6 %all-to-all-start.5 = ((bf16[32,8,256]{2,1,0:T(8,128)(2,1)}), bf16[32,8,256]{2,1,0:T(8,128)(2,1)S(1)}, u32[]{:S(2)}, u32[]{:S(2)}) async-start(bf16[32,8,256]{2,1,0:T(8,128)(2,1)} %bitcast.21), calls=%async_computation.5 | async-start | bytes 262144 | tf_op jit(solution)/shard_map/all_to_all | solution.py:149
  233.0 0.1 dynamic-slice_reduce_fusion
  233.2 0.1 reshape.524
  233.3 2.4 %scatter_custom_fusion.1 = bf16[256,256]{1,0:T(8,128)(2,1)} fusion(s32[256]{0:T(256)S(1)} %bitcast.87, bf16[32,256,256]{2,1,0:T(8,128)(2,1)} %all-to-all-done.1, s32[]{:T(128)} %constant.81.clone.1, s32[]{:T(128)S(6)} %select_n.89, bf16[]{:T(256)} %constant.76.clone.1), kind=kCustom, calls=%fused_computation.51 | custom fusion | bytes 263172 | tf_op jit(solution)/shard_map/scatter | solution.py:64
  235.7 4.9 %all-to-all-done.5 = bf16[32,8,256]{2,1,0:T(8,128)(2,1)S(1)} async-done(((bf16[32,8,256]{2,1,0:T(8,128)(2,1)}), bf16[32,8,256]{2,1,0:T(8,128)(2,1)S(1)}, u32[]{:S(2)}, u32[]{:S(2)}) %all-to-all-start.5) | async-done | bytes 131104 | tf_op jit(solution)/shard_map/all_to_all | solution.py:149
  240.7 2.1 scatter_custom_fusion
  (36 shorter events, 0.2 us)
Async XLA Ops:
  0.6 176.8 %copy-start = (bf16[384,2048]{1,0:T(8,128)(2,1)S(1)}, bf16[384,2048]{1,0:T(8,128)(2,1)}, u32[]{:S(2)}) copy-start(bf16[384,2048]{1,0:T(8,128)(2,1)} %param.29) | copy-start | bytes 4718596
  0.6 14.5 %copy-start.6 = (s32[256]{0:T(256)S(1)}, s32[256]{0:T(256)}, u32[]{:S(2)}) copy-start(s32[256]{0:T(256)} %param.16) | copy-start | bytes 3076
  0.7 14.6 %copy-start.3 = (bf16[256,2048]{1,0:T(8,128)(2,1)S(1)}, bf16[256,2048]{1,0:T(8,128)(2,1)}, u32[]{:S(2)}) copy-start(bf16[256,2048]{1,0:T(8,128)(2,1)} %param.15) | copy-start | bytes 3145732
  0.7 14.6 %copy-start.10 = (f32[2048]{0:T(1024)S(1)}, f32[2048]{0:T(1024)}, u32[]{:S(2)}) copy-start(f32[2048]{0:T(1024)} %param.19) | copy-start | bytes 24580
  0.7 14.2 %copy-start.11 = (s32[8]{0:T(128)S(1)}, s32[8]{0:T(128)}, u32[]{:S(2)}) copy-start(s32[8]{0:T(128)} %param.17) | copy-start | bytes 100
  2.2 16.4 %all-to-all-start = ((s32[32,1,256]{2,1,0:T(1,128)}), s32[32,1,256]{2,1,0:T(1,128)S(1)}, u32[]{:S(2)}, u32[]{:S(2)}) async-start(s32[32,1,256]{2,1,0:T(1,128)} %broadcast_in_dim.34), calls=%async_computation | async-start | bytes 65536 | tf_op jit(solution)/shard_map/all_to_all | solution.py:39
  12.9 3.9 %copy-start.8 = (f32[128]{0:T(128)S(1)}, f32[128]{0:T(128)}, u32[]{:S(2)}) copy-start(f32[128]{0:T(128)} %param.24) | copy-start | bytes 1540
  21.0 58.4 %all-to-all-start.1 = ((bf16[32,256,256]{2,1,0:T(8,128)(2,1)}), bf16[32,256,256]{2,1,0:T(8,128)(2,1)}, u32[]{:S(2)}, u32[]{:S(2)}) async-start(bf16[32,256,256]{2,1,0:T(8,128)(2,1)} %broadcast_in_dim.43), calls=%async_computation.1 | async-start | bytes 8388608 | tf_op jit(solution)/shard_map/all_to_all | solution.py:39
  27.9 2.6 %copy-start.9 = (f32[128]{0:T(128)S(1)}, f32[128]{0:T(128)}, u32[]{:S(2)}) copy-start(f32[128]{0:T(128)} %param.23) | copy-start | bytes 1540
  79.4 11.4 %copy-start.2 = (pred[256,8192]{1,0:T(8,128)(4,1)S(1)}, pred[256,8192]{1,0:T(8,128)(4,1)}, u32[]{:S(2)}) copy-start(pred[256,8192]{1,0:T(8,128)(4,1)} %compare_and_fusion) | copy-start | bytes 6291460
  85.1 5.7 %copy-start.1 = (f32[256,2,8192]{2,0,1:T(8,128)}, f32[256,2,8192]{2,0,1:T(8,128)S(1)}, u32[]{:S(2)}) copy-start(f32[256,2,8192]{2,0,1:T(8,128)S(1)} %get-tuple-element.13) | copy-start | bytes 50331652
  96.1 10.1 %copy-start.5 = (bf16[256,2048]{1,0:T(8,128)(2,1)S(1)}, bf16[256,2048]{1,0:T(8,128)(2,1)}, u32[]{:S(2)}) copy-start(bf16[256,2048]{1,0:T(8,128)(2,1)} %param.25) | copy-start | bytes 3145732
  107.8 36.7 %all-to-all-start.2 = ((bf16[8,256,256]{2,1,0:T(8,128)(2,1)}), bf16[8,256,256]{2,1,0:T(8,128)(2,1)}, u32[]{:S(2)}, u32[]{:S(2)}) async-start(bf16[8,256,256]{2,1,0:T(8,128)(2,1)} %bitcast.76), calls=%async_computation.2 | async-start | bytes 2097152 | tf_op jit(solution)/shard_map/all_to_all | solution.py:45
  146.9 28.6 %copy-start.7 = (f32[2048]{0:T(1024)S(1)}, f32[2048]{0:T(1024)}, u32[]{:S(2)}) copy-start(f32[2048]{0:T(1024)} %param.26) | copy-start | bytes 24580
  175.3 1.4 copy-start.4
  181.2 11.8 %copy-start.12 = (s32[64]{0:T(128)S(1)}, s32[64]{0:T(128)}, u32[]{:S(2)}) copy-start(s32[64]{0:T(128)} %param.18) | copy-start | bytes 772
  183.6 35.8 %all-to-all-start.4 = ((bf16[8,256,256]{2,1,0:T(8,128)(2,1)}), bf16[8,256,256]{2,1,0:T(8,128)(2,1)S(1)}, u32[]{:S(2)}, u32[]{:S(2)}) async-start(bf16[8,256,256]{2,1,0:T(8,128)(2,1)} %bitcast.75), calls=%async_computation.4 | async-start | bytes 2097152 | tf_op jit(solution)/shard_map/all_to_all | solution.py:45
  221.4 19.3 %all-to-all-start.5 = ((bf16[32,8,256]{2,1,0:T(8,128)(2,1)}), bf16[32,8,256]{2,1,0:T(8,128)(2,1)S(1)}, u32[]{:S(2)}, u32[]{:S(2)}) async-start(bf16[32,8,256]{2,1,0:T(8,128)(2,1)} %bitcast.21), calls=%async_computation.5 | async-start | bytes 262144 | tf_op jit(solution)/shard_map/all_to_all | solution.py:149

commit v4 on v3

--- a/solution.py
+++ b/solution.py
@@ -39,18 +39,44 @@
     return lax.all_to_all(copies, "seq", split_axis=0, concat_axis=0, tiled=True)
 
 
+def chip_shift(tp_count, shift):
+    chips = tp_count // 2
+    return [(i, ((i // 2 + shift) % chips) * 2 + i % 2) for i in range(tp_count)]
+
+
 def scatter_sum_tp(terms, tp_count):
     rows, width = terms.shape
-    split = terms.astype(jnp.bfloat16).reshape(rows, tp_count, width // tp_count).transpose(1, 0, 2)
-    arrived = lax.all_to_all(split, "tp", split_axis=0, concat_axis=0, tiled=True)
-    return jnp.sum(arrived.astype(jnp.float32), axis=0)
+    chips = tp_count // 2
+    part = width // tp_count
+    index = lax.axis_index("tp")
+    chip, core = index // 2, index % 2
+    blocks = terms.astype(jnp.bfloat16).reshape(rows, chips, 2, part)
+    mine = lax.dynamic_index_in_dim(blocks, core, axis=2, keepdims=False)
+    other = lax.dynamic_index_in_dim(blocks, 1 - core, axis=2, keepdims=False)
+    sibling = lax.ppermute(other, "tp", [(i, i ^ 1) for i in range(tp_count)])
+    chip_sum = mine.astype(jnp.float32) + sibling.astype(jnp.float32)
+    total = lax.dynamic_index_in_dim(chip_sum, chip, axis=1, keepdims=False)
+    outgoing = chip_sum.astype(jnp.bfloat16)
+    for shift in range(1, chips):
+        piece = lax.dynamic_index_in_dim(outgoing, (chip + shift) % chips, axis=1, keepdims=False)
+        total = total + lax.ppermute(piece, "tp", chip_shift(tp_count, shift)).astype(jnp.float32)
+    return total
 
 
 def gather_tp(block, tp_count):
     rows, part = block.shape
-    copies = jnp.broadcast_to(block[None], (tp_count,) + block.shape)
-    arrived = lax.all_to_all(copies, "tp", split_axis=0, concat_axis=0, tiled=True)
-    return arrived.transpose(1, 0, 2).reshape(rows, tp_count * part)
+    chips = tp_count // 2
+    index = lax.axis_index("tp")
+    chip, core = index // 2, index % 2
+    arrived = [block] + [
+        lax.ppermute(block, "tp", chip_shift(tp_count, shift)) for shift in range(1, chips)
+    ]
+    by_shift = jnp.stack(arrived, axis=0)
+    order = (chip - jnp.arange(chips, dtype=jnp.int32)) % chips
+    own_core = jnp.take(by_shift, order, axis=0)
+    other_core = lax.ppermute(own_core, "tp", [(i, i ^ 1) for i in range(tp_count)])
+    both = jnp.where(core == 0, jnp.stack([own_core, other_core]), jnp.stack([other_core, own_core]))
+    return both.transpose(2, 1, 0, 3).reshape(rows, tp_count * part)
 
 
 def build_cache(pieces, piece_tokens, rows, seq_count):

time: 243 us -> 223 us (0.918)
  blocking collectives: 28.2 us -> 0 us
  waiting for transfers between devices: 102 us -> 80.2 us
  starting transfers between devices: 47.4 us -> 57.3 us
  local copies, waits for them, and re-layouts: 21.8 us -> 31.4 us
  other arithmetic: 16.3 us -> 25.2 us
    all_to_all x2 -> x0, waiting for transfers between devices: 49.8 us -> none  [scatter_sum_tp(): lax.all_to_all(split, 'tp', split_axis=0, concat_axis=0, tiled=True)]
    ppermute x0 -> x12, waiting for transfers between devices: none -> 28.4 us  [the longest x6 17.8 us: scatter_sum_tp(): lax.ppermute(piece, 'tp', chip_shift(tp_count, shift)).astype(jnp.float32)]
    ppermute x0 -> x12, starting transfers between devices: none -> 28.3 us  [the longest x6 15.9 us: scatter_sum_tp(): lax.ppermute(piece, 'tp', chip_shift(tp_count, shift)).astype(jnp.float32)]
    all_to_all x1 -> x0, blocking collectives: 28.2 us -> none  [gather_tp(): lax.all_to_all(copies, 'tp', split_axis=0, concat_axis=0, tiled=True)]
    all_to_all x2 -> x0, starting transfers between devices: 19.7 us -> none  [scatter_sum_tp(): lax.all_to_all(split, 'tp', split_axis=0, concat_axis=0, tiled=True)]
    dynamic_slice x0 -> x2, local copies, waits for them, and re-layouts: none -> 6.3 us  [scatter_sum_tp(): mine = lax.dynamic_index_in_dim(blocks, core, axis=2, keepdims=False)]
    convert_element_type x0 -> x3, other arithmetic: none -> 6.07 us  [the longest x2 4.5 us: scatter_sum_tp(): outgoing = chip_sum.astype(jnp.bfloat16)]
    convert_element_type x1, local copies, waits for them, and re-layouts: 0.1 us -> 2.92 us  [body(): mid_full.astype(jnp.float32)]
  transfers between devices with their start and end apart: 5 -> 15, of which waited for: 5 -> 13; matrix products, arithmetic and copies ran while one was open for 7% -> 8% of each run, Pallas kernels for 0% -> 0%
where the time goes in v4:
time: 223 us; the launch traced here: 222 us
  waiting for transfers between devices  80.2 us (36%)
  starting transfers between devices  57.3 us (26%)
  local copies, waits for them, and re-layouts  31.4 us (14%)
  matrix products  27.2 us (12%)
  other arithmetic  25.2 us (11%)
    all_to_all x2, waiting for transfers between devices, gather_seq(): lax.all_to_all(copies, 'seq', split_axis=0, concat_axis=0, tiled=True)  46.9 us
    ppermute x6, waiting for transfers between devices, scatter_sum_tp(): lax.ppermute(piece, 'tp', chip_shift(tp_count, shift)).astype(jnp.float32)  17.8 us
    all_to_all x2, starting transfers between devices, gather_seq(): lax.all_to_all(copies, 'seq', split_axis=0, concat_axis=0, tiled=True)  16.1 us
    ppermute x6, starting transfers between devices, scatter_sum_tp(): lax.ppermute(piece, 'tp', chip_shift(tp_count, shift)).astype(jnp.float32)  15.9 us
    all_to_all x1, starting transfers between devices, body(): lax.all_to_all(out[send_rows], 'seq', split_axis=0, concat_axis=0, tiled=...  12.9 us
    dot_general x1, matrix products, body(): jnp.dot(weights.astype(jnp.bfloat16).reshape(rows * group, seq_count * ro...  10.1 us
    ppermute x3, starting transfers between devices, gather_tp(): lax.ppermute(block, 'tp', chip_shift(tp_count, shift))  8.07 us
    ppermute x3, waiting for transfers between devices, gather_tp(): lax.ppermute(block, 'tp', chip_shift(tp_count, shift))  7.04 us
  transfers between devices with their start and end apart: 15, of which 13 were waited for; matrix products, arithmetic and copies ran while one was open for 8% of the time, Pallas kernels for 0%

profile of v4, /device:TPU:1, one launch (start us, length us, event | category | flops | bytes accessed | tf_op | source)
XLA Modules:
  0.0 222.4 jit_solution(11497123093236259151)
XLA Ops:
  0.7 1.5 broadcast_in_dim.47
  2.2 9.2 %all-to-all-start = ((s32[32,1,256]{2,1,0:T(1,128)}), s32[32,1,256]{2,1,0:T(1,128)S(1)}, u32[]{:S(2)}, u32[]{:S(2)}) async-start(s32[32,1,256]{2,1,0:T(1,128)} %broadcast_in_dim.47), calls=%async_computation | async-start | bytes 65536 | tf_op jit(solution)/shard_map/all_to_all | solution.py:39
  11.4 1.5 multiply_reduce_fusion
  12.9 2.0 multiply_reduce_fusion.2
  14.9 0.2 reduce-window.9
  15.2 1.6 fusion.11
  17.0 0.3 fusion.51
  17.4 1.2 all-to-all-done
  18.6 2.4 %broadcast_in_dim.55 = bf16[32,256,256]{2,1,0:T(8,128)(2,1)} broadcast(bf16[256,256]{1,0:T(8,128)(2,1)S(1)} %copy.44), dimensions={1,2} | broadcast | bytes 4325376 | tf_op jit(solution)/shard_map/broadcast_in_dim | solution.py:38
  21.0 6.9 %all-to-all-start.1 = ((bf16[32,256,256]{2,1,0:T(8,128)(2,1)}), bf16[32,256,256]{2,1,0:T(8,128)(2,1)}, u32[]{:S(2)}, u32[]{:S(2)}) async-start(bf16[32,256,256]{2,1,0:T(8,128)(2,1)} %broadcast_in_dim.55), calls=%async_computation.1 | async-start | bytes 8388608 | tf_op jit(solution)/shard_map/all_to_all | solution.py:39
  27.9 1.9 multiply_reduce_fusion.1
  30.0 0.5 multiply_cosine_fusion
  30.8 2.9 %compare_and_fusion = pred[256,8192]{1,0:T(8,128)(4,1)} fusion(s32[8192]{0:T(1024)S(1)} %bitcast.127, s32[256]{0:T(256)S(1)} %copy-done.8, s32[256]{0:T(256)S(1)} %select_reduce_fusion), kind=kLoop, calls=%fused_computation.12 | loop fusion | flops 6291456 | bytes 2131968 | tf_op jit(solution)/shard_map/and | solution.py:137
  33.7 45.7 %all-to-all-done.1 = bf16[32,256,256]{2,1,0:T(8,128)(2,1)} async-done(((bf16[32,256,256]{2,1,0:T(8,128)(2,1)}), bf16[32,256,256]{2,1,0:T(8,128)(2,1)}, u32[]{:S(2)}, u32[]{:S(2)}) %all-to-all-start.1) | async-done | bytes 4194336 | tf_op jit(solution)/shard_map/all_to_all | solution.py:39
  79.4 5.7 %fusion = (f32[256,2]{0,1:T(2,128)S(1)}, f32[256,2,8192]{2,0,1:T(8,128)S(1)}) fusion(pred[256,8192]{1,0:T(8,128)(4,1)} %compare_and_fusion, bf16[8192,256]{1,0:T(8,128)(2,1)} %bitcast.12, bf16[256,2,64]{2,0,1:T(8,128)(2,1)S(1)} %get-tuple-element.17, bf16[256,2,64]{2,0,1:T(8,128)(2,1)S(1)} %get-tuple-element.16), kind=kOutput, calls=%fused_computation.7 | convolution fusion | flops 1086586368 | bytes 21104640 | tf_op jit(solution)/shard_map/dot_general | solution.py:144
  85.2 5.7 %copy-done.1 = f32[256,2,8192]{2,0,1:T(8,128)} copy-done((f32[256,2,8192]{2,0,1:T(8,128)}, f32[256,2,8192]{2,0,1:T(8,128)S(1)}, u32[]{:S(2)}) %copy-start.1) | copy-done | bytes 16777240
  90.9 5.3 %fusion.1 = f32[256,2]{0,1:T(2,128)S(1)} fusion(f32[256,2,8192]{2,0,1:T(8,128)S(1)} %get-tuple-element.27, f32[256,2]{0,1:T(2,128)S(1)} %broadcast_maximum_fusion, pred[256,8192]{1,0:T(8,128)(4,1)S(1)} %copy-done.2), kind=kLoop, calls=%fused_computation.8 | loop fusion | flops 20971008 | bytes 18878464 | tf_op jit(solution)/shard_map/reduce_sum | solution.py:150
  96.2 10.1 %fusion.15 = bf16[256,2,128]{0,2,1:T(8,128)(2,1)S(1)} fusion(bf16[8192,256]{1,0:T(8,128)(2,1)} %bitcast.12, f32[256,2,8192]{2,0,1:T(8,128)} %copy-done.1, f32[256,2]{0,1:T(2,128)S(1)} %broadcast_maximum_fusion, pred[256,8192]{1,0:T(8,128)(4,1)S(1)} %copy-done.2, f32[256,2]{0,1:T(2,128)S(1)} %fusion.1), kind=kOutput, calls=%fused_computation.31 | convolution fusion | flops 1094844416 | bytes 21106688 | tf_op jit(solution)/shard_map/dot_general | solution.py:151
  106.3 1.4 convolution_convert_fusion.1
  107.7 1.8 reshape.586
  109.5 3.1 %constant_dynamic-slice_fusion.3 = (bf16[256,4,1,256]{3,2,1,0:T(2,128)(2,1)}, bf16[256,4,1,256]{3,2,1,0:T(2,128)(2,1)S(1)}) fusion(bf16[256,4,2,256]{3,2,1,0:T(2,128)(2,1)S(1)} %reshape.586, s32[]{:T(128)S(6)} %select_n.212, s32[]{:T(128)S(6)} %select_n.213), kind=kLoop, calls=%fused_computation.113 | loop fusion | bytes 2097160 | tf_op jit(solution)/shard_map/jit(dynamic_index_in_dim)/dynamic_slice | solution.py:54
  112.7 0.2 copy.68
  112.9 3.0 %collective-permute-start = (bf16[256,4,256]{2,0,1:T(8,128)(2,1)S(1)}, bf16[256,4,256]{2,0,1:T(8,128)(2,1)}, u32[]{:S(2)}, u32[]{:S(2)}) collective-permute-start(bf16[256,4,256]{2,0,1:T(8,128)(2,1)S(1)} %bitcast.123), channel_id=1, source_target_pairs={{0,1},{1,0},{2,3},{3,2},{4,5},{5,4},{6,7},{7,6},{8,9},{9,8},{10,11... | collective-permute-start | bytes 1572872 | tf_op jit(solution)/shard_map/ppermute | solution.py:56
  115.9 1.7 collective-permute-done
  117.5 2.2 %fusion.65 = (bf16[256,4,256]{2,0,1:T(8,128)(2,1)S(1)}, f32[256,4,256]{2,0,1:T(8,128)}) fusion(bf16[256,4,256]{2,0,1:T(8,128)(2,1)} %collective-permute-done, bf16[256,4,1,256]{3,2,1,0:T(2,128)(2,1)S(1)} %copy-done.3), kind=kLoop, calls=%fused_computation.149 | loop fusion | flops 1048576 | bytes 2621440 | tf_op jit(solution)/shard_map/convert_element_type | solution.py:59
  119.8 3.1 %collective-permute-start.1 = (bf16[256,256]{1,0:T(8,128)(2,1)S(1)}, bf16[256,256]{1,0:T(8,128)(2,1)S(1)}, u32[]{:S(2)}, u32[]{:S(2)}) collective-permute-start(bf16[256,256]{1,0:T(8,128)(2,1)S(1)} %get-tuple-element.13), channel_id=1, source_target_pairs={{0,2},{1,3},{2,4},{3,5},{4,6},{5,7},{6,0},{7,1},{8,10},{9,11},{10,... | collective-permute-start | bytes 393224 | tf_op jit(solution)/shard_map/ppermute | solution.py:62
  122.9 4.2 %collective-permute-start.2 = (bf16[256,256]{1,0:T(8,128)(2,1)S(1)}, bf16[256,256]{1,0:T(8,128)(2,1)S(1)}, u32[]{:S(2)}, u32[]{:S(2)}) collective-permute-start(bf16[256,256]{1,0:T(8,128)(2,1)S(1)} %get-tuple-element.15), channel_id=1, source_target_pairs={{0,4},{1,5},{2,6},{3,7},{4,0},{5,1},{6,2},{7,3},{8,12},{9,13},{10,... | collective-permute-start | bytes 393224 | tf_op jit(solution)/shard_map/ppermute | solution.py:62
  127.1 2.4 %collective-permute-start.3 = (bf16[256,256]{1,0:T(8,128)(2,1)S(1)}, bf16[256,256]{1,0:T(8,128)(2,1)S(1)}, u32[]{:S(2)}, u32[]{:S(2)}) collective-permute-start(bf16[256,256]{1,0:T(8,128)(2,1)S(1)} %get-tuple-element.14), channel_id=1, source_target_pairs={{0,6},{1,7},{2,0},{3,1},{4,2},{5,3},{6,4},{7,5},{8,14},{9,15},{10,... | collective-permute-start | bytes 393224 | tf_op jit(solution)/shard_map/ppermute | solution.py:62
  129.5 2.8 %convert_element_type.109 = f32[256,2048]{1,0:T(8,128)} convert(bf16[256,2048]{1,0:T(8,128)(2,1)} %param.15) | non-fusion elementwise | flops 524288 | bytes 3145728 | tf_op jit(solution)/shard_map/convert_element_type | solution.py:118
  132.3 3.7 %collective-permute-done.2 = bf16[256,256]{1,0:T(8,128)(2,1)S(1)} collective-permute-done((bf16[256,256]{1,0:T(8,128)(2,1)S(1)}, bf16[256,256]{1,0:T(8,128)(2,1)S(1)}, u32[]{:S(2)}, u32[]{:S(2)}) %collective-permute-start.2) | collective-permute-done | bytes 131104 | tf_op jit(solution)/shard_map/ppermute | solution.py:62
  136.1 3.2 %collective-permute-done.3 = bf16[256,256]{1,0:T(8,128)(2,1)S(1)} collective-permute-done((bf16[256,256]{1,0:T(8,128)(2,1)S(1)}, bf16[256,256]{1,0:T(8,128)(2,1)S(1)}, u32[]{:S(2)}, u32[]{:S(2)}) %collective-permute-start.3) | collective-permute-done | bytes 131104 | tf_op jit(solution)/shard_map/ppermute | solution.py:62
  139.3 1.1 fusion.30
  140.4 1.5 collective-permute-start.4
  141.9 4.0 %collective-permute-start.5 = (bf16[256,256]{1,0:T(8,128)(2,1)S(1)}, bf16[256,256]{1,0:T(8,128)(2,1)S(1)}, u32[]{:S(2)}, u32[]{:S(2)}) collective-permute-start(bf16[256,256]{1,0:T(8,128)(2,1)S(1)} %fusion.30), channel_id=1, source_target_pairs={{0,4},{1,5},{2,6},{3,7},{4,0},{5,1},{6,2},{7,3},{8,12},{9,13},{10,... | collective-permute-start | bytes 393224 | tf_op jit(solution)/shard_map/ppermute | solution.py:72
  145.9 2.6 %collective-permute-start.6 = (bf16[256,256]{1,0:T(8,128)(2,1)S(1)}, bf16[256,256]{1,0:T(8,128)(2,1)S(1)}, u32[]{:S(2)}, u32[]{:S(2)}) collective-permute-start(bf16[256,256]{1,0:T(8,128)(2,1)S(1)} %fusion.30), channel_id=1, source_target_pairs={{0,6},{1,7},{2,0},{3,1},{4,2},{5,3},{6,4},{7,5},{8,14},{9,15},{10,... | collective-permute-start | bytes 393224 | tf_op jit(solution)/shard_map/ppermute | solution.py:72
  148.5 0.5 collective-permute-done.4
  149.0 5.3 %collective-permute-done.5 = bf16[256,256]{1,0:T(8,128)(2,1)S(1)} collective-permute-done((bf16[256,256]{1,0:T(8,128)(2,1)S(1)}, bf16[256,256]{1,0:T(8,128)(2,1)S(1)}, u32[]{:S(2)}, u32[]{:S(2)}) %collective-permute-start.5) | collective-permute-done | bytes 131104 | tf_op jit(solution)/shard_map/ppermute | solution.py:72
  154.3 1.2 collective-permute-done.6
  155.6 0.6 gather_fusion.1
  156.3 0.6 collective-permute-start.7
  157.5 1.0 collective-permute-done.7
  158.4 0.4 fusion.6
  158.8 1.6 convert_bitcast_fusion
  160.3 2.9 %copy.48 = f32[256,4,2,256]{0,3,2,1:T(8,128)} copy(f32[256,4,2,256]{3,0,1,2:T(8,128)} %convert_bitcast_fusion) | data formatting | bytes 4194304 | tf_op jit(solution)/shard_map/convert_element_type | solution.py:163
  163.3 2.0 fusion.9
  165.3 0.8 fusion.66
  166.1 3.8 %convolution_convert_fusion = bf16[256,2048]{1,0:T(8,128)(2,1)} fusion(bf16[384,2048]{1,0:T(8,128)(2,1)S(1)} %copy-done, bf16[256,2048]{0,1:T(8,128)(2,1)S(1)} %fusion.9, bf16[2048,384]{1,0:T(8,128)(2,1)} %param.28, f32[256,384]{1,0:T(8,128)S(1)} %fusion.66), kind=kOutput, calls=%fused_computation.15 | convolution fusion | flops 806420480 | bytes 5636096 | tf_op jit(solution)/shard_map/dot_general | solution.py:167
  169.9 1.8 reshape.587
  171.7 3.1 %constant_dynamic-slice_fusion.1 = (bf16[256,4,1,256]{3,2,1,0:T(2,128)(2,1)}, bf16[256,4,1,256]{3,2,1,0:T(2,128)(2,1)S(1)}) fusion(bf16[256,4,2,256]{3,2,1,0:T(2,128)(2,1)S(1)} %reshape.587, s32[]{:T(128)S(6)} %select_n.212, s32[]{:T(128)S(6)} %select_n.213), kind=kLoop, calls=%fused_computation.111 | loop fusion | bytes 2097160 | tf_op jit(solution)/shard_map/jit(dynamic_index_in_dim)/dynamic_slice | solution.py:54
  175.0 0.7 collective-permute-start.8
  175.9 0.6 gather_fusion
  176.5 0.9 collective-permute-done.8
  177.4 2.3 %fusion.64 = (bf16[256,4,256]{2,0,1:T(8,128)(2,1)S(1)}, f32[256,4,256]{2,0,1:T(8,128)}) fusion(bf16[256,4,256]{2,0,1:T(8,128)(2,1)} %collective-permute-done.8, bf16[256,4,1,256]{3,2,1,0:T(2,128)(2,1)S(1)} %copy-done.4), kind=kLoop, calls=%fused_computation.148 | loop fusion | flops 1048576 | bytes 2621440 | tf_op jit(solution)/shard_map/convert_element_type | solution.py:59
  179.7 3.8 %collective-permute-start.10 = (bf16[256,256]{1,0:T(8,128)(2,1)S(1)}, bf16[256,256]{1,0:T(8,128)(2,1)S(1)}, u32[]{:S(2)}, u32[]{:S(2)}) collective-permute-start(bf16[256,256]{1,0:T(8,128)(2,1)S(1)} %get-tuple-element.12), channel_id=1, source_target_pairs={{0,4},{1,5},{2,6},{3,7},{4,0},{5,1},{6,2},{7,3},{8,12},{9,13},{10,... | collective-permute-start | bytes 393224 | tf_op jit(solution)/shard_map/ppermute | solution.py:62
  183.6 1.8 collective-permute-start.11
  185.3 0.6 collective-permute-start.9
  186.1 2.3 %collective-permute-done.10 = bf16[256,256]{1,0:T(8,128)(2,1)S(1)} collective-permute-done((bf16[256,256]{1,0:T(8,128)(2,1)S(1)}, bf16[256,256]{1,0:T(8,128)(2,1)S(1)}, u32[]{:S(2)}, u32[]{:S(2)}) %collective-permute-start.10) | collective-permute-done | bytes 131104 | tf_op jit(solution)/shard_map/ppermute | solution.py:62
  188.4 8.5 %collective-permute-done.11 = bf16[256,256]{1,0:T(8,128)(2,1)S(1)} collective-permute-done((bf16[256,256]{1,0:T(8,128)(2,1)S(1)}, bf16[256,256]{1,0:T(8,128)(2,1)S(1)}, u32[]{:S(2)}, u32[]{:S(2)}) %collective-permute-start.11) | collective-permute-done | bytes 131104 | tf_op jit(solution)/shard_map/ppermute | solution.py:62
  197.0 1.0 fusion.26
  198.0 1.8 gather_fusion.2
  199.8 12.9 %all-to-all-start.2 = ((bf16[32,8,256]{2,1,0:T(8,128)(2,1)}), bf16[32,8,256]{2,1,0:T(8,128)(2,1)S(1)}, u32[]{:S(2)}, u32[]{:S(2)}) async-start(bf16[32,8,256]{2,1,0:T(8,128)(2,1)} %bitcast.38), calls=%async_computation.2 | async-start | bytes 262144 | tf_op jit(solution)/shard_map/all_to_all | solution.py:175
  213.0 2.4 %scatter_custom_fusion.1 = bf16[256,256]{1,0:T(8,128)(2,1)} fusion(s32[256]{0:T(256)S(1)} %bitcast.136, bf16[32,256,256]{2,1,0:T(8,128)(2,1)} %all-to-all-done.1, s32[]{:T(128)} %constant.185.clone.1, s32[]{:T(128)S(6)} %select_n.204, bf16[]{:T(256)} %constant.180.clone.1), kind=kCustom, calls=%fused_computation.68 | custom fusion | bytes 263172 | tf_op jit(solution)/shard_map/scatter | solution.py:90
  215.4 4.9 %all-to-all-done.2 = bf16[32,8,256]{2,1,0:T(8,128)(2,1)S(1)} async-done(((bf16[32,8,256]{2,1,0:T(8,128)(2,1)}), bf16[32,8,256]{2,1,0:T(8,128)(2,1)S(1)}, u32[]{:S(2)}, u32[]{:S(2)}) %all-to-all-start.2) | async-done | bytes 131104 | tf_op jit(solution)/shard_map/all_to_all | solution.py:175
  220.3 2.1 scatter_custom_fusion
  (72 shorter events, 2.4 us)
Async XLA Ops:
  0.6 165.5 %copy-start = (bf16[384,2048]{1,0:T(8,128)(2,1)S(1)}, bf16[384,2048]{1,0:T(8,128)(2,1)}, u32[]{:S(2)}) copy-start(bf16[384,2048]{1,0:T(8,128)(2,1)} %param.29) | copy-start | bytes 4718596
  0.6 14.5 %copy-start.8 = (s32[256]{0:T(256)S(1)}, s32[256]{0:T(256)}, u32[]{:S(2)}) copy-start(s32[256]{0:T(256)} %param.16) | copy-start | bytes 3076
  0.7 14.6 %copy-start.5 = (bf16[256,2048]{1,0:T(8,128)(2,1)S(1)}, bf16[256,2048]{1,0:T(8,128)(2,1)}, u32[]{:S(2)}) copy-start(bf16[256,2048]{1,0:T(8,128)(2,1)} %param.15) | copy-start | bytes 3145732
  0.7 14.6 %copy-start.12 = (f32[2048]{0:T(1024)S(1)}, f32[2048]{0:T(1024)}, u32[]{:S(2)}) copy-start(f32[2048]{0:T(1024)} %param.19) | copy-start | bytes 24580
  0.7 14.2 %copy-start.13 = (s32[8]{0:T(128)S(1)}, s32[8]{0:T(128)}, u32[]{:S(2)}) copy-start(s32[8]{0:T(128)} %param.17) | copy-start | bytes 100
  2.2 16.4 %all-to-all-start = ((s32[32,1,256]{2,1,0:T(1,128)}), s32[32,1,256]{2,1,0:T(1,128)S(1)}, u32[]{:S(2)}, u32[]{:S(2)}) async-start(s32[32,1,256]{2,1,0:T(1,128)} %broadcast_in_dim.47), calls=%async_computation | async-start | bytes 65536 | tf_op jit(solution)/shard_map/all_to_all | solution.py:39
  12.9 3.9 %copy-start.10 = (f32[128]{0:T(128)S(1)}, f32[128]{0:T(128)}, u32[]{:S(2)}) copy-start(f32[128]{0:T(128)} %param.24) | copy-start | bytes 1540
  21.0 58.4 %all-to-all-start.1 = ((bf16[32,256,256]{2,1,0:T(8,128)(2,1)}), bf16[32,256,256]{2,1,0:T(8,128)(2,1)}, u32[]{:S(2)}, u32[]{:S(2)}) async-start(bf16[32,256,256]{2,1,0:T(8,128)(2,1)} %broadcast_in_dim.55), calls=%async_computation.1 | async-start | bytes 8388608 | tf_op jit(solution)/shard_map/all_to_all | solution.py:39
  27.9 2.6 %copy-start.11 = (f32[128]{0:T(128)S(1)}, f32[128]{0:T(128)}, u32[]{:S(2)}) copy-start(f32[128]{0:T(128)} %param.23) | copy-start | bytes 1540
  79.4 11.4 %copy-start.2 = (pred[256,8192]{1,0:T(8,128)(4,1)S(1)}, pred[256,8192]{1,0:T(8,128)(4,1)}, u32[]{:S(2)}) copy-start(pred[256,8192]{1,0:T(8,128)(4,1)} %compare_and_fusion) | copy-start | bytes 6291460
  85.1 5.7 %copy-start.1 = (f32[256,2,8192]{2,0,1:T(8,128)}, f32[256,2,8192]{2,0,1:T(8,128)S(1)}, u32[]{:S(2)}) copy-start(f32[256,2,8192]{2,0,1:T(8,128)S(1)} %get-tuple-element.27) | copy-start | bytes 50331652
  96.2 10.1 %copy-start.7 = (bf16[256,2048]{1,0:T(8,128)(2,1)S(1)}, bf16[256,2048]{1,0:T(8,128)(2,1)}, u32[]{:S(2)}) copy-start(bf16[256,2048]{1,0:T(8,128)(2,1)} %param.25) | copy-start | bytes 3145732
  112.7 4.8 %copy-start.3 = (bf16[256,4,1,256]{3,2,1,0:T(2,128)(2,1)S(1)}, bf16[256,4,1,256]{3,2,1,0:T(2,128)(2,1)}, u32[]{:S(2)}) copy-start(bf16[256,4,1,256]{3,2,1,0:T(2,128)(2,1)} %get-tuple-element.8) | copy-start | bytes 1572868
  112.9 4.7 %collective-permute-start = (bf16[256,4,256]{2,0,1:T(8,128)(2,1)S(1)}, bf16[256,4,256]{2,0,1:T(8,128)(2,1)}, u32[]{:S(2)}, u32[]{:S(2)}) collective-permute-start(bf16[256,4,256]{2,0,1:T(8,128)(2,1)S(1)} %bitcast.123), channel_id=1, source_target_pairs={{0,1},{1,0},{2,3},{3,2},{4,5},{5,4},{6,7},{7,6},{8,9},{9,8},{10,11... | collective-permute-start | bytes 1572872 | tf_op jit(solution)/shard_map/ppermute | solution.py:56
  119.8 12.5 %collective-permute-start.1 = (bf16[256,256]{1,0:T(8,128)(2,1)S(1)}, bf16[256,256]{1,0:T(8,128)(2,1)S(1)}, u32[]{:S(2)}, u32[]{:S(2)}) collective-permute-start(bf16[256,256]{1,0:T(8,128)(2,1)S(1)} %get-tuple-element.13), channel_id=1, source_target_pairs={{0,2},{1,3},{2,4},{3,5},{4,6},{5,7},{6,0},{7,1},{8,10},{9,11},{10,... | collective-permute-start | bytes 393224 | tf_op jit(solution)/shard_map/ppermute | solution.py:62
  122.9 13.2 %collective-permute-start.2 = (bf16[256,256]{1,0:T(8,128)(2,1)S(1)}, bf16[256,256]{1,0:T(8,128)(2,1)S(1)}, u32[]{:S(2)}, u32[]{:S(2)}) collective-permute-start(bf16[256,256]{1,0:T(8,128)(2,1)S(1)} %get-tuple-element.15), channel_id=1, source_target_pairs={{0,4},{1,5},{2,6},{3,7},{4,0},{5,1},{6,2},{7,3},{8,12},{9,13},{10,... | collective-permute-start | bytes 393224 | tf_op jit(solution)/shard_map/ppermute | solution.py:62
  127.1 12.2 %collective-permute-start.3 = (bf16[256,256]{1,0:T(8,128)(2,1)S(1)}, bf16[256,256]{1,0:T(8,128)(2,1)S(1)}, u32[]{:S(2)}, u32[]{:S(2)}) collective-permute-start(bf16[256,256]{1,0:T(8,128)(2,1)S(1)} %get-tuple-element.14), channel_id=1, source_target_pairs={{0,6},{1,7},{2,0},{3,1},{4,2},{5,3},{6,4},{7,5},{8,14},{9,15},{10,... | collective-permute-start | bytes 393224 | tf_op jit(solution)/shard_map/ppermute | solution.py:62
  139.3 17.6 %copy-start.14 = (s32[64]{0:T(128)S(1)}, s32[64]{0:T(128)}, u32[]{:S(2)}) copy-start(s32[64]{0:T(128)} %param.18) | copy-start | bytes 772
  140.4 8.6 %collective-permute-start.4 = (bf16[256,256]{1,0:T(8,128)(2,1)S(1)}, bf16[256,256]{1,0:T(8,128)(2,1)S(1)}, u32[]{:S(2)}, u32[]{:S(2)}) collective-permute-start(bf16[256,256]{1,0:T(8,128)(2,1)S(1)} %fusion.30), channel_id=1, source_target_pairs={{0,2},{1,3},{2,4},{3,5},{4,6},{5,7},{6,0},{7,1},{8,10},{9,11},{10,... | collective-permute-start | bytes 393224 | tf_op jit(solution)/shard_map/ppermute | solution.py:72
  141.9 12.4 %collective-permute-start.5 = (bf16[256,256]{1,0:T(8,128)(2,1)S(1)}, bf16[256,256]{1,0:T(8,128)(2,1)S(1)}, u32[]{:S(2)}, u32[]{:S(2)}) collective-permute-start(bf16[256,256]{1,0:T(8,128)(2,1)S(1)} %fusion.30), channel_id=1, source_target_pairs={{0,4},{1,5},{2,6},{3,7},{4,0},{5,1},{6,2},{7,3},{8,12},{9,13},{10,... | collective-permute-start | bytes 393224 | tf_op jit(solution)/shard_map/ppermute | solution.py:72
  145.9 9.7 %collective-permute-start.6 = (bf16[256,256]{1,0:T(8,128)(2,1)S(1)}, bf16[256,256]{1,0:T(8,128)(2,1)S(1)}, u32[]{:S(2)}, u32[]{:S(2)}) collective-permute-start(bf16[256,256]{1,0:T(8,128)(2,1)S(1)} %fusion.30), channel_id=1, source_target_pairs={{0,6},{1,7},{2,0},{3,1},{4,2},{5,3},{6,4},{7,5},{8,14},{9,15},{10,... | collective-permute-start | bytes 393224 | tf_op jit(solution)/shard_map/ppermute | solution.py:72
  156.3 2.1 collective-permute-start.7
  160.3 2.9 %copy-start.9 = (f32[2048]{0:T(1024)S(1)}, f32[2048]{0:T(1024)}, u32[]{:S(2)}) copy-start(f32[2048]{0:T(1024)} %param.26) | copy-start | bytes 24580
  163.3 2.1 copy-start.6
  174.9 2.6 %copy-start.4 = (bf16[256,4,1,256]{3,2,1,0:T(2,128)(2,1)S(1)}, bf16[256,4,1,256]{3,2,1,0:T(2,128)(2,1)}, u32[]{:S(2)}) copy-start(bf16[256,4,1,256]{3,2,1,0:T(2,128)(2,1)} %get-tuple-element.6) | copy-start | bytes 1572868
  175.0 2.4 %collective-permute-start.8 = (bf16[256,4,256]{2,0,1:T(8,128)(2,1)S(1)}, bf16[256,4,256]{2,0,1:T(8,128)(2,1)}, u32[]{:S(2)}, u32[]{:S(2)}) collective-permute-start(bf16[256,4,256]{2,0,1:T(8,128)(2,1)S(1)} %bitcast.124), channel_id=1, source_target_pairs={{0,1},{1,0},{2,3},{3,2},{4,5},{5,4},{6,7},{7,6},{8,9},{9,8},{10,11... | collective-permute-start | bytes 1572872 | tf_op jit(solution)/shard_map/ppermute | solution.py:56
  179.7 8.7 %collective-permute-start.10 = (bf16[256,256]{1,0:T(8,128)(2,1)S(1)}, bf16[256,256]{1,0:T(8,128)(2,1)S(1)}, u32[]{:S(2)}, u32[]{:S(2)}) collective-permute-start(bf16[256,256]{1,0:T(8,128)(2,1)S(1)} %get-tuple-element.12), channel_id=1, source_target_pairs={{0,4},{1,5},{2,6},{3,7},{4,0},{5,1},{6,2},{7,3},{8,12},{9,13},{10,... | collective-permute-start | bytes 393224 | tf_op jit(solution)/shard_map/ppermute | solution.py:62
  183.6 13.4 %collective-permute-start.11 = (bf16[256,256]{1,0:T(8,128)(2,1)S(1)}, bf16[256,256]{1,0:T(8,128)(2,1)S(1)}, u32[]{:S(2)}, u32[]{:S(2)}) collective-permute-start(bf16[256,256]{1,0:T(8,128)(2,1)S(1)} %get-tuple-element.11), channel_id=1, source_target_pairs={{0,6},{1,7},{2,0},{3,1},{4,2},{5,3},{6,4},{7,5},{8,14},{9,15},{10,... | collective-permute-start | bytes 393224 | tf_op jit(solution)/shard_map/ppermute | solution.py:62
  185.3 11.6 %collective-permute-start.9 = (bf16[256,256]{1,0:T(8,128)(2,1)S(1)}, bf16[256,256]{1,0:T(8,128)(2,1)S(1)}, u32[]{:S(2)}, u32[]{:S(2)}) collective-permute-start(bf16[256,256]{1,0:T(8,128)(2,1)S(1)} %get-tuple-element.10), channel_id=1, source_target_pairs={{0,2},{1,3},{2,4},{3,5},{4,6},{5,7},{6,0},{7,1},{8,10},{9,11},{10,... | collective-permute-start | bytes 393224 | tf_op jit(solution)/shard_map/ppermute | solution.py:62
  199.8 20.5 %all-to-all-start.2 = ((bf16[32,8,256]{2,1,0:T(8,128)(2,1)}), bf16[32,8,256]{2,1,0:T(8,128)(2,1)S(1)}, u32[]{:S(2)}, u32[]{:S(2)}) async-start(bf16[32,8,256]{2,1,0:T(8,128)(2,1)} %bitcast.38), calls=%async_computation.2 | async-start | bytes 262144 | tf_op jit(solution)/shard_map/all_to_all | solution.py:175

commit v5 on v4

--- a/solution.py
+++ b/solution.py
@@ -1,6 +1,7 @@
 import jax
 import jax.numpy as jnp
 from jax import lax
+from jax.experimental import pallas as pl
 from jax.sharding import PartitionSpec as P
 
 HD = 128
@@ -89,6 +90,73 @@
     target = local_slot * BLK + anchor % BLK
     cache = jnp.zeros(arrived.shape, jnp.bfloat16).at[target].set(arrived)
     return cache.reshape(rows // BLK, BLK, arrived.shape[1])
+
+
+KEY_CHUNK = 512
+QUERY_TILE = 256
+
+
+def attend_kernel(q_ref, qtok_ref, qbeg_ref, kv_ref, ktok_ref, out_ref):
+    query = q_ref[...]
+    qtok = qtok_ref[...]
+    qbeg = qbeg_ref[...]
+    tile = query.shape[0]
+    chunks = kv_ref.shape[0] // KEY_CHUNK
+    scale = 1.0 / HD**0.5
+
+    def scores(chunk):
+        start = pl.multiple_of(chunk * KEY_CHUNK, KEY_CHUNK)
+        keys = kv_ref[pl.ds(start, KEY_CHUNK), pl.ds(0, HD)]
+        ktok = ktok_ref[:, pl.ds(start, KEY_CHUNK)]
+        raw = lax.dot_general(
+            query, keys, (((1,), (1,)), ((), ())), preferred_element_type=jnp.float32
+        ) * scale
+        mask = (ktok >= qbeg) & (ktok <= qtok)
+        return jnp.where(mask, raw, -1e30), mask, start
+
+    def find_top(chunk, top):
+        score, _, _ = scores(chunk)
+        return jnp.maximum(top, jnp.max(score, axis=1, keepdims=True))
+
+    top = lax.fori_loop(0, chunks, find_top, jnp.full((tile, 1), -1e30, jnp.float32))
+
+    def accumulate(chunk, carry):
+        total, accum = carry
+        score, mask, start = scores(chunk)
+        weights = jnp.where(mask, jnp.exp(score - top), 0.0)
+        values = kv_ref[pl.ds(start, KEY_CHUNK), pl.ds(HD, HD)]
+        total = total + jnp.sum(weights, axis=1, keepdims=True)
+        accum = accum + jnp.dot(
+            weights.astype(jnp.bfloat16), values, preferred_element_type=jnp.float32
+        )
+        return total, accum
+
+    total, accum = lax.fori_loop(
+        0,
+        chunks,
+        accumulate,
+        (jnp.zeros((tile, 1), jnp.float32), jnp.zeros((tile, HD), jnp.float32)),
+    )
+    out_ref[...] = (accum / total).astype(out_ref.dtype)
+
+
+def attend(query, query_tokens, query_begins, flat, key_tokens, head):
+    count = query.shape[0]
+    keys = flat.shape[0]
+    tile = min(QUERY_TILE, count)
+    return pl.pallas_call(
+        attend_kernel,
+        grid=(count // tile,),
+        in_specs=[
+            pl.BlockSpec((tile, HD), lambda i: (i, 0)),
+            pl.BlockSpec((tile, 1), lambda i: (i, 0)),
+            pl.BlockSpec((tile, 1), lambda i: (i, 0)),
+            pl.BlockSpec((keys, 2 * HD), lambda i: (0, head)),
+            pl.BlockSpec((1, keys), lambda i: (0, 0)),
+        ],
+        out_specs=pl.BlockSpec((tile, HD), lambda i: (i, 0)),
+        out_shape=jax.ShapeDtypeStruct((count, HD), jnp.bfloat16),
+    )(query, query_tokens, query_begins, flat, key_tokens)
 
 
 def body(
@@ -129,31 +197,19 @@
     qnorm = rotary(rms(query, q_gain), pos).astype(jnp.bfloat16).reshape(rows, kv_heads, group, HD)
     knorm = rotary(rms(keys, k_gain), pos).astype(jnp.bfloat16)
     stacked = jnp.stack([knorm, values], axis=2).reshape(rows, kv_heads * 2 * HD)
-    scale = 1.0 / HD**0.5
     pieces = gather_seq(stacked, seq_count)
-    piece_tokens = gather_seq(token_order, seq_count)
+    stacked, order_late = lax.optimization_barrier((stacked, token_order))
+    piece_tokens = gather_seq(order_late, seq_count)
     flat = pieces.reshape(seq_count * rows, kv_heads * 2 * HD)
-    piece_order = piece_tokens.reshape(seq_count * rows)
-    mask = (piece_order[None, :] >= begin[:, None]) & (piece_order[None, :] <= token_order[:, None])
-    mask = mask[:, None, :]
+    key_tokens = piece_tokens.reshape(1, seq_count * rows)
+    query_tokens = jnp.repeat(token_order, group)[:, None]
+    query_begins = jnp.repeat(begin, group)[:, None]
     heads_out = []
     for head in range(kv_heads):
-        piece_keys = flat[:, (2 * head) * HD : (2 * head + 1) * HD]
-        piece_values = flat[:, (2 * head + 1) * HD : (2 * head + 2) * HD]
         qhead = qnorm[:, head].reshape(rows * group, HD)
-        score = lax.dot_general(
-            qhead, piece_keys, (((1,), (1,)), ((), ())), preferred_element_type=jnp.float32
-        ).reshape(rows, group, seq_count * rows) * scale
-        score = jnp.where(mask, score, -1e30)
-        best = jnp.maximum(jnp.max(score, axis=-1), -1e30)
-        weights = jnp.where(mask, jnp.exp(score - best[..., None]), 0.0)
-        total = jnp.sum(weights, axis=-1)
-        accum = jnp.dot(
-            weights.astype(jnp.bfloat16).reshape(rows * group, seq_count * rows),
-            piece_values,
-            preferred_element_type=jnp.float32,
-        ).reshape(rows, group, HD)
-        heads_out.append((accum / total[..., None]).astype(jnp.bfloat16))
+        heads_out.append(
+            attend(qhead, query_tokens, query_begins, flat, key_tokens, head).reshape(rows, group, HD)
+        )
     attn = jnp.stack(heads_out, axis=1).reshape(rows, q_heads * HD)
     terms = jnp.dot(attn, o_weight, preferred_element_type=jnp.float32)
     column = lax.axis_index("tp") * part

time: 223 us -> 228 us (1.022)
  Pallas kernels: 0 us -> 29.7 us
  matrix products: 27.2 us -> 10.4 us
  other arithmetic: 25.2 us -> 20.2 us
  local copies, waits for them, and re-layouts: 31.4 us -> 28.6 us
    pallas_call x0 -> x1, Pallas kernels: none -> 29.7 us  [attend(): pl.pallas_call(attend_kernel, grid=(count // tile,), in_specs=[pl.BlockSp...]
    dot_general x2 -> x0, matrix products: 15.8 us -> none  [the longest x1 10.1 us: body(): jnp.dot(weights.astype(jnp.bfloat16).reshape(rows * group, seq_count * ro...]
    unnamed x32, local copies, waits for them, and re-layouts: 6.11 us -> 0.39 us
    reduce_sum x1 -> x0, other arithmetic: 5.29 us -> none  [body(): total = jnp.sum(weights, axis=-1)]
    and x1 -> x0, other arithmetic: 2.88 us -> none  [body(): (piece_order[None, :] >= begin[:, None]) & (piece_order[None, :] <= token...]
    another operation x0 -> x5, local copies, waits for them, and re-layouts: none -> 2.84 us  [the longest x1 0.95 us: body(): attn = jnp.stack(heads_out, axis=1).reshape(rows, q_heads * HD)]
  transfers between devices with their start and end apart: 15 -> 15, of which waited for: 13 -> 12; matrix products, arithmetic and copies ran while one was open for 8% -> 9% of each run, Pallas kernels for 0% -> 0%
where the time goes in v5:
time: 228 us; the launch traced here: 227 us
  waiting for transfers between devices  79.8 us (35%)
  starting transfers between devices  57.4 us (25%)
  Pallas kernels  29.7 us (13%)
  local copies, waits for them, and re-layouts  28.6 us (13%)
  other arithmetic  20.2 us (9%)
  matrix products  10.4 us (5%)
    all_to_all x2, waiting for transfers between devices, gather_seq(): lax.all_to_all(copies, 'seq', split_axis=0, concat_axis=0, tiled=True)  46.5 us
    pallas_call x1, Pallas kernels, attend(): pl.pallas_call(attend_kernel, grid=(count // tile,), in_specs=[pl.BlockSp...  29.7 us
    ppermute x6, waiting for transfers between devices, scatter_sum_tp(): lax.ppermute(piece, 'tp', chip_shift(tp_count, shift)).astype(jnp.float32)  17.7 us
    all_to_all x2, starting transfers between devices, gather_seq(): lax.all_to_all(copies, 'seq', split_axis=0, concat_axis=0, tiled=True)  17.1 us
    ppermute x6, starting transfers between devices, scatter_sum_tp(): lax.ppermute(piece, 'tp', chip_shift(tp_count, shift)).astype(jnp.float32)  15.9 us
    all_to_all x1, starting transfers between devices, body(): lax.all_to_all(out[send_rows], 'seq', split_axis=0, concat_axis=0, tiled=...  12.3 us
    ppermute x3, starting transfers between devices, gather_tp(): lax.ppermute(block, 'tp', chip_shift(tp_count, shift))  8.26 us
    ppermute x3, waiting for transfers between devices, gather_tp(): lax.ppermute(block, 'tp', chip_shift(tp_count, shift))  7.03 us
  transfers between devices with their start and end apart: 15, of which 12 were waited for; matrix products, arithmetic and copies ran while one was open for 9% of the time, Pallas kernels for 0%

profile of v5, /device:TPU:1, one launch (start us, length us, event | category | flops | bytes accessed | tf_op | source)
XLA Modules:
  0.0 227.1 jit_solution(2806036311486574562)
XLA Ops:
  0.7 1.5 broadcast_in_dim.33
  2.1 9.2 %all-to-all-start = ((s32[32,1,256]{2,1,0:T(1,128)}), s32[32,1,256]{2,1,0:T(1,128)S(1)}, u32[]{:S(2)}, u32[]{:S(2)}) async-start(s32[32,1,256]{2,1,0:T(1,128)} %broadcast_in_dim.33), calls=%async_computation | async-start | bytes 65536 | tf_op jit(solution)/shard_map/all_to_all | solution.py:40
  11.4 1.5 multiply_reduce_fusion
  12.9 0.8 reduce-window.9
  13.7 0.7 bitcast_subtract_fusion
  14.5 0.8 select_reduce_fusion
  15.2 0.7 subtract_convert_fusion.1
  15.9 2.0 multiply_reduce_fusion.2
  17.9 0.6 fusion.4
  18.6 0.3 fusion.35
  19.1 2.5 %broadcast_in_dim.42 = bf16[32,256,256]{2,1,0:T(8,128)(2,1)} broadcast(bf16[256,256]{1,0:T(8,128)(2,1)S(1)} %copy.48), dimensions={1,2} | broadcast | bytes 4325376 | tf_op jit(solution)/shard_map/broadcast_in_dim | solution.py:39
  21.5 7.9 %all-to-all-start.1 = ((bf16[32,256,256]{2,1,0:T(8,128)(2,1)}), bf16[32,256,256]{2,1,0:T(8,128)(2,1)}, u32[]{:S(2)}, u32[]{:S(2)}) async-start(bf16[32,256,256]{2,1,0:T(8,128)(2,1)} %broadcast_in_dim.42), calls=%async_computation.1 | async-start | bytes 8388608 | tf_op jit(solution)/shard_map/all_to_all | solution.py:40
  29.4 1.9 multiply_reduce_fusion.1
  32.2 0.8 broadcast_in_dim_reshape.11.qbeg_ref
  33.1 0.8 broadcast_in_dim_reshape.10.qtok_ref
  33.9 0.8 pad_maximum_fusion.1.q_ref
  34.7 46.5 %all-to-all-done.1 = bf16[32,256,256]{2,1,0:T(8,128)(2,1)} async-done(((bf16[32,256,256]{2,1,0:T(8,128)(2,1)}), bf16[32,256,256]{2,1,0:T(8,128)(2,1)}, u32[]{:S(2)}, u32[]{:S(2)}) %all-to-all-start.1) | async-done | bytes 4194336 | tf_op jit(solution)/shard_map/all_to_all | solution.py:40
  81.2 29.7 %shard_map.158 = bf16[512,128]{1,0:T(8,128)(2,1)} custom-call(bf16[512,128]{1,0:T(8,128)(2,1)} %pad_maximum_fusion.1.q_ref, s32[512,1]{1,0:T(8,128)} %broadcast_in_dim_reshape.10.qtok_ref, s32[512,1]{1,0:T(8,128)} %broadcast_in_dim_reshape.11.qbeg_ref, bf16[8192,256]{1,0:T(8,128)(2,1)} %bitcast.13.kv_ref, s32[1,8192]{1,0:T(1,128)} %bitcast.119), custom_call_target="tpu_custom_call" | custom-call | tf_op jit(solution)/shard_map/pallas_call | solution.py:147
  110.9 1.0 reshape_stack_reshape.3
  111.9 1.4 convolution_convert_fusion.1
  113.3 1.8 reshape.529
  115.1 3.1 %constant_dynamic-slice_fusion.3 = (bf16[256,4,1,256]{3,2,1,0:T(2,128)(2,1)}, bf16[256,4,1,256]{3,2,1,0:T(2,128)(2,1)S(1)}) fusion(bf16[256,4,2,256]{3,2,1,0:T(2,128)(2,1)S(1)} %reshape.529, s32[]{:T(128)S(6)} %select_n.203, s32[]{:T(128)S(6)} %select_n.204), kind=kLoop, calls=%fused_computation.98 | loop fusion | bytes 2097160 | tf_op jit(solution)/shard_map/jit(dynamic_index_in_dim)/dynamic_slice | solution.py:55
  118.4 2.8 %collective-permute-start = (bf16[256,4,256]{2,0,1:T(8,128)(2,1)S(1)}, bf16[256,4,256]{2,0,1:T(8,128)(2,1)}, u32[]{:S(2)}, u32[]{:S(2)}) collective-permute-start(bf16[256,4,256]{2,0,1:T(8,128)(2,1)S(1)} %bitcast.113), channel_id=1, source_target_pairs={{0,1},{1,0},{2,3},{3,2},{4,5},{5,4},{6,7},{7,6},{8,9},{9,8},{10,11... | collective-permute-start | bytes 1572872 | tf_op jit(solution)/shard_map/ppermute | solution.py:57
  121.2 1.7 collective-permute-done
  122.8 2.3 fusion.45
  125.1 3.0 %collective-permute-start.1 = (bf16[256,256]{1,0:T(8,128)(2,1)S(1)}, bf16[256,256]{1,0:T(8,128)(2,1)S(1)}, u32[]{:S(2)}, u32[]{:S(2)}) collective-permute-start(bf16[256,256]{1,0:T(8,128)(2,1)S(1)} %get-tuple-element.13), channel_id=1, source_target_pairs={{0,2},{1,3},{2,4},{3,5},{4,6},{5,7},{6,0},{7,1},{8,10},{9,11},{10,... | collective-permute-start | bytes 393224 | tf_op jit(solution)/shard_map/ppermute | solution.py:63
  128.2 4.2 %collective-permute-start.2 = (bf16[256,256]{1,0:T(8,128)(2,1)S(1)}, bf16[256,256]{1,0:T(8,128)(2,1)S(1)}, u32[]{:S(2)}, u32[]{:S(2)}) collective-permute-start(bf16[256,256]{1,0:T(8,128)(2,1)S(1)} %get-tuple-element.15), channel_id=1, source_target_pairs={{0,4},{1,5},{2,6},{3,7},{4,0},{5,1},{6,2},{7,3},{8,12},{9,13},{10,... | collective-permute-start | bytes 393224 | tf_op jit(solution)/shard_map/ppermute | solution.py:63
  132.4 2.4 %collective-permute-start.3 = (bf16[256,256]{1,0:T(8,128)(2,1)S(1)}, bf16[256,256]{1,0:T(8,128)(2,1)S(1)}, u32[]{:S(2)}, u32[]{:S(2)}) collective-permute-start(bf16[256,256]{1,0:T(8,128)(2,1)S(1)} %get-tuple-element.14), channel_id=1, source_target_pairs={{0,6},{1,7},{2,0},{3,1},{4,2},{5,3},{6,4},{7,5},{8,14},{9,15},{10,... | collective-permute-start | bytes 393224 | tf_op jit(solution)/shard_map/ppermute | solution.py:63
  134.8 2.8 %convert_element_type.102 = f32[256,2048]{1,0:T(8,128)} convert(bf16[256,2048]{1,0:T(8,128)(2,1)} %param.15) | non-fusion elementwise | flops 524288 | bytes 3145728 | tf_op jit(solution)/shard_map/convert_element_type | solution.py:186
  137.6 3.7 %collective-permute-done.2 = bf16[256,256]{1,0:T(8,128)(2,1)S(1)} collective-permute-done((bf16[256,256]{1,0:T(8,128)(2,1)S(1)}, bf16[256,256]{1,0:T(8,128)(2,1)S(1)}, u32[]{:S(2)}, u32[]{:S(2)}) %collective-permute-start.2) | collective-permute-done | bytes 131104 | tf_op jit(solution)/shard_map/ppermute | solution.py:63
  141.3 3.1 %collective-permute-done.3 = bf16[256,256]{1,0:T(8,128)(2,1)S(1)} collective-permute-done((bf16[256,256]{1,0:T(8,128)(2,1)S(1)}, bf16[256,256]{1,0:T(8,128)(2,1)S(1)}, u32[]{:S(2)}, u32[]{:S(2)}) %collective-permute-start.3) | collective-permute-done | bytes 131104 | tf_op jit(solution)/shard_map/ppermute | solution.py:63
  144.5 1.1 fusion.17
  145.6 1.6 collective-permute-start.4
  147.3 4.0 %collective-permute-start.5 = (bf16[256,256]{1,0:T(8,128)(2,1)S(1)}, bf16[256,256]{1,0:T(8,128)(2,1)S(1)}, u32[]{:S(2)}, u32[]{:S(2)}) collective-permute-start(bf16[256,256]{1,0:T(8,128)(2,1)S(1)} %fusion.17), channel_id=1, source_target_pairs={{0,4},{1,5},{2,6},{3,7},{4,0},{5,1},{6,2},{7,3},{8,12},{9,13},{10,... | collective-permute-start | bytes 393224 | tf_op jit(solution)/shard_map/ppermute | solution.py:73
  151.3 2.6 %collective-permute-start.6 = (bf16[256,256]{1,0:T(8,128)(2,1)S(1)}, bf16[256,256]{1,0:T(8,128)(2,1)S(1)}, u32[]{:S(2)}, u32[]{:S(2)}) collective-permute-start(bf16[256,256]{1,0:T(8,128)(2,1)S(1)} %fusion.17), channel_id=1, source_target_pairs={{0,6},{1,7},{2,0},{3,1},{4,2},{5,3},{6,4},{7,5},{8,14},{9,15},{10,... | collective-permute-start | bytes 393224 | tf_op jit(solution)/shard_map/ppermute | solution.py:73
  153.9 0.5 collective-permute-done.4
  154.4 5.3 %collective-permute-done.5 = bf16[256,256]{1,0:T(8,128)(2,1)S(1)} collective-permute-done((bf16[256,256]{1,0:T(8,128)(2,1)S(1)}, bf16[256,256]{1,0:T(8,128)(2,1)S(1)}, u32[]{:S(2)}, u32[]{:S(2)}) %collective-permute-start.5) | collective-permute-done | bytes 131104 | tf_op jit(solution)/shard_map/ppermute | solution.py:73
  159.7 1.3 collective-permute-done.6
  161.0 0.6 gather_fusion.1
  161.7 0.6 collective-permute-start.7
  162.9 1.0 collective-permute-done.7
  163.8 0.4 fusion
  164.2 1.6 convert_bitcast_fusion
  165.8 3.0 %copy.53 = f32[256,4,2,256]{0,3,2,1:T(8,128)} copy(f32[256,4,2,256]{3,0,1,2:T(8,128)} %convert_bitcast_fusion) | data formatting | bytes 4194304 | tf_op jit(solution)/shard_map/convert_element_type | solution.py:219
  168.8 2.0 fusion.2
  170.8 0.8 fusion.46
  171.6 3.8 %convolution_convert_fusion = bf16[256,2048]{1,0:T(8,128)(2,1)} fusion(bf16[384,2048]{1,0:T(8,128)(2,1)S(1)} %copy-done, bf16[256,2048]{0,1:T(8,128)(2,1)S(1)} %fusion.2, bf16[2048,384]{1,0:T(8,128)(2,1)} %param.28, f32[256,384]{1,0:T(8,128)S(1)} %fusion.46), kind=kOutput, calls=%fused_computation.7 | convolution fusion | flops 806420480 | bytes 5636096 | tf_op jit(solution)/shard_map/dot_general | solution.py:223
  175.3 1.8 reshape.530
  177.2 3.1 %constant_dynamic-slice_fusion.1 = (bf16[256,4,1,256]{3,2,1,0:T(2,128)(2,1)}, bf16[256,4,1,256]{3,2,1,0:T(2,128)(2,1)S(1)}) fusion(bf16[256,4,2,256]{3,2,1,0:T(2,128)(2,1)S(1)} %reshape.530, s32[]{:T(128)S(6)} %select_n.203, s32[]{:T(128)S(6)} %select_n.204), kind=kLoop, calls=%fused_computation.96 | loop fusion | bytes 2097160 | tf_op jit(solution)/shard_map/jit(dynamic_index_in_dim)/dynamic_slice | solution.py:55
  180.5 0.5 collective-permute-start.8
  181.2 0.6 gather_fusion
  181.7 0.9 collective-permute-done.8
  182.6 2.2 fusion.44
  184.9 3.9 %collective-permute-start.10 = (bf16[256,256]{1,0:T(8,128)(2,1)S(1)}, bf16[256,256]{1,0:T(8,128)(2,1)S(1)}, u32[]{:S(2)}, u32[]{:S(2)}) collective-permute-start(bf16[256,256]{1,0:T(8,128)(2,1)S(1)} %get-tuple-element.12), channel_id=1, source_target_pairs={{0,4},{1,5},{2,6},{3,7},{4,0},{5,1},{6,2},{7,3},{8,12},{9,13},{10,... | collective-permute-start | bytes 393224 | tf_op jit(solution)/shard_map/ppermute | solution.py:63
  188.8 1.7 collective-permute-start.11
  190.5 0.6 collective-permute-start.9
  191.3 2.3 %collective-permute-done.10 = bf16[256,256]{1,0:T(8,128)(2,1)S(1)} collective-permute-done((bf16[256,256]{1,0:T(8,128)(2,1)S(1)}, bf16[256,256]{1,0:T(8,128)(2,1)S(1)}, u32[]{:S(2)}, u32[]{:S(2)}) %collective-permute-start.10) | collective-permute-done | bytes 131104 | tf_op jit(solution)/shard_map/ppermute | solution.py:63
  193.6 8.5 %collective-permute-done.11 = bf16[256,256]{1,0:T(8,128)(2,1)S(1)} collective-permute-done((bf16[256,256]{1,0:T(8,128)(2,1)S(1)}, bf16[256,256]{1,0:T(8,128)(2,1)S(1)}, u32[]{:S(2)}, u32[]{:S(2)}) %collective-permute-start.11) | collective-permute-done | bytes 131104 | tf_op jit(solution)/shard_map/ppermute | solution.py:63
  202.2 1.0 fusion.13
  203.2 1.8 gather_fusion.2
  205.0 12.3 %all-to-all-start.2 = ((bf16[32,8,256]{2,1,0:T(8,128)(2,1)}), bf16[32,8,256]{2,1,0:T(8,128)(2,1)S(1)}, u32[]{:S(2)}, u32[]{:S(2)}) async-start(bf16[32,8,256]{2,1,0:T(8,128)(2,1)} %bitcast.37), calls=%async_computation.2 | async-start | bytes 262144 | tf_op jit(solution)/shard_map/all_to_all | solution.py:231
  217.6 2.4 %scatter_custom_fusion.1 = bf16[256,256]{1,0:T(8,128)(2,1)} fusion(s32[256]{0:T(256)S(1)} %bitcast.126, bf16[32,256,256]{2,1,0:T(8,128)(2,1)} %all-to-all-done.1, s32[]{:T(128)} %constant.181.clone.1, s32[]{:T(128)S(6)} %select_n.197, bf16[]{:T(256)} %constant.176.clone.1), kind=kCustom, calls=%fused_computation.49 | custom fusion | bytes 263172 | tf_op jit(solution)/shard_map/scatter | solution.py:91
  220.0 5.0 %all-to-all-done.2 = bf16[32,8,256]{2,1,0:T(8,128)(2,1)S(1)} async-done(((bf16[32,8,256]{2,1,0:T(8,128)(2,1)}), bf16[32,8,256]{2,1,0:T(8,128)(2,1)S(1)}, u32[]{:S(2)}, u32[]{:S(2)}) %all-to-all-start.2) | async-done | bytes 131104 | tf_op jit(solution)/shard_map/all_to_all | solution.py:231
  225.0 2.1 scatter_custom_fusion
  (75 shorter events, 2.9 us)
Async XLA Ops:
  0.6 170.9 %copy-start = (bf16[384,2048]{1,0:T(8,128)(2,1)S(1)}, bf16[384,2048]{1,0:T(8,128)(2,1)}, u32[]{:S(2)}) copy-start(bf16[384,2048]{1,0:T(8,128)(2,1)} %param.29) | copy-start | bytes 4718596
  0.6 17.2 %copy-start.3 = (bf16[256,2048]{1,0:T(8,128)(2,1)S(1)}, bf16[256,2048]{1,0:T(8,128)(2,1)}, u32[]{:S(2)}) copy-start(bf16[256,2048]{1,0:T(8,128)(2,1)} %param.15) | copy-start | bytes 3145732
  0.7 17.2 %copy-start.13 = (f32[2048]{0:T(1024)S(1)}, f32[2048]{0:T(1024)}, u32[]{:S(2)}) copy-start(f32[2048]{0:T(1024)} %param.19) | copy-start | bytes 24580
  2.1 16.9 %all-to-all-start = ((s32[32,1,256]{2,1,0:T(1,128)}), s32[32,1,256]{2,1,0:T(1,128)S(1)}, u32[]{:S(2)}, u32[]{:S(2)}) async-start(s32[32,1,256]{2,1,0:T(1,128)} %broadcast_in_dim.33), calls=%async_computation | async-start | bytes 65536 | tf_op jit(solution)/shard_map/all_to_all | solution.py:40
  13.7 4.2 %copy-start.12 = (bf16[2048,128]{1,0:T(8,128)(2,1)S(1)}, bf16[2048,128]{1,0:T(8,128)(2,1)}, u32[]{:S(2)}) copy-start(bf16[2048,128]{1,0:T(8,128)(2,1)} %param.22) | copy-start | bytes 1572868
  15.9 2.6 %copy-start.10 = (f32[128]{0:T(128)S(1)}, f32[128]{0:T(128)}, u32[]{:S(2)}) copy-start(f32[128]{0:T(128)} %param.24) | copy-start | bytes 1540
  19.0 2.5 %copy-start.6 = (s32[32,1,256]{2,1,0:T(1,128)}, s32[32,1,256]{2,1,0:T(1,128)S(1)}, u32[]{:S(2)}) copy-start(s32[32,1,256]{2,1,0:T(1,128)S(1)} %all-to-all-done) | copy-start | bytes 98308
  21.5 59.7 %all-to-all-start.1 = ((bf16[32,256,256]{2,1,0:T(8,128)(2,1)}), bf16[32,256,256]{2,1,0:T(8,128)(2,1)}, u32[]{:S(2)}, u32[]{:S(2)}) async-start(bf16[32,256,256]{2,1,0:T(8,128)(2,1)} %broadcast_in_dim.42), calls=%async_computation.1 | async-start | bytes 8388608 | tf_op jit(solution)/shard_map/all_to_all | solution.py:40
  29.4 2.3 copy-start.11
  29.4 3.6 %copy-start.8 = (s32[256]{0:T(256)S(1)}, s32[256]{0:T(256)}, u32[]{:S(2)}) copy-start(s32[256]{0:T(256)} %param.16) | copy-start | bytes 3076
  81.2 30.7 %copy-start.5 = (bf16[256,2048]{1,0:T(8,128)(2,1)S(1)}, bf16[256,2048]{1,0:T(8,128)(2,1)}, u32[]{:S(2)}) copy-start(bf16[256,2048]{1,0:T(8,128)(2,1)} %param.25) | copy-start | bytes 3145732
  118.2 4.6 %copy-start.1 = (bf16[256,4,1,256]{3,2,1,0:T(2,128)(2,1)S(1)}, bf16[256,4,1,256]{3,2,1,0:T(2,128)(2,1)}, u32[]{:S(2)}) copy-start(bf16[256,4,1,256]{3,2,1,0:T(2,128)(2,1)} %get-tuple-element.8) | copy-start | bytes 1572868
  118.4 4.4 %collective-permute-start = (bf16[256,4,256]{2,0,1:T(8,128)(2,1)S(1)}, bf16[256,4,256]{2,0,1:T(8,128)(2,1)}, u32[]{:S(2)}, u32[]{:S(2)}) collective-permute-start(bf16[256,4,256]{2,0,1:T(8,128)(2,1)S(1)} %bitcast.113), channel_id=1, source_target_pairs={{0,1},{1,0},{2,3},{3,2},{4,5},{5,4},{6,7},{7,6},{8,9},{9,8},{10,11... | collective-permute-start | bytes 1572872 | tf_op jit(solution)/shard_map/ppermute | solution.py:57
  125.1 12.5 %collective-permute-start.1 = (bf16[256,256]{1,0:T(8,128)(2,1)S(1)}, bf16[256,256]{1,0:T(8,128)(2,1)S(1)}, u32[]{:S(2)}, u32[]{:S(2)}) collective-permute-start(bf16[256,256]{1,0:T(8,128)(2,1)S(1)} %get-tuple-element.13), channel_id=1, source_target_pairs={{0,2},{1,3},{2,4},{3,5},{4,6},{5,7},{6,0},{7,1},{8,10},{9,11},{10,... | collective-permute-start | bytes 393224 | tf_op jit(solution)/shard_map/ppermute | solution.py:63
  128.2 13.2 %collective-permute-start.2 = (bf16[256,256]{1,0:T(8,128)(2,1)S(1)}, bf16[256,256]{1,0:T(8,128)(2,1)S(1)}, u32[]{:S(2)}, u32[]{:S(2)}) collective-permute-start(bf16[256,256]{1,0:T(8,128)(2,1)S(1)} %get-tuple-element.15), channel_id=1, source_target_pairs={{0,4},{1,5},{2,6},{3,7},{4,0},{5,1},{6,2},{7,3},{8,12},{9,13},{10,... | collective-permute-start | bytes 393224 | tf_op jit(solution)/shard_map/ppermute | solution.py:63
  132.4 12.1 %collective-permute-start.3 = (bf16[256,256]{1,0:T(8,128)(2,1)S(1)}, bf16[256,256]{1,0:T(8,128)(2,1)S(1)}, u32[]{:S(2)}, u32[]{:S(2)}) collective-permute-start(bf16[256,256]{1,0:T(8,128)(2,1)S(1)} %get-tuple-element.14), channel_id=1, source_target_pairs={{0,6},{1,7},{2,0},{3,1},{4,2},{5,3},{6,4},{7,5},{8,14},{9,15},{10,... | collective-permute-start | bytes 393224 | tf_op jit(solution)/shard_map/ppermute | solution.py:63
  144.5 17.8 %copy-start.14 = (s32[64]{0:T(128)S(1)}, s32[64]{0:T(128)}, u32[]{:S(2)}) copy-start(s32[64]{0:T(128)} %param.18) | copy-start | bytes 772
  145.6 8.8 %collective-permute-start.4 = (bf16[256,256]{1,0:T(8,128)(2,1)S(1)}, bf16[256,256]{1,0:T(8,128)(2,1)S(1)}, u32[]{:S(2)}, u32[]{:S(2)}) collective-permute-start(bf16[256,256]{1,0:T(8,128)(2,1)S(1)} %fusion.17), channel_id=1, source_target_pairs={{0,2},{1,3},{2,4},{3,5},{4,6},{5,7},{6,0},{7,1},{8,10},{9,11},{10,... | collective-permute-start | bytes 393224 | tf_op jit(solution)/shard_map/ppermute | solution.py:73
  147.3 12.4 %collective-permute-start.5 = (bf16[256,256]{1,0:T(8,128)(2,1)S(1)}, bf16[256,256]{1,0:T(8,128)(2,1)S(1)}, u32[]{:S(2)}, u32[]{:S(2)}) collective-permute-start(bf16[256,256]{1,0:T(8,128)(2,1)S(1)} %fusion.17), channel_id=1, source_target_pairs={{0,4},{1,5},{2,6},{3,7},{4,0},{5,1},{6,2},{7,3},{8,12},{9,13},{10,... | collective-permute-start | bytes 393224 | tf_op jit(solution)/shard_map/ppermute | solution.py:73
  151.3 9.7 %collective-permute-start.6 = (bf16[256,256]{1,0:T(8,128)(2,1)S(1)}, bf16[256,256]{1,0:T(8,128)(2,1)S(1)}, u32[]{:S(2)}, u32[]{:S(2)}) collective-permute-start(bf16[256,256]{1,0:T(8,128)(2,1)S(1)} %fusion.17), channel_id=1, source_target_pairs={{0,6},{1,7},{2,0},{3,1},{4,2},{5,3},{6,4},{7,5},{8,14},{9,15},{10,... | collective-permute-start | bytes 393224 | tf_op jit(solution)/shard_map/ppermute | solution.py:73
  161.7 2.1 collective-permute-start.7
  165.8 3.0 %copy-start.9 = (f32[2048]{0:T(1024)S(1)}, f32[2048]{0:T(1024)}, u32[]{:S(2)}) copy-start(f32[2048]{0:T(1024)} %param.26) | copy-start | bytes 24580
  168.8 2.1 copy-start.4
  177.2 3.9 %copy-start.7 = (s32[32,1,256]{2,1,0:T(1,128)S(1)}, s32[32,1,256]{2,1,0:T(1,128)}, u32[]{:S(2)}) copy-start(s32[32,1,256]{2,1,0:T(1,128)} %copy-done.6) | copy-start | bytes 98308
  180.3 2.3 %copy-start.2 = (bf16[256,4,1,256]{3,2,1,0:T(2,128)(2,1)S(1)}, bf16[256,4,1,256]{3,2,1,0:T(2,128)(2,1)}, u32[]{:S(2)}) copy-start(bf16[256,4,1,256]{3,2,1,0:T(2,128)(2,1)} %get-tuple-element.6) | copy-start | bytes 1572868
  180.5 2.1 collective-permute-start.8
  184.9 8.7 %collective-permute-start.10 = (bf16[256,256]{1,0:T(8,128)(2,1)S(1)}, bf16[256,256]{1,0:T(8,128)(2,1)S(1)}, u32[]{:S(2)}, u32[]{:S(2)}) collective-permute-start(bf16[256,256]{1,0:T(8,128)(2,1)S(1)} %get-tuple-element.12), channel_id=1, source_target_pairs={{0,4},{1,5},{2,6},{3,7},{4,0},{5,1},{6,2},{7,3},{8,12},{9,13},{10,... | collective-permute-start | bytes 393224 | tf_op jit(solution)/shard_map/ppermute | solution.py:63
  188.8 13.4 %collective-permute-start.11 = (bf16[256,256]{1,0:T(8,128)(2,1)S(1)}, bf16[256,256]{1,0:T(8,128)(2,1)S(1)}, u32[]{:S(2)}, u32[]{:S(2)}) collective-permute-start(bf16[256,256]{1,0:T(8,128)(2,1)S(1)} %get-tuple-element.11), channel_id=1, source_target_pairs={{0,6},{1,7},{2,0},{3,1},{4,2},{5,3},{6,4},{7,5},{8,14},{9,15},{10,... | collective-permute-start | bytes 393224 | tf_op jit(solution)/shard_map/ppermute | solution.py:63
  190.5 11.6 %collective-permute-start.9 = (bf16[256,256]{1,0:T(8,128)(2,1)S(1)}, bf16[256,256]{1,0:T(8,128)(2,1)S(1)}, u32[]{:S(2)}, u32[]{:S(2)}) collective-permute-start(bf16[256,256]{1,0:T(8,128)(2,1)S(1)} %get-tuple-element.10), channel_id=1, source_target_pairs={{0,2},{1,3},{2,4},{3,5},{4,6},{5,7},{6,0},{7,1},{8,10},{9,11},{10,... | collective-permute-start | bytes 393224 | tf_op jit(solution)/shard_map/ppermute | solution.py:63
  205.0 20.0 %all-to-all-start.2 = ((bf16[32,8,256]{2,1,0:T(8,128)(2,1)}), bf16[32,8,256]{2,1,0:T(8,128)(2,1)S(1)}, u32[]{:S(2)}, u32[]{:S(2)}) async-start(bf16[32,8,256]{2,1,0:T(8,128)(2,1)} %bitcast.37), calls=%async_computation.2 | async-start | bytes 262144 | tf_op jit(solution)/shard_map/all_to_all | solution.py:231

commit v6 on v4

--- a/solution.py
+++ b/solution.py
@@ -77,6 +77,22 @@
     other_core = lax.ppermute(own_core, "tp", [(i, i ^ 1) for i in range(tp_count)])
     both = jnp.where(core == 0, jnp.stack([own_core, other_core]), jnp.stack([other_core, own_core]))
     return both.transpose(2, 1, 0, 3).reshape(rows, tp_count * part)
+
+
+TOKEN_BASE = 64
+PAYLOAD_ROWS = 16
+
+
+def gather_with_tokens(stacked, token_order, seq_count):
+    rows, width = stacked.shape
+    high = (token_order // TOKEN_BASE).astype(jnp.bfloat16)
+    low = (token_order % TOKEN_BASE).astype(jnp.bfloat16)
+    token_rows = jnp.stack([high, low]).reshape(2 * rows // width, width)
+    padding = jnp.zeros((PAYLOAD_ROWS - token_rows.shape[0], width), jnp.bfloat16)
+    arrived = gather_seq(jnp.concatenate([stacked, token_rows, padding], axis=0), seq_count)
+    coded = arrived[:, rows : rows + token_rows.shape[0], :].reshape(seq_count, 2, rows)
+    tokens = coded[:, 0].astype(jnp.int32) * TOKEN_BASE + coded[:, 1].astype(jnp.int32)
+    return arrived[:, :rows, :], tokens
 
 
 def build_cache(pieces, piece_tokens, rows, seq_count):
@@ -130,8 +146,7 @@
     knorm = rotary(rms(keys, k_gain), pos).astype(jnp.bfloat16)
     stacked = jnp.stack([knorm, values], axis=2).reshape(rows, kv_heads * 2 * HD)
     scale = 1.0 / HD**0.5
-    pieces = gather_seq(stacked, seq_count)
-    piece_tokens = gather_seq(token_order, seq_count)
+    pieces, piece_tokens = gather_with_tokens(stacked, token_order, seq_count)
     flat = pieces.reshape(seq_count * rows, kv_heads * 2 * HD)
     piece_order = piece_tokens.reshape(seq_count * rows)
     mask = (piece_order[None, :] >= begin[:, None]) & (piece_order[None, :] <= token_order[:, None])

time: 223 us -> 225 us (level)
  starting transfers between devices: 57.3 us -> 44.8 us
  local copies, waits for them, and re-layouts: 31.4 us -> 38.6 us
  waiting for transfers between devices: 80.2 us -> 84.4 us
  other arithmetic: 25.2 us -> 29 us
    all_to_all x2 -> x1, waiting for transfers between devices: 46.9 us -> 54.2 us  [gather_seq(): lax.all_to_all(copies, 'seq', split_axis=0, concat_axis=0, tiled=True)]
    all_to_all x2 -> x1, starting transfers between devices: 16.1 us -> 9.51 us  [gather_seq(): lax.all_to_all(copies, 'seq', split_axis=0, concat_axis=0, tiled=True)]
    slice x0 -> x2, local copies, waits for them, and re-layouts: none -> 5.61 us  [the longest x1 4.58 us: gather_with_tokens(): return (arrived[:, :rows, :], tokens)]
    all_to_all x1, starting transfers between devices: 12.9 us -> 8.12 us  [body(): lax.all_to_all(out[send_rows], 'seq', split_axis=0, concat_axis=0, tiled=...]
    ppermute x6, waiting for transfers between devices: 17.8 us -> 13.8 us  [scatter_sum_tp(): lax.ppermute(piece, 'tp', chip_shift(tp_count, shift)).astype(jnp.float32)]
    ppermute x3, waiting for transfers between devices: 7.04 us -> 9.7 us  [gather_tp(): lax.ppermute(block, 'tp', chip_shift(tp_count, shift))]
    unnamed x32 -> x35, local copies, waits for them, and re-layouts: 6.11 us -> 6.4 us
  transfers between devices with their start and end apart: 15 -> 14, of which waited for: 13 -> 9; matrix products, arithmetic and copies ran while one was open for 8% -> 6% of each run, Pallas kernels for 0% -> 0%
where the time goes in v6:
time: 225 us; the launch traced here: 224 us
  waiting for transfers between devices  84.4 us (38%)
  starting transfers between devices  44.8 us (20%)
  local copies, waits for them, and re-layouts  38.6 us (17%)
  other arithmetic  29 us (13%)
  matrix products  25.7 us (11%)
    all_to_all x1, waiting for transfers between devices, gather_seq(): lax.all_to_all(copies, 'seq', split_axis=0, concat_axis=0, tiled=True)  54.2 us
    ppermute x6, starting transfers between devices, scatter_sum_tp(): lax.ppermute(piece, 'tp', chip_shift(tp_count, shift)).astype(jnp.float32)  15.2 us
    ppermute x6, waiting for transfers between devices, scatter_sum_tp(): lax.ppermute(piece, 'tp', chip_shift(tp_count, shift)).astype(jnp.float32)  13.8 us
    dot_general x1, matrix products, body(): jnp.dot(weights.astype(jnp.bfloat16).reshape(rows * group, seq_count * ro...  10.1 us
    ppermute x3, waiting for transfers between devices, gather_tp(): lax.ppermute(block, 'tp', chip_shift(tp_count, shift))  9.7 us
    all_to_all x1, starting transfers between devices, gather_seq(): lax.all_to_all(copies, 'seq', split_axis=0, concat_axis=0, tiled=True)  9.51 us
    ppermute x3, starting transfers between devices, gather_tp(): lax.ppermute(block, 'tp', chip_shift(tp_count, shift))  8.37 us
    all_to_all x1, starting transfers between devices, body(): lax.all_to_all(out[send_rows], 'seq', split_axis=0, concat_axis=0, tiled=...  8.12 us
  transfers between devices with their start and end apart: 14, of which 9 were waited for; matrix products, arithmetic and copies ran while one was open for 6% of the time, Pallas kernels for 0%

profile of v6, /device:TPU:1, one launch (start us, length us, event | category | flops | bytes accessed | tf_op | source)
XLA Modules:
  0.0 223.6 jit_solution(816251559414120509)
XLA Ops:
  0.7 1.0 reduce-window.9
  1.7 0.7 bitcast_subtract_fusion
  2.4 0.8 select_reduce_fusion
  3.1 0.7 subtract_convert_fusion.1
  4.0 1.5 multiply_reduce_fusion
  5.6 2.0 fusion.11
  7.6 0.6 multiply_reduce_fusion.2
  8.9 2.4 %broadcast_in_dim.50 = bf16[32,272,256]{2,1,0:T(8,128)(2,1)} broadcast(bf16[272,256]{1,0:T(8,128)(2,1)S(1)} %copy.53), dimensions={1,2} | broadcast | bytes 4595712 | tf_op jit(solution)/shard_map/broadcast_in_dim | solution.py:38
  11.3 9.5 %all-to-all-start = ((bf16[32,272,256]{2,1,0:T(8,128)(2,1)}), bf16[32,272,256]{2,1,0:T(8,128)(2,1)}, u32[]{:S(2)}, u32[]{:S(2)}) async-start(bf16[32,272,256]{2,1,0:T(8,128)(2,1)} %broadcast_in_dim.50), calls=%async_computation | async-start | bytes 8912896 | tf_op jit(solution)/shard_map/all_to_all | solution.py:39
  20.9 1.9 multiply_reduce_fusion.1
  22.9 0.5 multiply_cosine_fusion
  23.8 54.2 %all-to-all-done = bf16[32,272,256]{2,1,0:T(8,128)(2,1)} async-done(((bf16[32,272,256]{2,1,0:T(8,128)(2,1)}), bf16[32,272,256]{2,1,0:T(8,128)(2,1)}, u32[]{:S(2)}, u32[]{:S(2)}) %all-to-all-start) | async-done | bytes 4456480 | tf_op jit(solution)/shard_map/all_to_all | solution.py:39
  78.0 1.0 fusion.69
  79.4 1.9 compare_and_fusion
  81.3 4.6 %slice.51 = bf16[32,256,256]{2,1,0:T(8,128)(2,1)} slice(bf16[32,272,256]{2,1,0:T(8,128)(2,1)} %all-to-all-done), slice={[0:32], [0:256], [0:256]} | slice | bytes 8388608 | tf_op jit(solution)/shard_map/slice | solution.py:95
  85.9 5.2 %fusion = (f32[256,2]{0,1:T(2,128)S(1)}, f32[256,2,8192]{2,0,1:T(8,128)S(1)}) fusion(pred[256,8192]{1,0:T(8,128)(4,1)S(1)} %compare_and_fusion, bf16[8192,256]{1,0:T(8,128)(2,1)} %bitcast.125, bf16[256,2,64]{2,0,1:T(8,128)(2,1)S(1)} %get-tuple-element.19, bf16[256,2,64]{2,0,1:T(8,128)(2,1)S(1)} %get-tuple-element.18), kind=kOutput, calls=%fused_computation.7 | convolution fusion | flops 1086586368 | bytes 21104640 | tf_op jit(solution)/shard_map/dot_general | solution.py:159
  91.2 5.7 %copy-done.1 = f32[256,2,8192]{2,0,1:T(8,128)} copy-done((f32[256,2,8192]{2,0,1:T(8,128)}, f32[256,2,8192]{2,0,1:T(8,128)S(1)}, u32[]{:S(2)}) %copy-start.1) | copy-done | bytes 16777240
  96.9 5.3 %fusion.1 = f32[256,2]{0,1:T(2,128)S(1)} fusion(f32[256,2,8192]{2,0,1:T(8,128)S(1)} %get-tuple-element.34, f32[256,2]{0,1:T(2,128)S(1)} %broadcast_maximum_fusion, pred[256,8192]{1,0:T(8,128)(4,1)S(1)} %compare_and_fusion), kind=kLoop, calls=%fused_computation.8 | loop fusion | flops 20971008 | bytes 18878464 | tf_op jit(solution)/shard_map/reduce_sum | solution.py:165
  102.2 10.1 %fusion.15 = bf16[256,2,128]{0,2,1:T(8,128)(2,1)S(1)} fusion(bf16[8192,256]{1,0:T(8,128)(2,1)} %bitcast.126, f32[256,2,8192]{2,0,1:T(8,128)} %copy-done.1, f32[256,2]{0,1:T(2,128)S(1)} %broadcast_maximum_fusion, pred[256,8192]{1,0:T(8,128)(4,1)S(1)} %compare_and_fusion, f32[256,2]{0,1:T(2,128)S(1)} %fusion.1), kind=kOutput, calls=%fused_computation.31 | convolution fusion | flops 1094844416 | bytes 21106688 | tf_op jit(solution)/shard_map/dot_general | solution.py:166
  112.3 1.4 convolution_convert_fusion.1
  113.7 2.0 reshape.600
  115.8 3.1 %constant_dynamic-slice_fusion.4 = (bf16[256,4,1,256]{3,2,1,0:T(2,128)(2,1)}, bf16[256,4,1,256]{3,2,1,0:T(2,128)(2,1)S(1)}) fusion(bf16[256,4,2,256]{3,2,1,0:T(2,128)(2,1)S(1)} %reshape.600, s32[]{:T(128)S(6)} %select_n.221, s32[]{:T(128)S(6)} %select_n.222), kind=kLoop, calls=%fused_computation.115 | loop fusion | bytes 2097160 | tf_op jit(solution)/shard_map/jit(dynamic_index_in_dim)/dynamic_slice | solution.py:54
  119.1 1.9 collective-permute-start
  121.0 1.7 collective-permute-done
  122.6 2.2 %fusion.68 = (bf16[256,4,256]{2,0,1:T(8,128)(2,1)S(1)}, f32[256,4,256]{2,0,1:T(8,128)}) fusion(bf16[256,4,256]{2,0,1:T(8,128)(2,1)} %collective-permute-done, bf16[256,4,1,256]{3,2,1,0:T(2,128)(2,1)S(1)} %copy-done.2), kind=kLoop, calls=%fused_computation.161 | loop fusion | flops 1048576 | bytes 2621440 | tf_op jit(solution)/shard_map/convert_element_type | solution.py:59
  124.9 5.2 %collective-permute-start.3 = (bf16[256,256]{1,0:T(8,128)(2,1)S(1)}, bf16[256,256]{1,0:T(8,128)(2,1)S(1)}, u32[]{:S(2)}, u32[]{:S(2)}) collective-permute-start(bf16[256,256]{1,0:T(8,128)(2,1)S(1)} %get-tuple-element.16), channel_id=1, source_target_pairs={{0,6},{1,7},{2,0},{3,1},{4,2},{5,3},{6,4},{7,5},{8,14},{9,15},{10,... | collective-permute-start | bytes 393224 | tf_op jit(solution)/shard_map/ppermute | solution.py:62
  130.1 1.2 collective-permute-start.2
  131.3 2.1 collective-permute-start.1
  133.4 2.8 %convert_element_type.133 = f32[256,2048]{1,0:T(8,128)} convert(bf16[256,2048]{1,0:T(8,128)(2,1)} %param.15) | non-fusion elementwise | flops 524288 | bytes 3145728 | tf_op jit(solution)/shard_map/convert_element_type | solution.py:134
  136.2 6.4 %collective-permute-done.2 = bf16[256,256]{1,0:T(8,128)(2,1)S(1)} collective-permute-done((bf16[256,256]{1,0:T(8,128)(2,1)S(1)}, bf16[256,256]{1,0:T(8,128)(2,1)S(1)}, u32[]{:S(2)}, u32[]{:S(2)}) %collective-permute-start.2) | collective-permute-done | bytes 131104 | tf_op jit(solution)/shard_map/ppermute | solution.py:62
  142.7 1.1 fusion.30
  143.8 4.7 %collective-permute-start.6 = (bf16[256,256]{1,0:T(8,128)(2,1)S(1)}, bf16[256,256]{1,0:T(8,128)(2,1)S(1)}, u32[]{:S(2)}, u32[]{:S(2)}) collective-permute-start(bf16[256,256]{1,0:T(8,128)(2,1)S(1)} %fusion.30), channel_id=1, source_target_pairs={{0,6},{1,7},{2,0},{3,1},{4,2},{5,3},{6,4},{7,5},{8,14},{9,15},{10,... | collective-permute-start | bytes 393224 | tf_op jit(solution)/shard_map/ppermute | solution.py:72
  148.4 2.0 collective-permute-start.5
  150.4 1.8 collective-permute-start.4
  152.2 5.3 %collective-permute-done.6 = bf16[256,256]{1,0:T(8,128)(2,1)S(1)} collective-permute-done((bf16[256,256]{1,0:T(8,128)(2,1)S(1)}, bf16[256,256]{1,0:T(8,128)(2,1)S(1)}, u32[]{:S(2)}, u32[]{:S(2)}) %collective-permute-start.6) | collective-permute-done | bytes 131104 | tf_op jit(solution)/shard_map/ppermute | solution.py:72
  157.5 3.3 %collective-permute-done.5 = bf16[256,256]{1,0:T(8,128)(2,1)S(1)} collective-permute-done((bf16[256,256]{1,0:T(8,128)(2,1)S(1)}, bf16[256,256]{1,0:T(8,128)(2,1)S(1)}, u32[]{:S(2)}, u32[]{:S(2)}) %collective-permute-start.5) | collective-permute-done | bytes 131104 | tf_op jit(solution)/shard_map/ppermute | solution.py:72
  160.8 1.1 collective-permute-done.4
  162.0 0.6 gather_fusion.1
  162.7 1.6 collective-permute-start.7
  164.8 0.7 mul.249
  165.5 0.8 bitcast_select_fusion
  166.3 1.6 convert_bitcast_fusion
  168.2 3.2 %copy.62 = f32[256,4,2,256]{0,3,2,1:T(8,128)} copy(f32[256,4,2,256]{3,0,1,2:T(8,128)} %convert_bitcast_fusion) | data formatting | bytes 4194304 | tf_op jit(solution)/shard_map/convert_element_type | solution.py:178
  171.4 2.0 fusion.9
  173.5 0.8 fusion.70
  174.3 3.8 %convolution_convert_fusion = bf16[256,2048]{1,0:T(8,128)(2,1)} fusion(bf16[384,2048]{1,0:T(8,128)(2,1)S(1)} %copy-done, bf16[256,2048]{0,1:T(8,128)(2,1)S(1)} %fusion.9, bf16[2048,384]{1,0:T(8,128)(2,1)} %param.28, f32[256,384]{1,0:T(8,128)S(1)} %fusion.70), kind=kOutput, calls=%fused_computation.15 | convolution fusion | flops 806420480 | bytes 5636096 | tf_op jit(solution)/shard_map/dot_general | solution.py:182
  178.0 1.8 reshape.601
  179.9 3.1 %constant_dynamic-slice_fusion.2 = (bf16[256,4,1,256]{3,2,1,0:T(2,128)(2,1)}, bf16[256,4,1,256]{3,2,1,0:T(2,128)(2,1)S(1)}) fusion(bf16[256,4,2,256]{3,2,1,0:T(2,128)(2,1)S(1)} %reshape.601, s32[]{:T(128)S(6)} %select_n.221, s32[]{:T(128)S(6)} %select_n.222), kind=kLoop, calls=%fused_computation.113 | loop fusion | bytes 2097160 | tf_op jit(solution)/shard_map/jit(dynamic_index_in_dim)/dynamic_slice | solution.py:54
  183.3 0.7 iota_add_fusion
  184.0 0.9 add.304
  184.9 0.9 add.342
  186.0 2.3 %fusion.67 = (bf16[256,4,256]{2,0,1:T(8,128)(2,1)S(1)}, f32[256,4,256]{2,0,1:T(8,128)}) fusion(bf16[256,4,256]{2,0,1:T(8,128)(2,1)} %collective-permute-done.8, bf16[256,4,1,256]{3,2,1,0:T(2,128)(2,1)S(1)} %copy-done.3), kind=kLoop, calls=%fused_computation.160 | loop fusion | flops 1048576 | bytes 2621440 | tf_op jit(solution)/shard_map/convert_element_type | solution.py:59
  188.3 3.0 %collective-permute-start.11 = (bf16[256,256]{1,0:T(8,128)(2,1)S(1)}, bf16[256,256]{1,0:T(8,128)(2,1)S(1)}, u32[]{:S(2)}, u32[]{:S(2)}) collective-permute-start(bf16[256,256]{1,0:T(8,128)(2,1)S(1)} %get-tuple-element.13), channel_id=1, source_target_pairs={{0,6},{1,7},{2,0},{3,1},{4,2},{5,3},{6,4},{7,5},{8,14},{9,15},{10,... | collective-permute-start | bytes 393224 | tf_op jit(solution)/shard_map/ppermute | solution.py:62
  191.3 1.9 collective-permute-start.10
  193.2 1.9 collective-permute-start.9
  195.1 0.6 gather_fusion
  195.7 4.4 %collective-permute-done.10 = bf16[256,256]{1,0:T(8,128)(2,1)S(1)} collective-permute-done((bf16[256,256]{1,0:T(8,128)(2,1)S(1)}, bf16[256,256]{1,0:T(8,128)(2,1)S(1)}, u32[]{:S(2)}, u32[]{:S(2)}) %collective-permute-start.10) | collective-permute-done | bytes 131104 | tf_op jit(solution)/shard_map/ppermute | solution.py:62
  200.1 2.9 %collective-permute-done.9 = bf16[256,256]{1,0:T(8,128)(2,1)S(1)} collective-permute-done((bf16[256,256]{1,0:T(8,128)(2,1)S(1)}, bf16[256,256]{1,0:T(8,128)(2,1)S(1)}, u32[]{:S(2)}, u32[]{:S(2)}) %collective-permute-start.9) | collective-permute-done | bytes 131104 | tf_op jit(solution)/shard_map/ppermute | solution.py:62
  203.0 1.0 fusion.26
  204.1 1.8 gather_fusion.2
  205.9 8.1 %all-to-all-start.1 = ((bf16[32,8,256]{2,1,0:T(8,128)(2,1)}), bf16[32,8,256]{2,1,0:T(8,128)(2,1)S(1)}, u32[]{:S(2)}, u32[]{:S(2)}) async-start(bf16[32,8,256]{2,1,0:T(8,128)(2,1)} %bitcast.37), calls=%async_computation.1 | async-start | bytes 262144 | tf_op jit(solution)/shard_map/all_to_all | solution.py:190
  214.2 2.4 %scatter_custom_fusion.1 = bf16[256,256]{1,0:T(8,128)(2,1)} fusion(s32[256]{0:T(256)S(1)} %bitcast.143, bf16[32,256,256]{2,1,0:T(8,128)(2,1)} %slice.51, s32[]{:T(128)} %constant.204.clone.1, s32[]{:T(128)S(6)} %select_n.214, bf16[]{:T(256)} %constant.199.clone.1), kind=kCustom, calls=%fused_computation.69 | custom fusion | bytes 263172 | tf_op jit(solution)/shard_map/scatter | solution.py:106
  216.6 5.0 %all-to-all-done.1 = bf16[32,8,256]{2,1,0:T(8,128)(2,1)S(1)} async-done(((bf16[32,8,256]{2,1,0:T(8,128)(2,1)}), bf16[32,8,256]{2,1,0:T(8,128)(2,1)S(1)}, u32[]{:S(2)}, u32[]{:S(2)}) %all-to-all-start.1) | async-done | bytes 131104 | tf_op jit(solution)/shard_map/all_to_all | solution.py:190
  221.6 2.1 scatter_custom_fusion
  (80 shorter events, 3.9 us)
Async XLA Ops:
  0.6 173.6 %copy-start = (bf16[384,2048]{1,0:T(8,128)(2,1)S(1)}, bf16[384,2048]{1,0:T(8,128)(2,1)}, u32[]{:S(2)}) copy-start(bf16[384,2048]{1,0:T(8,128)(2,1)} %param.29) | copy-start | bytes 4718596
  0.6 6.9 %copy-start.4 = (bf16[256,2048]{1,0:T(8,128)(2,1)S(1)}, bf16[256,2048]{1,0:T(8,128)(2,1)}, u32[]{:S(2)}) copy-start(bf16[256,2048]{1,0:T(8,128)(2,1)} %param.15) | copy-start | bytes 3145732
  0.7 6.9 %copy-start.13 = (f32[2048]{0:T(1024)S(1)}, f32[2048]{0:T(1024)}, u32[]{:S(2)}) copy-start(f32[2048]{0:T(1024)} %param.19) | copy-start | bytes 24580
  1.7 5.9 %copy-start.12 = (bf16[2048,128]{1,0:T(8,128)(2,1)S(1)}, bf16[2048,128]{1,0:T(8,128)(2,1)}, u32[]{:S(2)}) copy-start(bf16[2048,128]{1,0:T(8,128)(2,1)} %param.21) | copy-start | bytes 1572868
  5.6 2.7 %copy-start.10 = (f32[128]{0:T(128)S(1)}, f32[128]{0:T(128)}, u32[]{:S(2)}) copy-start(f32[128]{0:T(128)} %param.24) | copy-start | bytes 1540
  11.3 66.7 %all-to-all-start = ((bf16[32,272,256]{2,1,0:T(8,128)(2,1)}), bf16[32,272,256]{2,1,0:T(8,128)(2,1)}, u32[]{:S(2)}, u32[]{:S(2)}) async-start(bf16[32,272,256]{2,1,0:T(8,128)(2,1)} %broadcast_in_dim.50), calls=%async_computation | async-start | bytes 8912896 | tf_op jit(solution)/shard_map/all_to_all | solution.py:39
  20.8 2.6 %copy-start.11 = (f32[128]{0:T(128)S(1)}, f32[128]{0:T(128)}, u32[]{:S(2)}) copy-start(f32[128]{0:T(128)} %param.23) | copy-start | bytes 1540
  22.7 56.7 %copy-start.7 = (s32[256]{0:T(256)S(1)}, s32[256]{0:T(256)}, u32[]{:S(2)}) copy-start(s32[256]{0:T(256)} %param.16) | copy-start | bytes 3076
  91.1 5.7 %copy-start.1 = (f32[256,2,8192]{2,0,1:T(8,128)}, f32[256,2,8192]{2,0,1:T(8,128)S(1)}, u32[]{:S(2)}) copy-start(f32[256,2,8192]{2,0,1:T(8,128)S(1)} %get-tuple-element.34) | copy-start | bytes 50331652
  102.2 10.1 %copy-start.6 = (bf16[256,2048]{1,0:T(8,128)(2,1)S(1)}, bf16[256,2048]{1,0:T(8,128)(2,1)}, u32[]{:S(2)}) copy-start(bf16[256,2048]{1,0:T(8,128)(2,1)} %param.25) | copy-start | bytes 3145732
  118.9 3.7 %copy-start.2 = (bf16[256,4,1,256]{3,2,1,0:T(2,128)(2,1)S(1)}, bf16[256,4,1,256]{3,2,1,0:T(2,128)(2,1)}, u32[]{:S(2)}) copy-start(bf16[256,4,1,256]{3,2,1,0:T(2,128)(2,1)} %get-tuple-element.10) | copy-start | bytes 1572868
  119.1 3.6 %collective-permute-start = (bf16[256,4,256]{2,0,1:T(8,128)(2,1)S(1)}, bf16[256,4,256]{2,0,1:T(8,128)(2,1)}, u32[]{:S(2)}, u32[]{:S(2)}) collective-permute-start(bf16[256,4,256]{2,0,1:T(8,128)(2,1)S(1)} %bitcast.130), channel_id=1, source_target_pairs={{0,1},{1,0},{2,3},{3,2},{4,5},{5,4},{6,7},{7,6},{8,9},{9,8},{10,11... | collective-permute-start | bytes 1572872 | tf_op jit(solution)/shard_map/ppermute | solution.py:56
  124.9 11.3 %collective-permute-start.3 = (bf16[256,256]{1,0:T(8,128)(2,1)S(1)}, bf16[256,256]{1,0:T(8,128)(2,1)S(1)}, u32[]{:S(2)}, u32[]{:S(2)}) collective-permute-start(bf16[256,256]{1,0:T(8,128)(2,1)S(1)} %get-tuple-element.16), channel_id=1, source_target_pairs={{0,6},{1,7},{2,0},{3,1},{4,2},{5,3},{6,4},{7,5},{8,14},{9,15},{10,... | collective-permute-start | bytes 393224 | tf_op jit(solution)/shard_map/ppermute | solution.py:62
  130.1 12.5 %collective-permute-start.2 = (bf16[256,256]{1,0:T(8,128)(2,1)S(1)}, bf16[256,256]{1,0:T(8,128)(2,1)S(1)}, u32[]{:S(2)}, u32[]{:S(2)}) collective-permute-start(bf16[256,256]{1,0:T(8,128)(2,1)S(1)} %get-tuple-element.17), channel_id=1, source_target_pairs={{0,4},{1,5},{2,6},{3,7},{4,0},{5,1},{6,2},{7,3},{8,12},{9,13},{10,... | collective-permute-start | bytes 393224 | tf_op jit(solution)/shard_map/ppermute | solution.py:62
  131.3 11.4 %collective-permute-start.1 = (bf16[256,256]{1,0:T(8,128)(2,1)S(1)}, bf16[256,256]{1,0:T(8,128)(2,1)S(1)}, u32[]{:S(2)}, u32[]{:S(2)}) collective-permute-start(bf16[256,256]{1,0:T(8,128)(2,1)S(1)} %get-tuple-element.15), channel_id=1, source_target_pairs={{0,2},{1,3},{2,4},{3,5},{4,6},{5,7},{6,0},{7,1},{8,10},{9,11},{10,... | collective-permute-start | bytes 393224 | tf_op jit(solution)/shard_map/ppermute | solution.py:62
  142.7 21.6 %copy-start.14 = (s32[64]{0:T(128)S(1)}, s32[64]{0:T(128)}, u32[]{:S(2)}) copy-start(s32[64]{0:T(128)} %param.18) | copy-start | bytes 772
  143.8 13.7 %collective-permute-start.6 = (bf16[256,256]{1,0:T(8,128)(2,1)S(1)}, bf16[256,256]{1,0:T(8,128)(2,1)S(1)}, u32[]{:S(2)}, u32[]{:S(2)}) collective-permute-start(bf16[256,256]{1,0:T(8,128)(2,1)S(1)} %fusion.30), channel_id=1, source_target_pairs={{0,6},{1,7},{2,0},{3,1},{4,2},{5,3},{6,4},{7,5},{8,14},{9,15},{10,... | collective-permute-start | bytes 393224 | tf_op jit(solution)/shard_map/ppermute | solution.py:72
  148.4 12.4 %collective-permute-start.5 = (bf16[256,256]{1,0:T(8,128)(2,1)S(1)}, bf16[256,256]{1,0:T(8,128)(2,1)S(1)}, u32[]{:S(2)}, u32[]{:S(2)}) collective-permute-start(bf16[256,256]{1,0:T(8,128)(2,1)S(1)} %fusion.30), channel_id=1, source_target_pairs={{0,4},{1,5},{2,6},{3,7},{4,0},{5,1},{6,2},{7,3},{8,12},{9,13},{10,... | collective-permute-start | bytes 393224 | tf_op jit(solution)/shard_map/ppermute | solution.py:72
  150.4 11.5 %collective-permute-start.4 = (bf16[256,256]{1,0:T(8,128)(2,1)S(1)}, bf16[256,256]{1,0:T(8,128)(2,1)S(1)}, u32[]{:S(2)}, u32[]{:S(2)}) collective-permute-start(bf16[256,256]{1,0:T(8,128)(2,1)S(1)} %fusion.30), channel_id=1, source_target_pairs={{0,2},{1,3},{2,4},{3,5},{4,6},{5,7},{6,0},{7,1},{8,10},{9,11},{10,... | collective-permute-start | bytes 393224 | tf_op jit(solution)/shard_map/ppermute | solution.py:72
  152.2 12.1 %copy-start.9 = (pred[4]{0:T(512)(128)(4,1)}, pred[4]{0:T(512)(128)(4,1)S(1)}, u32[]{:S(2)}) copy-start(pred[4]{0:T(512)(128)(4,1)S(1)} %compare_and_fusion.1) | copy-start | bytes 16
  162.7 3.7 %collective-permute-start.7 = (bf16[4,256,256]{2,1,0:T(8,128)(2,1)S(1)}, bf16[4,256,256]{2,1,0:T(8,128)(2,1)S(1)}, u32[]{:S(2)}, u32[]{:S(2)}) collective-permute-start(bf16[4,256,256]{2,1,0:T(8,128)(2,1)S(1)} %broadcast_select_fusion), channel_id=1, source_target_pairs={{0,1},{1,0},{2,3},{3,2},{4,5},{5,4},{6,7},{7,6},{8,9},{9,8},{10,11... | collective-permute-start | bytes 1572872 | tf_op jit(solution)/shard_map/ppermute | solution.py:77
  168.2 3.2 %copy-start.8 = (f32[2048]{0:T(1024)S(1)}, f32[2048]{0:T(1024)}, u32[]{:S(2)}) copy-start(f32[2048]{0:T(1024)} %param.26) | copy-start | bytes 24580
  171.4 2.1 copy-start.5
  183.0 3.0 %copy-start.3 = (bf16[256,4,1,256]{3,2,1,0:T(2,128)(2,1)S(1)}, bf16[256,4,1,256]{3,2,1,0:T(2,128)(2,1)}, u32[]{:S(2)}) copy-start(bf16[256,4,1,256]{3,2,1,0:T(2,128)(2,1)} %get-tuple-element.8) | copy-start | bytes 1572868
  183.2 2.8 %collective-permute-start.8 = (bf16[256,4,256]{2,0,1:T(8,128)(2,1)S(1)}, bf16[256,4,256]{2,0,1:T(8,128)(2,1)}, u32[]{:S(2)}, u32[]{:S(2)}) collective-permute-start(bf16[256,4,256]{2,0,1:T(8,128)(2,1)S(1)} %bitcast.131), channel_id=1, source_target_pairs={{0,1},{1,0},{2,3},{3,2},{4,5},{5,4},{6,7},{7,6},{8,9},{9,8},{10,11... | collective-permute-start | bytes 1572872 | tf_op jit(solution)/shard_map/ppermute | solution.py:56
  188.3 7.3 %collective-permute-start.11 = (bf16[256,256]{1,0:T(8,128)(2,1)S(1)}, bf16[256,256]{1,0:T(8,128)(2,1)S(1)}, u32[]{:S(2)}, u32[]{:S(2)}) collective-permute-start(bf16[256,256]{1,0:T(8,128)(2,1)S(1)} %get-tuple-element.13), channel_id=1, source_target_pairs={{0,6},{1,7},{2,0},{3,1},{4,2},{5,3},{6,4},{7,5},{8,14},{9,15},{10,... | collective-permute-start | bytes 393224 | tf_op jit(solution)/shard_map/ppermute | solution.py:62
  191.3 8.8 %collective-permute-start.10 = (bf16[256,256]{1,0:T(8,128)(2,1)S(1)}, bf16[256,256]{1,0:T(8,128)(2,1)S(1)}, u32[]{:S(2)}, u32[]{:S(2)}) collective-permute-start(bf16[256,256]{1,0:T(8,128)(2,1)S(1)} %get-tuple-element.14), channel_id=1, source_target_pairs={{0,4},{1,5},{2,6},{3,7},{4,0},{5,1},{6,2},{7,3},{8,12},{9,13},{10,... | collective-permute-start | bytes 393224 | tf_op jit(solution)/shard_map/ppermute | solution.py:62
  193.2 9.8 %collective-permute-start.9 = (bf16[256,256]{1,0:T(8,128)(2,1)S(1)}, bf16[256,256]{1,0:T(8,128)(2,1)S(1)}, u32[]{:S(2)}, u32[]{:S(2)}) collective-permute-start(bf16[256,256]{1,0:T(8,128)(2,1)S(1)} %get-tuple-element.12), channel_id=1, source_target_pairs={{0,2},{1,3},{2,4},{3,5},{4,6},{5,7},{6,0},{7,1},{8,10},{9,11},{10,... | collective-permute-start | bytes 393224 | tf_op jit(solution)/shard_map/ppermute | solution.py:62
  205.9 15.7 %all-to-all-start.1 = ((bf16[32,8,256]{2,1,0:T(8,128)(2,1)}), bf16[32,8,256]{2,1,0:T(8,128)(2,1)S(1)}, u32[]{:S(2)}, u32[]{:S(2)}) async-start(bf16[32,8,256]{2,1,0:T(8,128)(2,1)} %bitcast.37), calls=%async_computation.1 | async-start | bytes 262144 | tf_op jit(solution)/shard_map/all_to_all | solution.py:190

commit v7 on v4

--- a/solution.py
+++ b/solution.py
@@ -44,21 +44,22 @@
     return [(i, ((i // 2 + shift) % chips) * 2 + i % 2) for i in range(tp_count)]
 
 
-def scatter_sum_tp(terms, tp_count):
-    rows, width = terms.shape
+def project_reduce_tp(acts, weight, tp_count):
+    width = weight.shape[1]
     chips = tp_count // 2
     part = width // tp_count
     index = lax.axis_index("tp")
     chip, core = index // 2, index % 2
-    blocks = terms.astype(jnp.bfloat16).reshape(rows, chips, 2, part)
-    mine = lax.dynamic_index_in_dim(blocks, core, axis=2, keepdims=False)
-    other = lax.dynamic_index_in_dim(blocks, 1 - core, axis=2, keepdims=False)
+    split = weight.reshape(weight.shape[0], chips, 2, part)
+    terms = jnp.einsum("rk,kcip->icrp", acts, split, preferred_element_type=jnp.float32)
+    mine = lax.dynamic_index_in_dim(terms, core, axis=0, keepdims=False)
+    other = lax.dynamic_index_in_dim(terms, 1 - core, axis=0, keepdims=False).astype(jnp.bfloat16)
     sibling = lax.ppermute(other, "tp", [(i, i ^ 1) for i in range(tp_count)])
-    chip_sum = mine.astype(jnp.float32) + sibling.astype(jnp.float32)
-    total = lax.dynamic_index_in_dim(chip_sum, chip, axis=1, keepdims=False)
+    chip_sum = mine + sibling.astype(jnp.float32)
+    total = lax.dynamic_index_in_dim(chip_sum, chip, axis=0, keepdims=False)
     outgoing = chip_sum.astype(jnp.bfloat16)
     for shift in range(1, chips):
-        piece = lax.dynamic_index_in_dim(outgoing, (chip + shift) % chips, axis=1, keepdims=False)
+        piece = lax.dynamic_index_in_dim(outgoing, (chip + shift) % chips, axis=0, keepdims=False)
         total = total + lax.ppermute(piece, "tp", chip_shift(tp_count, shift)).astype(jnp.float32)
     return total
 
@@ -155,16 +156,15 @@
         ).reshape(rows, group, HD)
         heads_out.append((accum / total[..., None]).astype(jnp.bfloat16))
     attn = jnp.stack(heads_out, axis=1).reshape(rows, q_heads * HD)
-    terms = jnp.dot(attn, o_weight, preferred_element_type=jnp.float32)
     column = lax.axis_index("tp") * part
     own_input = lax.dynamic_slice_in_dim(xfull, column, part, 1)
-    mid = (own_input + scatter_sum_tp(terms, tp_count)).astype(jnp.bfloat16)
+    mid = (own_input + project_reduce_tp(attn, o_weight, tp_count)).astype(jnp.bfloat16)
     mid_full = gather_tp(mid, tp_count)
     normed_mid = rms(mid_full.astype(jnp.float32), norm_mid).astype(jnp.bfloat16)
     gate = jnp.dot(normed_mid, gate_weight, preferred_element_type=jnp.float32)
     upper = jnp.dot(normed_mid, up_weight, preferred_element_type=jnp.float32)
     act = (jax.nn.silu(gate) * upper).astype(jnp.bfloat16)
-    feed = scatter_sum_tp(jnp.dot(act, down_weight, preferred_element_type=jnp.float32), tp_count)
+    feed = project_reduce_tp(act, down_weight, tp_count)
     out = (mid.astype(jnp.float32) + feed).astype(jnp.bfloat16)
     blocks_dev = rows // BLK
     share = BLK // seq_count

time: 223 us -> 216 us (0.969)
  waiting for transfers between devices: 80.2 us -> 77 us
  other arithmetic: 25.2 us -> 22.4 us
    dynamic_slice x2 -> x0, local copies, waits for them, and re-layouts: 6.3 us -> none  [scatter_sum_tp(): mine = lax.dynamic_index_in_dim(blocks, core, axis=2, keepdims=False)]
    reshape x2, local copies, waits for them, and re-layouts: 3.65 us -> 6.49 us  [project_reduce_tp(): split = weight.reshape(weight.shape[0], chips, 2, part)]
    all_to_all x2, waiting for transfers between devices: 46.9 us -> 44.4 us  [gather_seq(): lax.all_to_all(copies, 'seq', split_axis=0, concat_axis=0, tiled=True)]
    unnamed x32 -> x28, local copies, waits for them, and re-layouts: 6.11 us -> 7.11 us
  transfers between devices with their start and end apart: 15 -> 15, of which waited for: 13 -> 14; matrix products, arithmetic and copies ran while one was open for 8% -> 11% of each run, Pallas kernels for 0% -> 0%
where the time goes in v7:
time: 216 us; the launch traced here: 215 us
  waiting for transfers between devices  77 us (36%)
  starting transfers between devices  57.5 us (27%)
  local copies, waits for them, and re-layouts  30.9 us (14%)
  matrix products  26.6 us (12%)
  other arithmetic  22.4 us (10%)
    all_to_all x2, waiting for transfers between devices, gather_seq(): lax.all_to_all(copies, 'seq', split_axis=0, concat_axis=0, tiled=True)  44.4 us
    ppermute x6, waiting for transfers between devices, project_reduce_tp(): lax.ppermute(piece, 'tp', chip_shift(tp_count, shift)).astype(jnp.float32)  18 us
    all_to_all x2, starting transfers between devices, gather_seq(): lax.all_to_all(copies, 'seq', split_axis=0, concat_axis=0, tiled=True)  16.1 us
    ppermute x6, starting transfers between devices, project_reduce_tp(): lax.ppermute(piece, 'tp', chip_shift(tp_count, shift)).astype(jnp.float32)  15.7 us
    all_to_all x1, starting transfers between devices, body(): lax.all_to_all(out[send_rows], 'seq', split_axis=0, concat_axis=0, tiled=...  14 us
    dot_general x1, matrix products, body(): jnp.dot(weights.astype(jnp.bfloat16).reshape(rows * group, seq_count * ro...  10.1 us
    ppermute x3, starting transfers between devices, gather_tp(): lax.ppermute(block, 'tp', chip_shift(tp_count, shift))  8.07 us
    unnamed x28, local copies, waits for them, and re-layouts  7.11 us
  transfers between devices with their start and end apart: 15, of which 14 were waited for; matrix products, arithmetic and copies ran while one was open for 11% of the time, Pallas kernels for 0%

profile of v7, /device:TPU:1, one launch (start us, length us, event | category | flops | bytes accessed | tf_op | source)
XLA Modules:
  0.0 215.5 jit_solution(15405569827569404745)
XLA Ops:
  0.7 1.5 broadcast_in_dim.47
  2.2 9.2 %all-to-all-start = ((s32[32,1,256]{2,1,0:T(1,128)}), s32[32,1,256]{2,1,0:T(1,128)S(1)}, u32[]{:S(2)}, u32[]{:S(2)}) async-start(s32[32,1,256]{2,1,0:T(1,128)} %broadcast_in_dim.47), calls=%async_computation | async-start | bytes 65536 | tf_op jit(solution)/shard_map/all_to_all | solution.py:39
  11.4 1.5 multiply_reduce_fusion
  12.9 2.0 multiply_reduce_fusion.2
  14.9 0.2 reduce-window.9
  15.2 1.6 fusion.14
  17.0 0.3 fusion.58
  17.4 1.2 all-to-all-done
  18.6 2.4 %broadcast_in_dim.55 = bf16[32,256,256]{2,1,0:T(8,128)(2,1)} broadcast(bf16[256,256]{1,0:T(8,128)(2,1)S(1)} %copy.51), dimensions={1,2} | broadcast | bytes 4325376 | tf_op jit(solution)/shard_map/broadcast_in_dim | solution.py:38
  21.0 6.9 %all-to-all-start.1 = ((bf16[32,256,256]{2,1,0:T(8,128)(2,1)}), bf16[32,256,256]{2,1,0:T(8,128)(2,1)}, u32[]{:S(2)}, u32[]{:S(2)}) async-start(bf16[32,256,256]{2,1,0:T(8,128)(2,1)} %broadcast_in_dim.55), calls=%async_computation.1 | async-start | bytes 8388608 | tf_op jit(solution)/shard_map/all_to_all | solution.py:39
  27.9 1.9 multiply_reduce_fusion.1
  29.9 2.6 %reshape.584 = bf16[256,4,2,256]{3,2,1,0:T(2,128)(2,1)} reshape(bf16[256,2048]{1,0:T(8,128)(2,1)} %param.25) | data formatting | bytes 2097152 | tf_op jit(solution)/shard_map/reshape | solution.py:53
  32.6 0.5 multiply_cosine_fusion
  33.1 0.1 multiply_multiply_fusion
  33.3 0.2 subtract_convert_fusion
  33.4 2.9 %compare_and_fusion = pred[256,8192]{1,0:T(8,128)(4,1)} fusion(s32[8192]{0:T(1024)S(1)} %bitcast.135, s32[256]{0:T(256)S(1)} %copy-done.7, s32[256]{0:T(256)S(1)} %select_reduce_fusion), kind=kLoop, calls=%fused_computation.12 | loop fusion | flops 6291456 | bytes 2131968 | tf_op jit(solution)/shard_map/and | solution.py:138
  36.3 43.2 %all-to-all-done.1 = bf16[32,256,256]{2,1,0:T(8,128)(2,1)} async-done(((bf16[32,256,256]{2,1,0:T(8,128)(2,1)}), bf16[32,256,256]{2,1,0:T(8,128)(2,1)}, u32[]{:S(2)}, u32[]{:S(2)}) %all-to-all-start.1) | async-done | bytes 4194336 | tf_op jit(solution)/shard_map/all_to_all | solution.py:39
  79.5 5.7 %fusion = (f32[256,2]{0,1:T(2,128)S(1)}, f32[256,2,8192]{2,0,1:T(8,128)S(1)}) fusion(pred[256,8192]{1,0:T(8,128)(4,1)} %compare_and_fusion, bf16[8192,256]{1,0:T(8,128)(2,1)} %bitcast.12, bf16[256,2,64]{2,0,1:T(8,128)(2,1)S(1)} %get-tuple-element.13, bf16[256,2,64]{2,0,1:T(8,128)(2,1)S(1)} %get-tuple-element.12), kind=kOutput, calls=%fused_computation.7 | convolution fusion | flops 1086586368 | bytes 21104640 | tf_op jit(solution)/shard_map/dot_general | solution.py:145
  85.2 5.7 %copy-done.1 = f32[256,2,8192]{2,0,1:T(8,128)} copy-done((f32[256,2,8192]{2,0,1:T(8,128)}, f32[256,2,8192]{2,0,1:T(8,128)S(1)}, u32[]{:S(2)}) %copy-start.1) | copy-done | bytes 16777240
  90.9 5.3 %fusion.1 = f32[256,2]{0,1:T(2,128)S(1)} fusion(f32[256,2,8192]{2,0,1:T(8,128)S(1)} %get-tuple-element.23, f32[256,2]{0,1:T(2,128)S(1)} %broadcast_maximum_fusion, pred[256,8192]{1,0:T(8,128)(4,1)S(1)} %copy-done.2), kind=kLoop, calls=%fused_computation.8 | loop fusion | flops 20971008 | bytes 18878464 | tf_op jit(solution)/shard_map/reduce_sum | solution.py:151
  96.2 10.1 %fusion.18 = bf16[256,2,128]{0,2,1:T(8,128)(2,1)S(1)} fusion(bf16[8192,256]{1,0:T(8,128)(2,1)} %bitcast.12, f32[256,2,8192]{2,0,1:T(8,128)} %copy-done.1, f32[256,2]{0,1:T(2,128)S(1)} %broadcast_maximum_fusion, pred[256,8192]{1,0:T(8,128)(4,1)S(1)} %copy-done.2, f32[256,2]{0,1:T(2,128)S(1)} %fusion.1), kind=kOutput, calls=%fused_computation.32 | convolution fusion | flops 1094844416 | bytes 21106688 | tf_op jit(solution)/shard_map/dot_general | solution.py:152
  106.3 0.5 fusion.21
  106.8 1.3 copy-done.3
  108.1 2.8 %collective-permute-start = (bf16[4,256,256]{2,1,0:T(8,128)(2,1)S(1)}, bf16[4,256,256]{2,1,0:T(8,128)(2,1)}, u32[]{:S(2)}, u32[]{:S(2)}) collective-permute-start(bf16[4,256,256]{2,1,0:T(8,128)(2,1)S(1)} %fusion.23), channel_id=1, source_target_pairs={{0,1},{1,0},{2,3},{3,2},{4,5},{5,4},{6,7},{7,6},{8,9},{9,8},{10,11... | collective-permute-start | bytes 1572872 | tf_op jit(solution)/shard_map/ppermute | solution.py:57
  110.9 1.7 collective-permute-done
  112.6 2.5 %fusion.72 = (bf16[4,256,256]{2,1,0:T(8,128)(2,1)S(1)}, f32[4,256,256]{2,1,0:T(8,128)}) fusion(bf16[4,256,256]{2,1,0:T(8,128)(2,1)} %collective-permute-done, f32[256,4,2,256]{3,0,2,1:T(8,128)} %copy-done.3, s32[]{:T(128)S(6)} %select_n.212), kind=kLoop, calls=%fused_computation.148 | loop fusion | flops 786432 | bytes 3145732 | tf_op jit(solution)/shard_map/convert_element_type | solution.py:60
  115.1 3.1 %collective-permute-start.1 = (bf16[256,256]{1,0:T(8,128)(2,1)S(1)}, bf16[256,256]{1,0:T(8,128)(2,1)S(1)}, u32[]{:S(2)}, u32[]{:S(2)}) collective-permute-start(bf16[256,256]{1,0:T(8,128)(2,1)S(1)} %get-tuple-element.9), channel_id=1, source_target_pairs={{0,2},{1,3},{2,4},{3,5},{4,6},{5,7},{6,0},{7,1},{8,10},{9,11},{10,... | collective-permute-start | bytes 393224 | tf_op jit(solution)/shard_map/ppermute | solution.py:63
  118.2 4.2 %collective-permute-start.2 = (bf16[256,256]{1,0:T(8,128)(2,1)S(1)}, bf16[256,256]{1,0:T(8,128)(2,1)S(1)}, u32[]{:S(2)}, u32[]{:S(2)}) collective-permute-start(bf16[256,256]{1,0:T(8,128)(2,1)S(1)} %get-tuple-element.11), channel_id=1, source_target_pairs={{0,4},{1,5},{2,6},{3,7},{4,0},{5,1},{6,2},{7,3},{8,12},{9,13},{10,... | collective-permute-start | bytes 393224 | tf_op jit(solution)/shard_map/ppermute | solution.py:63
  122.4 2.4 %collective-permute-start.3 = (bf16[256,256]{1,0:T(8,128)(2,1)S(1)}, bf16[256,256]{1,0:T(8,128)(2,1)S(1)}, u32[]{:S(2)}, u32[]{:S(2)}) collective-permute-start(bf16[256,256]{1,0:T(8,128)(2,1)S(1)} %get-tuple-element.10), channel_id=1, source_target_pairs={{0,6},{1,7},{2,0},{3,1},{4,2},{5,3},{6,4},{7,5},{8,14},{9,15},{10,... | collective-permute-start | bytes 393224 | tf_op jit(solution)/shard_map/ppermute | solution.py:63
  124.8 1.6 convert_element_type.109
  126.4 0.3 collective-permute-done.1
  126.7 4.7 %collective-permute-done.2 = bf16[256,256]{1,0:T(8,128)(2,1)S(1)} collective-permute-done((bf16[256,256]{1,0:T(8,128)(2,1)S(1)}, bf16[256,256]{1,0:T(8,128)(2,1)S(1)}, u32[]{:S(2)}, u32[]{:S(2)}) %collective-permute-start.2) | collective-permute-done | bytes 131104 | tf_op jit(solution)/shard_map/ppermute | solution.py:63
  131.4 3.2 %collective-permute-done.3 = bf16[256,256]{1,0:T(8,128)(2,1)S(1)} collective-permute-done((bf16[256,256]{1,0:T(8,128)(2,1)S(1)}, bf16[256,256]{1,0:T(8,128)(2,1)S(1)}, u32[]{:S(2)}, u32[]{:S(2)}) %collective-permute-start.3) | collective-permute-done | bytes 131104 | tf_op jit(solution)/shard_map/ppermute | solution.py:63
  134.6 1.1 fusion.37
  135.7 1.5 collective-permute-start.4
  137.2 4.0 %collective-permute-start.5 = (bf16[256,256]{1,0:T(8,128)(2,1)S(1)}, bf16[256,256]{1,0:T(8,128)(2,1)S(1)}, u32[]{:S(2)}, u32[]{:S(2)}) collective-permute-start(bf16[256,256]{1,0:T(8,128)(2,1)S(1)} %fusion.37), channel_id=1, source_target_pairs={{0,4},{1,5},{2,6},{3,7},{4,0},{5,1},{6,2},{7,3},{8,12},{9,13},{10,... | collective-permute-start | bytes 393224 | tf_op jit(solution)/shard_map/ppermute | solution.py:73
  141.2 2.6 %collective-permute-start.6 = (bf16[256,256]{1,0:T(8,128)(2,1)S(1)}, bf16[256,256]{1,0:T(8,128)(2,1)S(1)}, u32[]{:S(2)}, u32[]{:S(2)}) collective-permute-start(bf16[256,256]{1,0:T(8,128)(2,1)S(1)} %fusion.37), channel_id=1, source_target_pairs={{0,6},{1,7},{2,0},{3,1},{4,2},{5,3},{6,4},{7,5},{8,14},{9,15},{10,... | collective-permute-start | bytes 393224 | tf_op jit(solution)/shard_map/ppermute | solution.py:73
  143.8 0.5 collective-permute-done.4
  144.3 5.3 %collective-permute-done.5 = bf16[256,256]{1,0:T(8,128)(2,1)S(1)} collective-permute-done((bf16[256,256]{1,0:T(8,128)(2,1)S(1)}, bf16[256,256]{1,0:T(8,128)(2,1)S(1)}, u32[]{:S(2)}, u32[]{:S(2)}) %collective-permute-start.5) | collective-permute-done | bytes 131104 | tf_op jit(solution)/shard_map/ppermute | solution.py:73
  149.6 1.3 collective-permute-done.6
  150.9 0.6 gather_fusion.1
  151.7 0.6 collective-permute-start.7
  152.7 3.9 %reshape.585 = bf16[384,4,2,256]{3,2,1,0:T(2,128)(2,1)} reshape(bf16[384,2048]{1,0:T(8,128)(2,1)} %param.29) | data formatting | bytes 3145728 | tf_op jit(solution)/shard_map/reshape | solution.py:53
  156.7 0.4 fusion.6
  157.1 1.6 convert_bitcast_fusion
  158.7 2.9 %copy.56 = f32[256,4,2,256]{0,3,2,1:T(8,128)} copy(f32[256,4,2,256]{3,0,1,2:T(8,128)} %convert_bitcast_fusion) | data formatting | bytes 4194304 | tf_op jit(solution)/shard_map/convert_element_type | solution.py:163
  161.6 2.0 fusion.9
  163.7 0.7 fusion.73
  164.4 4.1 %fusion.10 = f32[256,4,2,256]{3,0,2,1:T(8,128)} fusion(bf16[384,4,2,256]{3,2,1,0:T(2,128)(2,1)} %reshape.585, bf16[256,2048]{0,1:T(8,128)(2,1)S(1)} %fusion.9, bf16[2048,384]{1,0:T(8,128)(2,1)S(1)} %copy-done, f32[256,384]{1,0:T(8,128)S(1)} %fusion.73), kind=kOutput, calls=%fused_computation.24 | convolution fusion | flops 805896192 | bytes 6684672 | tf_op jit(solution)/shard_map/rk,kcip->icrp/dot_general | solution.py:54
  168.6 1.3 fusion.24
  170.2 0.6 gather_fusion
  170.7 1.1 collective-permute-done.8
  171.8 1.4 fusion.71
  173.2 0.7 dynamic-slice_bitcast_fusion.2
  173.9 3.7 %collective-permute-start.10 = (bf16[256,256]{1,0:T(8,128)(2,1)}, bf16[256,256]{1,0:T(8,128)(2,1)S(1)}, u32[]{:S(2)}, u32[]{:S(2)}) collective-permute-start(bf16[256,256]{1,0:T(8,128)(2,1)} %get-tuple-element.8), channel_id=1, source_target_pairs={{0,4},{1,5},{2,6},{3,7},{4,0},{5,1},{6,2},{7,3},{8,12},{9,13},{10,... | collective-permute-start | bytes 393224 | tf_op jit(solution)/shard_map/ppermute | solution.py:63
  177.6 1.7 collective-permute-start.11
  179.3 0.6 collective-permute-start.9
  180.1 2.8 %collective-permute-done.10 = bf16[256,256]{1,0:T(8,128)(2,1)S(1)} collective-permute-done((bf16[256,256]{1,0:T(8,128)(2,1)}, bf16[256,256]{1,0:T(8,128)(2,1)S(1)}, u32[]{:S(2)}, u32[]{:S(2)}) %collective-permute-start.10) | collective-permute-done | bytes 131104 | tf_op jit(solution)/shard_map/ppermute | solution.py:63
  183.0 6.8 %collective-permute-done.11 = bf16[256,256]{1,0:T(8,128)(2,1)S(1)} collective-permute-done((bf16[256,256]{1,0:T(8,128)(2,1)S(1)}, bf16[256,256]{1,0:T(8,128)(2,1)S(1)}, u32[]{:S(2)}, u32[]{:S(2)}) %collective-permute-start.11) | collective-permute-done | bytes 131104 | tf_op jit(solution)/shard_map/ppermute | solution.py:63
  190.0 1.8 gather_fusion.2
  191.8 14.0 %all-to-all-start.2 = ((bf16[32,8,256]{2,1,0:T(8,128)(2,1)}), bf16[32,8,256]{2,1,0:T(8,128)(2,1)S(1)}, u32[]{:S(2)}, u32[]{:S(2)}) async-start(bf16[32,8,256]{2,1,0:T(8,128)(2,1)} %bitcast.45), calls=%async_computation.2 | async-start | bytes 262144 | tf_op jit(solution)/shard_map/all_to_all | solution.py:175
  206.1 2.4 %scatter_custom_fusion.1 = bf16[256,256]{1,0:T(8,128)(2,1)} fusion(s32[256]{0:T(256)S(1)} %bitcast.144, bf16[32,256,256]{2,1,0:T(8,128)(2,1)} %all-to-all-done.1, s32[]{:T(128)} %constant.185.clone.1, s32[]{:T(128)S(6)} %select_n.204, bf16[]{:T(256)} %constant.180.clone.1), kind=kCustom, calls=%fused_computation.71 | custom fusion | bytes 263172 | tf_op jit(solution)/shard_map/scatter | solution.py:91
  208.6 4.9 %all-to-all-done.2 = bf16[32,8,256]{2,1,0:T(8,128)(2,1)S(1)} async-done(((bf16[32,8,256]{2,1,0:T(8,128)(2,1)}), bf16[32,8,256]{2,1,0:T(8,128)(2,1)S(1)}, u32[]{:S(2)}, u32[]{:S(2)}) %all-to-all-start.2) | async-done | bytes 131104 | tf_op jit(solution)/shard_map/all_to_all | solution.py:175
  213.4 2.1 scatter_custom_fusion
  (68 shorter events, 2.3 us)
Async XLA Ops:
  0.6 163.8 %copy-start = (bf16[2048,384]{1,0:T(8,128)(2,1)S(1)}, bf16[2048,384]{1,0:T(8,128)(2,1)}, u32[]{:S(2)}) copy-start(bf16[2048,384]{1,0:T(8,128)(2,1)} %param.28) | copy-start | bytes 4718596
  0.6 14.5 %copy-start.7 = (s32[256]{0:T(256)S(1)}, s32[256]{0:T(256)}, u32[]{:S(2)}) copy-start(s32[256]{0:T(256)} %param.16) | copy-start | bytes 3076
  0.7 14.6 %copy-start.4 = (bf16[256,2048]{1,0:T(8,128)(2,1)S(1)}, bf16[256,2048]{1,0:T(8,128)(2,1)}, u32[]{:S(2)}) copy-start(bf16[256,2048]{1,0:T(8,128)(2,1)} %param.15) | copy-start | bytes 3145732
  0.7 14.6 %copy-start.11 = (f32[2048]{0:T(1024)S(1)}, f32[2048]{0:T(1024)}, u32[]{:S(2)}) copy-start(f32[2048]{0:T(1024)} %param.19) | copy-start | bytes 24580
  0.7 14.2 %copy-start.12 = (s32[8]{0:T(128)S(1)}, s32[8]{0:T(128)}, u32[]{:S(2)}) copy-start(s32[8]{0:T(128)} %param.17) | copy-start | bytes 100
  2.2 16.4 %all-to-all-start = ((s32[32,1,256]{2,1,0:T(1,128)}), s32[32,1,256]{2,1,0:T(1,128)S(1)}, u32[]{:S(2)}, u32[]{:S(2)}) async-start(s32[32,1,256]{2,1,0:T(1,128)} %broadcast_in_dim.47), calls=%async_computation | async-start | bytes 65536 | tf_op jit(solution)/shard_map/all_to_all | solution.py:39
  12.9 3.9 %copy-start.9 = (f32[128]{0:T(128)S(1)}, f32[128]{0:T(128)}, u32[]{:S(2)}) copy-start(f32[128]{0:T(128)} %param.24) | copy-start | bytes 1540
  21.0 58.4 %all-to-all-start.1 = ((bf16[32,256,256]{2,1,0:T(8,128)(2,1)}), bf16[32,256,256]{2,1,0:T(8,128)(2,1)}, u32[]{:S(2)}, u32[]{:S(2)}) async-start(bf16[32,256,256]{2,1,0:T(8,128)(2,1)} %broadcast_in_dim.55), calls=%async_computation.1 | async-start | bytes 8388608 | tf_op jit(solution)/shard_map/all_to_all | solution.py:39
  29.8 3.3 %copy-start.10 = (f32[128]{0:T(128)S(1)}, f32[128]{0:T(128)}, u32[]{:S(2)}) copy-start(f32[128]{0:T(128)} %param.23) | copy-start | bytes 1540
  79.5 11.4 %copy-start.2 = (pred[256,8192]{1,0:T(8,128)(4,1)S(1)}, pred[256,8192]{1,0:T(8,128)(4,1)}, u32[]{:S(2)}) copy-start(pred[256,8192]{1,0:T(8,128)(4,1)} %compare_and_fusion) | copy-start | bytes 6291460
  85.2 5.7 %copy-start.1 = (f32[256,2,8192]{2,0,1:T(8,128)}, f32[256,2,8192]{2,0,1:T(8,128)S(1)}, u32[]{:S(2)}) copy-start(f32[256,2,8192]{2,0,1:T(8,128)S(1)} %get-tuple-element.23) | copy-start | bytes 50331652
  96.2 10.1 %copy-start.5 = (bf16[256,4,2,256]{3,2,1,0:T(2,128)(2,1)S(1)}, bf16[256,4,2,256]{3,2,1,0:T(2,128)(2,1)}, u32[]{:S(2)}) copy-start(bf16[256,4,2,256]{3,2,1,0:T(2,128)(2,1)} %reshape.584) | copy-start | bytes 3145732
  106.8 1.3 copy-start.3
  108.1 4.4 %collective-permute-start = (bf16[4,256,256]{2,1,0:T(8,128)(2,1)S(1)}, bf16[4,256,256]{2,1,0:T(8,128)(2,1)}, u32[]{:S(2)}, u32[]{:S(2)}) collective-permute-start(bf16[4,256,256]{2,1,0:T(8,128)(2,1)S(1)} %fusion.23), channel_id=1, source_target_pairs={{0,1},{1,0},{2,3},{3,2},{4,5},{5,4},{6,7},{7,6},{8,9},{9,8},{10,11... | collective-permute-start | bytes 1572872 | tf_op jit(solution)/shard_map/ppermute | solution.py:57
  115.1 11.6 %collective-permute-start.1 = (bf16[256,256]{1,0:T(8,128)(2,1)S(1)}, bf16[256,256]{1,0:T(8,128)(2,1)S(1)}, u32[]{:S(2)}, u32[]{:S(2)}) collective-permute-start(bf16[256,256]{1,0:T(8,128)(2,1)S(1)} %get-tuple-element.9), channel_id=1, source_target_pairs={{0,2},{1,3},{2,4},{3,5},{4,6},{5,7},{6,0},{7,1},{8,10},{9,11},{10,... | collective-permute-start | bytes 393224 | tf_op jit(solution)/shard_map/ppermute | solution.py:63
  118.2 13.2 %collective-permute-start.2 = (bf16[256,256]{1,0:T(8,128)(2,1)S(1)}, bf16[256,256]{1,0:T(8,128)(2,1)S(1)}, u32[]{:S(2)}, u32[]{:S(2)}) collective-permute-start(bf16[256,256]{1,0:T(8,128)(2,1)S(1)} %get-tuple-element.11), channel_id=1, source_target_pairs={{0,4},{1,5},{2,6},{3,7},{4,0},{5,1},{6,2},{7,3},{8,12},{9,13},{10,... | collective-permute-start | bytes 393224 | tf_op jit(solution)/shard_map/ppermute | solution.py:63
  122.4 12.2 %collective-permute-start.3 = (bf16[256,256]{1,0:T(8,128)(2,1)S(1)}, bf16[256,256]{1,0:T(8,128)(2,1)S(1)}, u32[]{:S(2)}, u32[]{:S(2)}) collective-permute-start(bf16[256,256]{1,0:T(8,128)(2,1)S(1)} %get-tuple-element.10), channel_id=1, source_target_pairs={{0,6},{1,7},{2,0},{3,1},{4,2},{5,3},{6,4},{7,5},{8,14},{9,15},{10,... | collective-permute-start | bytes 393224 | tf_op jit(solution)/shard_map/ppermute | solution.py:63
  134.6 17.7 %copy-start.13 = (s32[64]{0:T(128)S(1)}, s32[64]{0:T(128)}, u32[]{:S(2)}) copy-start(s32[64]{0:T(128)} %param.18) | copy-start | bytes 772
  135.7 8.6 %collective-permute-start.4 = (bf16[256,256]{1,0:T(8,128)(2,1)S(1)}, bf16[256,256]{1,0:T(8,128)(2,1)S(1)}, u32[]{:S(2)}, u32[]{:S(2)}) collective-permute-start(bf16[256,256]{1,0:T(8,128)(2,1)S(1)} %fusion.37), channel_id=1, source_target_pairs={{0,2},{1,3},{2,4},{3,5},{4,6},{5,7},{6,0},{7,1},{8,10},{9,11},{10,... | collective-permute-start | bytes 393224 | tf_op jit(solution)/shard_map/ppermute | solution.py:73
  137.2 12.4 %collective-permute-start.5 = (bf16[256,256]{1,0:T(8,128)(2,1)S(1)}, bf16[256,256]{1,0:T(8,128)(2,1)S(1)}, u32[]{:S(2)}, u32[]{:S(2)}) collective-permute-start(bf16[256,256]{1,0:T(8,128)(2,1)S(1)} %fusion.37), channel_id=1, source_target_pairs={{0,4},{1,5},{2,6},{3,7},{4,0},{5,1},{6,2},{7,3},{8,12},{9,13},{10,... | collective-permute-start | bytes 393224 | tf_op jit(solution)/shard_map/ppermute | solution.py:73
  141.2 9.7 %collective-permute-start.6 = (bf16[256,256]{1,0:T(8,128)(2,1)S(1)}, bf16[256,256]{1,0:T(8,128)(2,1)S(1)}, u32[]{:S(2)}, u32[]{:S(2)}) collective-permute-start(bf16[256,256]{1,0:T(8,128)(2,1)S(1)} %fusion.37), channel_id=1, source_target_pairs={{0,6},{1,7},{2,0},{3,1},{4,2},{5,3},{6,4},{7,5},{8,14},{9,15},{10,... | collective-permute-start | bytes 393224 | tf_op jit(solution)/shard_map/ppermute | solution.py:73
  151.7 5.1 %collective-permute-start.7 = (bf16[4,256,256]{2,1,0:T(8,128)(2,1)S(1)}, bf16[4,256,256]{2,1,0:T(8,128)(2,1)S(1)}, u32[]{:S(2)}, u32[]{:S(2)}) collective-permute-start(bf16[4,256,256]{2,1,0:T(8,128)(2,1)S(1)} %broadcast_select_fusion), channel_id=1, source_target_pairs={{0,1},{1,0},{2,3},{3,2},{4,5},{5,4},{6,7},{7,6},{8,9},{9,8},{10,11... | collective-permute-start | bytes 1572872 | tf_op jit(solution)/shard_map/ppermute | solution.py:78
  158.7 2.9 %copy-start.8 = (f32[2048]{0:T(1024)S(1)}, f32[2048]{0:T(1024)}, u32[]{:S(2)}) copy-start(f32[2048]{0:T(1024)} %param.26) | copy-start | bytes 24580
  161.6 2.1 copy-start.6
  169.8 2.0 collective-permute-start.8
  173.9 9.1 %collective-permute-start.10 = (bf16[256,256]{1,0:T(8,128)(2,1)}, bf16[256,256]{1,0:T(8,128)(2,1)S(1)}, u32[]{:S(2)}, u32[]{:S(2)}) collective-permute-start(bf16[256,256]{1,0:T(8,128)(2,1)} %get-tuple-element.8), channel_id=1, source_target_pairs={{0,4},{1,5},{2,6},{3,7},{4,0},{5,1},{6,2},{7,3},{8,12},{9,13},{10,... | collective-permute-start | bytes 393224 | tf_op jit(solution)/shard_map/ppermute | solution.py:63
  177.6 12.2 %collective-permute-start.11 = (bf16[256,256]{1,0:T(8,128)(2,1)S(1)}, bf16[256,256]{1,0:T(8,128)(2,1)S(1)}, u32[]{:S(2)}, u32[]{:S(2)}) collective-permute-start(bf16[256,256]{1,0:T(8,128)(2,1)S(1)} %get-tuple-element.7), channel_id=1, source_target_pairs={{0,6},{1,7},{2,0},{3,1},{4,2},{5,3},{6,4},{7,5},{8,14},{9,15},{10,... | collective-permute-start | bytes 393224 | tf_op jit(solution)/shard_map/ppermute | solution.py:63
  179.3 10.6 %collective-permute-start.9 = (bf16[256,256]{1,0:T(8,128)(2,1)S(1)}, bf16[256,256]{1,0:T(8,128)(2,1)S(1)}, u32[]{:S(2)}, u32[]{:S(2)}) collective-permute-start(bf16[256,256]{1,0:T(8,128)(2,1)S(1)} %get-tuple-element.6), channel_id=1, source_target_pairs={{0,2},{1,3},{2,4},{3,5},{4,6},{5,7},{6,0},{7,1},{8,10},{9,11},{10,... | collective-permute-start | bytes 393224 | tf_op jit(solution)/shard_map/ppermute | solution.py:63
  191.8 21.6 %all-to-all-start.2 = ((bf16[32,8,256]{2,1,0:T(8,128)(2,1)}), bf16[32,8,256]{2,1,0:T(8,128)(2,1)S(1)}, u32[]{:S(2)}, u32[]{:S(2)}) async-start(bf16[32,8,256]{2,1,0:T(8,128)(2,1)} %bitcast.45), calls=%async_computation.2 | async-start | bytes 262144 | tf_op jit(solution)/shard_map/all_to_all | solution.py:175

commit v8 on v5

--- a/solution.py
+++ b/solution.py
@@ -45,21 +45,22 @@
     return [(i, ((i // 2 + shift) % chips) * 2 + i % 2) for i in range(tp_count)]
 
 
-def scatter_sum_tp(terms, tp_count):
-    rows, width = terms.shape
+def project_reduce_tp(acts, weight, tp_count):
+    width = weight.shape[1]
     chips = tp_count // 2
     part = width // tp_count
     index = lax.axis_index("tp")
     chip, core = index // 2, index % 2
-    blocks = terms.astype(jnp.bfloat16).reshape(rows, chips, 2, part)
-    mine = lax.dynamic_index_in_dim(blocks, core, axis=2, keepdims=False)
-    other = lax.dynamic_index_in_dim(blocks, 1 - core, axis=2, keepdims=False)
+    split = weight.reshape(weight.shape[0], chips, 2, part)
+    terms = jnp.einsum("rk,kcip->icrp", acts, split, preferred_element_type=jnp.float32)
+    mine = lax.dynamic_index_in_dim(terms, core, axis=0, keepdims=False)
+    other = lax.dynamic_index_in_dim(terms, 1 - core, axis=0, keepdims=False).astype(jnp.bfloat16)
     sibling = lax.ppermute(other, "tp", [(i, i ^ 1) for i in range(tp_count)])
-    chip_sum = mine.astype(jnp.float32) + sibling.astype(jnp.float32)
-    total = lax.dynamic_index_in_dim(chip_sum, chip, axis=1, keepdims=False)
+    chip_sum = mine + sibling.astype(jnp.float32)
+    total = lax.dynamic_index_in_dim(chip_sum, chip, axis=0, keepdims=False)
     outgoing = chip_sum.astype(jnp.bfloat16)
     for shift in range(1, chips):
-        piece = lax.dynamic_index_in_dim(outgoing, (chip + shift) % chips, axis=1, keepdims=False)
+        piece = lax.dynamic_index_in_dim(outgoing, (chip + shift) % chips, axis=0, keepdims=False)
         total = total + lax.ppermute(piece, "tp", chip_shift(tp_count, shift)).astype(jnp.float32)
     return total
 
@@ -92,8 +93,9 @@
     return cache.reshape(rows // BLK, BLK, arrived.shape[1])
 
 
-KEY_CHUNK = 512
+KEY_CHUNK = 2048
 QUERY_TILE = 256
+UNROLL = 4
 
 
 def attend_kernel(q_ref, qtok_ref, qbeg_ref, kv_ref, ktok_ref, out_ref):
@@ -112,18 +114,20 @@
             query, keys, (((1,), (1,)), ((), ())), preferred_element_type=jnp.float32
         ) * scale
         mask = (ktok >= qbeg) & (ktok <= qtok)
-        return jnp.where(mask, raw, -1e30), mask, start
+        return jnp.where(mask, raw, -1e30), start
 
     def find_top(chunk, top):
-        score, _, _ = scores(chunk)
+        score, _ = scores(chunk)
         return jnp.maximum(top, jnp.max(score, axis=1, keepdims=True))
 
-    top = lax.fori_loop(0, chunks, find_top, jnp.full((tile, 1), -1e30, jnp.float32))
+    top = lax.fori_loop(
+        0, chunks, find_top, jnp.full((tile, 1), -1e30, jnp.float32), unroll=UNROLL
+    )
 
     def accumulate(chunk, carry):
         total, accum = carry
-        score, mask, start = scores(chunk)
-        weights = jnp.where(mask, jnp.exp(score - top), 0.0)
+        score, start = scores(chunk)
+        weights = jnp.exp(score - top)
         values = kv_ref[pl.ds(start, KEY_CHUNK), pl.ds(HD, HD)]
         total = total + jnp.sum(weights, axis=1, keepdims=True)
         accum = accum + jnp.dot(
@@ -136,6 +140,7 @@
         chunks,
         accumulate,
         (jnp.zeros((tile, 1), jnp.float32), jnp.zeros((tile, HD), jnp.float32)),
+        unroll=UNROLL,
     )
     out_ref[...] = (accum / total).astype(out_ref.dtype)
 
@@ -198,8 +203,7 @@
     knorm = rotary(rms(keys, k_gain), pos).astype(jnp.bfloat16)
     stacked = jnp.stack([knorm, values], axis=2).reshape(rows, kv_heads * 2 * HD)
     pieces = gather_seq(stacked, seq_count)
-    stacked, order_late = lax.optimization_barrier((stacked, token_order))
-    piece_tokens = gather_seq(order_late, seq_count)
+    piece_tokens = gather_seq(token_order, seq_count)
     flat = pieces.reshape(seq_count * rows, kv_heads * 2 * HD)
     key_tokens = piece_tokens.reshape(1, seq_count * rows)
     query_tokens = jnp.repeat(token_order, group)[:, None]
@@ -211,16 +215,15 @@
             attend(qhead, query_tokens, query_begins, flat, key_tokens, head).reshape(rows, group, HD)
         )
     attn = jnp.stack(heads_out, axis=1).reshape(rows, q_heads * HD)
-    terms = jnp.dot(attn, o_weight, preferred_element_type=jnp.float32)
     column = lax.axis_index("tp") * part
     own_input = lax.dynamic_slice_in_dim(xfull, column, part, 1)
-    mid = (own_input + scatter_sum_tp(terms, tp_count)).astype(jnp.bfloat16)
+    mid = (own_input + project_reduce_tp(attn, o_weight, tp_count)).astype(jnp.bfloat16)
     mid_full = gather_tp(mid, tp_count)
     normed_mid = rms(mid_full.astype(jnp.float32), norm_mid).astype(jnp.bfloat16)
     gate = jnp.dot(normed_mid, gate_weight, preferred_element_type=jnp.float32)
     upper = jnp.dot(normed_mid, up_weight, preferred_element_type=jnp.float32)
     act = (jax.nn.silu(gate) * upper).astype(jnp.bfloat16)
-    feed = scatter_sum_tp(jnp.dot(act, down_weight, preferred_element_type=jnp.float32), tp_count)
+    feed = project_reduce_tp(act, down_weight, tp_count)
     out = (mid.astype(jnp.float32) + feed).astype(jnp.bfloat16)
     blocks_dev = rows // BLK
     share = BLK // seq_count

time: 228 us -> 207 us (0.908)
  Pallas kernels: 29.7 us -> 13.3 us
  other arithmetic: 20.2 us -> 17.4 us
    pallas_call x1, Pallas kernels: 29.7 us -> 13.3 us  [attend(): pl.pallas_call(attend_kernel, grid=(count // tile,), in_specs=[pl.BlockSp...]
    dynamic_slice x2 -> x0, local copies, waits for them, and re-layouts: 6.27 us -> none  [scatter_sum_tp(): mine = lax.dynamic_index_in_dim(blocks, core, axis=2, keepdims=False)]
    reshape x2, local copies, waits for them, and re-layouts: 3.65 us -> 6.47 us  [project_reduce_tp(): split = weight.reshape(weight.shape[0], chips, 2, part)]
    all_to_all x2, waiting for transfers between devices: 46.5 us -> 43.9 us  [gather_seq(): lax.all_to_all(copies, 'seq', split_axis=0, concat_axis=0, tiled=True)]
  transfers between devices with their start and end apart: 15 -> 15, of which waited for: 12 -> 12; matrix products, arithmetic and copies ran while one was open for 9% -> 12% of each run, Pallas kernels for 0% -> 0%
where the time goes in v8:
time: 207 us; the launch traced here: 206 us
  waiting for transfers between devices  78.4 us (38%)
  starting transfers between devices  56.7 us (27%)
  local copies, waits for them, and re-layouts  28.1 us (14%)
  other arithmetic  17.4 us (8%)
  Pallas kernels  13.3 us (6%)
  matrix products  11 us (5%)
    all_to_all x2, waiting for transfers between devices, gather_seq(): lax.all_to_all(copies, 'seq', split_axis=0, concat_axis=0, tiled=True)  43.9 us
    ppermute x6, waiting for transfers between devices, project_reduce_tp(): lax.ppermute(piece, 'tp', chip_shift(tp_count, shift)).astype(jnp.float32)  19.7 us
    all_to_all x2, starting transfers between devices, gather_seq(): lax.all_to_all(copies, 'seq', split_axis=0, concat_axis=0, tiled=True)  17.1 us
    ppermute x6, starting transfers between devices, project_reduce_tp(): lax.ppermute(piece, 'tp', chip_shift(tp_count, shift)).astype(jnp.float32)  15.5 us
    pallas_call x1, Pallas kernels, attend(): pl.pallas_call(attend_kernel, grid=(count // tile,), in_specs=[pl.BlockSp...  13.3 us
    all_to_all x1, starting transfers between devices, body(): lax.all_to_all(out[send_rows], 'seq', split_axis=0, concat_axis=0, tiled=...  12.7 us
    ppermute x3, starting transfers between devices, gather_tp(): lax.ppermute(block, 'tp', chip_shift(tp_count, shift))  7.88 us
    ppermute x3, waiting for transfers between devices, gather_tp(): lax.ppermute(block, 'tp', chip_shift(tp_count, shift))  7.23 us
  transfers between devices with their start and end apart: 15, of which 12 were waited for; matrix products, arithmetic and copies ran while one was open for 12% of the time, Pallas kernels for 0%

profile of v8, /device:TPU:1, one launch (start us, length us, event | category | flops | bytes accessed | tf_op | source)
XLA Modules:
  0.0 206.0 jit_solution(4748160204254022140)
XLA Ops:
  0.7 1.5 broadcast_in_dim.33
  2.1 9.2 %all-to-all-start = ((s32[32,1,256]{2,1,0:T(1,128)}), s32[32,1,256]{2,1,0:T(1,128)S(1)}, u32[]{:S(2)}, u32[]{:S(2)}) async-start(s32[32,1,256]{2,1,0:T(1,128)} %broadcast_in_dim.33), calls=%async_computation | async-start | bytes 65536 | tf_op jit(solution)/shard_map/all_to_all | solution.py:40
  11.4 1.5 multiply_reduce_fusion
  12.9 0.8 reduce-window.9
  13.7 0.7 bitcast_subtract_fusion
  14.5 0.8 select_reduce_fusion
  15.2 0.7 subtract_convert_fusion.1
  15.9 2.0 multiply_reduce_fusion.2
  17.9 0.6 fusion.7
  18.6 0.3 fusion.43
  19.1 2.4 %broadcast_in_dim.42 = bf16[32,256,256]{2,1,0:T(8,128)(2,1)} broadcast(bf16[256,256]{1,0:T(8,128)(2,1)S(1)} %copy.52), dimensions={1,2} | broadcast | bytes 4325376 | tf_op jit(solution)/shard_map/broadcast_in_dim | solution.py:39
  21.5 7.9 %all-to-all-start.1 = ((bf16[32,256,256]{2,1,0:T(8,128)(2,1)}), bf16[32,256,256]{2,1,0:T(8,128)(2,1)}, u32[]{:S(2)}, u32[]{:S(2)}) async-start(bf16[32,256,256]{2,1,0:T(8,128)(2,1)} %broadcast_in_dim.42), calls=%async_computation.1 | async-start | bytes 8388608 | tf_op jit(solution)/shard_map/all_to_all | solution.py:40
  29.4 1.9 multiply_reduce_fusion.1
  31.3 0.3 multiply_cosine_fusion.1
  32.1 0.8 broadcast_in_dim_reshape.11.qbeg_ref
  33.1 0.8 broadcast_in_dim_reshape.10.qtok_ref
  33.9 2.6 %reshape.526 = bf16[256,4,2,256]{3,2,1,0:T(2,128)(2,1)} reshape(bf16[256,2048]{1,0:T(8,128)(2,1)} %param.25) | data formatting | bytes 2097152 | tf_op jit(solution)/shard_map/reshape | solution.py:54
  36.5 0.8 pad_maximum_fusion.1.q_ref
  37.3 43.9 %all-to-all-done.1 = bf16[32,256,256]{2,1,0:T(8,128)(2,1)} async-done(((bf16[32,256,256]{2,1,0:T(8,128)(2,1)}), bf16[32,256,256]{2,1,0:T(8,128)(2,1)}, u32[]{:S(2)}, u32[]{:S(2)}) %all-to-all-start.1) | async-done | bytes 4194336 | tf_op jit(solution)/shard_map/all_to_all | solution.py:40
  81.2 13.3 %shard_map.158 = bf16[512,128]{1,0:T(8,128)(2,1)} custom-call(bf16[512,128]{1,0:T(8,128)(2,1)} %pad_maximum_fusion.1.q_ref, s32[512,1]{1,0:T(8,128)} %broadcast_in_dim_reshape.10.qtok_ref, s32[512,1]{1,0:T(8,128)} %broadcast_in_dim_reshape.11.qbeg_ref, bf16[8192,256]{1,0:T(8,128)(2,1)} %bitcast.13.kv_ref, s32[1,8192]{1,0:T(1,128)} %bitcast.127), custom_call_target="tpu_custom_call" | custom-call | tf_op jit(solution)/shard_map/pallas_call | solution.py:152
  94.5 1.0 reshape.573
  95.4 1.7 fusion.8
  97.1 1.3 copy-done.1
  98.5 2.8 %collective-permute-start = (bf16[4,256,256]{2,1,0:T(8,128)(2,1)S(1)}, bf16[4,256,256]{2,1,0:T(8,128)(2,1)}, u32[]{:S(2)}, u32[]{:S(2)}) collective-permute-start(bf16[4,256,256]{2,1,0:T(8,128)(2,1)S(1)} %fusion.10), channel_id=1, source_target_pairs={{0,1},{1,0},{2,3},{3,2},{4,5},{5,4},{6,7},{7,6},{8,9},{9,8},{10,11... | collective-permute-start | bytes 1572872 | tf_op jit(solution)/shard_map/ppermute | solution.py:58
  101.3 1.7 collective-permute-done
  102.9 2.5 %fusion.53 = (bf16[4,256,256]{2,1,0:T(8,128)(2,1)S(1)}, f32[4,256,256]{2,1,0:T(8,128)}) fusion(bf16[4,256,256]{2,1,0:T(8,128)(2,1)} %collective-permute-done, f32[256,4,2,256]{3,0,2,1:T(8,128)} %copy-done.1, s32[]{:T(128)S(6)} %select_n.203), kind=kLoop, calls=%fused_computation.129 | loop fusion | flops 786432 | bytes 3145732 | tf_op jit(solution)/shard_map/convert_element_type | solution.py:61
  105.5 3.1 %collective-permute-start.1 = (bf16[256,256]{1,0:T(8,128)(2,1)S(1)}, bf16[256,256]{1,0:T(8,128)(2,1)S(1)}, u32[]{:S(2)}, u32[]{:S(2)}) collective-permute-start(bf16[256,256]{1,0:T(8,128)(2,1)S(1)} %get-tuple-element.9), channel_id=1, source_target_pairs={{0,2},{1,3},{2,4},{3,5},{4,6},{5,7},{6,0},{7,1},{8,10},{9,11},{10,... | collective-permute-start | bytes 393224 | tf_op jit(solution)/shard_map/ppermute | solution.py:64
  108.6 4.2 %collective-permute-start.2 = (bf16[256,256]{1,0:T(8,128)(2,1)S(1)}, bf16[256,256]{1,0:T(8,128)(2,1)S(1)}, u32[]{:S(2)}, u32[]{:S(2)}) collective-permute-start(bf16[256,256]{1,0:T(8,128)(2,1)S(1)} %get-tuple-element.11), channel_id=1, source_target_pairs={{0,4},{1,5},{2,6},{3,7},{4,0},{5,1},{6,2},{7,3},{8,12},{9,13},{10,... | collective-permute-start | bytes 393224 | tf_op jit(solution)/shard_map/ppermute | solution.py:64
  112.8 2.4 %collective-permute-start.3 = (bf16[256,256]{1,0:T(8,128)(2,1)S(1)}, bf16[256,256]{1,0:T(8,128)(2,1)S(1)}, u32[]{:S(2)}, u32[]{:S(2)}) collective-permute-start(bf16[256,256]{1,0:T(8,128)(2,1)S(1)} %get-tuple-element.10), channel_id=1, source_target_pairs={{0,6},{1,7},{2,0},{3,1},{4,2},{5,3},{6,4},{7,5},{8,14},{9,15},{10,... | collective-permute-start | bytes 393224 | tf_op jit(solution)/shard_map/ppermute | solution.py:64
  115.2 1.6 convert_element_type.102
  116.7 0.3 collective-permute-done.1
  117.1 4.7 %collective-permute-done.2 = bf16[256,256]{1,0:T(8,128)(2,1)S(1)} collective-permute-done((bf16[256,256]{1,0:T(8,128)(2,1)S(1)}, bf16[256,256]{1,0:T(8,128)(2,1)S(1)}, u32[]{:S(2)}, u32[]{:S(2)}) %collective-permute-start.2) | collective-permute-done | bytes 131104 | tf_op jit(solution)/shard_map/ppermute | solution.py:64
  121.8 3.3 %collective-permute-done.3 = bf16[256,256]{1,0:T(8,128)(2,1)S(1)} collective-permute-done((bf16[256,256]{1,0:T(8,128)(2,1)S(1)}, bf16[256,256]{1,0:T(8,128)(2,1)S(1)}, u32[]{:S(2)}, u32[]{:S(2)}) %collective-permute-start.3) | collective-permute-done | bytes 131104 | tf_op jit(solution)/shard_map/ppermute | solution.py:64
  125.1 1.1 fusion.24
  126.2 1.3 collective-permute-start.4
  127.5 4.2 %collective-permute-start.5 = (bf16[256,256]{1,0:T(8,128)(2,1)S(1)}, bf16[256,256]{1,0:T(8,128)(2,1)S(1)}, u32[]{:S(2)}, u32[]{:S(2)}) collective-permute-start(bf16[256,256]{1,0:T(8,128)(2,1)S(1)} %fusion.24), channel_id=1, source_target_pairs={{0,4},{1,5},{2,6},{3,7},{4,0},{5,1},{6,2},{7,3},{8,12},{9,13},{10,... | collective-permute-start | bytes 393224 | tf_op jit(solution)/shard_map/ppermute | solution.py:74
  131.7 2.4 %collective-permute-start.6 = (bf16[256,256]{1,0:T(8,128)(2,1)S(1)}, bf16[256,256]{1,0:T(8,128)(2,1)S(1)}, u32[]{:S(2)}, u32[]{:S(2)}) collective-permute-start(bf16[256,256]{1,0:T(8,128)(2,1)S(1)} %fusion.24), channel_id=1, source_target_pairs={{0,6},{1,7},{2,0},{3,1},{4,2},{5,3},{6,4},{7,5},{8,14},{9,15},{10,... | collective-permute-start | bytes 393224 | tf_op jit(solution)/shard_map/ppermute | solution.py:74
  134.1 0.7 collective-permute-done.4
  134.8 5.7 %collective-permute-done.5 = bf16[256,256]{1,0:T(8,128)(2,1)S(1)} collective-permute-done((bf16[256,256]{1,0:T(8,128)(2,1)S(1)}, bf16[256,256]{1,0:T(8,128)(2,1)S(1)}, u32[]{:S(2)}, u32[]{:S(2)}) %collective-permute-start.5) | collective-permute-done | bytes 131104 | tf_op jit(solution)/shard_map/ppermute | solution.py:74
  140.4 0.9 collective-permute-done.6
  141.4 0.6 gather_fusion.1
  142.1 0.6 collective-permute-start.7
  143.1 3.8 %reshape.527 = bf16[384,4,2,256]{3,2,1,0:T(2,128)(2,1)} reshape(bf16[384,2048]{1,0:T(8,128)(2,1)} %param.29) | data formatting | bytes 3145728 | tf_op jit(solution)/shard_map/reshape | solution.py:54
  147.1 0.4 fusion
  147.5 1.6 convert_bitcast_fusion
  149.0 2.9 %copy.57 = f32[256,4,2,256]{0,3,2,1:T(8,128)} copy(f32[256,4,2,256]{3,0,1,2:T(8,128)} %convert_bitcast_fusion) | data formatting | bytes 4194304 | tf_op jit(solution)/shard_map/convert_element_type | solution.py:222
  152.0 2.0 fusion.2
  154.1 0.7 fusion.54
  154.8 4.1 %fusion.3 = f32[256,4,2,256]{3,0,2,1:T(8,128)} fusion(bf16[384,4,2,256]{3,2,1,0:T(2,128)(2,1)} %reshape.527, bf16[256,2048]{0,1:T(8,128)(2,1)S(1)} %fusion.2, bf16[2048,384]{1,0:T(8,128)(2,1)S(1)} %copy-done, f32[256,384]{1,0:T(8,128)S(1)} %fusion.54), kind=kOutput, calls=%fused_computation.13 | convolution fusion | flops 805896192 | bytes 6684672 | tf_op jit(solution)/shard_map/rk,kcip->icrp/dot_general | solution.py:55
  159.0 1.3 fusion.11
  160.6 0.6 gather_fusion
  161.2 1.1 collective-permute-done.8
  162.3 1.4 fusion.52
  163.6 0.7 dynamic-slice_bitcast_fusion.2
  164.3 3.5 %collective-permute-start.10 = (bf16[256,256]{1,0:T(8,128)(2,1)}, bf16[256,256]{1,0:T(8,128)(2,1)S(1)}, u32[]{:S(2)}, u32[]{:S(2)}) collective-permute-start(bf16[256,256]{1,0:T(8,128)(2,1)} %get-tuple-element.8), channel_id=1, source_target_pairs={{0,4},{1,5},{2,6},{3,7},{4,0},{5,1},{6,2},{7,3},{8,12},{9,13},{10,... | collective-permute-start | bytes 393224 | tf_op jit(solution)/shard_map/ppermute | solution.py:64
  167.9 1.9 collective-permute-start.11
  169.7 0.5 collective-permute-start.9
  170.4 3.0 %collective-permute-done.10 = bf16[256,256]{1,0:T(8,128)(2,1)S(1)} collective-permute-done((bf16[256,256]{1,0:T(8,128)(2,1)}, bf16[256,256]{1,0:T(8,128)(2,1)S(1)}, u32[]{:S(2)}, u32[]{:S(2)}) %collective-permute-start.10) | collective-permute-done | bytes 131104 | tf_op jit(solution)/shard_map/ppermute | solution.py:64
  173.4 8.3 %collective-permute-done.11 = bf16[256,256]{1,0:T(8,128)(2,1)S(1)} collective-permute-done((bf16[256,256]{1,0:T(8,128)(2,1)S(1)}, bf16[256,256]{1,0:T(8,128)(2,1)S(1)}, u32[]{:S(2)}, u32[]{:S(2)}) %collective-permute-start.11) | collective-permute-done | bytes 131104 | tf_op jit(solution)/shard_map/ppermute | solution.py:64
  181.8 1.8 gather_fusion.2
  183.6 12.7 %all-to-all-start.2 = ((bf16[32,8,256]{2,1,0:T(8,128)(2,1)}), bf16[32,8,256]{2,1,0:T(8,128)(2,1)S(1)}, u32[]{:S(2)}, u32[]{:S(2)}) async-start(bf16[32,8,256]{2,1,0:T(8,128)(2,1)} %bitcast.44), calls=%async_computation.2 | async-start | bytes 262144 | tf_op jit(solution)/shard_map/all_to_all | solution.py:234
  196.6 2.4 %scatter_custom_fusion.1 = bf16[256,256]{1,0:T(8,128)(2,1)} fusion(s32[256]{0:T(256)S(1)} %bitcast.134, bf16[32,256,256]{2,1,0:T(8,128)(2,1)} %all-to-all-done.1, s32[]{:T(128)} %constant.181.clone.1, s32[]{:T(128)S(6)} %select_n.197, bf16[]{:T(256)} %constant.176.clone.1), kind=kCustom, calls=%fused_computation.52 | custom fusion | bytes 263172 | tf_op jit(solution)/shard_map/scatter | solution.py:92
  199.0 4.9 %all-to-all-done.2 = bf16[32,8,256]{2,1,0:T(8,128)(2,1)S(1)} async-done(((bf16[32,8,256]{2,1,0:T(8,128)(2,1)}), bf16[32,8,256]{2,1,0:T(8,128)(2,1)S(1)}, u32[]{:S(2)}, u32[]{:S(2)}) %all-to-all-start.2) | async-done | bytes 131104 | tf_op jit(solution)/shard_map/all_to_all | solution.py:234
  204.0 2.1 %scatter_custom_fusion = bf16[256,256]{1,0:T(8,128)(2,1)} fusion(s32[256]{0:T(256)S(1)} %bitcast.133, bf16[32,8,256]{2,1,0:T(8,128)(2,1)S(1)} %all-to-all-done.2, bf16[]{:T(256)} %constant.176.clone.1), kind=kCustom, calls=%fused_computation.54 | custom fusion | bytes 262146 | tf_op jit(solution)/shard_map/scatter | solution.py:239
  (69 shorter events, 2.5 us)
Async XLA Ops:
  0.6 154.2 %copy-start = (bf16[2048,384]{1,0:T(8,128)(2,1)S(1)}, bf16[2048,384]{1,0:T(8,128)(2,1)}, u32[]{:S(2)}) copy-start(bf16[2048,384]{1,0:T(8,128)(2,1)} %param.28) | copy-start | bytes 4718596
  0.6 17.2 %copy-start.2 = (bf16[256,2048]{1,0:T(8,128)(2,1)S(1)}, bf16[256,2048]{1,0:T(8,128)(2,1)}, u32[]{:S(2)}) copy-start(bf16[256,2048]{1,0:T(8,128)(2,1)} %param.15) | copy-start | bytes 3145732
  0.7 17.2 %copy-start.11 = (f32[2048]{0:T(1024)S(1)}, f32[2048]{0:T(1024)}, u32[]{:S(2)}) copy-start(f32[2048]{0:T(1024)} %param.19) | copy-start | bytes 24580
  2.1 16.9 %all-to-all-start = ((s32[32,1,256]{2,1,0:T(1,128)}), s32[32,1,256]{2,1,0:T(1,128)S(1)}, u32[]{:S(2)}, u32[]{:S(2)}) async-start(s32[32,1,256]{2,1,0:T(1,128)} %broadcast_in_dim.33), calls=%async_computation | async-start | bytes 65536 | tf_op jit(solution)/shard_map/all_to_all | solution.py:40
  13.7 4.2 %copy-start.10 = (bf16[2048,128]{1,0:T(8,128)(2,1)S(1)}, bf16[2048,128]{1,0:T(8,128)(2,1)}, u32[]{:S(2)}) copy-start(bf16[2048,128]{1,0:T(8,128)(2,1)} %param.22) | copy-start | bytes 1572868
  15.9 2.6 %copy-start.8 = (f32[128]{0:T(128)S(1)}, f32[128]{0:T(128)}, u32[]{:S(2)}) copy-start(f32[128]{0:T(128)} %param.24) | copy-start | bytes 1540
  19.1 2.5 %copy-start.4 = (s32[32,1,256]{2,1,0:T(1,128)}, s32[32,1,256]{2,1,0:T(1,128)S(1)}, u32[]{:S(2)}) copy-start(s32[32,1,256]{2,1,0:T(1,128)S(1)} %all-to-all-done) | copy-start | bytes 98308
  21.5 59.6 %all-to-all-start.1 = ((bf16[32,256,256]{2,1,0:T(8,128)(2,1)}), bf16[32,256,256]{2,1,0:T(8,128)(2,1)}, u32[]{:S(2)}, u32[]{:S(2)}) async-start(bf16[32,256,256]{2,1,0:T(8,128)(2,1)} %broadcast_in_dim.42), calls=%async_computation.1 | async-start | bytes 8388608 | tf_op jit(solution)/shard_map/all_to_all | solution.py:40
  29.4 2.3 %copy-start.9 = (f32[128]{0:T(128)S(1)}, f32[128]{0:T(128)}, u32[]{:S(2)}) copy-start(f32[128]{0:T(128)} %param.23) | copy-start | bytes 1540
  29.4 3.6 %copy-start.6 = (s32[256]{0:T(256)S(1)}, s32[256]{0:T(256)}, u32[]{:S(2)}) copy-start(s32[256]{0:T(256)} %param.16) | copy-start | bytes 3076
  97.1 1.3 copy-start.1
  98.5 4.4 %collective-permute-start = (bf16[4,256,256]{2,1,0:T(8,128)(2,1)S(1)}, bf16[4,256,256]{2,1,0:T(8,128)(2,1)}, u32[]{:S(2)}, u32[]{:S(2)}) collective-permute-start(bf16[4,256,256]{2,1,0:T(8,128)(2,1)S(1)} %fusion.10), channel_id=1, source_target_pairs={{0,1},{1,0},{2,3},{3,2},{4,5},{5,4},{6,7},{7,6},{8,9},{9,8},{10,11... | collective-permute-start | bytes 1572872 | tf_op jit(solution)/shard_map/ppermute | solution.py:58
  105.5 11.6 %collective-permute-start.1 = (bf16[256,256]{1,0:T(8,128)(2,1)S(1)}, bf16[256,256]{1,0:T(8,128)(2,1)S(1)}, u32[]{:S(2)}, u32[]{:S(2)}) collective-permute-start(bf16[256,256]{1,0:T(8,128)(2,1)S(1)} %get-tuple-element.9), channel_id=1, source_target_pairs={{0,2},{1,3},{2,4},{3,5},{4,6},{5,7},{6,0},{7,1},{8,10},{9,11},{10,... | collective-permute-start | bytes 393224 | tf_op jit(solution)/shard_map/ppermute | solution.py:64
  108.6 13.2 %collective-permute-start.2 = (bf16[256,256]{1,0:T(8,128)(2,1)S(1)}, bf16[256,256]{1,0:T(8,128)(2,1)S(1)}, u32[]{:S(2)}, u32[]{:S(2)}) collective-permute-start(bf16[256,256]{1,0:T(8,128)(2,1)S(1)} %get-tuple-element.11), channel_id=1, source_target_pairs={{0,4},{1,5},{2,6},{3,7},{4,0},{5,1},{6,2},{7,3},{8,12},{9,13},{10,... | collective-permute-start | bytes 393224 | tf_op jit(solution)/shard_map/ppermute | solution.py:64
  112.8 12.3 %collective-permute-start.3 = (bf16[256,256]{1,0:T(8,128)(2,1)S(1)}, bf16[256,256]{1,0:T(8,128)(2,1)S(1)}, u32[]{:S(2)}, u32[]{:S(2)}) collective-permute-start(bf16[256,256]{1,0:T(8,128)(2,1)S(1)} %get-tuple-element.10), channel_id=1, source_target_pairs={{0,6},{1,7},{2,0},{3,1},{4,2},{5,3},{6,4},{7,5},{8,14},{9,15},{10,... | collective-permute-start | bytes 393224 | tf_op jit(solution)/shard_map/ppermute | solution.py:64
  125.1 17.6 %copy-start.12 = (s32[64]{0:T(128)S(1)}, s32[64]{0:T(128)}, u32[]{:S(2)}) copy-start(s32[64]{0:T(128)} %param.18) | copy-start | bytes 772
  126.2 8.6 %collective-permute-start.4 = (bf16[256,256]{1,0:T(8,128)(2,1)S(1)}, bf16[256,256]{1,0:T(8,128)(2,1)S(1)}, u32[]{:S(2)}, u32[]{:S(2)}) collective-permute-start(bf16[256,256]{1,0:T(8,128)(2,1)S(1)} %fusion.24), channel_id=1, source_target_pairs={{0,2},{1,3},{2,4},{3,5},{4,6},{5,7},{6,0},{7,1},{8,10},{9,11},{10,... | collective-permute-start | bytes 393224 | tf_op jit(solution)/shard_map/ppermute | solution.py:74
  127.5 13.0 %collective-permute-start.5 = (bf16[256,256]{1,0:T(8,128)(2,1)S(1)}, bf16[256,256]{1,0:T(8,128)(2,1)S(1)}, u32[]{:S(2)}, u32[]{:S(2)}) collective-permute-start(bf16[256,256]{1,0:T(8,128)(2,1)S(1)} %fusion.24), channel_id=1, source_target_pairs={{0,4},{1,5},{2,6},{3,7},{4,0},{5,1},{6,2},{7,3},{8,12},{9,13},{10,... | collective-permute-start | bytes 393224 | tf_op jit(solution)/shard_map/ppermute | solution.py:74
  131.7 9.7 %collective-permute-start.6 = (bf16[256,256]{1,0:T(8,128)(2,1)S(1)}, bf16[256,256]{1,0:T(8,128)(2,1)S(1)}, u32[]{:S(2)}, u32[]{:S(2)}) collective-permute-start(bf16[256,256]{1,0:T(8,128)(2,1)S(1)} %fusion.24), channel_id=1, source_target_pairs={{0,6},{1,7},{2,0},{3,1},{4,2},{5,3},{6,4},{7,5},{8,14},{9,15},{10,... | collective-permute-start | bytes 393224 | tf_op jit(solution)/shard_map/ppermute | solution.py:74
  142.1 5.0 %collective-permute-start.7 = (bf16[4,256,256]{2,1,0:T(8,128)(2,1)S(1)}, bf16[4,256,256]{2,1,0:T(8,128)(2,1)S(1)}, u32[]{:S(2)}, u32[]{:S(2)}) collective-permute-start(bf16[4,256,256]{2,1,0:T(8,128)(2,1)S(1)} %broadcast_select_fusion), channel_id=1, source_target_pairs={{0,1},{1,0},{2,3},{3,2},{4,5},{5,4},{6,7},{7,6},{8,9},{9,8},{10,11... | collective-permute-start | bytes 1572872 | tf_op jit(solution)/shard_map/ppermute | solution.py:79
  149.0 3.0 %copy-start.7 = (f32[2048]{0:T(1024)S(1)}, f32[2048]{0:T(1024)}, u32[]{:S(2)}) copy-start(f32[2048]{0:T(1024)} %param.26) | copy-start | bytes 24580
  152.0 2.1 copy-start.3
  154.8 5.7 %copy-start.5 = (s32[32,1,256]{2,1,0:T(1,128)S(1)}, s32[32,1,256]{2,1,0:T(1,128)}, u32[]{:S(2)}) copy-start(s32[32,1,256]{2,1,0:T(1,128)} %copy-done.4) | copy-start | bytes 98308
  160.3 2.0 collective-permute-start.8
  164.3 9.1 %collective-permute-start.10 = (bf16[256,256]{1,0:T(8,128)(2,1)}, bf16[256,256]{1,0:T(8,128)(2,1)S(1)}, u32[]{:S(2)}, u32[]{:S(2)}) collective-permute-start(bf16[256,256]{1,0:T(8,128)(2,1)} %get-tuple-element.8), channel_id=1, source_target_pairs={{0,4},{1,5},{2,6},{3,7},{4,0},{5,1},{6,2},{7,3},{8,12},{9,13},{10,... | collective-permute-start | bytes 393224 | tf_op jit(solution)/shard_map/ppermute | solution.py:64
  167.9 13.9 %collective-permute-start.11 = (bf16[256,256]{1,0:T(8,128)(2,1)S(1)}, bf16[256,256]{1,0:T(8,128)(2,1)S(1)}, u32[]{:S(2)}, u32[]{:S(2)}) collective-permute-start(bf16[256,256]{1,0:T(8,128)(2,1)S(1)} %get-tuple-element.7), channel_id=1, source_target_pairs={{0,6},{1,7},{2,0},{3,1},{4,2},{5,3},{6,4},{7,5},{8,14},{9,15},{10,... | collective-permute-start | bytes 393224 | tf_op jit(solution)/shard_map/ppermute | solution.py:64
  169.7 12.0 %collective-permute-start.9 = (bf16[256,256]{1,0:T(8,128)(2,1)S(1)}, bf16[256,256]{1,0:T(8,128)(2,1)S(1)}, u32[]{:S(2)}, u32[]{:S(2)}) collective-permute-start(bf16[256,256]{1,0:T(8,128)(2,1)S(1)} %get-tuple-element.6), channel_id=1, source_target_pairs={{0,2},{1,3},{2,4},{3,5},{4,6},{5,7},{6,0},{7,1},{8,10},{9,11},{10,... | collective-permute-start | bytes 393224 | tf_op jit(solution)/shard_map/ppermute | solution.py:64
  183.6 20.4 %all-to-all-start.2 = ((bf16[32,8,256]{2,1,0:T(8,128)(2,1)}), bf16[32,8,256]{2,1,0:T(8,128)(2,1)S(1)}, u32[]{:S(2)}, u32[]{:S(2)}) async-start(bf16[32,8,256]{2,1,0:T(8,128)(2,1)} %bitcast.44), calls=%async_computation.2 | async-start | bytes 262144 | tf_op jit(solution)/shard_map/all_to_all | solution.py:234

commit v9 on v8

--- a/solution.py
+++ b/solution.py
@@ -73,12 +73,13 @@
     arrived = [block] + [
         lax.ppermute(block, "tp", chip_shift(tp_count, shift)) for shift in range(1, chips)
     ]
-    by_shift = jnp.stack(arrived, axis=0)
-    order = (chip - jnp.arange(chips, dtype=jnp.int32)) % chips
-    own_core = jnp.take(by_shift, order, axis=0)
-    other_core = lax.ppermute(own_core, "tp", [(i, i ^ 1) for i in range(tp_count)])
-    both = jnp.where(core == 0, jnp.stack([own_core, other_core]), jnp.stack([other_core, own_core]))
-    return both.transpose(2, 1, 0, 3).reshape(rows, tp_count * part)
+    other_core = lax.ppermute(jnp.stack(arrived), "tp", [(i, i ^ 1) for i in range(tp_count)])
+    full = jnp.zeros((rows, tp_count * part), block.dtype)
+    for shift in range(chips):
+        source = (chip - shift) % chips
+        full = lax.dynamic_update_slice(full, arrived[shift], (0, (2 * source + core) * part))
+        full = lax.dynamic_update_slice(full, other_core[shift], (0, (2 * source + 1 - core) * part))
+    return full
 
 
 def build_cache(pieces, piece_tokens, rows, seq_count):

time: 207 us -> 205 us (level)
  other arithmetic: 17.4 us -> 15.3 us
    convert_element_type x3 -> x0, other arithmetic: 4.72 us -> none  [the longest x1 2.05 us: body(): rms(mid_full.astype(jnp.float32), norm_mid).astype(jnp.bfloat16)]
    convert_element_type x1 -> x0, local copies, waits for them, and re-layouts: 2.95 us -> none  [body(): mid_full.astype(jnp.float32)]
  transfers between devices with their start and end apart: 15 -> 15, of which waited for: 12 -> 12; matrix products, arithmetic and copies ran while one was open for 12% -> 14% of each run, Pallas kernels for 0% -> 0%
where the time goes in v9:
time: 205 us; the launch traced here: 203 us
  waiting for transfers between devices  76.6 us (37%)
  starting transfers between devices  57 us (28%)
  local copies, waits for them, and re-layouts  29.1 us (14%)
  other arithmetic  15.3 us (7%)
  Pallas kernels  13.3 us (6%)
  matrix products  11.1 us (5%)
    all_to_all x2, waiting for transfers between devices, gather_seq(): lax.all_to_all(copies, 'seq', split_axis=0, concat_axis=0, tiled=True)  44.2 us
    ppermute x6, waiting for transfers between devices, project_reduce_tp(): lax.ppermute(piece, 'tp', chip_shift(tp_count, shift)).astype(jnp.float32)  17.6 us
    all_to_all x2, starting transfers between devices, gather_seq(): lax.all_to_all(copies, 'seq', split_axis=0, concat_axis=0, tiled=True)  17.1 us
    ppermute x6, starting transfers between devices, project_reduce_tp(): lax.ppermute(piece, 'tp', chip_shift(tp_count, shift)).astype(jnp.float32)  16.1 us
    pallas_call x1, Pallas kernels, attend(): pl.pallas_call(attend_kernel, grid=(count // tile,), in_specs=[pl.BlockSp...  13.3 us
    all_to_all x1, starting transfers between devices, body(): lax.all_to_all(out[send_rows], 'seq', split_axis=0, concat_axis=0, tiled=...  12.2 us
    ppermute x3, starting transfers between devices, gather_tp(): lax.ppermute(block, 'tp', chip_shift(tp_count, shift))  8.17 us
    ppermute x3, waiting for transfers between devices, gather_tp(): lax.ppermute(block, 'tp', chip_shift(tp_count, shift))  7.07 us
  transfers between devices with their start and end apart: 15, of which 12 were waited for; matrix products, arithmetic and copies ran while one was open for 14% of the time, Pallas kernels for 0%

profile of v9, /device:TPU:1, one launch (start us, length us, event | category | flops | bytes accessed | tf_op | source)
XLA Modules:
  0.0 203.5 jit_solution(1860579129301330535)
XLA Ops:
  0.7 1.5 broadcast_in_dim.24
  2.1 9.2 %all-to-all-start = ((s32[32,1,256]{2,1,0:T(1,128)}), s32[32,1,256]{2,1,0:T(1,128)S(1)}, u32[]{:S(2)}, u32[]{:S(2)}) async-start(s32[32,1,256]{2,1,0:T(1,128)} %broadcast_in_dim.24), calls=%async_computation | async-start | bytes 65536 | tf_op jit(solution)/shard_map/all_to_all | solution.py:40
  11.4 1.5 multiply_reduce_fusion
  12.9 0.8 reduce-window.9
  13.7 0.7 bitcast_subtract_fusion
  14.5 0.8 select_reduce_fusion
  15.2 0.7 subtract_convert_fusion.1
  15.9 2.0 multiply_reduce_fusion.2
  17.9 0.6 fusion.5
  19.1 2.5 %broadcast_in_dim.30 = bf16[32,256,256]{2,1,0:T(8,128)(2,1)} broadcast(bf16[256,256]{1,0:T(8,128)(2,1)S(1)} %copy.58), dimensions={1,2} | broadcast | bytes 4325376 | tf_op jit(solution)/shard_map/broadcast_in_dim | solution.py:39
  21.5 7.9 %all-to-all-start.1 = ((bf16[32,256,256]{2,1,0:T(8,128)(2,1)}), bf16[32,256,256]{2,1,0:T(8,128)(2,1)}, u32[]{:S(2)}, u32[]{:S(2)}) async-start(bf16[32,256,256]{2,1,0:T(8,128)(2,1)} %broadcast_in_dim.30), calls=%async_computation.1 | async-start | bytes 8388608 | tf_op jit(solution)/shard_map/all_to_all | solution.py:40
  29.4 1.9 multiply_reduce_fusion.1
  32.1 0.8 broadcast_in_dim_reshape.11.qbeg_ref
  33.1 0.8 broadcast_in_dim_reshape.10.qtok_ref
  33.9 2.3 %copy.71 = bf16[256,2048]{0,1:T(8,128)(2,1)} copy(bf16[256,2048]{1,0:T(8,128)(2,1)} %param.25) | data formatting | bytes 2097152 | tf_op jit(solution)/shard_map/reshape | solution.py:54
  36.2 0.8 pad_maximum_fusion.1.q_ref
  37.0 44.2 %all-to-all-done.1 = bf16[32,256,256]{2,1,0:T(8,128)(2,1)} async-done(((bf16[32,256,256]{2,1,0:T(8,128)(2,1)}), bf16[32,256,256]{2,1,0:T(8,128)(2,1)}, u32[]{:S(2)}, u32[]{:S(2)}) %all-to-all-start.1) | async-done | bytes 4194336 | tf_op jit(solution)/shard_map/all_to_all | solution.py:40
  81.2 13.3 %shard_map.158 = bf16[512,128]{1,0:T(8,128)(2,1)} custom-call(bf16[512,128]{1,0:T(8,128)(2,1)} %pad_maximum_fusion.1.q_ref, s32[512,1]{1,0:T(8,128)} %broadcast_in_dim_reshape.10.qtok_ref, s32[512,1]{1,0:T(8,128)} %broadcast_in_dim_reshape.11.qbeg_ref, bf16[8192,256]{1,0:T(8,128)(2,1)} %bitcast.13.kv_ref, s32[1,8192]{1,0:T(1,128)} %bitcast.130), custom_call_target="tpu_custom_call" | custom-call | tf_op jit(solution)/shard_map/pallas_call | solution.py:153
  94.5 1.0 reshape.500
  95.4 1.7 fusion.36
  97.1 1.3 copy-done.1
  98.5 2.8 %collective-permute-start = (bf16[4,256,256]{1,2,0:T(8,128)(2,1)S(1)}, bf16[4,256,256]{1,2,0:T(8,128)(2,1)}, u32[]{:S(2)}, u32[]{:S(2)}) collective-permute-start(bf16[4,256,256]{1,2,0:T(8,128)(2,1)S(1)} %fusion.6), channel_id=1, source_target_pairs={{0,1},{1,0},{2,3},{3,2},{4,5},{5,4},{6,7},{7,6},{8,9},{9,8},{10,11... | collective-permute-start | bytes 1572872 | tf_op jit(solution)/shard_map/ppermute | solution.py:58
  101.3 1.7 collective-permute-done
  103.0 2.5 %fusion.58 = (bf16[4,256,256]{1,2,0:T(8,128)(2,1)S(1)}, f32[4,256,256]{1,2,0:T(8,128)}) fusion(bf16[4,256,256]{1,2,0:T(8,128)(2,1)} %collective-permute-done, f32[256,4,2,256]{0,3,2,1:T(8,128)} %copy-done.1, s32[]{:T(128)S(6)} %select_n.189), kind=kLoop, calls=%fused_computation.119 | loop fusion | flops 786432 | bytes 3145732 | tf_op jit(solution)/shard_map/convert_element_type | solution.py:61
  105.6 3.1 %collective-permute-start.1 = (bf16[256,256]{1,0:T(8,128)(2,1)S(1)}, bf16[256,256]{1,0:T(8,128)(2,1)S(1)}, u32[]{:S(2)}, u32[]{:S(2)}) collective-permute-start(bf16[256,256]{1,0:T(8,128)(2,1)S(1)} %bitcast.131), channel_id=1, source_target_pairs={{0,2},{1,3},{2,4},{3,5},{4,6},{5,7},{6,0},{7,1},{8,10},{9,11},{10,... | collective-permute-start | bytes 393224 | tf_op jit(solution)/shard_map/ppermute | solution.py:64
  108.8 4.5 %collective-permute-start.2 = (bf16[256,256]{1,0:T(8,128)(2,1)S(1)}, bf16[256,256]{1,0:T(8,128)(2,1)}, u32[]{:S(2)}, u32[]{:S(2)}) collective-permute-start(bf16[256,256]{1,0:T(8,128)(2,1)S(1)} %bitcast.132), channel_id=1, source_target_pairs={{0,4},{1,5},{2,6},{3,7},{4,0},{5,1},{6,2},{7,3},{8,12},{9,13},{10,... | collective-permute-start | bytes 393224 | tf_op jit(solution)/shard_map/ppermute | solution.py:64
  113.4 2.5 %collective-permute-start.3 = (bf16[256,256]{1,0:T(8,128)(2,1)S(1)}, bf16[256,256]{1,0:T(8,128)(2,1)S(1)}, u32[]{:S(2)}, u32[]{:S(2)}) collective-permute-start(bf16[256,256]{1,0:T(8,128)(2,1)S(1)} %bitcast.133), channel_id=1, source_target_pairs={{0,6},{1,7},{2,0},{3,1},{4,2},{5,3},{6,4},{7,5},{8,14},{9,15},{10,... | collective-permute-start | bytes 393224 | tf_op jit(solution)/shard_map/ppermute | solution.py:64
  115.8 1.6 convert_element_type.92
  117.4 1.0 constant_dynamic-slice_fusion.3
  118.6 3.5 %collective-permute-done.2 = bf16[256,256]{1,0:T(8,128)(2,1)} collective-permute-done((bf16[256,256]{1,0:T(8,128)(2,1)S(1)}, bf16[256,256]{1,0:T(8,128)(2,1)}, u32[]{:S(2)}, u32[]{:S(2)}) %collective-permute-start.2) | collective-permute-done | bytes 131104 | tf_op jit(solution)/shard_map/ppermute | solution.py:64
  122.1 3.3 %collective-permute-done.3 = bf16[256,256]{1,0:T(8,128)(2,1)S(1)} collective-permute-done((bf16[256,256]{1,0:T(8,128)(2,1)S(1)}, bf16[256,256]{1,0:T(8,128)(2,1)S(1)}, u32[]{:S(2)}, u32[]{:S(2)}) %collective-permute-start.3) | collective-permute-done | bytes 131104 | tf_op jit(solution)/shard_map/ppermute | solution.py:64
  125.4 1.1 constant_dynamic-update-slice_fusion.3
  126.5 1.6 collective-permute-start.4
  128.1 3.9 %collective-permute-start.5 = (bf16[256,256]{1,0:T(8,128)(2,1)S(1)}, bf16[256,256]{1,0:T(8,128)(2,1)S(1)}, u32[]{:S(2)}, u32[]{:S(2)}) collective-permute-start(bf16[256,256]{1,0:T(8,128)(2,1)S(1)} %get-tuple-element.5), channel_id=1, source_target_pairs={{0,4},{1,5},{2,6},{3,7},{4,0},{5,1},{6,2},{7,3},{8,12},{9,13},{10,... | collective-permute-start | bytes 393224 | tf_op jit(solution)/shard_map/ppermute | solution.py:74
  132.0 2.7 %collective-permute-start.6 = (bf16[256,256]{1,0:T(8,128)(2,1)S(1)}, bf16[256,256]{1,0:T(8,128)(2,1)S(1)}, u32[]{:S(2)}, u32[]{:S(2)}) collective-permute-start(bf16[256,256]{1,0:T(8,128)(2,1)S(1)} %get-tuple-element.5), channel_id=1, source_target_pairs={{0,6},{1,7},{2,0},{3,1},{4,2},{5,3},{6,4},{7,5},{8,14},{9,15},{10,... | collective-permute-start | bytes 393224 | tf_op jit(solution)/shard_map/ppermute | solution.py:74
  135.1 5.5 %collective-permute-done.5 = bf16[256,256]{1,0:T(8,128)(2,1)S(1)} collective-permute-done((bf16[256,256]{1,0:T(8,128)(2,1)S(1)}, bf16[256,256]{1,0:T(8,128)(2,1)S(1)}, u32[]{:S(2)}, u32[]{:S(2)}) %collective-permute-start.5) | collective-permute-done | bytes 131104 | tf_op jit(solution)/shard_map/ppermute | solution.py:74
  140.6 1.2 collective-permute-done.6
  141.8 0.9 pad_maximum_fusion
  142.6 0.5 collective-permute-start.7
  143.1 0.5 broadcast_multiply_fusion
  143.6 0.7 mul.249
  144.4 0.7 iota_add_fusion
  145.1 0.9 add.367
  146.0 0.9 add.311
  146.9 3.8 %reshape.463 = bf16[384,4,2,256]{3,2,1,0:T(2,128)(2,1)} reshape(bf16[384,2048]{1,0:T(8,128)(2,1)} %param.29) | data formatting | bytes 3145728 | tf_op jit(solution)/shard_map/reshape | solution.py:54
  150.7 1.0 constant_dynamic-update-slice_fusion.2
  152.2 0.8 fusion.10
  153.0 4.2 %fusion.3 = f32[256,4,2,256]{3,0,2,1:T(8,128)} fusion(bf16[384,4,2,256]{3,2,1,0:T(2,128)(2,1)} %reshape.463, bf16[2048,384]{1,0:T(8,128)(2,1)S(1)} %copy-done, bf16[256,2048]{1,0:T(8,128)(2,1)S(1)} %fusion.28, f32[2048]{0:T(1024)S(1)} %copy-done.12, f32[256]{0:T(256)S(1)} %add_rsqrt_fusion.1, f32[256,384]{1,0:T(8,128)S(1)} %fusion.10), kind=kOutput, calls=%fused_computation.11 | convolution fusion | flops 807993344 | bytes 6693888 | tf_op jit(solution)/shard_map/rk,kcip->icrp/dot_general | solution.py:55
  157.2 1.3 fusion.7
  158.8 0.6 gather_fusion
  159.3 1.1 collective-permute-done.8
  160.4 1.4 fusion.56
  161.8 0.7 dynamic-slice_bitcast_fusion.2
  162.5 3.8 %collective-permute-start.10 = (bf16[256,256]{1,0:T(8,128)(2,1)}, bf16[256,256]{1,0:T(8,128)(2,1)S(1)}, u32[]{:S(2)}, u32[]{:S(2)}) collective-permute-start(bf16[256,256]{1,0:T(8,128)(2,1)} %get-tuple-element.10), channel_id=1, source_target_pairs={{0,4},{1,5},{2,6},{3,7},{4,0},{5,1},{6,2},{7,3},{8,12},{9,13},{10,... | collective-permute-start | bytes 393224 | tf_op jit(solution)/shard_map/ppermute | solution.py:64
  166.3 1.7 collective-permute-start.11
  167.9 0.7 collective-permute-start.9
  168.8 2.8 %collective-permute-done.10 = bf16[256,256]{1,0:T(8,128)(2,1)S(1)} collective-permute-done((bf16[256,256]{1,0:T(8,128)(2,1)}, bf16[256,256]{1,0:T(8,128)(2,1)S(1)}, u32[]{:S(2)}, u32[]{:S(2)}) %collective-permute-start.10) | collective-permute-done | bytes 131104 | tf_op jit(solution)/shard_map/ppermute | solution.py:64
  171.6 6.2 %collective-permute-done.11 = bf16[256,256]{1,0:T(8,128)(2,1)S(1)} collective-permute-done((bf16[256,256]{1,0:T(8,128)(2,1)S(1)}, bf16[256,256]{1,0:T(8,128)(2,1)S(1)}, u32[]{:S(2)}, u32[]{:S(2)}) %collective-permute-start.11) | collective-permute-done | bytes 131104 | tf_op jit(solution)/shard_map/ppermute | solution.py:64
  177.8 1.9 collective-permute-done.9
  179.8 1.8 gather_fusion.1
  181.6 12.2 %all-to-all-start.2 = ((bf16[32,8,256]{2,1,0:T(8,128)(2,1)}), bf16[32,8,256]{2,1,0:T(8,128)(2,1)S(1)}, u32[]{:S(2)}, u32[]{:S(2)}) async-start(bf16[32,8,256]{2,1,0:T(8,128)(2,1)} %bitcast.44), calls=%async_computation.2 | async-start | bytes 262144 | tf_op jit(solution)/shard_map/all_to_all | solution.py:235
  194.1 2.4 %scatter_custom_fusion.1 = bf16[256,256]{1,0:T(8,128)(2,1)} fusion(s32[256]{0:T(256)S(1)} %bitcast.137, bf16[32,256,256]{2,1,0:T(8,128)(2,1)} %all-to-all-done.1, s32[]{:T(128)} %constant.179.clone.1, s32[]{:T(128)S(6)} %select_n.183, bf16[]{:T(256)} %constant.174.clone.1), kind=kCustom, calls=%fused_computation.49 | custom fusion | bytes 263172 | tf_op jit(solution)/shard_map/scatter | solution.py:93
  196.5 4.9 %all-to-all-done.2 = bf16[32,8,256]{2,1,0:T(8,128)(2,1)S(1)} async-done(((bf16[32,8,256]{2,1,0:T(8,128)(2,1)}), bf16[32,8,256]{2,1,0:T(8,128)(2,1)S(1)}, u32[]{:S(2)}, u32[]{:S(2)}) %all-to-all-start.2) | async-done | bytes 131104 | tf_op jit(solution)/shard_map/all_to_all | solution.py:235
  201.4 2.1 %scatter_custom_fusion = bf16[256,256]{1,0:T(8,128)(2,1)} fusion(s32[256]{0:T(256)S(1)} %bitcast.136, bf16[32,8,256]{2,1,0:T(8,128)(2,1)S(1)} %all-to-all-done.2, bf16[]{:T(256)} %constant.174.clone.1), kind=kCustom, calls=%fused_computation.51 | custom fusion | bytes 262146 | tf_op jit(solution)/shard_map/scatter | solution.py:240
  (75 shorter events, 3.7 us)
Async XLA Ops:
  0.6 152.3 %copy-start = (bf16[2048,384]{1,0:T(8,128)(2,1)S(1)}, bf16[2048,384]{1,0:T(8,128)(2,1)}, u32[]{:S(2)}) copy-start(bf16[2048,384]{1,0:T(8,128)(2,1)} %param.28) | copy-start | bytes 4718596
  0.6 17.2 %copy-start.2 = (bf16[256,2048]{1,0:T(8,128)(2,1)S(1)}, bf16[256,2048]{1,0:T(8,128)(2,1)}, u32[]{:S(2)}) copy-start(bf16[256,2048]{1,0:T(8,128)(2,1)} %param.15) | copy-start | bytes 3145732
  0.7 17.2 %copy-start.11 = (f32[2048]{0:T(1024)S(1)}, f32[2048]{0:T(1024)}, u32[]{:S(2)}) copy-start(f32[2048]{0:T(1024)} %param.19) | copy-start | bytes 24580
  2.1 16.9 %all-to-all-start = ((s32[32,1,256]{2,1,0:T(1,128)}), s32[32,1,256]{2,1,0:T(1,128)S(1)}, u32[]{:S(2)}, u32[]{:S(2)}) async-start(s32[32,1,256]{2,1,0:T(1,128)} %broadcast_in_dim.24), calls=%async_computation | async-start | bytes 65536 | tf_op jit(solution)/shard_map/all_to_all | solution.py:40
  13.7 4.2 %copy-start.10 = (bf16[2048,128]{1,0:T(8,128)(2,1)S(1)}, bf16[2048,128]{1,0:T(8,128)(2,1)}, u32[]{:S(2)}) copy-start(bf16[2048,128]{1,0:T(8,128)(2,1)} %param.22) | copy-start | bytes 1572868
  15.9 2.6 %copy-start.7 = (f32[128]{0:T(128)S(1)}, f32[128]{0:T(128)}, u32[]{:S(2)}) copy-start(f32[128]{0:T(128)} %param.24) | copy-start | bytes 1540
  19.1 2.5 %copy-start.4 = (s32[32,1,256]{2,1,0:T(1,128)}, s32[32,1,256]{2,1,0:T(1,128)S(1)}, u32[]{:S(2)}) copy-start(s32[32,1,256]{2,1,0:T(1,128)S(1)} %all-to-all-done) | copy-start | bytes 98308
  21.5 59.6 %all-to-all-start.1 = ((bf16[32,256,256]{2,1,0:T(8,128)(2,1)}), bf16[32,256,256]{2,1,0:T(8,128)(2,1)}, u32[]{:S(2)}, u32[]{:S(2)}) async-start(bf16[32,256,256]{2,1,0:T(8,128)(2,1)} %broadcast_in_dim.30), calls=%async_computation.1 | async-start | bytes 8388608 | tf_op jit(solution)/shard_map/all_to_all | solution.py:40
  29.4 2.3 %copy-start.8 = (f32[128]{0:T(128)S(1)}, f32[128]{0:T(128)}, u32[]{:S(2)}) copy-start(f32[128]{0:T(128)} %param.23) | copy-start | bytes 1540
  29.4 3.6 %copy-start.6 = (s32[256]{0:T(256)S(1)}, s32[256]{0:T(256)}, u32[]{:S(2)}) copy-start(s32[256]{0:T(256)} %param.16) | copy-start | bytes 3076
  97.1 1.4 copy-start.1
  98.5 4.4 %collective-permute-start = (bf16[4,256,256]{1,2,0:T(8,128)(2,1)S(1)}, bf16[4,256,256]{1,2,0:T(8,128)(2,1)}, u32[]{:S(2)}, u32[]{:S(2)}) collective-permute-start(bf16[4,256,256]{1,2,0:T(8,128)(2,1)S(1)} %fusion.6), channel_id=1, source_target_pairs={{0,1},{1,0},{2,3},{3,2},{4,5},{5,4},{6,7},{7,6},{8,9},{9,8},{10,11... | collective-permute-start | bytes 1572872 | tf_op jit(solution)/shard_map/ppermute | solution.py:58
  105.6 12.9 %collective-permute-start.1 = (bf16[256,256]{1,0:T(8,128)(2,1)S(1)}, bf16[256,256]{1,0:T(8,128)(2,1)S(1)}, u32[]{:S(2)}, u32[]{:S(2)}) collective-permute-start(bf16[256,256]{1,0:T(8,128)(2,1)S(1)} %bitcast.131), channel_id=1, source_target_pairs={{0,2},{1,3},{2,4},{3,5},{4,6},{5,7},{6,0},{7,1},{8,10},{9,11},{10,... | collective-permute-start | bytes 393224 | tf_op jit(solution)/shard_map/ppermute | solution.py:64
  108.8 13.2 %collective-permute-start.2 = (bf16[256,256]{1,0:T(8,128)(2,1)S(1)}, bf16[256,256]{1,0:T(8,128)(2,1)}, u32[]{:S(2)}, u32[]{:S(2)}) collective-permute-start(bf16[256,256]{1,0:T(8,128)(2,1)S(1)} %bitcast.132), channel_id=1, source_target_pairs={{0,4},{1,5},{2,6},{3,7},{4,0},{5,1},{6,2},{7,3},{8,12},{9,13},{10,... | collective-permute-start | bytes 393224 | tf_op jit(solution)/shard_map/ppermute | solution.py:64
  113.4 11.9 %collective-permute-start.3 = (bf16[256,256]{1,0:T(8,128)(2,1)S(1)}, bf16[256,256]{1,0:T(8,128)(2,1)S(1)}, u32[]{:S(2)}, u32[]{:S(2)}) collective-permute-start(bf16[256,256]{1,0:T(8,128)(2,1)S(1)} %bitcast.133), channel_id=1, source_target_pairs={{0,6},{1,7},{2,0},{3,1},{4,2},{5,3},{6,4},{7,5},{8,14},{9,15},{10,... | collective-permute-start | bytes 393224 | tf_op jit(solution)/shard_map/ppermute | solution.py:64
  118.4 24.7 %copy-start.13 = (s32[64]{0:T(128)S(1)}, s32[64]{0:T(128)}, u32[]{:S(2)}) copy-start(s32[64]{0:T(128)} %param.18) | copy-start | bytes 772
  126.5 8.6 %collective-permute-start.4 = (bf16[256,256]{1,0:T(8,128)(2,1)S(1)}, bf16[256,256]{1,0:T(8,128)(2,1)S(1)}, u32[]{:S(2)}, u32[]{:S(2)}) collective-permute-start(bf16[256,256]{1,0:T(8,128)(2,1)S(1)} %get-tuple-element.5), channel_id=1, source_target_pairs={{0,2},{1,3},{2,4},{3,5},{4,6},{5,7},{6,0},{7,1},{8,10},{9,11},{10,... | collective-permute-start | bytes 393224 | tf_op jit(solution)/shard_map/ppermute | solution.py:74
  128.1 12.5 %collective-permute-start.5 = (bf16[256,256]{1,0:T(8,128)(2,1)S(1)}, bf16[256,256]{1,0:T(8,128)(2,1)S(1)}, u32[]{:S(2)}, u32[]{:S(2)}) collective-permute-start(bf16[256,256]{1,0:T(8,128)(2,1)S(1)} %get-tuple-element.5), channel_id=1, source_target_pairs={{0,4},{1,5},{2,6},{3,7},{4,0},{5,1},{6,2},{7,3},{8,12},{9,13},{10,... | collective-permute-start | bytes 393224 | tf_op jit(solution)/shard_map/ppermute | solution.py:74
  132.0 9.8 %collective-permute-start.6 = (bf16[256,256]{1,0:T(8,128)(2,1)S(1)}, bf16[256,256]{1,0:T(8,128)(2,1)S(1)}, u32[]{:S(2)}, u32[]{:S(2)}) collective-permute-start(bf16[256,256]{1,0:T(8,128)(2,1)S(1)} %get-tuple-element.5), channel_id=1, source_target_pairs={{0,6},{1,7},{2,0},{3,1},{4,2},{5,3},{6,4},{7,5},{8,14},{9,15},{10,... | collective-permute-start | bytes 393224 | tf_op jit(solution)/shard_map/ppermute | solution.py:74
  135.1 6.7 %copy-start.3 = (bf16[256,256]{1,0:T(8,128)(2,1)}, bf16[256,256]{1,0:T(8,128)(2,1)S(1)}, u32[]{:S(2)}) copy-start(bf16[256,256]{1,0:T(8,128)(2,1)S(1)} %collective-permute-done.4) | copy-start | bytes 393220
  142.6 8.1 %collective-permute-start.7 = (bf16[4,256,256]{2,1,0:T(8,128)(2,1)}, bf16[4,256,256]{2,1,0:T(8,128)(2,1)S(1)}, u32[]{:S(2)}, u32[]{:S(2)}) collective-permute-start(bf16[4,256,256]{2,1,0:T(8,128)(2,1)} %pad_maximum_fusion), channel_id=1, source_target_pairs={{0,1},{1,0},{2,3},{3,2},{4,5},{5,4},{6,7},{7,6},{8,9},{9,8},{10,11... | collective-permute-start | bytes 1572872 | tf_op jit(solution)/shard_map/ppermute | solution.py:76
  150.7 1.5 copy-start.12
  150.7 1.5 copy-start.9
  153.0 5.7 %copy-start.5 = (s32[32,1,256]{2,1,0:T(1,128)S(1)}, s32[32,1,256]{2,1,0:T(1,128)}, u32[]{:S(2)}) copy-start(s32[32,1,256]{2,1,0:T(1,128)} %copy-done.4) | copy-start | bytes 98308
  158.4 2.0 collective-permute-start.8
  162.5 9.1 %collective-permute-start.10 = (bf16[256,256]{1,0:T(8,128)(2,1)}, bf16[256,256]{1,0:T(8,128)(2,1)S(1)}, u32[]{:S(2)}, u32[]{:S(2)}) collective-permute-start(bf16[256,256]{1,0:T(8,128)(2,1)} %get-tuple-element.10), channel_id=1, source_target_pairs={{0,4},{1,5},{2,6},{3,7},{4,0},{5,1},{6,2},{7,3},{8,12},{9,13},{10,... | collective-permute-start | bytes 393224 | tf_op jit(solution)/shard_map/ppermute | solution.py:64
  166.3 11.6 %collective-permute-start.11 = (bf16[256,256]{1,0:T(8,128)(2,1)S(1)}, bf16[256,256]{1,0:T(8,128)(2,1)S(1)}, u32[]{:S(2)}, u32[]{:S(2)}) collective-permute-start(bf16[256,256]{1,0:T(8,128)(2,1)S(1)} %get-tuple-element.9), channel_id=1, source_target_pairs={{0,6},{1,7},{2,0},{3,1},{4,2},{5,3},{6,4},{7,5},{8,14},{9,15},{10,... | collective-permute-start | bytes 393224 | tf_op jit(solution)/shard_map/ppermute | solution.py:64
  167.9 11.8 %collective-permute-start.9 = (bf16[256,256]{1,0:T(8,128)(2,1)S(1)}, bf16[256,256]{1,0:T(8,128)(2,1)S(1)}, u32[]{:S(2)}, u32[]{:S(2)}) collective-permute-start(bf16[256,256]{1,0:T(8,128)(2,1)S(1)} %get-tuple-element.8), channel_id=1, source_target_pairs={{0,2},{1,3},{2,4},{3,5},{4,6},{5,7},{6,0},{7,1},{8,10},{9,11},{10,... | collective-permute-start | bytes 393224 | tf_op jit(solution)/shard_map/ppermute | solution.py:64
  181.6 19.8 %all-to-all-start.2 = ((bf16[32,8,256]{2,1,0:T(8,128)(2,1)}), bf16[32,8,256]{2,1,0:T(8,128)(2,1)S(1)}, u32[]{:S(2)}, u32[]{:S(2)}) async-start(bf16[32,8,256]{2,1,0:T(8,128)(2,1)} %bitcast.44), calls=%async_computation.2 | async-start | bytes 262144 | tf_op jit(solution)/shard_map/all_to_all | solution.py:235

commit v10 on v9

--- a/solution.py
+++ b/solution.py
@@ -46,12 +46,12 @@
 
 
 def project_reduce_tp(acts, weight, tp_count):
-    width = weight.shape[1]
+    width = weight.shape[1] * weight.shape[2] * weight.shape[3]
     chips = tp_count // 2
     part = width // tp_count
     index = lax.axis_index("tp")
     chip, core = index // 2, index % 2
-    split = weight.reshape(weight.shape[0], chips, 2, part)
+    split = weight
     terms = jnp.einsum("rk,kcip->icrp", acts, split, preferred_element_type=jnp.float32)
     mine = lax.dynamic_index_in_dim(terms, core, axis=0, keepdims=False)
     other = lax.dynamic_index_in_dim(terms, 1 - core, axis=0, keepdims=False).astype(jnp.bfloat16)
@@ -204,6 +204,10 @@
     knorm = rotary(rms(keys, k_gain), pos).astype(jnp.bfloat16)
     stacked = jnp.stack([knorm, values], axis=2).reshape(rows, kv_heads * 2 * HD)
     pieces = gather_seq(stacked, seq_count)
+    blocks = (tp_count // 2, 2, width // tp_count)
+    o_split = o_weight.reshape((o_weight.shape[0],) + blocks)
+    down_split = down_weight.reshape((down_weight.shape[0],) + blocks)
+    pieces, o_split, down_split = lax.optimization_barrier((pieces, o_split, down_split))
     piece_tokens = gather_seq(token_order, seq_count)
     flat = pieces.reshape(seq_count * rows, kv_heads * 2 * HD)
     key_tokens = piece_tokens.reshape(1, seq_count * rows)
@@ -218,13 +222,13 @@
     attn = jnp.stack(heads_out, axis=1).reshape(rows, q_heads * HD)
     column = lax.axis_index("tp") * part
     own_input = lax.dynamic_slice_in_dim(xfull, column, part, 1)
-    mid = (own_input + project_reduce_tp(attn, o_weight, tp_count)).astype(jnp.bfloat16)
+    mid = (own_input + project_reduce_tp(attn, o_split, tp_count)).astype(jnp.bfloat16)
     mid_full = gather_tp(mid, tp_count)
     normed_mid = rms(mid_full.astype(jnp.float32), norm_mid).astype(jnp.bfloat16)
     gate = jnp.dot(normed_mid, gate_weight, preferred_element_type=jnp.float32)
     upper = jnp.dot(normed_mid, up_weight, preferred_element_type=jnp.float32)
     act = (jax.nn.silu(gate) * upper).astype(jnp.bfloat16)
-    feed = project_reduce_tp(act, down_weight, tp_count)
+    feed = project_reduce_tp(act, down_split, tp_count)
     out = (mid.astype(jnp.float32) + feed).astype(jnp.bfloat16)
     blocks_dev = rows // BLK
     share = BLK // seq_count

time: 205 us -> 203 us (level)
  starting transfers between devices: 57 us -> 48.6 us
  waiting for transfers between devices: 76.6 us -> 80.9 us
  local copies, waits for them, and re-layouts: 29.1 us -> 31.6 us
    all_to_all x1, starting transfers between devices: 12.2 us -> 3.86 us  [body(): lax.all_to_all(out[send_rows], 'seq', split_axis=0, concat_axis=0, tiled=...]
    all_to_all x2, waiting for transfers between devices: 44.2 us -> 49.1 us  [gather_seq(): lax.all_to_all(copies, 'seq', split_axis=0, concat_axis=0, tiled=True)]
    dynamic_slice x4 -> x8, local copies, waits for them, and re-layouts: 0.32 us -> 2.64 us  [project_reduce_tp(): lax.dynamic_index_in_dim(outgoing, (chip + shift) % chips, axis=0, keepdi...]
  transfers between devices with their start and end apart: 15 -> 15, of which waited for: 12 -> 13; matrix products, arithmetic and copies ran while one was open for 14% -> 12% of each run, Pallas kernels for 0% -> 0%
where the time goes in v10:
time: 203 us
  waiting for transfers between devices  80.9 us (40%)
  starting transfers between devices  48.6 us (24%)
  local copies, waits for them, and re-layouts  31.6 us (16%)
  other arithmetic  15.5 us (8%)
  Pallas kernels  13.3 us (7%)
  matrix products  11.4 us (6%)
    all_to_all x2, waiting for transfers between devices, gather_seq(): lax.all_to_all(copies, 'seq', split_axis=0, concat_axis=0, tiled=True)  49.1 us
    all_to_all x2, starting transfers between devices, gather_seq(): lax.all_to_all(copies, 'seq', split_axis=0, concat_axis=0, tiled=True)  17.9 us
    ppermute x6, waiting for transfers between devices, project_reduce_tp(): lax.ppermute(piece, 'tp', chip_shift(tp_count, shift)).astype(jnp.float32)  17.2 us
    ppermute x6, starting transfers between devices, project_reduce_tp(): lax.ppermute(piece, 'tp', chip_shift(tp_count, shift)).astype(jnp.float32)  16.1 us
    pallas_call x1, Pallas kernels, attend(): pl.pallas_call(attend_kernel, grid=(count // tile,), in_specs=[pl.BlockSp...  13.3 us
    ppermute x3, starting transfers between devices, gather_tp(): lax.ppermute(block, 'tp', chip_shift(tp_count, shift))  8.13 us
    ppermute x3, waiting for transfers between devices, gather_tp(): lax.ppermute(block, 'tp', chip_shift(tp_count, shift))  7.07 us
    dot_general x2, matrix products, project_reduce_tp(): jnp.einsum('rk,kcip->icrp', acts, split, preferred_element_type=jnp.float32)  6.16 us
  transfers between devices with their start and end apart: 15, of which 13 were waited for; matrix products, arithmetic and copies ran while one was open for 12% of the time, Pallas kernels for 0%

profile of v10, /device:TPU:1, one launch (start us, length us, event | category | flops | bytes accessed | tf_op | source)
XLA Modules:
  0.0 202.6 jit_solution(11630531998315989006)
XLA Ops:
  0.7 1.7 multiply_reduce_fusion
  2.4 0.8 reduce-window.9
  3.2 0.7 bitcast_subtract_fusion
  3.9 0.8 select_reduce_fusion
  4.6 0.7 subtract_convert_fusion.1
  5.3 2.0 multiply_reduce_fusion.2
  8.5 2.5 %broadcast_in_dim.28 = bf16[32,256,256]{2,1,0:T(8,128)(2,1)} broadcast(bf16[256,256]{1,0:T(8,128)(2,1)S(1)} %copy.64), dimensions={1,2} | broadcast | bytes 4325376 | tf_op jit(solution)/shard_map/broadcast_in_dim | solution.py:39
  10.9 9.4 %all-to-all-start.1 = ((bf16[32,256,256]{2,1,0:T(8,128)(2,1)}), bf16[32,256,256]{2,1,0:T(8,128)(2,1)}, u32[]{:S(2)}, u32[]{:S(2)}) async-start(bf16[32,256,256]{2,1,0:T(8,128)(2,1)} %broadcast_in_dim.28), calls=%async_computation.1 | async-start | bytes 8388608 | tf_op jit(solution)/shard_map/all_to_all | solution.py:40
  20.3 1.9 multiply_reduce_fusion.1
  22.9 3.8 %reshape.460 = bf16[384,4,2,256]{3,2,1,0:T(2,128)(2,1)} reshape(bf16[384,2048]{1,0:T(8,128)(2,1)} %param.29) | data formatting | bytes 3145728 | tf_op jit(solution)/shard_map/reshape | solution.py:209
  26.8 2.6 %reshape.459 = bf16[256,4,2,256]{3,2,1,0:T(2,128)(2,1)} reshape(bf16[256,2048]{1,0:T(8,128)(2,1)} %param.25) | data formatting | bytes 2097152 | tf_op jit(solution)/shard_map/reshape | solution.py:208
  29.5 0.8 broadcast_in_dim_reshape.11.qbeg_ref
  30.4 0.8 broadcast_in_dim_reshape.10.qtok_ref
  31.2 42.6 %all-to-all-done.1 = bf16[32,256,256]{2,1,0:T(8,128)(2,1)} async-done(((bf16[32,256,256]{2,1,0:T(8,128)(2,1)}), bf16[32,256,256]{2,1,0:T(8,128)(2,1)}, u32[]{:S(2)}, u32[]{:S(2)}) %all-to-all-start.1) | async-done | bytes 4194336 | tf_op jit(solution)/shard_map/all_to_all | solution.py:40
  73.8 0.6 broadcast_in_dim.24
  74.4 8.5 %all-to-all-start = ((s32[32,1,256]{2,1,0:T(1,128)}), s32[32,1,256]{2,1,0:T(1,128)S(1)}, u32[]{:S(2)}, u32[]{:S(2)}) async-start(s32[32,1,256]{2,1,0:T(1,128)} %broadcast_in_dim.24), calls=%async_computation | async-start | bytes 65536 | tf_op jit(solution)/shard_map/all_to_all | solution.py:40
  83.0 0.8 pad_maximum_fusion.2.q_ref
  83.7 6.4 %all-to-all-done = s32[32,1,256]{2,1,0:T(1,128)S(1)} async-done(((s32[32,1,256]{2,1,0:T(1,128)}), s32[32,1,256]{2,1,0:T(1,128)S(1)}, u32[]{:S(2)}, u32[]{:S(2)}) %all-to-all-start) | async-done | bytes 32800 | tf_op jit(solution)/shard_map/all_to_all | solution.py:40
  90.8 13.3 %shard_map.158 = bf16[512,128]{1,0:T(8,128)(2,1)} custom-call(bf16[512,128]{1,0:T(8,128)(2,1)} %pad_maximum_fusion.2.q_ref, s32[512,1]{1,0:T(8,128)} %broadcast_in_dim_reshape.10.qtok_ref, s32[512,1]{1,0:T(8,128)} %broadcast_in_dim_reshape.11.qbeg_ref, bf16[8192,256]{1,0:T(8,128)(2,1)} %bitcast.13.kv_ref, s32[1,8192]{1,0:T(1,128)} %bitcast.124), custom_call_target="tpu_custom_call" | custom-call | tf_op jit(solution)/shard_map/pallas_call | solution.py:153
  104.1 1.0 reshape.500
  105.0 1.8 fusion.6
  106.8 1.4 copy-done.1
  108.2 2.1 %collective-permute-start = (bf16[4,256,256]{1,2,0:T(8,128)(2,1)S(1)}, bf16[4,256,256]{1,2,0:T(8,128)(2,1)}, u32[]{:S(2)}, u32[]{:S(2)}) collective-permute-start(bf16[4,256,256]{1,2,0:T(8,128)(2,1)S(1)} %fusion.8), channel_id=1, source_target_pairs={{0,1},{1,0},{2,3},{3,2},{4,5},{5,4},{6,7},{7,6},{8,9},{9,8},{10,11... | collective-permute-start | bytes 1572872 | tf_op jit(solution)/shard_map/ppermute | solution.py:58
  110.3 1.7 collective-permute-done
  112.0 2.5 %fusion.59 = (bf16[4,256,256]{1,2,0:T(8,128)(2,1)S(1)}, f32[4,256,256]{1,2,0:T(8,128)}) fusion(bf16[4,256,256]{1,2,0:T(8,128)(2,1)} %collective-permute-done, f32[4,2,256,256]{3,2,1,0:T(8,128)} %copy-done.1, s32[]{:T(128)S(6)} %select_n.189), kind=kLoop, calls=%fused_computation.121 | loop fusion | flops 786432 | bytes 3145732 | tf_op jit(solution)/shard_map/convert_element_type | solution.py:61
  114.6 3.2 %collective-permute-start.1 = (bf16[256,256]{1,0:T(8,128)(2,1)S(1)}, bf16[256,256]{1,0:T(8,128)(2,1)S(1)}, u32[]{:S(2)}, u32[]{:S(2)}) collective-permute-start(bf16[256,256]{1,0:T(8,128)(2,1)S(1)} %bitcast.125), channel_id=1, source_target_pairs={{0,2},{1,3},{2,4},{3,5},{4,6},{5,7},{6,0},{7,1},{8,10},{9,11},{10,... | collective-permute-start | bytes 393224 | tf_op jit(solution)/shard_map/ppermute | solution.py:64
  118.0 4.3 %collective-permute-start.2 = (bf16[256,256]{1,0:T(8,128)(2,1)S(1)}, bf16[256,256]{1,0:T(8,128)(2,1)}, u32[]{:S(2)}, u32[]{:S(2)}) collective-permute-start(bf16[256,256]{1,0:T(8,128)(2,1)S(1)} %bitcast.126), channel_id=1, source_target_pairs={{0,4},{1,5},{2,6},{3,7},{4,0},{5,1},{6,2},{7,3},{8,12},{9,13},{10,... | collective-permute-start | bytes 393224 | tf_op jit(solution)/shard_map/ppermute | solution.py:64
  122.4 2.4 %collective-permute-start.3 = (bf16[256,256]{1,0:T(8,128)(2,1)S(1)}, bf16[256,256]{1,0:T(8,128)(2,1)S(1)}, u32[]{:S(2)}, u32[]{:S(2)}) collective-permute-start(bf16[256,256]{1,0:T(8,128)(2,1)S(1)} %bitcast.127), channel_id=1, source_target_pairs={{0,6},{1,7},{2,0},{3,1},{4,2},{5,3},{6,4},{7,5},{8,14},{9,15},{10,... | collective-permute-start | bytes 393224 | tf_op jit(solution)/shard_map/ppermute | solution.py:64
  124.8 1.6 convert_element_type.92
  126.4 1.0 constant_dynamic-slice_fusion.7
  127.5 3.4 %collective-permute-done.2 = bf16[256,256]{1,0:T(8,128)(2,1)} collective-permute-done((bf16[256,256]{1,0:T(8,128)(2,1)S(1)}, bf16[256,256]{1,0:T(8,128)(2,1)}, u32[]{:S(2)}, u32[]{:S(2)}) %collective-permute-start.2) | collective-permute-done | bytes 131104 | tf_op jit(solution)/shard_map/ppermute | solution.py:64
  131.0 3.7 %collective-permute-done.3 = bf16[256,256]{1,0:T(8,128)(2,1)S(1)} collective-permute-done((bf16[256,256]{1,0:T(8,128)(2,1)S(1)}, bf16[256,256]{1,0:T(8,128)(2,1)S(1)}, u32[]{:S(2)}, u32[]{:S(2)}) %collective-permute-start.3) | collective-permute-done | bytes 131104 | tf_op jit(solution)/shard_map/ppermute | solution.py:64
  134.7 0.7 copy-done.6
  135.5 1.2 constant_dynamic-update-slice_fusion.3
  136.6 1.5 collective-permute-start.4
  138.2 3.9 %collective-permute-start.5 = (bf16[256,256]{1,0:T(8,128)(2,1)S(1)}, bf16[256,256]{1,0:T(8,128)(2,1)S(1)}, u32[]{:S(2)}, u32[]{:S(2)}) collective-permute-start(bf16[256,256]{1,0:T(8,128)(2,1)S(1)} %get-tuple-element.11), channel_id=1, source_target_pairs={{0,4},{1,5},{2,6},{3,7},{4,0},{5,1},{6,2},{7,3},{8,12},{9,13},{10,... | collective-permute-start | bytes 393224 | tf_op jit(solution)/shard_map/ppermute | solution.py:74
  142.1 2.7 %collective-permute-start.6 = (bf16[256,256]{1,0:T(8,128)(2,1)S(1)}, bf16[256,256]{1,0:T(8,128)(2,1)S(1)}, u32[]{:S(2)}, u32[]{:S(2)}) collective-permute-start(bf16[256,256]{1,0:T(8,128)(2,1)S(1)} %get-tuple-element.11), channel_id=1, source_target_pairs={{0,6},{1,7},{2,0},{3,1},{4,2},{5,3},{6,4},{7,5},{8,14},{9,15},{10,... | collective-permute-start | bytes 393224 | tf_op jit(solution)/shard_map/ppermute | solution.py:74
  145.2 5.4 %collective-permute-done.5 = bf16[256,256]{1,0:T(8,128)(2,1)S(1)} collective-permute-done((bf16[256,256]{1,0:T(8,128)(2,1)S(1)}, bf16[256,256]{1,0:T(8,128)(2,1)S(1)}, u32[]{:S(2)}, u32[]{:S(2)}) %collective-permute-start.5) | collective-permute-done | bytes 131104 | tf_op jit(solution)/shard_map/ppermute | solution.py:74
  150.6 1.2 collective-permute-done.6
  151.8 0.9 pad_maximum_fusion
  153.7 0.7 mul.249
  154.5 0.7 iota_add_fusion
  155.2 0.9 add.367
  156.1 0.9 add.311
  157.0 1.0 constant_dynamic-update-slice_fusion.2
  158.5 0.8 fusion.12
  159.3 4.4 %fusion.3 = f32[4,2,256,256]{3,2,1,0:T(8,128)} fusion(bf16[384,4,2,256]{3,2,1,0:T(2,128)(2,1)} %reshape.460, bf16[2048,384]{1,0:T(8,128)(2,1)S(1)} %copy-done, bf16[256,2048]{1,0:T(8,128)(2,1)S(1)} %fusion.30, f32[2048]{0:T(1024)S(1)} %copy-done.13, f32[256]{0:T(256)S(1)} %add_rsqrt_fusion.1, f32[256,384]{1,0:T(8,128)S(1)} %fusion.12), kind=kOutput, calls=%fused_computation.11 | convolution fusion | flops 807993344 | bytes 6693888 | tf_op jit(solution)/shard_map/rk,kcip->icrp/dot_general | solution.py:55
  163.7 1.3 fusion.9
  165.9 1.1 collective-permute-done.8
  167.0 1.4 fusion.57
  168.4 0.8 copy.79
  169.2 3.8 %collective-permute-start.10 = (bf16[256,256]{1,0:T(8,128)(2,1)}, bf16[256,256]{1,0:T(8,128)(2,1)S(1)}, u32[]{:S(2)}, u32[]{:S(2)}) collective-permute-start(bf16[256,256]{1,0:T(8,128)(2,1)} %bitcast.40), channel_id=1, source_target_pairs={{0,4},{1,5},{2,6},{3,7},{4,0},{5,1},{6,2},{7,3},{8,12},{9,13},{10,... | collective-permute-start | bytes 393224 | tf_op jit(solution)/shard_map/ppermute | solution.py:64
  172.9 0.8 copy.80
  173.7 1.7 collective-permute-start.11
  175.4 0.8 copy.78
  176.1 0.7 collective-permute-start.9
  177.2 1.1 collective-permute-done.10
  178.3 6.2 %collective-permute-done.11 = bf16[256,256]{1,0:T(8,128)(2,1)S(1)} collective-permute-done((bf16[256,256]{1,0:T(8,128)(2,1)}, bf16[256,256]{1,0:T(8,128)(2,1)S(1)}, u32[]{:S(2)}, u32[]{:S(2)}) %collective-permute-start.11) | collective-permute-done | bytes 131104 | tf_op jit(solution)/shard_map/ppermute | solution.py:64
  184.5 2.7 %collective-permute-done.9 = bf16[256,256]{1,0:T(8,128)(2,1)S(1)} collective-permute-done((bf16[256,256]{1,0:T(8,128)(2,1)}, bf16[256,256]{1,0:T(8,128)(2,1)S(1)}, u32[]{:S(2)}, u32[]{:S(2)}) %collective-permute-start.9) | collective-permute-done | bytes 131104 | tf_op jit(solution)/shard_map/ppermute | solution.py:64
  187.3 1.8 gather_fusion.1
  189.1 3.9 %all-to-all-start.2 = ((bf16[32,8,256]{2,1,0:T(8,128)(2,1)}), bf16[32,8,256]{2,1,0:T(8,128)(2,1)S(1)}, u32[]{:S(2)}, u32[]{:S(2)}) async-start(bf16[32,8,256]{2,1,0:T(8,128)(2,1)} %bitcast.43), calls=%async_computation.2 | async-start | bytes 262144 | tf_op jit(solution)/shard_map/all_to_all | solution.py:239
  193.2 2.4 %scatter_custom_fusion.1 = bf16[256,256]{1,0:T(8,128)(2,1)} fusion(s32[256]{0:T(256)S(1)} %bitcast.131, bf16[32,256,256]{2,1,0:T(8,128)(2,1)} %all-to-all-done.1, s32[]{:T(128)} %constant.179.clone.1, s32[]{:T(128)S(6)} %select_n.183, bf16[]{:T(256)} %constant.174.clone.1), kind=kCustom, calls=%fused_computation.51 | custom fusion | bytes 263172 | tf_op jit(solution)/shard_map/scatter | solution.py:93
  195.6 4.9 %all-to-all-done.2 = bf16[32,8,256]{2,1,0:T(8,128)(2,1)S(1)} async-done(((bf16[32,8,256]{2,1,0:T(8,128)(2,1)}), bf16[32,8,256]{2,1,0:T(8,128)(2,1)S(1)}, u32[]{:S(2)}, u32[]{:S(2)}) %all-to-all-start.2) | async-done | bytes 131104 | tf_op jit(solution)/shard_map/all_to_all | solution.py:239
  200.5 2.1 %scatter_custom_fusion = bf16[256,256]{1,0:T(8,128)(2,1)} fusion(s32[256]{0:T(256)S(1)} %bitcast.130, bf16[32,8,256]{2,1,0:T(8,128)(2,1)S(1)} %all-to-all-done.2, bf16[]{:T(256)} %constant.174.clone.1), kind=kCustom, calls=%fused_computation.53 | custom fusion | bytes 262146 | tf_op jit(solution)/shard_map/scatter | solution.py:244
  (82 shorter events, 6.6 us)
Async XLA Ops:
  0.6 158.7 %copy-start = (bf16[2048,384]{1,0:T(8,128)(2,1)S(1)}, bf16[2048,384]{1,0:T(8,128)(2,1)}, u32[]{:S(2)}) copy-start(bf16[2048,384]{1,0:T(8,128)(2,1)} %param.28) | copy-start | bytes 4718596
  0.6 6.6 %copy-start.2 = (bf16[256,2048]{1,0:T(8,128)(2,1)S(1)}, bf16[256,2048]{1,0:T(8,128)(2,1)}, u32[]{:S(2)}) copy-start(bf16[256,2048]{1,0:T(8,128)(2,1)} %param.15) | copy-start | bytes 3145732
  0.7 6.6 %copy-start.12 = (f32[2048]{0:T(1024)S(1)}, f32[2048]{0:T(1024)}, u32[]{:S(2)}) copy-start(f32[2048]{0:T(1024)} %param.19) | copy-start | bytes 24580
  0.7 6.6 %copy-start.11 = (bf16[2048,128]{1,0:T(8,128)(2,1)S(1)}, bf16[2048,128]{1,0:T(8,128)(2,1)}, u32[]{:S(2)}) copy-start(bf16[2048,128]{1,0:T(8,128)(2,1)} %param.22) | copy-start | bytes 1572868
  5.3 2.6 %copy-start.8 = (f32[128]{0:T(128)S(1)}, f32[128]{0:T(128)}, u32[]{:S(2)}) copy-start(f32[128]{0:T(128)} %param.24) | copy-start | bytes 1540
  10.9 62.9 %all-to-all-start.1 = ((bf16[32,256,256]{2,1,0:T(8,128)(2,1)}), bf16[32,256,256]{2,1,0:T(8,128)(2,1)}, u32[]{:S(2)}, u32[]{:S(2)}) async-start(bf16[32,256,256]{2,1,0:T(8,128)(2,1)} %broadcast_in_dim.28), calls=%async_computation.1 | async-start | bytes 8388608 | tf_op jit(solution)/shard_map/all_to_all | solution.py:40
  20.3 2.2 %copy-start.9 = (f32[128]{0:T(128)S(1)}, f32[128]{0:T(128)}, u32[]{:S(2)}) copy-start(f32[128]{0:T(128)} %param.23) | copy-start | bytes 1540
  26.8 3.5 %copy-start.7 = (s32[256]{0:T(256)S(1)}, s32[256]{0:T(256)}, u32[]{:S(2)}) copy-start(s32[256]{0:T(256)} %param.16) | copy-start | bytes 3076
  74.4 15.7 %all-to-all-start = ((s32[32,1,256]{2,1,0:T(1,128)}), s32[32,1,256]{2,1,0:T(1,128)S(1)}, u32[]{:S(2)}, u32[]{:S(2)}) async-start(s32[32,1,256]{2,1,0:T(1,128)} %broadcast_in_dim.24), calls=%async_computation | async-start | bytes 65536 | tf_op jit(solution)/shard_map/all_to_all | solution.py:40
  90.2 0.6 copy-start.4
  106.8 1.4 copy-start.1
  108.2 3.7 %collective-permute-start = (bf16[4,256,256]{1,2,0:T(8,128)(2,1)S(1)}, bf16[4,256,256]{1,2,0:T(8,128)(2,1)}, u32[]{:S(2)}, u32[]{:S(2)}) collective-permute-start(bf16[4,256,256]{1,2,0:T(8,128)(2,1)S(1)} %fusion.8), channel_id=1, source_target_pairs={{0,1},{1,0},{2,3},{3,2},{4,5},{5,4},{6,7},{7,6},{8,9},{9,8},{10,11... | collective-permute-start | bytes 1572872 | tf_op jit(solution)/shard_map/ppermute | solution.py:58
  114.6 12.9 %collective-permute-start.1 = (bf16[256,256]{1,0:T(8,128)(2,1)S(1)}, bf16[256,256]{1,0:T(8,128)(2,1)S(1)}, u32[]{:S(2)}, u32[]{:S(2)}) collective-permute-start(bf16[256,256]{1,0:T(8,128)(2,1)S(1)} %bitcast.125), channel_id=1, source_target_pairs={{0,2},{1,3},{2,4},{3,5},{4,6},{5,7},{6,0},{7,1},{8,10},{9,11},{10,... | collective-permute-start | bytes 393224 | tf_op jit(solution)/shard_map/ppermute | solution.py:64
  118.0 13.0 %collective-permute-start.2 = (bf16[256,256]{1,0:T(8,128)(2,1)S(1)}, bf16[256,256]{1,0:T(8,128)(2,1)}, u32[]{:S(2)}, u32[]{:S(2)}) collective-permute-start(bf16[256,256]{1,0:T(8,128)(2,1)S(1)} %bitcast.126), channel_id=1, source_target_pairs={{0,4},{1,5},{2,6},{3,7},{4,0},{5,1},{6,2},{7,3},{8,12},{9,13},{10,... | collective-permute-start | bytes 393224 | tf_op jit(solution)/shard_map/ppermute | solution.py:64
  122.4 12.3 %collective-permute-start.3 = (bf16[256,256]{1,0:T(8,128)(2,1)S(1)}, bf16[256,256]{1,0:T(8,128)(2,1)S(1)}, u32[]{:S(2)}, u32[]{:S(2)}) collective-permute-start(bf16[256,256]{1,0:T(8,128)(2,1)S(1)} %bitcast.127), channel_id=1, source_target_pairs={{0,6},{1,7},{2,0},{3,1},{4,2},{5,3},{6,4},{7,5},{8,14},{9,15},{10,... | collective-permute-start | bytes 393224 | tf_op jit(solution)/shard_map/ppermute | solution.py:64
  127.4 25.8 %copy-start.14 = (s32[64]{0:T(128)S(1)}, s32[64]{0:T(128)}, u32[]{:S(2)}) copy-start(s32[64]{0:T(128)} %param.18) | copy-start | bytes 772
  134.7 0.7 copy-start.6
  136.6 8.6 %collective-permute-start.4 = (bf16[256,256]{1,0:T(8,128)(2,1)S(1)}, bf16[256,256]{1,0:T(8,128)(2,1)S(1)}, u32[]{:S(2)}, u32[]{:S(2)}) collective-permute-start(bf16[256,256]{1,0:T(8,128)(2,1)S(1)} %get-tuple-element.11), channel_id=1, source_target_pairs={{0,2},{1,3},{2,4},{3,5},{4,6},{5,7},{6,0},{7,1},{8,10},{9,11},{10,... | collective-permute-start | bytes 393224 | tf_op jit(solution)/shard_map/ppermute | solution.py:74
  138.2 12.5 %collective-permute-start.5 = (bf16[256,256]{1,0:T(8,128)(2,1)S(1)}, bf16[256,256]{1,0:T(8,128)(2,1)S(1)}, u32[]{:S(2)}, u32[]{:S(2)}) collective-permute-start(bf16[256,256]{1,0:T(8,128)(2,1)S(1)} %get-tuple-element.11), channel_id=1, source_target_pairs={{0,4},{1,5},{2,6},{3,7},{4,0},{5,1},{6,2},{7,3},{8,12},{9,13},{10,... | collective-permute-start | bytes 393224 | tf_op jit(solution)/shard_map/ppermute | solution.py:74
  142.1 9.7 %collective-permute-start.6 = (bf16[256,256]{1,0:T(8,128)(2,1)S(1)}, bf16[256,256]{1,0:T(8,128)(2,1)S(1)}, u32[]{:S(2)}, u32[]{:S(2)}) collective-permute-start(bf16[256,256]{1,0:T(8,128)(2,1)S(1)} %get-tuple-element.11), channel_id=1, source_target_pairs={{0,6},{1,7},{2,0},{3,1},{4,2},{5,3},{6,4},{7,5},{8,14},{9,15},{10,... | collective-permute-start | bytes 393224 | tf_op jit(solution)/shard_map/ppermute | solution.py:74
  145.2 6.7 %copy-start.3 = (bf16[256,256]{1,0:T(8,128)(2,1)}, bf16[256,256]{1,0:T(8,128)(2,1)S(1)}, u32[]{:S(2)}) copy-start(bf16[256,256]{1,0:T(8,128)(2,1)S(1)} %collective-permute-done.4) | copy-start | bytes 393220
  152.7 4.3 %collective-permute-start.7 = (bf16[4,256,256]{2,1,0:T(8,128)(2,1)}, bf16[4,256,256]{2,1,0:T(8,128)(2,1)S(1)}, u32[]{:S(2)}, u32[]{:S(2)}) collective-permute-start(bf16[4,256,256]{2,1,0:T(8,128)(2,1)} %pad_maximum_fusion), channel_id=1, source_target_pairs={{0,1},{1,0},{2,3},{3,2},{4,5},{5,4},{6,7},{7,6},{8,9},{9,8},{10,11... | collective-permute-start | bytes 1572872 | tf_op jit(solution)/shard_map/ppermute | solution.py:76
  155.2 3.3 %copy-start.13 = (f32[2048]{0:T(1024)S(1)}, f32[2048]{0:T(1024)}, u32[]{:S(2)}) copy-start(f32[2048]{0:T(1024)} %param.26) | copy-start | bytes 24580
  157.0 1.5 copy-start.10
  159.3 5.9 %copy-start.5 = (s32[32,1,256]{2,1,0:T(1,128)S(1)}, s32[32,1,256]{2,1,0:T(1,128)}, u32[]{:S(2)}) copy-start(s32[32,1,256]{2,1,0:T(1,128)} %copy-done.4) | copy-start | bytes 98308
  165.0 2.0 collective-permute-start.8
  169.2 9.1 %collective-permute-start.10 = (bf16[256,256]{1,0:T(8,128)(2,1)}, bf16[256,256]{1,0:T(8,128)(2,1)S(1)}, u32[]{:S(2)}, u32[]{:S(2)}) collective-permute-start(bf16[256,256]{1,0:T(8,128)(2,1)} %bitcast.40), channel_id=1, source_target_pairs={{0,4},{1,5},{2,6},{3,7},{4,0},{5,1},{6,2},{7,3},{8,12},{9,13},{10,... | collective-permute-start | bytes 393224 | tf_op jit(solution)/shard_map/ppermute | solution.py:64
  173.7 10.8 %collective-permute-start.11 = (bf16[256,256]{1,0:T(8,128)(2,1)}, bf16[256,256]{1,0:T(8,128)(2,1)S(1)}, u32[]{:S(2)}, u32[]{:S(2)}) collective-permute-start(bf16[256,256]{1,0:T(8,128)(2,1)} %bitcast.41), channel_id=1, source_target_pairs={{0,6},{1,7},{2,0},{3,1},{4,2},{5,3},{6,4},{7,5},{8,14},{9,15},{10,... | collective-permute-start | bytes 393224 | tf_op jit(solution)/shard_map/ppermute | solution.py:64
  176.1 11.0 %collective-permute-start.9 = (bf16[256,256]{1,0:T(8,128)(2,1)}, bf16[256,256]{1,0:T(8,128)(2,1)S(1)}, u32[]{:S(2)}, u32[]{:S(2)}) collective-permute-start(bf16[256,256]{1,0:T(8,128)(2,1)} %bitcast.39), channel_id=1, source_target_pairs={{0,2},{1,3},{2,4},{3,5},{4,6},{5,7},{6,0},{7,1},{8,10},{9,11},{10,... | collective-permute-start | bytes 393224 | tf_op jit(solution)/shard_map/ppermute | solution.py:64
  189.1 11.4 %all-to-all-start.2 = ((bf16[32,8,256]{2,1,0:T(8,128)(2,1)}), bf16[32,8,256]{2,1,0:T(8,128)(2,1)S(1)}, u32[]{:S(2)}, u32[]{:S(2)}) async-start(bf16[32,8,256]{2,1,0:T(8,128)(2,1)} %bitcast.43), calls=%async_computation.2 | async-start | bytes 262144 | tf_op jit(solution)/shard_map/all_to_all | solution.py:239

commit v11 on v10

--- a/solution.py
+++ b/solution.py
@@ -1,3 +1,5 @@
+import functools
+
 import jax
 import jax.numpy as jnp
 from jax import lax
@@ -82,6 +84,22 @@
     return full
 
 
+TOKEN_BASE = 64
+PAYLOAD_EXTRA = 16
+
+
+def gather_with_tokens(stacked, token_order, seq_count):
+    rows, width = stacked.shape
+    high = (token_order // TOKEN_BASE).astype(jnp.bfloat16)
+    low = (token_order % TOKEN_BASE).astype(jnp.bfloat16)
+    token_rows = jnp.stack([high, low]).reshape(2 * rows // width, width)
+    padding = jnp.zeros((PAYLOAD_EXTRA - token_rows.shape[0], width), jnp.bfloat16)
+    arrived = gather_seq(jnp.concatenate([stacked, token_rows, padding], axis=0), seq_count)
+    coded = arrived[:, rows : rows + token_rows.shape[0], :].reshape(seq_count, 2, rows)
+    tokens = coded[:, 0].astype(jnp.int32) * TOKEN_BASE + coded[:, 1].astype(jnp.int32)
+    return arrived, tokens
+
+
 def build_cache(pieces, piece_tokens, rows, seq_count):
     group_rows = rows // seq_count
     share = BLK // seq_count
@@ -99,17 +117,23 @@
 UNROLL = 4
 
 
-def attend_kernel(q_ref, qtok_ref, qbeg_ref, kv_ref, ktok_ref, out_ref):
+def attend_kernel(q_ref, qtok_ref, qbeg_ref, kv_ref, ktok_ref, out_ref, *, rows):
     query = q_ref[...]
     qtok = qtok_ref[...]
     qbeg = qbeg_ref[...]
     tile = query.shape[0]
-    chunks = kv_ref.shape[0] // KEY_CHUNK
+    per_chunk = KEY_CHUNK // rows
+    chunks = kv_ref.shape[0] // per_chunk
     scale = 1.0 / HD**0.5
+
+    def block(chunk, offset):
+        first = pl.multiple_of(chunk * per_chunk, per_chunk)
+        part = kv_ref[pl.ds(first, per_chunk), pl.ds(0, rows), pl.ds(offset, HD)]
+        return part.reshape(KEY_CHUNK, HD)
 
     def scores(chunk):
         start = pl.multiple_of(chunk * KEY_CHUNK, KEY_CHUNK)
-        keys = kv_ref[pl.ds(start, KEY_CHUNK), pl.ds(0, HD)]
+        keys = block(chunk, 0)
         ktok = ktok_ref[:, pl.ds(start, KEY_CHUNK)]
         raw = lax.dot_general(
             query, keys, (((1,), (1,)), ((), ())), preferred_element_type=jnp.float32
@@ -129,7 +153,7 @@
         total, accum = carry
         score, start = scores(chunk)
         weights = jnp.exp(score - top)
-        values = kv_ref[pl.ds(start, KEY_CHUNK), pl.ds(HD, HD)]
+        values = block(chunk, HD)
         total = total + jnp.sum(weights, axis=1, keepdims=True)
         accum = accum + jnp.dot(
             weights.astype(jnp.bfloat16), values, preferred_element_type=jnp.float32
@@ -146,23 +170,24 @@
     out_ref[...] = (accum / total).astype(out_ref.dtype)
 
 
-def attend(query, query_tokens, query_begins, flat, key_tokens, head):
+def attend(query, query_tokens, query_begins, pieces, key_tokens, head, rows):
     count = query.shape[0]
-    keys = flat.shape[0]
+    keys = key_tokens.shape[1]
     tile = min(QUERY_TILE, count)
+    sources, padded, _ = pieces.shape
     return pl.pallas_call(
-        attend_kernel,
+        functools.partial(attend_kernel, rows=rows),
         grid=(count // tile,),
         in_specs=[
             pl.BlockSpec((tile, HD), lambda i: (i, 0)),
             pl.BlockSpec((tile, 1), lambda i: (i, 0)),
             pl.BlockSpec((tile, 1), lambda i: (i, 0)),
-            pl.BlockSpec((keys, 2 * HD), lambda i: (0, head)),
+            pl.BlockSpec((sources, padded, 2 * HD), lambda i: (0, 0, head)),
             pl.BlockSpec((1, keys), lambda i: (0, 0)),
         ],
         out_specs=pl.BlockSpec((tile, HD), lambda i: (i, 0)),
         out_shape=jax.ShapeDtypeStruct((count, HD), jnp.bfloat16),
-    )(query, query_tokens, query_begins, flat, key_tokens)
+    )(query, query_tokens, query_begins, pieces, key_tokens)
 
 
 def body(
@@ -203,13 +228,11 @@
     qnorm = rotary(rms(query, q_gain), pos).astype(jnp.bfloat16).reshape(rows, kv_heads, group, HD)
     knorm = rotary(rms(keys, k_gain), pos).astype(jnp.bfloat16)
     stacked = jnp.stack([knorm, values], axis=2).reshape(rows, kv_heads * 2 * HD)
-    pieces = gather_seq(stacked, seq_count)
+    pieces, piece_tokens = gather_with_tokens(stacked, token_order, seq_count)
     blocks = (tp_count // 2, 2, width // tp_count)
     o_split = o_weight.reshape((o_weight.shape[0],) + blocks)
     down_split = down_weight.reshape((down_weight.shape[0],) + blocks)
     pieces, o_split, down_split = lax.optimization_barrier((pieces, o_split, down_split))
-    piece_tokens = gather_seq(token_order, seq_count)
-    flat = pieces.reshape(seq_count * rows, kv_heads * 2 * HD)
     key_tokens = piece_tokens.reshape(1, seq_count * rows)
     query_tokens = jnp.repeat(token_order, group)[:, None]
     query_begins = jnp.repeat(begin, group)[:, None]
@@ -217,7 +240,7 @@
     for head in range(kv_heads):
         qhead = qnorm[:, head].reshape(rows * group, HD)
         heads_out.append(
-            attend(qhead, query_tokens, query_begins, flat, key_tokens, head).reshape(rows, group, HD)
+            attend(qhead, query_tokens, query_begins, pieces, key_tokens, head, rows).reshape(rows, group, HD)
         )
     attn = jnp.stack(heads_out, axis=1).reshape(rows, q_heads * HD)
     column = lax.axis_index("tp") * part

time: 203 us -> 194 us (0.956)
  waiting for transfers between devices: 80.9 us -> 76.4 us
  starting transfers between devices: 48.6 us -> 45.2 us
  local copies, waits for them, and re-layouts: 31.6 us -> 28.8 us
    all_to_all x2 -> x1, starting transfers between devices: 17.9 us -> 9.34 us  [gather_seq(): lax.all_to_all(copies, 'seq', split_axis=0, concat_axis=0, tiled=True)]
    all_to_all x1, starting transfers between devices: 3.86 us -> 8.9 us  [body(): lax.all_to_all(out[send_rows], 'seq', split_axis=0, concat_axis=0, tiled=...]
    all_to_all x2 -> x1, waiting for transfers between devices: 49.1 us -> 45.6 us  [gather_seq(): lax.all_to_all(copies, 'seq', split_axis=0, concat_axis=0, tiled=True)]
  transfers between devices with their start and end apart: 15 -> 14, of which waited for: 13 -> 12; matrix products, arithmetic and copies ran while one was open for 12% -> 11% of each run, Pallas kernels for 0% -> 0%
where the time goes in v11:
time: 194 us; the launch traced here: 193 us
  waiting for transfers between devices  76.4 us (39%)
  starting transfers between devices  45.2 us (23%)
  local copies, waits for them, and re-layouts  28.8 us (15%)
  other arithmetic  16.7 us (9%)
  Pallas kernels  13.4 us (7%)
  matrix products  11.4 us (6%)
    all_to_all x1, waiting for transfers between devices, gather_seq(): lax.all_to_all(copies, 'seq', split_axis=0, concat_axis=0, tiled=True)  45.6 us
    ppermute x6, starting transfers between devices, project_reduce_tp(): lax.ppermute(piece, 'tp', chip_shift(tp_count, shift)).astype(jnp.float32)  16.1 us
    ppermute x6, waiting for transfers between devices, project_reduce_tp(): lax.ppermute(piece, 'tp', chip_shift(tp_count, shift)).astype(jnp.float32)  15.8 us
    pallas_call x1, Pallas kernels, attend(): pl.pallas_call(functools.partial(attend_kernel, rows=rows), grid=(count /...  13.4 us
    all_to_all x1, starting transfers between devices, gather_seq(): lax.all_to_all(copies, 'seq', split_axis=0, concat_axis=0, tiled=True)  9.34 us
    all_to_all x1, starting transfers between devices, body(): lax.all_to_all(out[send_rows], 'seq', split_axis=0, concat_axis=0, tiled=...  8.9 us
    ppermute x3, starting transfers between devices, gather_tp(): lax.ppermute(block, 'tp', chip_shift(tp_count, shift))  8.04 us
    ppermute x3, waiting for transfers between devices, gather_tp(): lax.ppermute(block, 'tp', chip_shift(tp_count, shift))  7.07 us
  transfers between devices with their start and end apart: 14, of which 12 were waited for; matrix products, arithmetic and copies ran while one was open for 11% of the time, Pallas kernels for 0%

profile of v11, /device:TPU:1, one launch (start us, length us, event | category | flops | bytes accessed | tf_op | source)
XLA Modules:
  0.0 193.2 jit_solution(7005269317316375462)
XLA Ops:
  0.7 1.7 multiply_reduce_fusion
  2.4 0.8 reduce-window.9
  3.2 0.7 bitcast_subtract_fusion
  3.9 0.8 select_reduce_fusion
  4.6 0.7 subtract_convert_fusion.1
  5.3 2.0 %multiply_reduce_fusion.2 = (f32[256]{0:T(256)S(1)}, f32[256,128]{0,1:T(8,128)S(1)}) fusion(bf16[2048,128]{1,0:T(8,128)(2,1)} %param.21, f32[2048]{0:T(1024)} %param.19, f32[256]{0:T(256)S(1)} %add_rsqrt_fusion.3, bf16[256,2048]{1,0:T(8,128)(2,1)} %param.15), kind=kOutput, calls=%fused_computation.61 | convolution fusion | flops 136380160 | bytes 1714176 | tf_op jit(solution)/shard_map/dot_general | solution.py:222
  7.3 0.6 fusion.5
  8.7 2.4 %broadcast_in_dim.24 = bf16[32,272,256]{2,1,0:T(8,128)(2,1)} broadcast(bf16[272,256]{1,0:T(8,128)(2,1)S(1)} %maximum_maximum_fusion), dimensions={1,2} | broadcast | bytes 4595712 | tf_op jit(solution)/shard_map/broadcast_in_dim | solution.py:41
  11.1 9.3 %all-to-all-start = ((bf16[32,272,256]{2,1,0:T(8,128)(2,1)}), bf16[32,272,256]{2,1,0:T(8,128)(2,1)}, u32[]{:S(2)}, u32[]{:S(2)}) async-start(bf16[32,272,256]{2,1,0:T(8,128)(2,1)} %broadcast_in_dim.24), calls=%async_computation | async-start | bytes 8912896 | tf_op jit(solution)/shard_map/all_to_all | solution.py:42
  20.5 1.9 multiply_reduce_fusion.1
  23.1 3.9 %reshape.488 = bf16[384,4,2,256]{3,2,1,0:T(2,128)(2,1)} reshape(bf16[384,2048]{1,0:T(8,128)(2,1)} %param.29) | data formatting | bytes 3145728 | tf_op jit(solution)/shard_map/reshape | solution.py:234
  26.9 2.6 %reshape.487 = bf16[256,4,2,256]{3,2,1,0:T(2,128)(2,1)} reshape(bf16[256,2048]{1,0:T(8,128)(2,1)} %param.25) | data formatting | bytes 2097152 | tf_op jit(solution)/shard_map/reshape | solution.py:233
  29.6 0.8 broadcast_in_dim_reshape.10.qbeg_ref
  30.6 0.8 broadcast_in_dim_reshape.9.qtok_ref
  31.4 0.8 pad_maximum_fusion.2.q_ref
  32.1 45.6 %all-to-all-done.kv_ref = bf16[32,272,256]{2,1,0:T(8,128)(2,1)} async-done(((bf16[32,272,256]{2,1,0:T(8,128)(2,1)}), bf16[32,272,256]{2,1,0:T(8,128)(2,1)}, u32[]{:S(2)}, u32[]{:S(2)}) %all-to-all-start) | async-done | bytes 4456480 | tf_op jit(solution)/shard_map/all_to_all | solution.py:42
  77.7 1.7 fusion.50
  79.4 13.4 %shard_map.158 = bf16[512,128]{1,0:T(8,128)(2,1)} custom-call(bf16[512,128]{1,0:T(8,128)(2,1)} %pad_maximum_fusion.2.q_ref, s32[512,1]{1,0:T(8,128)} %broadcast_in_dim_reshape.9.qtok_ref, s32[512,1]{1,0:T(8,128)} %broadcast_in_dim_reshape.10.qbeg_ref, bf16[32,272,256]{2,1,0:T(8,128)(2,1)} %all-to-all-done.kv_ref, s32[1,8192]{1,0:T(1,128)} %bitcast.123), custom_call_target="tpu_custom_call" | custom-call | tf_op jit(solution)/shard_map/pallas_call | solution.py:178
  92.8 1.0 reshape.526
  93.8 1.8 fusion.6
  95.5 1.4 copy-done.1
  97.0 1.9 collective-permute-start
  98.9 1.7 collective-permute-done
  100.5 2.5 %fusion.63 = (bf16[4,256,256]{1,2,0:T(8,128)(2,1)S(1)}, f32[4,256,256]{1,2,0:T(8,128)}) fusion(bf16[4,256,256]{1,2,0:T(8,128)(2,1)} %collective-permute-done, f32[4,2,256,256]{3,2,1,0:T(8,128)} %copy-done.1, s32[]{:T(128)S(6)} %select_n.200), kind=kLoop, calls=%fused_computation.135 | loop fusion | flops 786432 | bytes 3145732 | tf_op jit(solution)/shard_map/convert_element_type | solution.py:63
  103.2 3.3 %collective-permute-start.1 = (bf16[256,256]{1,0:T(8,128)(2,1)S(1)}, bf16[256,256]{1,0:T(8,128)(2,1)S(1)}, u32[]{:S(2)}, u32[]{:S(2)}) collective-permute-start(bf16[256,256]{1,0:T(8,128)(2,1)S(1)} %bitcast.124), channel_id=1, source_target_pairs={{0,2},{1,3},{2,4},{3,5},{4,6},{5,7},{6,0},{7,1},{8,10},{9,11},{10,... | collective-permute-start | bytes 393224 | tf_op jit(solution)/shard_map/ppermute | solution.py:66
  106.6 4.3 %collective-permute-start.2 = (bf16[256,256]{1,0:T(8,128)(2,1)S(1)}, bf16[256,256]{1,0:T(8,128)(2,1)}, u32[]{:S(2)}, u32[]{:S(2)}) collective-permute-start(bf16[256,256]{1,0:T(8,128)(2,1)S(1)} %bitcast.125), channel_id=1, source_target_pairs={{0,4},{1,5},{2,6},{3,7},{4,0},{5,1},{6,2},{7,3},{8,12},{9,13},{10,... | collective-permute-start | bytes 393224 | tf_op jit(solution)/shard_map/ppermute | solution.py:66
  110.9 2.5 %collective-permute-start.3 = (bf16[256,256]{1,0:T(8,128)(2,1)S(1)}, bf16[256,256]{1,0:T(8,128)(2,1)S(1)}, u32[]{:S(2)}, u32[]{:S(2)}) collective-permute-start(bf16[256,256]{1,0:T(8,128)(2,1)S(1)} %bitcast.126), channel_id=1, source_target_pairs={{0,6},{1,7},{2,0},{3,1},{4,2},{5,3},{6,4},{7,5},{8,14},{9,15},{10,... | collective-permute-start | bytes 393224 | tf_op jit(solution)/shard_map/ppermute | solution.py:66
  113.4 1.6 convert_element_type.122
  115.0 1.0 constant_dynamic-slice_fusion.7
  116.2 6.1 %collective-permute-done.2 = bf16[256,256]{1,0:T(8,128)(2,1)} collective-permute-done((bf16[256,256]{1,0:T(8,128)(2,1)S(1)}, bf16[256,256]{1,0:T(8,128)(2,1)}, u32[]{:S(2)}, u32[]{:S(2)}) %collective-permute-start.2) | collective-permute-done | bytes 131104 | tf_op jit(solution)/shard_map/ppermute | solution.py:66
  122.5 0.7 copy-done.5
  123.2 1.2 constant_dynamic-update-slice_fusion.3
  124.4 1.4 collective-permute-start.4
  125.8 4.0 %collective-permute-start.5 = (bf16[256,256]{1,0:T(8,128)(2,1)S(1)}, bf16[256,256]{1,0:T(8,128)(2,1)S(1)}, u32[]{:S(2)}, u32[]{:S(2)}) collective-permute-start(bf16[256,256]{1,0:T(8,128)(2,1)S(1)} %get-tuple-element.11), channel_id=1, source_target_pairs={{0,4},{1,5},{2,6},{3,7},{4,0},{5,1},{6,2},{7,3},{8,12},{9,13},{10,... | collective-permute-start | bytes 393224 | tf_op jit(solution)/shard_map/ppermute | solution.py:76
  129.8 2.6 %collective-permute-start.6 = (bf16[256,256]{1,0:T(8,128)(2,1)S(1)}, bf16[256,256]{1,0:T(8,128)(2,1)S(1)}, u32[]{:S(2)}, u32[]{:S(2)}) collective-permute-start(bf16[256,256]{1,0:T(8,128)(2,1)S(1)} %get-tuple-element.11), channel_id=1, source_target_pairs={{0,6},{1,7},{2,0},{3,1},{4,2},{5,3},{6,4},{7,5},{8,14},{9,15},{10,... | collective-permute-start | bytes 393224 | tf_op jit(solution)/shard_map/ppermute | solution.py:76
  132.5 5.8 %collective-permute-done.5 = bf16[256,256]{1,0:T(8,128)(2,1)S(1)} collective-permute-done((bf16[256,256]{1,0:T(8,128)(2,1)S(1)}, bf16[256,256]{1,0:T(8,128)(2,1)S(1)}, u32[]{:S(2)}, u32[]{:S(2)}) %collective-permute-start.5) | collective-permute-done | bytes 131104 | tf_op jit(solution)/shard_map/ppermute | solution.py:76
  138.2 1.3 collective-permute-done.6
  139.5 0.9 pad_maximum_fusion
  140.4 0.5 collective-permute-start.7
  140.9 0.5 broadcast_multiply_fusion
  141.4 0.7 mul.284
  142.2 0.4 collective-permute-done.7
  142.7 1.0 constant_dynamic-update-slice_fusion.2
  144.1 0.8 fusion.12
  144.9 4.4 %fusion.3 = f32[4,2,256,256]{3,2,1,0:T(8,128)} fusion(bf16[384,4,2,256]{3,2,1,0:T(2,128)(2,1)} %reshape.488, bf16[2048,384]{1,0:T(8,128)(2,1)S(1)} %copy-done, bf16[256,2048]{1,0:T(8,128)(2,1)S(1)} %fusion.30, f32[2048]{0:T(1024)S(1)} %copy-done.13, f32[256]{0:T(256)S(1)} %add_rsqrt_fusion.1, f32[256,384]{1,0:T(8,128)S(1)} %fusion.12), kind=kOutput, calls=%fused_computation.11 | convolution fusion | flops 807993344 | bytes 6693888 | tf_op jit(solution)/shard_map/rk,kcip->icrp/dot_general | solution.py:57
  149.3 1.3 fusion.9
  150.6 0.4 collective-permute-start.8
  151.7 0.9 collective-permute-done.8
  152.6 1.4 fusion.61
  154.0 0.8 copy.78
  154.8 3.7 %collective-permute-start.10 = (bf16[256,256]{1,0:T(8,128)(2,1)}, bf16[256,256]{1,0:T(8,128)(2,1)S(1)}, u32[]{:S(2)}, u32[]{:S(2)}) collective-permute-start(bf16[256,256]{1,0:T(8,128)(2,1)} %bitcast.39), channel_id=1, source_target_pairs={{0,4},{1,5},{2,6},{3,7},{4,0},{5,1},{6,2},{7,3},{8,12},{9,13},{10,... | collective-permute-start | bytes 393224 | tf_op jit(solution)/shard_map/ppermute | solution.py:66
  158.5 0.8 copy.79
  159.3 1.7 collective-permute-start.11
  160.9 0.8 copy.77
  161.7 0.7 collective-permute-start.9
  162.5 0.6 gather_fusion
  163.2 0.4 collective-permute-done.10
  163.6 6.4 %collective-permute-done.11 = bf16[256,256]{1,0:T(8,128)(2,1)S(1)} collective-permute-done((bf16[256,256]{1,0:T(8,128)(2,1)}, bf16[256,256]{1,0:T(8,128)(2,1)S(1)}, u32[]{:S(2)}, u32[]{:S(2)}) %collective-permute-start.11) | collective-permute-done | bytes 131104 | tf_op jit(solution)/shard_map/ppermute | solution.py:66
  170.1 2.7 %collective-permute-done.9 = bf16[256,256]{1,0:T(8,128)(2,1)S(1)} collective-permute-done((bf16[256,256]{1,0:T(8,128)(2,1)}, bf16[256,256]{1,0:T(8,128)(2,1)S(1)}, u32[]{:S(2)}, u32[]{:S(2)}) %collective-permute-start.9) | collective-permute-done | bytes 131104 | tf_op jit(solution)/shard_map/ppermute | solution.py:66
  172.8 1.8 gather_fusion.1
  174.6 8.9 %all-to-all-start.1 = ((bf16[32,8,256]{2,1,0:T(8,128)(2,1)}), bf16[32,8,256]{2,1,0:T(8,128)(2,1)S(1)}, u32[]{:S(2)}, u32[]{:S(2)}) async-start(bf16[32,8,256]{2,1,0:T(8,128)(2,1)} %bitcast.42), calls=%async_computation.1 | async-start | bytes 262144 | tf_op jit(solution)/shard_map/all_to_all | solution.py:262
  183.7 2.4 %scatter_custom_fusion.1 = bf16[256,256]{1,0:T(8,128)(2,1)} fusion(s32[256]{0:T(256)S(1)} %bitcast.130, bf16[32,272,256]{2,1,0:T(8,128)(2,1)} %all-to-all-done.kv_ref, s32[]{:T(128)} %constant.199.clone.1, s32[]{:T(128)S(6)} %select_n.227, bf16[]{:T(256)} %constant.194.clone.1), kind=kCustom, calls=%fused_computation.52 | custom fusion | bytes 263172 | tf_op jit(solution)/shard_map/scatter | solution.py:111
  186.2 4.9 %all-to-all-done.1 = bf16[32,8,256]{2,1,0:T(8,128)(2,1)S(1)} async-done(((bf16[32,8,256]{2,1,0:T(8,128)(2,1)}), bf16[32,8,256]{2,1,0:T(8,128)(2,1)S(1)}, u32[]{:S(2)}, u32[]{:S(2)}) %all-to-all-start.1) | async-done | bytes 131104 | tf_op jit(solution)/shard_map/all_to_all | solution.py:262
  191.1 2.1 %scatter_custom_fusion = bf16[256,256]{1,0:T(8,128)(2,1)} fusion(s32[256]{0:T(256)S(1)} %bitcast.129, bf16[32,8,256]{2,1,0:T(8,128)(2,1)S(1)} %all-to-all-done.1, bf16[]{:T(256)} %constant.194.clone.1), kind=kCustom, calls=%fused_computation.54 | custom fusion | bytes 262146 | tf_op jit(solution)/shard_map/scatter | solution.py:267
  (84 shorter events, 4.1 us)
Async XLA Ops:
  0.6 144.2 %copy-start = (bf16[2048,384]{1,0:T(8,128)(2,1)S(1)}, bf16[2048,384]{1,0:T(8,128)(2,1)}, u32[]{:S(2)}) copy-start(bf16[2048,384]{1,0:T(8,128)(2,1)} %param.28) | copy-start | bytes 4718596
  0.6 6.7 %copy-start.2 = (bf16[256,2048]{1,0:T(8,128)(2,1)S(1)}, bf16[256,2048]{1,0:T(8,128)(2,1)}, u32[]{:S(2)}) copy-start(bf16[256,2048]{1,0:T(8,128)(2,1)} %param.15) | copy-start | bytes 3145732
  0.7 6.7 %copy-start.11 = (f32[2048]{0:T(1024)S(1)}, f32[2048]{0:T(1024)}, u32[]{:S(2)}) copy-start(f32[2048]{0:T(1024)} %param.19) | copy-start | bytes 24580
  0.7 6.7 %copy-start.10 = (bf16[2048,128]{1,0:T(8,128)(2,1)S(1)}, bf16[2048,128]{1,0:T(8,128)(2,1)}, u32[]{:S(2)}) copy-start(bf16[2048,128]{1,0:T(8,128)(2,1)} %param.22) | copy-start | bytes 1572868
  5.3 2.6 %copy-start.7 = (f32[128]{0:T(128)S(1)}, f32[128]{0:T(128)}, u32[]{:S(2)}) copy-start(f32[128]{0:T(128)} %param.24) | copy-start | bytes 1540
  11.1 66.7 %all-to-all-start = ((bf16[32,272,256]{2,1,0:T(8,128)(2,1)}), bf16[32,272,256]{2,1,0:T(8,128)(2,1)}, u32[]{:S(2)}, u32[]{:S(2)}) async-start(bf16[32,272,256]{2,1,0:T(8,128)(2,1)} %broadcast_in_dim.24), calls=%async_computation | async-start | bytes 8912896 | tf_op jit(solution)/shard_map/all_to_all | solution.py:42
  20.4 2.3 %copy-start.8 = (f32[128]{0:T(128)S(1)}, f32[128]{0:T(128)}, u32[]{:S(2)}) copy-start(f32[128]{0:T(128)} %param.23) | copy-start | bytes 1540
  26.9 3.5 %copy-start.6 = (s32[256]{0:T(256)S(1)}, s32[256]{0:T(256)}, u32[]{:S(2)}) copy-start(s32[256]{0:T(256)} %param.16) | copy-start | bytes 3076
  95.5 1.4 copy-start.1
  97.0 3.6 %collective-permute-start = (bf16[4,256,256]{1,2,0:T(8,128)(2,1)S(1)}, bf16[4,256,256]{1,2,0:T(8,128)(2,1)}, u32[]{:S(2)}, u32[]{:S(2)}) collective-permute-start(bf16[4,256,256]{1,2,0:T(8,128)(2,1)S(1)} %fusion.8), channel_id=1, source_target_pairs={{0,1},{1,0},{2,3},{3,2},{4,5},{5,4},{6,7},{7,6},{8,9},{9,8},{10,11... | collective-permute-start | bytes 1572872 | tf_op jit(solution)/shard_map/ppermute | solution.py:60
  103.2 13.0 %collective-permute-start.1 = (bf16[256,256]{1,0:T(8,128)(2,1)S(1)}, bf16[256,256]{1,0:T(8,128)(2,1)S(1)}, u32[]{:S(2)}, u32[]{:S(2)}) collective-permute-start(bf16[256,256]{1,0:T(8,128)(2,1)S(1)} %bitcast.124), channel_id=1, source_target_pairs={{0,2},{1,3},{2,4},{3,5},{4,6},{5,7},{6,0},{7,1},{8,10},{9,11},{10,... | collective-permute-start | bytes 393224 | tf_op jit(solution)/shard_map/ppermute | solution.py:66
  106.6 15.7 %collective-permute-start.2 = (bf16[256,256]{1,0:T(8,128)(2,1)S(1)}, bf16[256,256]{1,0:T(8,128)(2,1)}, u32[]{:S(2)}, u32[]{:S(2)}) collective-permute-start(bf16[256,256]{1,0:T(8,128)(2,1)S(1)} %bitcast.125), channel_id=1, source_target_pairs={{0,4},{1,5},{2,6},{3,7},{4,0},{5,1},{6,2},{7,3},{8,12},{9,13},{10,... | collective-permute-start | bytes 393224 | tf_op jit(solution)/shard_map/ppermute | solution.py:66
  110.9 11.5 %collective-permute-start.3 = (bf16[256,256]{1,0:T(8,128)(2,1)S(1)}, bf16[256,256]{1,0:T(8,128)(2,1)S(1)}, u32[]{:S(2)}, u32[]{:S(2)}) collective-permute-start(bf16[256,256]{1,0:T(8,128)(2,1)S(1)} %bitcast.126), channel_id=1, source_target_pairs={{0,6},{1,7},{2,0},{3,1},{4,2},{5,3},{6,4},{7,5},{8,14},{9,15},{10,... | collective-permute-start | bytes 393224 | tf_op jit(solution)/shard_map/ppermute | solution.py:66
  116.0 24.9 %copy-start.14 = (s32[64]{0:T(128)S(1)}, s32[64]{0:T(128)}, u32[]{:S(2)}) copy-start(s32[64]{0:T(128)} %param.18) | copy-start | bytes 772
  122.5 0.7 copy-start.5
  124.4 8.0 %collective-permute-start.4 = (bf16[256,256]{1,0:T(8,128)(2,1)S(1)}, bf16[256,256]{1,0:T(8,128)(2,1)S(1)}, u32[]{:S(2)}, u32[]{:S(2)}) collective-permute-start(bf16[256,256]{1,0:T(8,128)(2,1)S(1)} %get-tuple-element.11), channel_id=1, source_target_pairs={{0,2},{1,3},{2,4},{3,5},{4,6},{5,7},{6,0},{7,1},{8,10},{9,11},{10,... | collective-permute-start | bytes 393224 | tf_op jit(solution)/shard_map/ppermute | solution.py:76
  125.8 12.4 %collective-permute-start.5 = (bf16[256,256]{1,0:T(8,128)(2,1)S(1)}, bf16[256,256]{1,0:T(8,128)(2,1)S(1)}, u32[]{:S(2)}, u32[]{:S(2)}) collective-permute-start(bf16[256,256]{1,0:T(8,128)(2,1)S(1)} %get-tuple-element.11), channel_id=1, source_target_pairs={{0,4},{1,5},{2,6},{3,7},{4,0},{5,1},{6,2},{7,3},{8,12},{9,13},{10,... | collective-permute-start | bytes 393224 | tf_op jit(solution)/shard_map/ppermute | solution.py:76
  129.8 9.7 %collective-permute-start.6 = (bf16[256,256]{1,0:T(8,128)(2,1)S(1)}, bf16[256,256]{1,0:T(8,128)(2,1)S(1)}, u32[]{:S(2)}, u32[]{:S(2)}) collective-permute-start(bf16[256,256]{1,0:T(8,128)(2,1)S(1)} %get-tuple-element.11), channel_id=1, source_target_pairs={{0,6},{1,7},{2,0},{3,1},{4,2},{5,3},{6,4},{7,5},{8,14},{9,15},{10,... | collective-permute-start | bytes 393224 | tf_op jit(solution)/shard_map/ppermute | solution.py:76
  132.4 7.1 %copy-start.3 = (bf16[256,256]{1,0:T(8,128)(2,1)}, bf16[256,256]{1,0:T(8,128)(2,1)S(1)}, u32[]{:S(2)}) copy-start(bf16[256,256]{1,0:T(8,128)(2,1)S(1)} %collective-permute-done.4) | copy-start | bytes 393220
  140.4 2.2 %collective-permute-start.7 = (bf16[4,256,256]{2,1,0:T(8,128)(2,1)}, bf16[4,256,256]{2,1,0:T(8,128)(2,1)S(1)}, u32[]{:S(2)}, u32[]{:S(2)}) collective-permute-start(bf16[4,256,256]{2,1,0:T(8,128)(2,1)} %pad_maximum_fusion), channel_id=1, source_target_pairs={{0,1},{1,0},{2,3},{3,2},{4,5},{5,4},{6,7},{7,6},{8,9},{9,8},{10,11... | collective-permute-start | bytes 1572872 | tf_op jit(solution)/shard_map/ppermute | solution.py:78
  142.2 1.8 copy-start.9
  142.2 1.8 copy-start.12
  144.0 0.8 copy-start.13
  144.9 6.6 %copy-start.4 = (s32[32,1,256]{2,1,0:T(1,128)S(1)}, s32[32,1,256]{2,1,0:T(1,128)}, u32[]{:S(2)}) copy-start(s32[32,1,256]{2,1,0:T(1,128)} %fusion.50) | copy-start | bytes 98308
  150.6 2.0 %collective-permute-start.8 = (bf16[4,256,256]{1,2,0:T(8,128)(2,1)S(1)}, bf16[4,256,256]{1,2,0:T(8,128)(2,1)S(1)}, u32[]{:S(2)}, u32[]{:S(2)}) collective-permute-start(bf16[4,256,256]{1,2,0:T(8,128)(2,1)S(1)} %fusion.9), channel_id=1, source_target_pairs={{0,1},{1,0},{2,3},{3,2},{4,5},{5,4},{6,7},{7,6},{8,9},{9,8},{10,11... | collective-permute-start | bytes 1572872 | tf_op jit(solution)/shard_map/ppermute | solution.py:60
  154.8 8.9 %collective-permute-start.10 = (bf16[256,256]{1,0:T(8,128)(2,1)}, bf16[256,256]{1,0:T(8,128)(2,1)S(1)}, u32[]{:S(2)}, u32[]{:S(2)}) collective-permute-start(bf16[256,256]{1,0:T(8,128)(2,1)} %bitcast.39), channel_id=1, source_target_pairs={{0,4},{1,5},{2,6},{3,7},{4,0},{5,1},{6,2},{7,3},{8,12},{9,13},{10,... | collective-permute-start | bytes 393224 | tf_op jit(solution)/shard_map/ppermute | solution.py:66
  159.3 10.8 %collective-permute-start.11 = (bf16[256,256]{1,0:T(8,128)(2,1)}, bf16[256,256]{1,0:T(8,128)(2,1)S(1)}, u32[]{:S(2)}, u32[]{:S(2)}) collective-permute-start(bf16[256,256]{1,0:T(8,128)(2,1)} %bitcast.40), channel_id=1, source_target_pairs={{0,6},{1,7},{2,0},{3,1},{4,2},{5,3},{6,4},{7,5},{8,14},{9,15},{10,... | collective-permute-start | bytes 393224 | tf_op jit(solution)/shard_map/ppermute | solution.py:66
  161.7 11.1 %collective-permute-start.9 = (bf16[256,256]{1,0:T(8,128)(2,1)}, bf16[256,256]{1,0:T(8,128)(2,1)S(1)}, u32[]{:S(2)}, u32[]{:S(2)}) collective-permute-start(bf16[256,256]{1,0:T(8,128)(2,1)} %bitcast.38), channel_id=1, source_target_pairs={{0,2},{1,3},{2,4},{3,5},{4,6},{5,7},{6,0},{7,1},{8,10},{9,11},{10,... | collective-permute-start | bytes 393224 | tf_op jit(solution)/shard_map/ppermute | solution.py:66
  174.6 16.5 %all-to-all-start.1 = ((bf16[32,8,256]{2,1,0:T(8,128)(2,1)}), bf16[32,8,256]{2,1,0:T(8,128)(2,1)S(1)}, u32[]{:S(2)}, u32[]{:S(2)}) async-start(bf16[32,8,256]{2,1,0:T(8,128)(2,1)} %bitcast.42), calls=%async_computation.1 | async-start | bytes 262144 | tf_op jit(solution)/shard_map/all_to_all | solution.py:262

commit v12 on v11

--- a/solution.py
+++ b/solution.py
@@ -4,6 +4,7 @@
 import jax.numpy as jnp
 from jax import lax
 from jax.experimental import pallas as pl
+from jax.experimental.pallas import tpu as pltpu
 from jax.sharding import PartitionSpec as P
 
 HD = 128
@@ -117,7 +118,7 @@
 UNROLL = 4
 
 
-def attend_kernel(q_ref, qtok_ref, qbeg_ref, kv_ref, ktok_ref, out_ref, *, rows):
+def attend_kernel(q_ref, qtok_ref, qbeg_ref, kv_ref, ktok_ref, out_ref, score_ref, *, rows):
     query = q_ref[...]
     qtok = qtok_ref[...]
     qbeg = qbeg_ref[...]
@@ -142,7 +143,8 @@
         return jnp.where(mask, raw, -1e30), start
 
     def find_top(chunk, top):
-        score, _ = scores(chunk)
+        score, start = scores(chunk)
+        score_ref[:, pl.ds(start, KEY_CHUNK)] = score
         return jnp.maximum(top, jnp.max(score, axis=1, keepdims=True))
 
     top = lax.fori_loop(
@@ -151,8 +153,8 @@
 
     def accumulate(chunk, carry):
         total, accum = carry
-        score, start = scores(chunk)
-        weights = jnp.exp(score - top)
+        start = pl.multiple_of(chunk * KEY_CHUNK, KEY_CHUNK)
+        weights = jnp.exp(score_ref[:, pl.ds(start, KEY_CHUNK)] - top)
         values = block(chunk, HD)
         total = total + jnp.sum(weights, axis=1, keepdims=True)
         accum = accum + jnp.dot(
@@ -187,6 +189,7 @@
         ],
         out_specs=pl.BlockSpec((tile, HD), lambda i: (i, 0)),
         out_shape=jax.ShapeDtypeStruct((count, HD), jnp.bfloat16),
+        scratch_shapes=[pltpu.VMEM((tile, keys), jnp.float32)],
     )(query, query_tokens, query_begins, pieces, key_tokens)
 
 

time: 194 us -> 194 us (level)
  no operation moved by 1% of the time
where the time goes in v12:
time: 194 us; the launch traced here: 193 us
  waiting for transfers between devices  76.4 us (39%)
  starting transfers between devices  45.2 us (23%)
  local copies, waits for them, and re-layouts  28.8 us (15%)
  other arithmetic  16.7 us (9%)
  Pallas kernels  13.4 us (7%)
  matrix products  11.4 us (6%)
    all_to_all x1, waiting for transfers between devices, gather_seq(): lax.all_to_all(copies, 'seq', split_axis=0, concat_axis=0, tiled=True)  45.6 us
    ppermute x6, starting transfers between devices, project_reduce_tp(): lax.ppermute(piece, 'tp', chip_shift(tp_count, shift)).astype(jnp.float32)  16.1 us
    ppermute x6, waiting for transfers between devices, project_reduce_tp(): lax.ppermute(piece, 'tp', chip_shift(tp_count, shift)).astype(jnp.float32)  15.8 us
    pallas_call x1, Pallas kernels, attend(): pl.pallas_call(functools.partial(attend_kernel, rows=rows), grid=(count /...  13.4 us
    all_to_all x1, starting transfers between devices, gather_seq(): lax.all_to_all(copies, 'seq', split_axis=0, concat_axis=0, tiled=True)  9.34 us
    all_to_all x1, starting transfers between devices, body(): lax.all_to_all(out[send_rows], 'seq', split_axis=0, concat_axis=0, tiled=...  8.9 us
    ppermute x3, starting transfers between devices, gather_tp(): lax.ppermute(block, 'tp', chip_shift(tp_count, shift))  8.04 us
    ppermute x3, waiting for transfers between devices, gather_tp(): lax.ppermute(block, 'tp', chip_shift(tp_count, shift))  7.07 us
  transfers between devices with their start and end apart: 14, of which 12 were waited for; matrix products, arithmetic and copies ran while one was open for 11% of the time, Pallas kernels for 0%

profile of v12, /device:TPU:1, one launch (start us, length us, event | category | flops | bytes accessed | tf_op | source)
XLA Modules:
  0.0 193.2 jit_solution(7005269317316375462)
XLA Ops:
  0.7 1.7 multiply_reduce_fusion
  2.4 0.8 reduce-window.9
  3.2 0.7 bitcast_subtract_fusion
  3.9 0.8 select_reduce_fusion
  4.6 0.7 subtract_convert_fusion.1
  5.3 2.0 %multiply_reduce_fusion.2 = (f32[256]{0:T(256)S(1)}, f32[256,128]{0,1:T(8,128)S(1)}) fusion(bf16[2048,128]{1,0:T(8,128)(2,1)} %param.21, f32[2048]{0:T(1024)} %param.19, f32[256]{0:T(256)S(1)} %add_rsqrt_fusion.3, bf16[256,2048]{1,0:T(8,128)(2,1)} %param.15), kind=kOutput, calls=%fused_computation.61 | convolution fusion | flops 136380160 | bytes 1714176 | tf_op jit(solution)/shard_map/dot_general | solution.py:225
  7.3 0.6 fusion.5
  8.7 2.4 %broadcast_in_dim.24 = bf16[32,272,256]{2,1,0:T(8,128)(2,1)} broadcast(bf16[272,256]{1,0:T(8,128)(2,1)S(1)} %maximum_maximum_fusion), dimensions={1,2} | broadcast | bytes 4595712 | tf_op jit(solution)/shard_map/broadcast_in_dim | solution.py:42
  11.1 9.3 %all-to-all-start = ((bf16[32,272,256]{2,1,0:T(8,128)(2,1)}), bf16[32,272,256]{2,1,0:T(8,128)(2,1)}, u32[]{:S(2)}, u32[]{:S(2)}) async-start(bf16[32,272,256]{2,1,0:T(8,128)(2,1)} %broadcast_in_dim.24), calls=%async_computation | async-start | bytes 8912896 | tf_op jit(solution)/shard_map/all_to_all | solution.py:43
  20.5 1.9 multiply_reduce_fusion.1
  23.1 3.9 %reshape.488 = bf16[384,4,2,256]{3,2,1,0:T(2,128)(2,1)} reshape(bf16[384,2048]{1,0:T(8,128)(2,1)} %param.29) | data formatting | bytes 3145728 | tf_op jit(solution)/shard_map/reshape | solution.py:237
  26.9 2.6 %reshape.487 = bf16[256,4,2,256]{3,2,1,0:T(2,128)(2,1)} reshape(bf16[256,2048]{1,0:T(8,128)(2,1)} %param.25) | data formatting | bytes 2097152 | tf_op jit(solution)/shard_map/reshape | solution.py:236
  29.6 0.8 broadcast_in_dim_reshape.10.qbeg_ref
  30.6 0.8 broadcast_in_dim_reshape.9.qtok_ref
  31.4 0.8 pad_maximum_fusion.2.q_ref
  32.1 45.6 %all-to-all-done.kv_ref = bf16[32,272,256]{2,1,0:T(8,128)(2,1)} async-done(((bf16[32,272,256]{2,1,0:T(8,128)(2,1)}), bf16[32,272,256]{2,1,0:T(8,128)(2,1)}, u32[]{:S(2)}, u32[]{:S(2)}) %all-to-all-start) | async-done | bytes 4456480 | tf_op jit(solution)/shard_map/all_to_all | solution.py:43
  77.7 1.7 fusion.50
  79.4 13.4 %shard_map.158 = bf16[512,128]{1,0:T(8,128)(2,1)} custom-call(bf16[512,128]{1,0:T(8,128)(2,1)} %pad_maximum_fusion.2.q_ref, s32[512,1]{1,0:T(8,128)} %broadcast_in_dim_reshape.9.qtok_ref, s32[512,1]{1,0:T(8,128)} %broadcast_in_dim_reshape.10.qbeg_ref, bf16[32,272,256]{2,1,0:T(8,128)(2,1)} %all-to-all-done.kv_ref, s32[1,8192]{1,0:T(1,128)} %bitcast.123), custom_call_target="tpu_custom_call" | custom-call | tf_op jit(solution)/shard_map/pallas_call | solution.py:180
  92.8 1.0 reshape.526
  93.8 1.8 fusion.6
  95.5 1.4 copy-done.1
  97.0 1.9 collective-permute-start
  98.9 1.7 collective-permute-done
  100.5 2.5 %fusion.63 = (bf16[4,256,256]{1,2,0:T(8,128)(2,1)S(1)}, f32[4,256,256]{1,2,0:T(8,128)}) fusion(bf16[4,256,256]{1,2,0:T(8,128)(2,1)} %collective-permute-done, f32[4,2,256,256]{3,2,1,0:T(8,128)} %copy-done.1, s32[]{:T(128)S(6)} %select_n.200), kind=kLoop, calls=%fused_computation.135 | loop fusion | flops 786432 | bytes 3145732 | tf_op jit(solution)/shard_map/convert_element_type | solution.py:64
  103.2 3.3 %collective-permute-start.1 = (bf16[256,256]{1,0:T(8,128)(2,1)S(1)}, bf16[256,256]{1,0:T(8,128)(2,1)S(1)}, u32[]{:S(2)}, u32[]{:S(2)}) collective-permute-start(bf16[256,256]{1,0:T(8,128)(2,1)S(1)} %bitcast.124), channel_id=1, source_target_pairs={{0,2},{1,3},{2,4},{3,5},{4,6},{5,7},{6,0},{7,1},{8,10},{9,11},{10,... | collective-permute-start | bytes 393224 | tf_op jit(solution)/shard_map/ppermute | solution.py:67
  106.6 4.3 %collective-permute-start.2 = (bf16[256,256]{1,0:T(8,128)(2,1)S(1)}, bf16[256,256]{1,0:T(8,128)(2,1)}, u32[]{:S(2)}, u32[]{:S(2)}) collective-permute-start(bf16[256,256]{1,0:T(8,128)(2,1)S(1)} %bitcast.125), channel_id=1, source_target_pairs={{0,4},{1,5},{2,6},{3,7},{4,0},{5,1},{6,2},{7,3},{8,12},{9,13},{10,... | collective-permute-start | bytes 393224 | tf_op jit(solution)/shard_map/ppermute | solution.py:67
  110.9 2.5 %collective-permute-start.3 = (bf16[256,256]{1,0:T(8,128)(2,1)S(1)}, bf16[256,256]{1,0:T(8,128)(2,1)S(1)}, u32[]{:S(2)}, u32[]{:S(2)}) collective-permute-start(bf16[256,256]{1,0:T(8,128)(2,1)S(1)} %bitcast.126), channel_id=1, source_target_pairs={{0,6},{1,7},{2,0},{3,1},{4,2},{5,3},{6,4},{7,5},{8,14},{9,15},{10,... | collective-permute-start | bytes 393224 | tf_op jit(solution)/shard_map/ppermute | solution.py:67
  113.4 1.6 convert_element_type.122
  115.0 1.0 constant_dynamic-slice_fusion.7
  116.2 6.1 %collective-permute-done.2 = bf16[256,256]{1,0:T(8,128)(2,1)} collective-permute-done((bf16[256,256]{1,0:T(8,128)(2,1)S(1)}, bf16[256,256]{1,0:T(8,128)(2,1)}, u32[]{:S(2)}, u32[]{:S(2)}) %collective-permute-start.2) | collective-permute-done | bytes 131104 | tf_op jit(solution)/shard_map/ppermute | solution.py:67
  122.5 0.7 copy-done.5
  123.2 1.2 constant_dynamic-update-slice_fusion.3
  124.4 1.4 collective-permute-start.4
  125.8 4.0 %collective-permute-start.5 = (bf16[256,256]{1,0:T(8,128)(2,1)S(1)}, bf16[256,256]{1,0:T(8,128)(2,1)S(1)}, u32[]{:S(2)}, u32[]{:S(2)}) collective-permute-start(bf16[256,256]{1,0:T(8,128)(2,1)S(1)} %get-tuple-element.11), channel_id=1, source_target_pairs={{0,4},{1,5},{2,6},{3,7},{4,0},{5,1},{6,2},{7,3},{8,12},{9,13},{10,... | collective-permute-start | bytes 393224 | tf_op jit(solution)/shard_map/ppermute | solution.py:77
  129.8 2.6 %collective-permute-start.6 = (bf16[256,256]{1,0:T(8,128)(2,1)S(1)}, bf16[256,256]{1,0:T(8,128)(2,1)S(1)}, u32[]{:S(2)}, u32[]{:S(2)}) collective-permute-start(bf16[256,256]{1,0:T(8,128)(2,1)S(1)} %get-tuple-element.11), channel_id=1, source_target_pairs={{0,6},{1,7},{2,0},{3,1},{4,2},{5,3},{6,4},{7,5},{8,14},{9,15},{10,... | collective-permute-start | bytes 393224 | tf_op jit(solution)/shard_map/ppermute | solution.py:77
  132.5 5.8 %collective-permute-done.5 = bf16[256,256]{1,0:T(8,128)(2,1)S(1)} collective-permute-done((bf16[256,256]{1,0:T(8,128)(2,1)S(1)}, bf16[256,256]{1,0:T(8,128)(2,1)S(1)}, u32[]{:S(2)}, u32[]{:S(2)}) %collective-permute-start.5) | collective-permute-done | bytes 131104 | tf_op jit(solution)/shard_map/ppermute | solution.py:77
  138.2 1.3 collective-permute-done.6
  139.5 0.9 pad_maximum_fusion
  140.4 0.5 collective-permute-start.7
  140.9 0.5 broadcast_multiply_fusion
  141.4 0.7 mul.284
  142.2 0.4 collective-permute-done.7
  142.7 1.0 constant_dynamic-update-slice_fusion.2
  144.1 0.8 fusion.12
  144.9 4.4 %fusion.3 = f32[4,2,256,256]{3,2,1,0:T(8,128)} fusion(bf16[384,4,2,256]{3,2,1,0:T(2,128)(2,1)} %reshape.488, bf16[2048,384]{1,0:T(8,128)(2,1)S(1)} %copy-done, bf16[256,2048]{1,0:T(8,128)(2,1)S(1)} %fusion.30, f32[2048]{0:T(1024)S(1)} %copy-done.13, f32[256]{0:T(256)S(1)} %add_rsqrt_fusion.1, f32[256,384]{1,0:T(8,128)S(1)} %fusion.12), kind=kOutput, calls=%fused_computation.11 | convolution fusion | flops 807993344 | bytes 6693888 | tf_op jit(solution)/shard_map/rk,kcip->icrp/dot_general | solution.py:58
  149.3 1.3 fusion.9
  150.6 0.4 collective-permute-start.8
  151.7 0.9 collective-permute-done.8
  152.6 1.4 fusion.61
  154.0 0.8 copy.78
  154.8 3.7 %collective-permute-start.10 = (bf16[256,256]{1,0:T(8,128)(2,1)}, bf16[256,256]{1,0:T(8,128)(2,1)S(1)}, u32[]{:S(2)}, u32[]{:S(2)}) collective-permute-start(bf16[256,256]{1,0:T(8,128)(2,1)} %bitcast.39), channel_id=1, source_target_pairs={{0,4},{1,5},{2,6},{3,7},{4,0},{5,1},{6,2},{7,3},{8,12},{9,13},{10,... | collective-permute-start | bytes 393224 | tf_op jit(solution)/shard_map/ppermute | solution.py:67
  158.5 0.8 copy.79
  159.3 1.7 collective-permute-start.11
  160.9 0.8 copy.77
  161.7 0.7 collective-permute-start.9
  162.5 0.6 gather_fusion
  163.2 0.4 collective-permute-done.10
  163.6 6.4 %collective-permute-done.11 = bf16[256,256]{1,0:T(8,128)(2,1)S(1)} collective-permute-done((bf16[256,256]{1,0:T(8,128)(2,1)}, bf16[256,256]{1,0:T(8,128)(2,1)S(1)}, u32[]{:S(2)}, u32[]{:S(2)}) %collective-permute-start.11) | collective-permute-done | bytes 131104 | tf_op jit(solution)/shard_map/ppermute | solution.py:67
  170.1 2.7 %collective-permute-done.9 = bf16[256,256]{1,0:T(8,128)(2,1)S(1)} collective-permute-done((bf16[256,256]{1,0:T(8,128)(2,1)}, bf16[256,256]{1,0:T(8,128)(2,1)S(1)}, u32[]{:S(2)}, u32[]{:S(2)}) %collective-permute-start.9) | collective-permute-done | bytes 131104 | tf_op jit(solution)/shard_map/ppermute | solution.py:67
  172.8 1.8 gather_fusion.1
  174.6 8.9 %all-to-all-start.1 = ((bf16[32,8,256]{2,1,0:T(8,128)(2,1)}), bf16[32,8,256]{2,1,0:T(8,128)(2,1)S(1)}, u32[]{:S(2)}, u32[]{:S(2)}) async-start(bf16[32,8,256]{2,1,0:T(8,128)(2,1)} %bitcast.42), calls=%async_computation.1 | async-start | bytes 262144 | tf_op jit(solution)/shard_map/all_to_all | solution.py:265
  183.7 2.4 %scatter_custom_fusion.1 = bf16[256,256]{1,0:T(8,128)(2,1)} fusion(s32[256]{0:T(256)S(1)} %bitcast.130, bf16[32,272,256]{2,1,0:T(8,128)(2,1)} %all-to-all-done.kv_ref, s32[]{:T(128)} %constant.199.clone.1, s32[]{:T(128)S(6)} %select_n.227, bf16[]{:T(256)} %constant.194.clone.1), kind=kCustom, calls=%fused_computation.52 | custom fusion | bytes 263172 | tf_op jit(solution)/shard_map/scatter | solution.py:112
  186.2 4.9 %all-to-all-done.1 = bf16[32,8,256]{2,1,0:T(8,128)(2,1)S(1)} async-done(((bf16[32,8,256]{2,1,0:T(8,128)(2,1)}), bf16[32,8,256]{2,1,0:T(8,128)(2,1)S(1)}, u32[]{:S(2)}, u32[]{:S(2)}) %all-to-all-start.1) | async-done | bytes 131104 | tf_op jit(solution)/shard_map/all_to_all | solution.py:265
  191.1 2.1 %scatter_custom_fusion = bf16[256,256]{1,0:T(8,128)(2,1)} fusion(s32[256]{0:T(256)S(1)} %bitcast.129, bf16[32,8,256]{2,1,0:T(8,128)(2,1)S(1)} %all-to-all-done.1, bf16[]{:T(256)} %constant.194.clone.1), kind=kCustom, calls=%fused_computation.54 | custom fusion | bytes 262146 | tf_op jit(solution)/shard_map/scatter | solution.py:270
  (84 shorter events, 4.1 us)
Async XLA Ops:
  0.6 144.2 %copy-start = (bf16[2048,384]{1,0:T(8,128)(2,1)S(1)}, bf16[2048,384]{1,0:T(8,128)(2,1)}, u32[]{:S(2)}) copy-start(bf16[2048,384]{1,0:T(8,128)(2,1)} %param.28) | copy-start | bytes 4718596
  0.6 6.7 %copy-start.2 = (bf16[256,2048]{1,0:T(8,128)(2,1)S(1)}, bf16[256,2048]{1,0:T(8,128)(2,1)}, u32[]{:S(2)}) copy-start(bf16[256,2048]{1,0:T(8,128)(2,1)} %param.15) | copy-start | bytes 3145732
  0.7 6.7 %copy-start.11 = (f32[2048]{0:T(1024)S(1)}, f32[2048]{0:T(1024)}, u32[]{:S(2)}) copy-start(f32[2048]{0:T(1024)} %param.19) | copy-start | bytes 24580
  0.7 6.7 %copy-start.10 = (bf16[2048,128]{1,0:T(8,128)(2,1)S(1)}, bf16[2048,128]{1,0:T(8,128)(2,1)}, u32[]{:S(2)}) copy-start(bf16[2048,128]{1,0:T(8,128)(2,1)} %param.22) | copy-start | bytes 1572868
  5.3 2.6 %copy-start.7 = (f32[128]{0:T(128)S(1)}, f32[128]{0:T(128)}, u32[]{:S(2)}) copy-start(f32[128]{0:T(128)} %param.24) | copy-start | bytes 1540
  11.1 66.7 %all-to-all-start = ((bf16[32,272,256]{2,1,0:T(8,128)(2,1)}), bf16[32,272,256]{2,1,0:T(8,128)(2,1)}, u32[]{:S(2)}, u32[]{:S(2)}) async-start(bf16[32,272,256]{2,1,0:T(8,128)(2,1)} %broadcast_in_dim.24), calls=%async_computation | async-start | bytes 8912896 | tf_op jit(solution)/shard_map/all_to_all | solution.py:43
  20.4 2.3 %copy-start.8 = (f32[128]{0:T(128)S(1)}, f32[128]{0:T(128)}, u32[]{:S(2)}) copy-start(f32[128]{0:T(128)} %param.23) | copy-start | bytes 1540
  26.9 3.5 %copy-start.6 = (s32[256]{0:T(256)S(1)}, s32[256]{0:T(256)}, u32[]{:S(2)}) copy-start(s32[256]{0:T(256)} %param.16) | copy-start | bytes 3076
  95.5 1.4 copy-start.1
  97.0 3.6 %collective-permute-start = (bf16[4,256,256]{1,2,0:T(8,128)(2,1)S(1)}, bf16[4,256,256]{1,2,0:T(8,128)(2,1)}, u32[]{:S(2)}, u32[]{:S(2)}) collective-permute-start(bf16[4,256,256]{1,2,0:T(8,128)(2,1)S(1)} %fusion.8), channel_id=1, source_target_pairs={{0,1},{1,0},{2,3},{3,2},{4,5},{5,4},{6,7},{7,6},{8,9},{9,8},{10,11... | collective-permute-start | bytes 1572872 | tf_op jit(solution)/shard_map/ppermute | solution.py:61
  103.2 13.0 %collective-permute-start.1 = (bf16[256,256]{1,0:T(8,128)(2,1)S(1)}, bf16[256,256]{1,0:T(8,128)(2,1)S(1)}, u32[]{:S(2)}, u32[]{:S(2)}) collective-permute-start(bf16[256,256]{1,0:T(8,128)(2,1)S(1)} %bitcast.124), channel_id=1, source_target_pairs={{0,2},{1,3},{2,4},{3,5},{4,6},{5,7},{6,0},{7,1},{8,10},{9,11},{10,... | collective-permute-start | bytes 393224 | tf_op jit(solution)/shard_map/ppermute | solution.py:67
  106.6 15.7 %collective-permute-start.2 = (bf16[256,256]{1,0:T(8,128)(2,1)S(1)}, bf16[256,256]{1,0:T(8,128)(2,1)}, u32[]{:S(2)}, u32[]{:S(2)}) collective-permute-start(bf16[256,256]{1,0:T(8,128)(2,1)S(1)} %bitcast.125), channel_id=1, source_target_pairs={{0,4},{1,5},{2,6},{3,7},{4,0},{5,1},{6,2},{7,3},{8,12},{9,13},{10,... | collective-permute-start | bytes 393224 | tf_op jit(solution)/shard_map/ppermute | solution.py:67
  110.9 11.5 %collective-permute-start.3 = (bf16[256,256]{1,0:T(8,128)(2,1)S(1)}, bf16[256,256]{1,0:T(8,128)(2,1)S(1)}, u32[]{:S(2)}, u32[]{:S(2)}) collective-permute-start(bf16[256,256]{1,0:T(8,128)(2,1)S(1)} %bitcast.126), channel_id=1, source_target_pairs={{0,6},{1,7},{2,0},{3,1},{4,2},{5,3},{6,4},{7,5},{8,14},{9,15},{10,... | collective-permute-start | bytes 393224 | tf_op jit(solution)/shard_map/ppermute | solution.py:67
  116.0 24.9 %copy-start.14 = (s32[64]{0:T(128)S(1)}, s32[64]{0:T(128)}, u32[]{:S(2)}) copy-start(s32[64]{0:T(128)} %param.18) | copy-start | bytes 772
  122.5 0.7 copy-start.5
  124.4 8.0 %collective-permute-start.4 = (bf16[256,256]{1,0:T(8,128)(2,1)S(1)}, bf16[256,256]{1,0:T(8,128)(2,1)S(1)}, u32[]{:S(2)}, u32[]{:S(2)}) collective-permute-start(bf16[256,256]{1,0:T(8,128)(2,1)S(1)} %get-tuple-element.11), channel_id=1, source_target_pairs={{0,2},{1,3},{2,4},{3,5},{4,6},{5,7},{6,0},{7,1},{8,10},{9,11},{10,... | collective-permute-start | bytes 393224 | tf_op jit(solution)/shard_map/ppermute | solution.py:77
  125.8 12.4 %collective-permute-start.5 = (bf16[256,256]{1,0:T(8,128)(2,1)S(1)}, bf16[256,256]{1,0:T(8,128)(2,1)S(1)}, u32[]{:S(2)}, u32[]{:S(2)}) collective-permute-start(bf16[256,256]{1,0:T(8,128)(2,1)S(1)} %get-tuple-element.11), channel_id=1, source_target_pairs={{0,4},{1,5},{2,6},{3,7},{4,0},{5,1},{6,2},{7,3},{8,12},{9,13},{10,... | collective-permute-start | bytes 393224 | tf_op jit(solution)/shard_map/ppermute | solution.py:77
  129.8 9.7 %collective-permute-start.6 = (bf16[256,256]{1,0:T(8,128)(2,1)S(1)}, bf16[256,256]{1,0:T(8,128)(2,1)S(1)}, u32[]{:S(2)}, u32[]{:S(2)}) collective-permute-start(bf16[256,256]{1,0:T(8,128)(2,1)S(1)} %get-tuple-element.11), channel_id=1, source_target_pairs={{0,6},{1,7},{2,0},{3,1},{4,2},{5,3},{6,4},{7,5},{8,14},{9,15},{10,... | collective-permute-start | bytes 393224 | tf_op jit(solution)/shard_map/ppermute | solution.py:77
  132.4 7.1 %copy-start.3 = (bf16[256,256]{1,0:T(8,128)(2,1)}, bf16[256,256]{1,0:T(8,128)(2,1)S(1)}, u32[]{:S(2)}) copy-start(bf16[256,256]{1,0:T(8,128)(2,1)S(1)} %collective-permute-done.4) | copy-start | bytes 393220
  140.4 2.2 %collective-permute-start.7 = (bf16[4,256,256]{2,1,0:T(8,128)(2,1)}, bf16[4,256,256]{2,1,0:T(8,128)(2,1)S(1)}, u32[]{:S(2)}, u32[]{:S(2)}) collective-permute-start(bf16[4,256,256]{2,1,0:T(8,128)(2,1)} %pad_maximum_fusion), channel_id=1, source_target_pairs={{0,1},{1,0},{2,3},{3,2},{4,5},{5,4},{6,7},{7,6},{8,9},{9,8},{10,11... | collective-permute-start | bytes 1572872 | tf_op jit(solution)/shard_map/ppermute | solution.py:79
  142.2 1.8 copy-start.9
  142.2 1.8 copy-start.12
  144.0 0.8 copy-start.13
  144.9 6.6 %copy-start.4 = (s32[32,1,256]{2,1,0:T(1,128)S(1)}, s32[32,1,256]{2,1,0:T(1,128)}, u32[]{:S(2)}) copy-start(s32[32,1,256]{2,1,0:T(1,128)} %fusion.50) | copy-start | bytes 98308
  150.6 2.0 %collective-permute-start.8 = (bf16[4,256,256]{1,2,0:T(8,128)(2,1)S(1)}, bf16[4,256,256]{1,2,0:T(8,128)(2,1)S(1)}, u32[]{:S(2)}, u32[]{:S(2)}) collective-permute-start(bf16[4,256,256]{1,2,0:T(8,128)(2,1)S(1)} %fusion.9), channel_id=1, source_target_pairs={{0,1},{1,0},{2,3},{3,2},{4,5},{5,4},{6,7},{7,6},{8,9},{9,8},{10,11... | collective-permute-start | bytes 1572872 | tf_op jit(solution)/shard_map/ppermute | solution.py:61
  154.8 8.9 %collective-permute-start.10 = (bf16[256,256]{1,0:T(8,128)(2,1)}, bf16[256,256]{1,0:T(8,128)(2,1)S(1)}, u32[]{:S(2)}, u32[]{:S(2)}) collective-permute-start(bf16[256,256]{1,0:T(8,128)(2,1)} %bitcast.39), channel_id=1, source_target_pairs={{0,4},{1,5},{2,6},{3,7},{4,0},{5,1},{6,2},{7,3},{8,12},{9,13},{10,... | collective-permute-start | bytes 393224 | tf_op jit(solution)/shard_map/ppermute | solution.py:67
  159.3 10.8 %collective-permute-start.11 = (bf16[256,256]{1,0:T(8,128)(2,1)}, bf16[256,256]{1,0:T(8,128)(2,1)S(1)}, u32[]{:S(2)}, u32[]{:S(2)}) collective-permute-start(bf16[256,256]{1,0:T(8,128)(2,1)} %bitcast.40), channel_id=1, source_target_pairs={{0,6},{1,7},{2,0},{3,1},{4,2},{5,3},{6,4},{7,5},{8,14},{9,15},{10,... | collective-permute-start | bytes 393224 | tf_op jit(solution)/shard_map/ppermute | solution.py:67
  161.7 11.1 %collective-permute-start.9 = (bf16[256,256]{1,0:T(8,128)(2,1)}, bf16[256,256]{1,0:T(8,128)(2,1)S(1)}, u32[]{:S(2)}, u32[]{:S(2)}) collective-permute-start(bf16[256,256]{1,0:T(8,128)(2,1)} %bitcast.38), channel_id=1, source_target_pairs={{0,2},{1,3},{2,4},{3,5},{4,6},{5,7},{6,0},{7,1},{8,10},{9,11},{10,... | collective-permute-start | bytes 393224 | tf_op jit(solution)/shard_map/ppermute | solution.py:67
  174.6 16.5 %all-to-all-start.1 = ((bf16[32,8,256]{2,1,0:T(8,128)(2,1)}), bf16[32,8,256]{2,1,0:T(8,128)(2,1)S(1)}, u32[]{:S(2)}, u32[]{:S(2)}) async-start(bf16[32,8,256]{2,1,0:T(8,128)(2,1)} %bitcast.42), calls=%async_computation.1 | async-start | bytes 262144 | tf_op jit(solution)/shard_map/all_to_all | solution.py:265

commit v13 on v11

--- a/solution.py
+++ b/solution.py
@@ -94,7 +94,9 @@
     low = (token_order % TOKEN_BASE).astype(jnp.bfloat16)
     token_rows = jnp.stack([high, low]).reshape(2 * rows // width, width)
     padding = jnp.zeros((PAYLOAD_EXTRA - token_rows.shape[0], width), jnp.bfloat16)
-    arrived = gather_seq(jnp.concatenate([stacked, token_rows, padding], axis=0), seq_count)
+    parts = [jnp.broadcast_to(x[None], (seq_count,) + x.shape) for x in (stacked, token_rows, padding)]
+    copies = jnp.concatenate(parts, axis=1)
+    arrived = lax.all_to_all(copies, "seq", split_axis=0, concat_axis=0, tiled=True)
     coded = arrived[:, rows : rows + token_rows.shape[0], :].reshape(seq_count, 2, rows)
     tokens = coded[:, 0].astype(jnp.int32) * TOKEN_BASE + coded[:, 1].astype(jnp.int32)
     return arrived, tokens

time: 194 us -> 196 us (1.010)
  other arithmetic: 16.7 us -> 19.9 us
    concatenate x1, other arithmetic: 0.11 us -> 3.35 us  [gather_with_tokens(): copies = jnp.concatenate(parts, axis=1)]
where the time goes in v13:
time: 196 us; the launch traced here: 195 us
  waiting for transfers between devices  76.4 us (39%)
  starting transfers between devices  45.2 us (23%)
  local copies, waits for them, and re-layouts  26.9 us (14%)
  other arithmetic  19.9 us (10%)
  Pallas kernels  13.4 us (7%)
  matrix products  11.4 us (6%)
    all_to_all x1, waiting for transfers between devices, gather_with_tokens(): lax.all_to_all(copies, 'seq', split_axis=0, concat_axis=0, tiled=True)  45.6 us
    ppermute x6, starting transfers between devices, project_reduce_tp(): lax.ppermute(piece, 'tp', chip_shift(tp_count, shift)).astype(jnp.float32)  16 us
    ppermute x6, waiting for transfers between devices, project_reduce_tp(): lax.ppermute(piece, 'tp', chip_shift(tp_count, shift)).astype(jnp.float32)  15.8 us
    pallas_call x1, Pallas kernels, attend(): pl.pallas_call(functools.partial(attend_kernel, rows=rows), grid=(count /...  13.4 us
    all_to_all x1, starting transfers between devices, gather_with_tokens(): lax.all_to_all(copies, 'seq', split_axis=0, concat_axis=0, tiled=True)  9.34 us
    all_to_all x1, starting transfers between devices, body(): lax.all_to_all(out[send_rows], 'seq', split_axis=0, concat_axis=0, tiled=...  8.89 us
    ppermute x3, starting transfers between devices, gather_tp(): lax.ppermute(block, 'tp', chip_shift(tp_count, shift))  8.04 us
    ppermute x3, waiting for transfers between devices, gather_tp(): lax.ppermute(block, 'tp', chip_shift(tp_count, shift))  7.07 us
  transfers between devices with their start and end apart: 14, of which 12 were waited for; matrix products, arithmetic and copies ran while one was open for 11% of the time, Pallas kernels for 0%

profile of v13, /device:TPU:1, one launch (start us, length us, event | category | flops | bytes accessed | tf_op | source)
XLA Modules:
  0.0 194.5 jit_solution(11164631798645828643)
XLA Ops:
  0.7 1.7 multiply_reduce_fusion
  2.4 0.8 reduce-window.9
  3.2 0.7 bitcast_subtract_fusion
  3.9 0.8 select_reduce_fusion
  4.6 0.7 subtract_convert_fusion.1
  5.3 2.0 %multiply_reduce_fusion.2 = (f32[256]{0:T(256)S(1)}, f32[256,128]{0,1:T(8,128)S(1)}) fusion(bf16[2048,128]{1,0:T(8,128)(2,1)} %param.21, f32[2048]{0:T(1024)} %param.19, f32[256]{0:T(256)S(1)} %add_rsqrt_fusion.3, bf16[256,2048]{1,0:T(8,128)(2,1)} %param.15), kind=kOutput, calls=%fused_computation.61 | convolution fusion | flops 136380160 | bytes 1714176 | tf_op jit(solution)/shard_map/dot_general | solution.py:224
  7.3 0.6 fusion.5
  8.6 0.5 broadcast_in_dim.26
  9.1 3.4 %maximum_maximum_fusion = bf16[32,272,256]{2,1,0:T(8,128)(2,1)} fusion(bf16[32,2,256]{2,1,0:T(2,128)(2,1)S(1)} %broadcast_in_dim.27, bf16[32,256,256]{2,1,0:T(8,128)(2,1)S(1)} %broadcast_in_dim.26, bf16[272]{0:T(512)(128)(2,1)S(1)} %pad.8.clone), kind=kLoop, calls=%fused_computation.4 | loop fusion | flops 13369344 | bytes 8684064 | tf_op jit(solution)/shard_map/concatenate | solution.py:98
  12.4 9.3 %all-to-all-start = ((bf16[32,272,256]{2,1,0:T(8,128)(2,1)}), bf16[32,272,256]{2,1,0:T(8,128)(2,1)}, u32[]{:S(2)}, u32[]{:S(2)}) async-start(bf16[32,272,256]{2,1,0:T(8,128)(2,1)} %maximum_maximum_fusion), calls=%async_computation | async-start | bytes 8912896 | tf_op jit(solution)/shard_map/all_to_all | solution.py:99
  21.8 1.9 multiply_reduce_fusion.1
  24.4 3.9 %reshape.485 = bf16[384,4,2,256]{3,2,1,0:T(2,128)(2,1)} reshape(bf16[384,2048]{1,0:T(8,128)(2,1)} %param.29) | data formatting | bytes 3145728 | tf_op jit(solution)/shard_map/reshape | solution.py:236
  28.3 2.6 %reshape.484 = bf16[256,4,2,256]{3,2,1,0:T(2,128)(2,1)} reshape(bf16[256,2048]{1,0:T(8,128)(2,1)} %param.25) | data formatting | bytes 2097152 | tf_op jit(solution)/shard_map/reshape | solution.py:235
  31.0 0.8 broadcast_in_dim_reshape.11.qbeg_ref
  31.9 0.8 broadcast_in_dim_reshape.10.qtok_ref
  32.7 0.8 pad_maximum_fusion.2.q_ref
  33.5 45.6 %all-to-all-done.kv_ref = bf16[32,272,256]{2,1,0:T(8,128)(2,1)} async-done(((bf16[32,272,256]{2,1,0:T(8,128)(2,1)}), bf16[32,272,256]{2,1,0:T(8,128)(2,1)}, u32[]{:S(2)}, u32[]{:S(2)}) %all-to-all-start) | async-done | bytes 4456480 | tf_op jit(solution)/shard_map/all_to_all | solution.py:99
  79.1 1.7 fusion.50
  80.8 13.4 %shard_map.158 = bf16[512,128]{1,0:T(8,128)(2,1)} custom-call(bf16[512,128]{1,0:T(8,128)(2,1)} %pad_maximum_fusion.2.q_ref, s32[512,1]{1,0:T(8,128)} %broadcast_in_dim_reshape.10.qtok_ref, s32[512,1]{1,0:T(8,128)} %broadcast_in_dim_reshape.11.qbeg_ref, bf16[32,272,256]{2,1,0:T(8,128)(2,1)} %all-to-all-done.kv_ref, s32[1,8192]{1,0:T(1,128)} %bitcast.123), custom_call_target="tpu_custom_call" | custom-call | tf_op jit(solution)/shard_map/pallas_call | solution.py:180
  94.2 1.0 reshape.523
  95.1 1.8 fusion.6
  96.9 1.4 copy-done.1
  98.3 2.1 %collective-permute-start = (bf16[4,256,256]{1,2,0:T(8,128)(2,1)S(1)}, bf16[4,256,256]{1,2,0:T(8,128)(2,1)}, u32[]{:S(2)}, u32[]{:S(2)}) collective-permute-start(bf16[4,256,256]{1,2,0:T(8,128)(2,1)S(1)} %fusion.8), channel_id=1, source_target_pairs={{0,1},{1,0},{2,3},{3,2},{4,5},{5,4},{6,7},{7,6},{8,9},{9,8},{10,11... | collective-permute-start | bytes 1572872 | tf_op jit(solution)/shard_map/ppermute | solution.py:60
  100.4 1.7 collective-permute-done
  102.1 2.5 %fusion.63 = (bf16[4,256,256]{1,2,0:T(8,128)(2,1)S(1)}, f32[4,256,256]{1,2,0:T(8,128)}) fusion(bf16[4,256,256]{1,2,0:T(8,128)(2,1)} %collective-permute-done, f32[4,2,256,256]{3,2,1,0:T(8,128)} %copy-done.1, s32[]{:T(128)S(6)} %select_n.200), kind=kLoop, calls=%fused_computation.136 | loop fusion | flops 786432 | bytes 3145732 | tf_op jit(solution)/shard_map/convert_element_type | solution.py:63
  104.7 3.1 %collective-permute-start.1 = (bf16[256,256]{1,0:T(8,128)(2,1)S(1)}, bf16[256,256]{1,0:T(8,128)(2,1)S(1)}, u32[]{:S(2)}, u32[]{:S(2)}) collective-permute-start(bf16[256,256]{1,0:T(8,128)(2,1)S(1)} %bitcast.124), channel_id=1, source_target_pairs={{0,2},{1,3},{2,4},{3,5},{4,6},{5,7},{6,0},{7,1},{8,10},{9,11},{10,... | collective-permute-start | bytes 393224 | tf_op jit(solution)/shard_map/ppermute | solution.py:66
  107.9 4.3 %collective-permute-start.2 = (bf16[256,256]{1,0:T(8,128)(2,1)S(1)}, bf16[256,256]{1,0:T(8,128)(2,1)}, u32[]{:S(2)}, u32[]{:S(2)}) collective-permute-start(bf16[256,256]{1,0:T(8,128)(2,1)S(1)} %bitcast.125), channel_id=1, source_target_pairs={{0,4},{1,5},{2,6},{3,7},{4,0},{5,1},{6,2},{7,3},{8,12},{9,13},{10,... | collective-permute-start | bytes 393224 | tf_op jit(solution)/shard_map/ppermute | solution.py:66
  112.3 2.5 %collective-permute-start.3 = (bf16[256,256]{1,0:T(8,128)(2,1)S(1)}, bf16[256,256]{1,0:T(8,128)(2,1)S(1)}, u32[]{:S(2)}, u32[]{:S(2)}) collective-permute-start(bf16[256,256]{1,0:T(8,128)(2,1)S(1)} %bitcast.126), channel_id=1, source_target_pairs={{0,6},{1,7},{2,0},{3,1},{4,2},{5,3},{6,4},{7,5},{8,14},{9,15},{10,... | collective-permute-start | bytes 393224 | tf_op jit(solution)/shard_map/ppermute | solution.py:66
  114.8 1.6 convert_element_type.122
  116.4 1.0 constant_dynamic-slice_fusion.7
  117.5 6.1 %collective-permute-done.2 = bf16[256,256]{1,0:T(8,128)(2,1)} collective-permute-done((bf16[256,256]{1,0:T(8,128)(2,1)S(1)}, bf16[256,256]{1,0:T(8,128)(2,1)}, u32[]{:S(2)}, u32[]{:S(2)}) %collective-permute-start.2) | collective-permute-done | bytes 131104 | tf_op jit(solution)/shard_map/ppermute | solution.py:66
  123.8 0.7 copy-done.5
  124.6 1.2 constant_dynamic-update-slice_fusion.3
  125.8 1.4 collective-permute-start.4
  127.2 4.0 %collective-permute-start.5 = (bf16[256,256]{1,0:T(8,128)(2,1)S(1)}, bf16[256,256]{1,0:T(8,128)(2,1)S(1)}, u32[]{:S(2)}, u32[]{:S(2)}) collective-permute-start(bf16[256,256]{1,0:T(8,128)(2,1)S(1)} %get-tuple-element.11), channel_id=1, source_target_pairs={{0,4},{1,5},{2,6},{3,7},{4,0},{5,1},{6,2},{7,3},{8,12},{9,13},{10,... | collective-permute-start | bytes 393224 | tf_op jit(solution)/shard_map/ppermute | solution.py:76
  131.2 2.6 %collective-permute-start.6 = (bf16[256,256]{1,0:T(8,128)(2,1)S(1)}, bf16[256,256]{1,0:T(8,128)(2,1)S(1)}, u32[]{:S(2)}, u32[]{:S(2)}) collective-permute-start(bf16[256,256]{1,0:T(8,128)(2,1)S(1)} %get-tuple-element.11), channel_id=1, source_target_pairs={{0,6},{1,7},{2,0},{3,1},{4,2},{5,3},{6,4},{7,5},{8,14},{9,15},{10,... | collective-permute-start | bytes 393224 | tf_op jit(solution)/shard_map/ppermute | solution.py:76
  133.8 5.8 %collective-permute-done.5 = bf16[256,256]{1,0:T(8,128)(2,1)S(1)} collective-permute-done((bf16[256,256]{1,0:T(8,128)(2,1)S(1)}, bf16[256,256]{1,0:T(8,128)(2,1)S(1)}, u32[]{:S(2)}, u32[]{:S(2)}) %collective-permute-start.5) | collective-permute-done | bytes 131104 | tf_op jit(solution)/shard_map/ppermute | solution.py:76
  139.6 1.3 collective-permute-done.6
  140.9 0.9 pad_maximum_fusion
  141.8 0.5 collective-permute-start.7
  142.3 0.5 broadcast_multiply_fusion
  142.8 0.7 mul.284
  143.6 0.4 collective-permute-done.7
  144.0 1.0 constant_dynamic-update-slice_fusion.2
  145.4 0.8 fusion.12
  146.2 4.4 %fusion.3 = f32[4,2,256,256]{3,2,1,0:T(8,128)} fusion(bf16[384,4,2,256]{3,2,1,0:T(2,128)(2,1)} %reshape.485, bf16[2048,384]{1,0:T(8,128)(2,1)S(1)} %copy-done, bf16[256,2048]{1,0:T(8,128)(2,1)S(1)} %fusion.30, f32[2048]{0:T(1024)S(1)} %copy-done.13, f32[256]{0:T(256)S(1)} %add_rsqrt_fusion.1, f32[256,384]{1,0:T(8,128)S(1)} %fusion.12), kind=kOutput, calls=%fused_computation.12 | convolution fusion | flops 807993344 | bytes 6693888 | tf_op jit(solution)/shard_map/rk,kcip->icrp/dot_general | solution.py:57
  150.7 1.3 fusion.9
  151.9 0.4 collective-permute-start.8
  153.0 0.9 collective-permute-done.8
  153.9 1.4 fusion.61
  155.4 0.8 copy.78
  156.1 3.7 %collective-permute-start.10 = (bf16[256,256]{1,0:T(8,128)(2,1)}, bf16[256,256]{1,0:T(8,128)(2,1)S(1)}, u32[]{:S(2)}, u32[]{:S(2)}) collective-permute-start(bf16[256,256]{1,0:T(8,128)(2,1)} %bitcast.39), channel_id=1, source_target_pairs={{0,4},{1,5},{2,6},{3,7},{4,0},{5,1},{6,2},{7,3},{8,12},{9,13},{10,... | collective-permute-start | bytes 393224 | tf_op jit(solution)/shard_map/ppermute | solution.py:66
  159.9 0.8 copy.79
  160.6 1.7 collective-permute-start.11
  162.3 0.8 copy.77
  163.1 0.7 collective-permute-start.9
  163.9 0.6 gather_fusion
  165.0 6.4 %collective-permute-done.11 = bf16[256,256]{1,0:T(8,128)(2,1)S(1)} collective-permute-done((bf16[256,256]{1,0:T(8,128)(2,1)}, bf16[256,256]{1,0:T(8,128)(2,1)S(1)}, u32[]{:S(2)}, u32[]{:S(2)}) %collective-permute-start.11) | collective-permute-done | bytes 131104 | tf_op jit(solution)/shard_map/ppermute | solution.py:66
  171.4 2.7 %collective-permute-done.9 = bf16[256,256]{1,0:T(8,128)(2,1)S(1)} collective-permute-done((bf16[256,256]{1,0:T(8,128)(2,1)}, bf16[256,256]{1,0:T(8,128)(2,1)S(1)}, u32[]{:S(2)}, u32[]{:S(2)}) %collective-permute-start.9) | collective-permute-done | bytes 131104 | tf_op jit(solution)/shard_map/ppermute | solution.py:66
  174.2 1.8 gather_fusion.1
  176.0 8.9 %all-to-all-start.1 = ((bf16[32,8,256]{2,1,0:T(8,128)(2,1)}), bf16[32,8,256]{2,1,0:T(8,128)(2,1)S(1)}, u32[]{:S(2)}, u32[]{:S(2)}) async-start(bf16[32,8,256]{2,1,0:T(8,128)(2,1)} %bitcast.42), calls=%async_computation.1 | async-start | bytes 262144 | tf_op jit(solution)/shard_map/all_to_all | solution.py:264
  185.1 2.4 %scatter_custom_fusion.1 = bf16[256,256]{1,0:T(8,128)(2,1)} fusion(s32[256]{0:T(256)S(1)} %bitcast.130, bf16[32,272,256]{2,1,0:T(8,128)(2,1)} %all-to-all-done.kv_ref, s32[]{:T(128)} %constant.199.clone.1, s32[]{:T(128)S(6)} %select_n.227, bf16[]{:T(256)} %constant.194.clone.1), kind=kCustom, calls=%fused_computation.52 | custom fusion | bytes 263172 | tf_op jit(solution)/shard_map/scatter | solution.py:113
  187.5 4.9 %all-to-all-done.1 = bf16[32,8,256]{2,1,0:T(8,128)(2,1)S(1)} async-done(((bf16[32,8,256]{2,1,0:T(8,128)(2,1)}), bf16[32,8,256]{2,1,0:T(8,128)(2,1)S(1)}, u32[]{:S(2)}, u32[]{:S(2)}) %all-to-all-start.1) | async-done | bytes 131104 | tf_op jit(solution)/shard_map/all_to_all | solution.py:264
  192.4 2.1 %scatter_custom_fusion = bf16[256,256]{1,0:T(8,128)(2,1)} fusion(s32[256]{0:T(256)S(1)} %bitcast.129, bf16[32,8,256]{2,1,0:T(8,128)(2,1)S(1)} %all-to-all-done.1, bf16[]{:T(256)} %constant.194.clone.1), kind=kCustom, calls=%fused_computation.54 | custom fusion | bytes 262146 | tf_op jit(solution)/shard_map/scatter | solution.py:269
  (86 shorter events, 4.4 us)
Async XLA Ops:
  0.6 145.6 %copy-start = (bf16[2048,384]{1,0:T(8,128)(2,1)S(1)}, bf16[2048,384]{1,0:T(8,128)(2,1)}, u32[]{:S(2)}) copy-start(bf16[2048,384]{1,0:T(8,128)(2,1)} %param.28) | copy-start | bytes 4718596
  0.6 6.7 %copy-start.2 = (bf16[256,2048]{1,0:T(8,128)(2,1)S(1)}, bf16[256,2048]{1,0:T(8,128)(2,1)}, u32[]{:S(2)}) copy-start(bf16[256,2048]{1,0:T(8,128)(2,1)} %param.15) | copy-start | bytes 3145732
  0.7 6.7 %copy-start.11 = (f32[2048]{0:T(1024)S(1)}, f32[2048]{0:T(1024)}, u32[]{:S(2)}) copy-start(f32[2048]{0:T(1024)} %param.19) | copy-start | bytes 24580
  0.7 6.7 %copy-start.10 = (bf16[2048,128]{1,0:T(8,128)(2,1)S(1)}, bf16[2048,128]{1,0:T(8,128)(2,1)}, u32[]{:S(2)}) copy-start(bf16[2048,128]{1,0:T(8,128)(2,1)} %param.22) | copy-start | bytes 1572868
  5.3 2.6 %copy-start.7 = (f32[128]{0:T(128)S(1)}, f32[128]{0:T(128)}, u32[]{:S(2)}) copy-start(f32[128]{0:T(128)} %param.24) | copy-start | bytes 1540
  12.4 66.7 %all-to-all-start = ((bf16[32,272,256]{2,1,0:T(8,128)(2,1)}), bf16[32,272,256]{2,1,0:T(8,128)(2,1)}, u32[]{:S(2)}, u32[]{:S(2)}) async-start(bf16[32,272,256]{2,1,0:T(8,128)(2,1)} %maximum_maximum_fusion), calls=%async_computation | async-start | bytes 8912896 | tf_op jit(solution)/shard_map/all_to_all | solution.py:99
  21.8 2.3 %copy-start.8 = (f32[128]{0:T(128)S(1)}, f32[128]{0:T(128)}, u32[]{:S(2)}) copy-start(f32[128]{0:T(128)} %param.23) | copy-start | bytes 1540
  28.3 3.5 %copy-start.6 = (s32[256]{0:T(256)S(1)}, s32[256]{0:T(256)}, u32[]{:S(2)}) copy-start(s32[256]{0:T(256)} %param.16) | copy-start | bytes 3076
  96.9 1.4 copy-start.1
  98.3 3.8 %collective-permute-start = (bf16[4,256,256]{1,2,0:T(8,128)(2,1)S(1)}, bf16[4,256,256]{1,2,0:T(8,128)(2,1)}, u32[]{:S(2)}, u32[]{:S(2)}) collective-permute-start(bf16[4,256,256]{1,2,0:T(8,128)(2,1)S(1)} %fusion.8), channel_id=1, source_target_pairs={{0,1},{1,0},{2,3},{3,2},{4,5},{5,4},{6,7},{7,6},{8,9},{9,8},{10,11... | collective-permute-start | bytes 1572872 | tf_op jit(solution)/shard_map/ppermute | solution.py:60
  104.7 12.8 %collective-permute-start.1 = (bf16[256,256]{1,0:T(8,128)(2,1)S(1)}, bf16[256,256]{1,0:T(8,128)(2,1)S(1)}, u32[]{:S(2)}, u32[]{:S(2)}) collective-permute-start(bf16[256,256]{1,0:T(8,128)(2,1)S(1)} %bitcast.124), channel_id=1, source_target_pairs={{0,2},{1,3},{2,4},{3,5},{4,6},{5,7},{6,0},{7,1},{8,10},{9,11},{10,... | collective-permute-start | bytes 393224 | tf_op jit(solution)/shard_map/ppermute | solution.py:66
  107.9 15.7 %collective-permute-start.2 = (bf16[256,256]{1,0:T(8,128)(2,1)S(1)}, bf16[256,256]{1,0:T(8,128)(2,1)}, u32[]{:S(2)}, u32[]{:S(2)}) collective-permute-start(bf16[256,256]{1,0:T(8,128)(2,1)S(1)} %bitcast.125), channel_id=1, source_target_pairs={{0,4},{1,5},{2,6},{3,7},{4,0},{5,1},{6,2},{7,3},{8,12},{9,13},{10,... | collective-permute-start | bytes 393224 | tf_op jit(solution)/shard_map/ppermute | solution.py:66
  112.3 11.5 %collective-permute-start.3 = (bf16[256,256]{1,0:T(8,128)(2,1)S(1)}, bf16[256,256]{1,0:T(8,128)(2,1)S(1)}, u32[]{:S(2)}, u32[]{:S(2)}) collective-permute-start(bf16[256,256]{1,0:T(8,128)(2,1)S(1)} %bitcast.126), channel_id=1, source_target_pairs={{0,6},{1,7},{2,0},{3,1},{4,2},{5,3},{6,4},{7,5},{8,14},{9,15},{10,... | collective-permute-start | bytes 393224 | tf_op jit(solution)/shard_map/ppermute | solution.py:66
  117.4 24.9 %copy-start.14 = (s32[64]{0:T(128)S(1)}, s32[64]{0:T(128)}, u32[]{:S(2)}) copy-start(s32[64]{0:T(128)} %param.18) | copy-start | bytes 772
  123.8 0.7 copy-start.5
  125.8 8.0 %collective-permute-start.4 = (bf16[256,256]{1,0:T(8,128)(2,1)S(1)}, bf16[256,256]{1,0:T(8,128)(2,1)S(1)}, u32[]{:S(2)}, u32[]{:S(2)}) collective-permute-start(bf16[256,256]{1,0:T(8,128)(2,1)S(1)} %get-tuple-element.11), channel_id=1, source_target_pairs={{0,2},{1,3},{2,4},{3,5},{4,6},{5,7},{6,0},{7,1},{8,10},{9,11},{10,... | collective-permute-start | bytes 393224 | tf_op jit(solution)/shard_map/ppermute | solution.py:76
  127.2 12.4 %collective-permute-start.5 = (bf16[256,256]{1,0:T(8,128)(2,1)S(1)}, bf16[256,256]{1,0:T(8,128)(2,1)S(1)}, u32[]{:S(2)}, u32[]{:S(2)}) collective-permute-start(bf16[256,256]{1,0:T(8,128)(2,1)S(1)} %get-tuple-element.11), channel_id=1, source_target_pairs={{0,4},{1,5},{2,6},{3,7},{4,0},{5,1},{6,2},{7,3},{8,12},{9,13},{10,... | collective-permute-start | bytes 393224 | tf_op jit(solution)/shard_map/ppermute | solution.py:76
  131.2 9.7 %collective-permute-start.6 = (bf16[256,256]{1,0:T(8,128)(2,1)S(1)}, bf16[256,256]{1,0:T(8,128)(2,1)S(1)}, u32[]{:S(2)}, u32[]{:S(2)}) collective-permute-start(bf16[256,256]{1,0:T(8,128)(2,1)S(1)} %get-tuple-element.11), channel_id=1, source_target_pairs={{0,6},{1,7},{2,0},{3,1},{4,2},{5,3},{6,4},{7,5},{8,14},{9,15},{10,... | collective-permute-start | bytes 393224 | tf_op jit(solution)/shard_map/ppermute | solution.py:76
  133.8 7.1 %copy-start.3 = (bf16[256,256]{1,0:T(8,128)(2,1)}, bf16[256,256]{1,0:T(8,128)(2,1)S(1)}, u32[]{:S(2)}) copy-start(bf16[256,256]{1,0:T(8,128)(2,1)S(1)} %collective-permute-done.4) | copy-start | bytes 393220
  141.8 2.2 %collective-permute-start.7 = (bf16[4,256,256]{2,1,0:T(8,128)(2,1)}, bf16[4,256,256]{2,1,0:T(8,128)(2,1)S(1)}, u32[]{:S(2)}, u32[]{:S(2)}) collective-permute-start(bf16[4,256,256]{2,1,0:T(8,128)(2,1)} %pad_maximum_fusion), channel_id=1, source_target_pairs={{0,1},{1,0},{2,3},{3,2},{4,5},{5,4},{6,7},{7,6},{8,9},{9,8},{10,11... | collective-permute-start | bytes 1572872 | tf_op jit(solution)/shard_map/ppermute | solution.py:78
  143.6 1.8 copy-start.9
  143.6 1.8 copy-start.12
  145.4 0.8 copy-start.13
  146.2 6.6 %copy-start.4 = (s32[32,1,256]{2,1,0:T(1,128)S(1)}, s32[32,1,256]{2,1,0:T(1,128)}, u32[]{:S(2)}) copy-start(s32[32,1,256]{2,1,0:T(1,128)} %fusion.50) | copy-start | bytes 98308
  151.9 2.0 %collective-permute-start.8 = (bf16[4,256,256]{1,2,0:T(8,128)(2,1)S(1)}, bf16[4,256,256]{1,2,0:T(8,128)(2,1)S(1)}, u32[]{:S(2)}, u32[]{:S(2)}) collective-permute-start(bf16[4,256,256]{1,2,0:T(8,128)(2,1)S(1)} %fusion.9), channel_id=1, source_target_pairs={{0,1},{1,0},{2,3},{3,2},{4,5},{5,4},{6,7},{7,6},{8,9},{9,8},{10,11... | collective-permute-start | bytes 1572872 | tf_op jit(solution)/shard_map/ppermute | solution.py:60
  156.1 8.9 %collective-permute-start.10 = (bf16[256,256]{1,0:T(8,128)(2,1)}, bf16[256,256]{1,0:T(8,128)(2,1)S(1)}, u32[]{:S(2)}, u32[]{:S(2)}) collective-permute-start(bf16[256,256]{1,0:T(8,128)(2,1)} %bitcast.39), channel_id=1, source_target_pairs={{0,4},{1,5},{2,6},{3,7},{4,0},{5,1},{6,2},{7,3},{8,12},{9,13},{10,... | collective-permute-start | bytes 393224 | tf_op jit(solution)/shard_map/ppermute | solution.py:66
  160.6 10.8 %collective-permute-start.11 = (bf16[256,256]{1,0:T(8,128)(2,1)}, bf16[256,256]{1,0:T(8,128)(2,1)S(1)}, u32[]{:S(2)}, u32[]{:S(2)}) collective-permute-start(bf16[256,256]{1,0:T(8,128)(2,1)} %bitcast.40), channel_id=1, source_target_pairs={{0,6},{1,7},{2,0},{3,1},{4,2},{5,3},{6,4},{7,5},{8,14},{9,15},{10,... | collective-permute-start | bytes 393224 | tf_op jit(solution)/shard_map/ppermute | solution.py:66
  163.1 11.1 %collective-permute-start.9 = (bf16[256,256]{1,0:T(8,128)(2,1)}, bf16[256,256]{1,0:T(8,128)(2,1)S(1)}, u32[]{:S(2)}, u32[]{:S(2)}) collective-permute-start(bf16[256,256]{1,0:T(8,128)(2,1)} %bitcast.38), channel_id=1, source_target_pairs={{0,2},{1,3},{2,4},{3,5},{4,6},{5,7},{6,0},{7,1},{8,10},{9,11},{10,... | collective-permute-start | bytes 393224 | tf_op jit(solution)/shard_map/ppermute | solution.py:66
  176.0 16.4 %all-to-all-start.1 = ((bf16[32,8,256]{2,1,0:T(8,128)(2,1)}), bf16[32,8,256]{2,1,0:T(8,128)(2,1)S(1)}, u32[]{:S(2)}, u32[]{:S(2)}) async-start(bf16[32,8,256]{2,1,0:T(8,128)(2,1)} %bitcast.42), calls=%async_computation.1 | async-start | bytes 262144 | tf_op jit(solution)/shard_map/all_to_all | solution.py:264

commit v14 on v11

--- a/solution.py
+++ b/solution.py
@@ -47,16 +47,22 @@
     return [(i, ((i // 2 + shift) % chips) * 2 + i % 2) for i in range(tp_count)]
 
 
-def project_reduce_tp(acts, weight, tp_count):
-    width = weight.shape[1] * weight.shape[2] * weight.shape[3]
+def core_halves(weight, tp_count):
+    core = lax.axis_index("tp") % 2
+    mine = lax.dynamic_index_in_dim(weight, core, axis=2, keepdims=False)
+    other = lax.dynamic_index_in_dim(weight, 1 - core, axis=2, keepdims=False)
+    return mine, other
+
+
+def project_reduce_tp(acts, halves, tp_count):
     chips = tp_count // 2
-    part = width // tp_count
     index = lax.axis_index("tp")
-    chip, core = index // 2, index % 2
-    split = weight
-    terms = jnp.einsum("rk,kcip->icrp", acts, split, preferred_element_type=jnp.float32)
-    mine = lax.dynamic_index_in_dim(terms, core, axis=0, keepdims=False)
-    other = lax.dynamic_index_in_dim(terms, 1 - core, axis=0, keepdims=False).astype(jnp.bfloat16)
+    chip = index // 2
+    w_mine, w_other = halves
+    other = jnp.einsum("rk,kcp->crp", acts, w_other, preferred_element_type=jnp.float32).astype(
+        jnp.bfloat16
+    )
+    mine = jnp.einsum("rk,kcp->crp", acts, w_mine, preferred_element_type=jnp.float32)
     sibling = lax.ppermute(other, "tp", [(i, i ^ 1) for i in range(tp_count)])
     chip_sum = mine + sibling.astype(jnp.float32)
     total = lax.dynamic_index_in_dim(chip_sum, chip, axis=0, keepdims=False)
@@ -232,6 +238,8 @@
     blocks = (tp_count // 2, 2, width // tp_count)
     o_split = o_weight.reshape((o_weight.shape[0],) + blocks)
     down_split = down_weight.reshape((down_weight.shape[0],) + blocks)
+    o_split = core_halves(o_split, tp_count)
+    down_split = core_halves(down_split, tp_count)
     pieces, o_split, down_split = lax.optimization_barrier((pieces, o_split, down_split))
     key_tokens = piece_tokens.reshape(1, seq_count * rows)
     query_tokens = jnp.repeat(token_order, group)[:, None]

time: 194 us -> 191 us (0.985)
  local copies, waits for them, and re-layouts: 28.8 us -> 47.9 us
  waiting for transfers between devices: 76.4 us -> 58.1 us
  other arithmetic: 16.7 us -> 13.8 us
  starting transfers between devices: 45.2 us -> 43.1 us
    dynamic_slice x0 -> x6, local copies, waits for them, and re-layouts: none -> 21.5 us  [the longest x4 13.2 us: core_halves(): other = lax.dynamic_index_in_dim(weight, 1 - core, axis=2, keepdims=False)]
    all_to_all x1, waiting for transfers between devices: 45.6 us -> 25.5 us  [gather_seq(): lax.all_to_all(copies, 'seq', split_axis=0, concat_axis=0, tiled=True)]
    convert_element_type x2 -> x0, other arithmetic: 3.86 us -> none  [project_reduce_tp(): outgoing = chip_sum.astype(jnp.bfloat16)]
    all_to_all x1, starting transfers between devices: 8.9 us -> 6.04 us  [body(): lax.all_to_all(out[send_rows], 'seq', split_axis=0, concat_axis=0, tiled=...]
    ppermute x3, waiting for transfers between devices: 7.07 us -> 9.75 us  [gather_tp(): lax.ppermute(block, 'tp', chip_shift(tp_count, shift))]
    dot_general x2 -> x5, matrix products: 6.18 us -> 6.36 us  [the longest x2 3.96 us: project_reduce_tp(): jnp.einsum('rk,kcp->crp', acts, w_mine, preferred_element_type=jnp.float32)]
  transfers between devices with their start and end apart: 14 -> 14, of which waited for: 12 -> 13; matrix products, arithmetic and copies ran while one was open for 11% -> 22% of each run, Pallas kernels for 0% -> 0%
where the time goes in v14:
time: 191 us; the launch traced here: 190 us
  waiting for transfers between devices  58.1 us (30%)
  local copies, waits for them, and re-layouts  47.9 us (25%)
  starting transfers between devices  43.1 us (23%)
  other arithmetic  13.8 us (7%)
  Pallas kernels  13.7 us (7%)
  matrix products  11.9 us (6%)
    all_to_all x1, waiting for transfers between devices, gather_seq(): lax.all_to_all(copies, 'seq', split_axis=0, concat_axis=0, tiled=True)  25.5 us
    ppermute x6, starting transfers between devices, project_reduce_tp(): lax.ppermute(piece, 'tp', chip_shift(tp_count, shift)).astype(jnp.float32)  15.9 us
    ppermute x6, waiting for transfers between devices, project_reduce_tp(): lax.ppermute(piece, 'tp', chip_shift(tp_count, shift)).astype(jnp.float32)  14.6 us
    pallas_call x1, Pallas kernels, attend(): pl.pallas_call(functools.partial(attend_kernel, rows=rows), grid=(count /...  13.7 us
    dynamic_slice x4, local copies, waits for them, and re-layouts, core_halves(): other = lax.dynamic_index_in_dim(weight, 1 - core, axis=2, keepdims=False)  13.2 us
    ppermute x3, waiting for transfers between devices, gather_tp(): lax.ppermute(block, 'tp', chip_shift(tp_count, shift))  9.75 us
    all_to_all x1, starting transfers between devices, gather_seq(): lax.all_to_all(copies, 'seq', split_axis=0, concat_axis=0, tiled=True)  9.34 us
    dynamic_slice x2, local copies, waits for them, and re-layouts, core_halves(): mine = lax.dynamic_index_in_dim(weight, core, axis=2, keepdims=False)  8.36 us
  transfers between devices with their start and end apart: 14, of which 13 were waited for; matrix products, arithmetic and copies ran while one was open for 22% of the time, Pallas kernels for 0%

profile of v14, /device:TPU:1, one launch (start us, length us, event | category | flops | bytes accessed | tf_op | source)
XLA Modules:
  0.0 189.7 jit_solution(16501197013946014237)
XLA Ops:
  0.7 1.0 reduce-window.9
  1.7 0.7 bitcast_subtract_fusion
  2.4 0.8 select_reduce_fusion
  3.1 0.7 subtract_convert_fusion.1
  3.9 1.5 multiply_reduce_fusion
  5.4 2.0 %fusion.5 = bf16[256,1,1,128]{0,3,2,1:T(8,128)(2,1)S(1)} fusion(bf16[2048,128]{1,0:T(8,128)(2,1)} %param.22, f32[2048]{0:T(1024)} %param.19, f32[256]{0:T(256)S(1)} %add_rsqrt_fusion.3, bf16[256,2048]{1,0:T(8,128)(2,1)} %param.15), kind=kOutput, calls=%fused_computation.18 | convolution fusion | flops 136347648 | bytes 1647616 | tf_op jit(solution)/shard_map/dot_general | solution.py:230
  8.7 2.4 %broadcast_in_dim.24 = bf16[32,272,256]{2,1,0:T(8,128)(2,1)} broadcast(bf16[272,256]{1,0:T(8,128)(2,1)S(1)} %maximum_maximum_fusion), dimensions={1,2} | broadcast | bytes 4595712 | tf_op jit(solution)/shard_map/broadcast_in_dim | solution.py:41
  11.1 9.3 %all-to-all-start = ((bf16[32,272,256]{2,1,0:T(8,128)(2,1)}), bf16[32,272,256]{2,1,0:T(8,128)(2,1)}, u32[]{:S(2)}, u32[]{:S(2)}) async-start(bf16[32,272,256]{2,1,0:T(8,128)(2,1)} %broadcast_in_dim.24), calls=%async_computation | async-start | bytes 8912896 | tf_op jit(solution)/shard_map/all_to_all | solution.py:42
  20.5 1.8 reshape.485
  22.3 3.5 %constant_dynamic-slice_fusion.10 = (bf16[256,4,1,256]{3,2,1,0:T(2,128)(2,1)}, bf16[256,4,1,256]{3,2,1,0:T(2,128)(2,1)}) fusion(bf16[256,4,2,256]{3,2,1,0:T(2,128)(2,1)S(1)} %reshape.485, s32[]{:T(128)S(6)} %select_n.202, s32[]{:T(128)S(6)} %select_n.201), kind=kLoop, calls=%fused_computation.98 | loop fusion | bytes 2097160 | tf_op jit(solution)/shard_map/jit(dynamic_index_in_dim)/dynamic_slice | solution.py:53
  25.8 3.6 %copy.64 = bf16[256,4,1,256]{0,3,1,2:T(8,128)(2,1)} copy(bf16[256,4,1,256]{3,2,1,0:T(2,128)(2,1)} %get-tuple-element.21) | data formatting | bytes 1048576 | tf_op jit(solution)/shard_map/jit(dynamic_index_in_dim)/dynamic_slice | solution.py:52
  29.4 2.0 %copy.65 = bf16[256,4,1,256]{0,3,1,2:T(8,128)(2,1)} copy(bf16[256,4,1,256]{3,2,1,0:T(2,128)(2,1)S(1)} %copy-done.4) | data formatting | bytes 1048576 | tf_op jit(solution)/shard_map/jit(dynamic_index_in_dim)/dynamic_slice | solution.py:53
  31.4 2.9 %reshape.486 = bf16[384,4,2,256]{3,2,1,0:T(2,128)(2,1)S(1)} reshape(bf16[384,2048]{1,0:T(8,128)(2,1)} %param.29) | data formatting | bytes 3145728 | tf_op jit(solution)/shard_map/reshape | solution.py:240
  34.2 4.9 %constant_dynamic-slice_fusion.8 = (bf16[384,4,1,256]{3,2,1,0:T(2,128)(2,1)}, bf16[384,4,1,256]{3,2,1,0:T(2,128)(2,1)}) fusion(bf16[384,4,2,256]{3,2,1,0:T(2,128)(2,1)S(1)} %reshape.486, s32[]{:T(128)S(6)} %select_n.202, s32[]{:T(128)S(6)} %select_n.201), kind=kLoop, calls=%fused_computation.96 | loop fusion | bytes 3145736 | tf_op jit(solution)/shard_map/jit(dynamic_index_in_dim)/dynamic_slice | solution.py:53
  39.1 4.8 %copy.66 = bf16[384,4,1,256]{0,3,1,2:T(8,128)(2,1)} copy(bf16[384,4,1,256]{3,2,1,0:T(2,128)(2,1)} %get-tuple-element.19) | data formatting | bytes 1572864 | tf_op jit(solution)/shard_map/jit(dynamic_index_in_dim)/dynamic_slice | solution.py:52
  43.9 2.8 %copy.67 = bf16[384,4,1,256]{0,3,1,2:T(8,128)(2,1)} copy(bf16[384,4,1,256]{3,2,1,0:T(2,128)(2,1)S(1)} %copy-done.1) | data formatting | bytes 1572864 | tf_op jit(solution)/shard_map/jit(dynamic_index_in_dim)/dynamic_slice | solution.py:53
  46.7 2.2 %multiply_reduce_fusion.1 = (f32[256,2]{0,1:T(2,128)S(1)}, f32[256,256]{0,1:T(8,128)S(1)}) fusion(bf16[2048,256]{1,0:T(8,128)(2,1)} %param.20, f32[2048]{0:T(1024)S(1)} %copy-done.18, f32[256]{0:T(256)S(1)} %add_rsqrt_fusion.3, bf16[256,2048]{1,0:T(8,128)(2,1)} %param.15), kind=kOutput, calls=%fused_computation.37 | convolution fusion | flops 270663168 | bytes 2370560 | tf_op jit(solution)/shard_map/dot_general | solution.py:227
  49.8 0.8 broadcast_in_dim_reshape.9.qtok_ref
  50.7 0.8 broadcast_in_dim_reshape.10.qbeg_ref
  51.5 0.8 pad_maximum_fusion.2.q_ref
  52.3 25.5 %all-to-all-done.kv_ref = bf16[32,272,256]{2,1,0:T(8,128)(2,1)} async-done(((bf16[32,272,256]{2,1,0:T(8,128)(2,1)}), bf16[32,272,256]{2,1,0:T(8,128)(2,1)}, u32[]{:S(2)}, u32[]{:S(2)}) %all-to-all-start) | async-done | bytes 4456480 | tf_op jit(solution)/shard_map/all_to_all | solution.py:42
  77.8 1.7 fusion.42
  79.5 13.7 %shard_map.158 = bf16[512,128]{1,0:T(8,128)(2,1)} custom-call(bf16[512,128]{1,0:T(8,128)(2,1)} %pad_maximum_fusion.2.q_ref, s32[512,1]{1,0:T(8,128)} %broadcast_in_dim_reshape.9.qtok_ref, s32[512,1]{1,0:T(8,128)} %broadcast_in_dim_reshape.10.qbeg_ref, bf16[32,272,256]{2,1,0:T(8,128)(2,1)} %all-to-all-done.kv_ref, s32[1,8192]{1,0:T(1,128)} %bitcast.118), custom_call_target="tpu_custom_call" | custom-call | tf_op jit(solution)/shard_map/pallas_call | solution.py:184
  93.1 1.0 reshape.524
  94.1 1.2 fusion.3
  95.3 1.8 collective-permute-start
  97.1 1.9 collective-permute-done
  99.0 2.3 %fusion.54 = (bf16[4,256,256]{1,2,0:T(8,128)(2,1)S(1)}, f32[4,256,256]{1,2,0:T(8,128)}) fusion(bf16[4,256,256]{1,2,0:T(8,128)(2,1)} %collective-permute-done, bf16[256,4,256]{0,2,1:T(8,128)(2,1)S(1)} %bitcast.109, bf16[256,256,1]{1,0,2:T(8,128)(2,1)S(1)} %reshape.524), kind=kOutput, calls=%fused_computation.134 | convolution fusion | flops 135004160 | bytes 2752512 | tf_op jit(solution)/shard_map/rk,kcp->crp/dot_general | solution.py:65
  101.5 5.2 %collective-permute-start.3 = (bf16[256,256]{1,0:T(8,128)(2,1)S(1)}, bf16[256,256]{1,0:T(8,128)(2,1)S(1)}, u32[]{:S(2)}, u32[]{:S(2)}) collective-permute-start(bf16[256,256]{1,0:T(8,128)(2,1)S(1)} %bitcast.119), channel_id=1, source_target_pairs={{0,6},{1,7},{2,0},{3,1},{4,2},{5,3},{6,4},{7,5},{8,14},{9,15},{10,... | collective-permute-start | bytes 393224 | tf_op jit(solution)/shard_map/ppermute | solution.py:72
  106.8 1.2 collective-permute-start.2
  108.1 2.2 %collective-permute-start.1 = (bf16[256,256]{1,0:T(8,128)(2,1)S(1)}, bf16[256,256]{1,0:T(8,128)(2,1)}, u32[]{:S(2)}, u32[]{:S(2)}) collective-permute-start(bf16[256,256]{1,0:T(8,128)(2,1)S(1)} %bitcast.121), channel_id=1, source_target_pairs={{0,2},{1,3},{2,4},{3,5},{4,6},{5,7},{6,0},{7,1},{8,10},{9,11},{10,... | collective-permute-start | bytes 393224 | tf_op jit(solution)/shard_map/ppermute | solution.py:72
  110.3 1.6 convert_element_type.116
  111.9 1.0 constant_dynamic-slice_fusion.7
  113.0 6.4 %collective-permute-done.2 = bf16[256,256]{1,0:T(8,128)(2,1)S(1)} collective-permute-done((bf16[256,256]{1,0:T(8,128)(2,1)S(1)}, bf16[256,256]{1,0:T(8,128)(2,1)S(1)}, u32[]{:S(2)}, u32[]{:S(2)}) %collective-permute-start.2) | collective-permute-done | bytes 131104 | tf_op jit(solution)/shard_map/ppermute | solution.py:72
  120.2 1.2 constant_dynamic-update-slice_fusion.3
  121.3 4.1 %collective-permute-start.6 = (bf16[256,256]{1,0:T(8,128)(2,1)S(1)}, bf16[256,256]{1,0:T(8,128)(2,1)S(1)}, u32[]{:S(2)}, u32[]{:S(2)}) collective-permute-start(bf16[256,256]{1,0:T(8,128)(2,1)S(1)} %get-tuple-element.15), channel_id=1, source_target_pairs={{0,6},{1,7},{2,0},{3,1},{4,2},{5,3},{6,4},{7,5},{8,14},{9,15},{10,... | collective-permute-start | bytes 393224 | tf_op jit(solution)/shard_map/ppermute | solution.py:82
  125.4 1.9 collective-permute-start.5
  127.3 2.1 %collective-permute-start.4 = (bf16[256,256]{1,0:T(8,128)(2,1)S(1)}, bf16[256,256]{1,0:T(8,128)(2,1)S(1)}, u32[]{:S(2)}, u32[]{:S(2)}) collective-permute-start(bf16[256,256]{1,0:T(8,128)(2,1)S(1)} %get-tuple-element.15), channel_id=1, source_target_pairs={{0,2},{1,3},{2,4},{3,5},{4,6},{5,7},{6,0},{7,1},{8,10},{9,11},{10,... | collective-permute-start | bytes 393224 | tf_op jit(solution)/shard_map/ppermute | solution.py:82
  129.3 4.8 %collective-permute-done.6 = bf16[256,256]{1,0:T(8,128)(2,1)S(1)} collective-permute-done((bf16[256,256]{1,0:T(8,128)(2,1)S(1)}, bf16[256,256]{1,0:T(8,128)(2,1)S(1)}, u32[]{:S(2)}, u32[]{:S(2)}) %collective-permute-start.6) | collective-permute-done | bytes 131104 | tf_op jit(solution)/shard_map/ppermute | solution.py:82
  134.1 4.8 %collective-permute-done.5 = bf16[256,256]{1,0:T(8,128)(2,1)S(1)} collective-permute-done((bf16[256,256]{1,0:T(8,128)(2,1)S(1)}, bf16[256,256]{1,0:T(8,128)(2,1)S(1)}, u32[]{:S(2)}, u32[]{:S(2)}) %collective-permute-start.5) | collective-permute-done | bytes 131104 | tf_op jit(solution)/shard_map/ppermute | solution.py:82
  139.1 0.7 copy-done.10
  139.8 0.9 pad_maximum_fusion
  140.6 1.5 collective-permute-start.7
  142.6 0.7 mul.284
  143.9 0.9 constant_dynamic-update-slice_fusion.2
  145.3 0.8 fusion.8
  146.6 0.8 fusion.12
  149.4 1.0 collective-permute-done.8
  150.4 1.6 fusion.52
  152.0 0.8 copy.79
  152.8 3.4 %collective-permute-start.11 = (bf16[256,256]{1,0:T(8,128)(2,1)}, bf16[256,256]{1,0:T(8,128)(2,1)S(1)}, u32[]{:S(2)}, u32[]{:S(2)}) collective-permute-start(bf16[256,256]{1,0:T(8,128)(2,1)} %bitcast.38), channel_id=1, source_target_pairs={{0,6},{1,7},{2,0},{3,1},{4,2},{5,3},{6,4},{7,5},{8,14},{9,15},{10,... | collective-permute-start | bytes 393224 | tf_op jit(solution)/shard_map/ppermute | solution.py:72
  156.2 0.8 copy.78
  157.0 1.6 collective-permute-start.10
  158.6 0.8 copy.77
  159.3 2.2 %collective-permute-start.9 = (bf16[256,256]{1,0:T(8,128)(2,1)}, bf16[256,256]{1,0:T(8,128)(2,1)}, u32[]{:S(2)}, u32[]{:S(2)}) collective-permute-start(bf16[256,256]{1,0:T(8,128)(2,1)} %bitcast.36), channel_id=1, source_target_pairs={{0,2},{1,3},{2,4},{3,5},{4,6},{5,7},{6,0},{7,1},{8,10},{9,11},{10,... | collective-permute-start | bytes 393224 | tf_op jit(solution)/shard_map/ppermute | solution.py:72
  161.6 0.9 copy.80
  163.3 4.1 %collective-permute-done.10 = bf16[256,256]{1,0:T(8,128)(2,1)} collective-permute-done((bf16[256,256]{1,0:T(8,128)(2,1)}, bf16[256,256]{1,0:T(8,128)(2,1)}, u32[]{:S(2)}, u32[]{:S(2)}) %collective-permute-start.10) | collective-permute-done | bytes 131104 | tf_op jit(solution)/shard_map/ppermute | solution.py:72
  167.4 3.7 %collective-permute-done.9 = bf16[256,256]{1,0:T(8,128)(2,1)} collective-permute-done((bf16[256,256]{1,0:T(8,128)(2,1)}, bf16[256,256]{1,0:T(8,128)(2,1)}, u32[]{:S(2)}, u32[]{:S(2)}) %collective-permute-start.9) | collective-permute-done | bytes 131104 | tf_op jit(solution)/shard_map/ppermute | solution.py:72
  171.2 1.0 fusion.18
  172.2 1.8 gather_fusion.1
  174.0 6.0 %all-to-all-start.1 = ((bf16[32,8,256]{2,1,0:T(8,128)(2,1)}), bf16[32,8,256]{2,1,0:T(8,128)(2,1)S(1)}, u32[]{:S(2)}, u32[]{:S(2)}) async-start(bf16[32,8,256]{2,1,0:T(8,128)(2,1)} %bitcast.40), calls=%async_computation.1 | async-start | bytes 262144 | tf_op jit(solution)/shard_map/all_to_all | solution.py:270
  180.2 2.4 %scatter_custom_fusion.1 = bf16[256,256]{1,0:T(8,128)(2,1)} fusion(s32[256]{0:T(256)S(1)} %bitcast.125, bf16[32,272,256]{2,1,0:T(8,128)(2,1)} %all-to-all-done.kv_ref, s32[]{:T(128)} %constant.201.clone.1, s32[]{:T(128)S(6)} %select_n.228, bf16[]{:T(256)} %constant.196.clone.1), kind=kCustom, calls=%fused_computation.49 | custom fusion | bytes 263172 | tf_op jit(solution)/shard_map/scatter | solution.py:117
  182.7 5.0 %all-to-all-done.1 = bf16[32,8,256]{2,1,0:T(8,128)(2,1)S(1)} async-done(((bf16[32,8,256]{2,1,0:T(8,128)(2,1)}), bf16[32,8,256]{2,1,0:T(8,128)(2,1)S(1)}, u32[]{:S(2)}, u32[]{:S(2)}) %all-to-all-start.1) | async-done | bytes 131104 | tf_op jit(solution)/shard_map/all_to_all | solution.py:270
  187.6 2.1 %scatter_custom_fusion = bf16[256,256]{1,0:T(8,128)(2,1)} fusion(s32[256]{0:T(256)S(1)} %bitcast.124, bf16[32,8,256]{2,1,0:T(8,128)(2,1)S(1)} %all-to-all-done.1, bf16[]{:T(256)} %constant.196.clone.1), kind=kCustom, calls=%fused_computation.51 | custom fusion | bytes 262146 | tf_op jit(solution)/shard_map/scatter | solution.py:275
  (101 shorter events, 8.6 us)
Async XLA Ops:
  0.6 144.6 %copy-start = (bf16[2048,384]{1,0:T(8,128)(2,1)S(1)}, bf16[2048,384]{1,0:T(8,128)(2,1)}, u32[]{:S(2)}) copy-start(bf16[2048,384]{1,0:T(8,128)(2,1)} %param.27) | copy-start | bytes 4718596
  0.6 6.7 %copy-start.2 = (bf16[256,2048]{1,0:T(8,128)(2,1)S(1)}, bf16[256,2048]{1,0:T(8,128)(2,1)}, u32[]{:S(2)}) copy-start(bf16[256,2048]{1,0:T(8,128)(2,1)} %param.15) | copy-start | bytes 3145732
  0.7 6.7 %copy-start.18 = (f32[2048]{0:T(1024)S(1)}, f32[2048]{0:T(1024)}, u32[]{:S(2)}) copy-start(f32[2048]{0:T(1024)} %param.19) | copy-start | bytes 24580
  1.7 5.7 %copy-start.17 = (bf16[2048,128]{1,0:T(8,128)(2,1)S(1)}, bf16[2048,128]{1,0:T(8,128)(2,1)}, u32[]{:S(2)}) copy-start(bf16[2048,128]{1,0:T(8,128)(2,1)} %param.21) | copy-start | bytes 1572868
  5.4 2.6 %copy-start.14 = (f32[128]{0:T(128)S(1)}, f32[128]{0:T(128)}, u32[]{:S(2)}) copy-start(f32[128]{0:T(128)} %param.24) | copy-start | bytes 1540
  11.1 66.7 %all-to-all-start = ((bf16[32,272,256]{2,1,0:T(8,128)(2,1)}), bf16[32,272,256]{2,1,0:T(8,128)(2,1)}, u32[]{:S(2)}, u32[]{:S(2)}) async-start(bf16[32,272,256]{2,1,0:T(8,128)(2,1)} %broadcast_in_dim.24), calls=%async_computation | async-start | bytes 8912896 | tf_op jit(solution)/shard_map/all_to_all | solution.py:42
  25.8 3.6 %copy-start.4 = (bf16[256,4,1,256]{3,2,1,0:T(2,128)(2,1)S(1)}, bf16[256,4,1,256]{3,2,1,0:T(2,128)(2,1)}, u32[]{:S(2)}) copy-start(bf16[256,4,1,256]{3,2,1,0:T(2,128)(2,1)} %get-tuple-element.20) | copy-start | bytes 1572868
  39.1 4.8 %copy-start.1 = (bf16[384,4,1,256]{3,2,1,0:T(2,128)(2,1)S(1)}, bf16[384,4,1,256]{3,2,1,0:T(2,128)(2,1)}, u32[]{:S(2)}) copy-start(bf16[384,4,1,256]{3,2,1,0:T(2,128)(2,1)} %get-tuple-element.18) | copy-start | bytes 2359300
  46.7 2.6 %copy-start.15 = (f32[128]{0:T(128)S(1)}, f32[128]{0:T(128)}, u32[]{:S(2)}) copy-start(f32[128]{0:T(128)} %param.23) | copy-start | bytes 1540
  46.7 3.0 %copy-start.13 = (s32[256]{0:T(256)S(1)}, s32[256]{0:T(256)}, u32[]{:S(2)}) copy-start(s32[256]{0:T(256)} %param.16) | copy-start | bytes 3076
  79.5 14.6 %copy-start.7 = (bf16[256,4,1,256]{0,3,1,2:T(8,128)(2,1)S(1)}, bf16[256,4,1,256]{0,3,1,2:T(8,128)(2,1)}, u32[]{:S(2)}) copy-start(bf16[256,4,1,256]{0,3,1,2:T(8,128)(2,1)} %copy.65) | copy-start | bytes 1572868
  79.5 19.5 %copy-start.8 = (bf16[256,4,1,256]{0,3,1,2:T(8,128)(2,1)S(1)}, bf16[256,4,1,256]{0,3,1,2:T(8,128)(2,1)}, u32[]{:S(2)}) copy-start(bf16[256,4,1,256]{0,3,1,2:T(8,128)(2,1)} %copy.64) | copy-start | bytes 1572868
  95.3 3.7 %collective-permute-start = (bf16[4,256,256]{1,2,0:T(8,128)(2,1)}, bf16[4,256,256]{1,2,0:T(8,128)(2,1)}, u32[]{:S(2)}, u32[]{:S(2)}) collective-permute-start(bf16[4,256,256]{1,2,0:T(8,128)(2,1)} %fusion.3), channel_id=1, source_target_pairs={{0,1},{1,0},{2,3},{3,2},{4,5},{5,4},{6,7},{7,6},{8,9},{9,8},{10,11... | collective-permute-start | bytes 1572872 | tf_op jit(solution)/shard_map/ppermute | solution.py:66
  97.1 13.2 %copy-start.3 = (bf16[256,2048]{1,0:T(8,128)(2,1)S(1)}, bf16[256,2048]{1,0:T(8,128)(2,1)}, u32[]{:S(2)}) copy-start(bf16[256,2048]{1,0:T(8,128)(2,1)} %param.15) | copy-start | bytes 3145732
  101.5 11.6 %collective-permute-start.3 = (bf16[256,256]{1,0:T(8,128)(2,1)S(1)}, bf16[256,256]{1,0:T(8,128)(2,1)S(1)}, u32[]{:S(2)}, u32[]{:S(2)}) collective-permute-start(bf16[256,256]{1,0:T(8,128)(2,1)S(1)} %bitcast.119), channel_id=1, source_target_pairs={{0,6},{1,7},{2,0},{3,1},{4,2},{5,3},{6,4},{7,5},{8,14},{9,15},{10,... | collective-permute-start | bytes 393224 | tf_op jit(solution)/shard_map/ppermute | solution.py:72
  106.8 12.6 %collective-permute-start.2 = (bf16[256,256]{1,0:T(8,128)(2,1)S(1)}, bf16[256,256]{1,0:T(8,128)(2,1)S(1)}, u32[]{:S(2)}, u32[]{:S(2)}) collective-permute-start(bf16[256,256]{1,0:T(8,128)(2,1)S(1)} %bitcast.120), channel_id=1, source_target_pairs={{0,4},{1,5},{2,6},{3,7},{4,0},{5,1},{6,2},{7,3},{8,12},{9,13},{10,... | collective-permute-start | bytes 393224 | tf_op jit(solution)/shard_map/ppermute | solution.py:72
  108.1 11.5 %collective-permute-start.1 = (bf16[256,256]{1,0:T(8,128)(2,1)S(1)}, bf16[256,256]{1,0:T(8,128)(2,1)}, u32[]{:S(2)}, u32[]{:S(2)}) collective-permute-start(bf16[256,256]{1,0:T(8,128)(2,1)S(1)} %bitcast.121), channel_id=1, source_target_pairs={{0,2},{1,3},{2,4},{3,5},{4,6},{5,7},{6,0},{7,1},{8,10},{9,11},{10,... | collective-permute-start | bytes 393224 | tf_op jit(solution)/shard_map/ppermute | solution.py:72
  112.9 29.3 %copy-start.20 = (s32[64]{0:T(128)S(1)}, s32[64]{0:T(128)}, u32[]{:S(2)}) copy-start(s32[64]{0:T(128)} %param.18) | copy-start | bytes 772
  119.4 0.7 copy-start.12
  121.3 12.8 %collective-permute-start.6 = (bf16[256,256]{1,0:T(8,128)(2,1)S(1)}, bf16[256,256]{1,0:T(8,128)(2,1)S(1)}, u32[]{:S(2)}, u32[]{:S(2)}) collective-permute-start(bf16[256,256]{1,0:T(8,128)(2,1)S(1)} %get-tuple-element.15), channel_id=1, source_target_pairs={{0,6},{1,7},{2,0},{3,1},{4,2},{5,3},{6,4},{7,5},{8,14},{9,15},{10,... | collective-permute-start | bytes 393224 | tf_op jit(solution)/shard_map/ppermute | solution.py:82
  125.4 13.5 %collective-permute-start.5 = (bf16[256,256]{1,0:T(8,128)(2,1)S(1)}, bf16[256,256]{1,0:T(8,128)(2,1)S(1)}, u32[]{:S(2)}, u32[]{:S(2)}) collective-permute-start(bf16[256,256]{1,0:T(8,128)(2,1)S(1)} %get-tuple-element.15), channel_id=1, source_target_pairs={{0,4},{1,5},{2,6},{3,7},{4,0},{5,1},{6,2},{7,3},{8,12},{9,13},{10,... | collective-permute-start | bytes 393224 | tf_op jit(solution)/shard_map/ppermute | solution.py:82
  127.3 11.8 %collective-permute-start.4 = (bf16[256,256]{1,0:T(8,128)(2,1)S(1)}, bf16[256,256]{1,0:T(8,128)(2,1)S(1)}, u32[]{:S(2)}, u32[]{:S(2)}) collective-permute-start(bf16[256,256]{1,0:T(8,128)(2,1)S(1)} %get-tuple-element.15), channel_id=1, source_target_pairs={{0,2},{1,3},{2,4},{3,5},{4,6},{5,7},{6,0},{7,1},{8,10},{9,11},{10,... | collective-permute-start | bytes 393224 | tf_op jit(solution)/shard_map/ppermute | solution.py:82
  139.1 0.7 copy-start.10
  140.6 3.3 %collective-permute-start.7 = (bf16[4,256,256]{2,1,0:T(8,128)(2,1)}, bf16[4,256,256]{2,1,0:T(8,128)(2,1)S(1)}, u32[]{:S(2)}, u32[]{:S(2)}) collective-permute-start(bf16[4,256,256]{2,1,0:T(8,128)(2,1)} %pad_maximum_fusion), channel_id=1, source_target_pairs={{0,1},{1,0},{2,3},{3,2},{4,5},{5,4},{6,7},{7,6},{8,9},{9,8},{10,11... | collective-permute-start | bytes 1572872 | tf_op jit(solution)/shard_map/ppermute | solution.py:84
  143.4 1.8 copy-start.19
  145.2 1.4 copy-start.16
  146.6 1.1 copy-start.5
  146.6 2.5 %copy-start.11 = (s32[32,1,256]{2,1,0:T(1,128)S(1)}, s32[32,1,256]{2,1,0:T(1,128)}, u32[]{:S(2)}) copy-start(s32[32,1,256]{2,1,0:T(1,128)} %fusion.42) | copy-start | bytes 98308
  147.8 1.6 copy-start.9
  147.8 2.6 %copy-start.6 = (bf16[384,4,1,256]{0,3,1,2:T(8,128)(2,1)S(1)}, bf16[384,4,1,256]{0,3,1,2:T(8,128)(2,1)}, u32[]{:S(2)}) copy-start(bf16[384,4,1,256]{0,3,1,2:T(8,128)(2,1)} %copy.66) | copy-start | bytes 2359300
  148.2 2.1 %collective-permute-start.8 = (bf16[4,256,256]{1,2,0:T(8,128)(2,1)S(1)}, bf16[4,256,256]{1,2,0:T(8,128)(2,1)}, u32[]{:S(2)}, u32[]{:S(2)}) collective-permute-start(bf16[4,256,256]{1,2,0:T(8,128)(2,1)S(1)} %fusion.4), channel_id=1, source_target_pairs={{0,1},{1,0},{2,3},{3,2},{4,5},{5,4},{6,7},{7,6},{8,9},{9,8},{10,11... | collective-permute-start | bytes 1572872 | tf_op jit(solution)/shard_map/ppermute | solution.py:66
  152.8 10.6 %collective-permute-start.11 = (bf16[256,256]{1,0:T(8,128)(2,1)}, bf16[256,256]{1,0:T(8,128)(2,1)S(1)}, u32[]{:S(2)}, u32[]{:S(2)}) collective-permute-start(bf16[256,256]{1,0:T(8,128)(2,1)} %bitcast.38), channel_id=1, source_target_pairs={{0,6},{1,7},{2,0},{3,1},{4,2},{5,3},{6,4},{7,5},{8,14},{9,15},{10,... | collective-permute-start | bytes 393224 | tf_op jit(solution)/shard_map/ppermute | solution.py:72
  157.0 10.5 %collective-permute-start.10 = (bf16[256,256]{1,0:T(8,128)(2,1)}, bf16[256,256]{1,0:T(8,128)(2,1)}, u32[]{:S(2)}, u32[]{:S(2)}) collective-permute-start(bf16[256,256]{1,0:T(8,128)(2,1)} %bitcast.37), channel_id=1, source_target_pairs={{0,4},{1,5},{2,6},{3,7},{4,0},{5,1},{6,2},{7,3},{8,12},{9,13},{10,... | collective-permute-start | bytes 393224 | tf_op jit(solution)/shard_map/ppermute | solution.py:72
  159.3 11.8 %collective-permute-start.9 = (bf16[256,256]{1,0:T(8,128)(2,1)}, bf16[256,256]{1,0:T(8,128)(2,1)}, u32[]{:S(2)}, u32[]{:S(2)}) collective-permute-start(bf16[256,256]{1,0:T(8,128)(2,1)} %bitcast.36), channel_id=1, source_target_pairs={{0,2},{1,3},{2,4},{3,5},{4,6},{5,7},{6,0},{7,1},{8,10},{9,11},{10,... | collective-permute-start | bytes 393224 | tf_op jit(solution)/shard_map/ppermute | solution.py:72
  174.0 13.6 %all-to-all-start.1 = ((bf16[32,8,256]{2,1,0:T(8,128)(2,1)}), bf16[32,8,256]{2,1,0:T(8,128)(2,1)S(1)}, u32[]{:S(2)}, u32[]{:S(2)}) async-start(bf16[32,8,256]{2,1,0:T(8,128)(2,1)} %bitcast.40), calls=%async_computation.1 | async-start | bytes 262144 | tf_op jit(solution)/shard_map/all_to_all | solution.py:270

commit v15 on v14

--- a/solution.py
+++ b/solution.py
@@ -81,7 +81,10 @@
     arrived = [block] + [
         lax.ppermute(block, "tp", chip_shift(tp_count, shift)) for shift in range(1, chips)
     ]
-    other_core = lax.ppermute(jnp.stack(arrived), "tp", [(i, i ^ 1) for i in range(tp_count)])
+    pairs = [(i, i ^ 1) for i in range(tp_count)]
+    other_core = [lax.ppermute(block, "tp", pairs)]
+    forwarded = lax.ppermute(jnp.stack(arrived[1:]), "tp", pairs)
+    other_core = other_core + [forwarded[shift] for shift in range(chips - 1)]
     full = jnp.zeros((rows, tp_count * part), block.dtype)
     for shift in range(chips):
         source = (chip - shift) % chips

time: 191 us -> 192 us (level)
  waiting for transfers between devices: 58.1 us -> 54.7 us
  starting transfers between devices: 43.1 us -> 46.2 us
  local copies, waits for them, and re-layouts: 47.9 us -> 50.2 us
    dynamic_update_slice x4, local copies, waits for them, and re-layouts: 0.06 us -> 3.68 us  [gather_tp(): lax.dynamic_update_slice(full, other_core[shift], (0, (2 * source + 1 - c...]
    ppermute x3, waiting for transfers between devices: 9.75 us -> 6.76 us  [gather_tp(): lax.ppermute(block, 'tp', chip_shift(tp_count, shift))]
    all_to_all x1, starting transfers between devices: 6.04 us -> 8.06 us  [body(): lax.all_to_all(out[send_rows], 'seq', split_axis=0, concat_axis=0, tiled=...]
  transfers between devices with their start and end apart: 14 -> 15, of which waited for: 13 -> 10; matrix products, arithmetic and copies ran while one was open for 22% -> 23% of each run, Pallas kernels for 0% -> 0%
where the time goes in v15:
time: 192 us; the launch traced here: 191 us
  waiting for transfers between devices  54.7 us (28%)
  local copies, waits for them, and re-layouts  50.2 us (26%)
  starting transfers between devices  46.2 us (24%)
  Pallas kernels  13.7 us (7%)
  other arithmetic  13 us (7%)
  matrix products  11.9 us (6%)
    all_to_all x1, waiting for transfers between devices, gather_seq(): lax.all_to_all(copies, 'seq', split_axis=0, concat_axis=0, tiled=True)  25.5 us
    ppermute x6, starting transfers between devices, project_reduce_tp(): lax.ppermute(piece, 'tp', chip_shift(tp_count, shift)).astype(jnp.float32)  14.4 us
    ppermute x6, waiting for transfers between devices, project_reduce_tp(): lax.ppermute(piece, 'tp', chip_shift(tp_count, shift)).astype(jnp.float32)  14.3 us
    pallas_call x1, Pallas kernels, attend(): pl.pallas_call(functools.partial(attend_kernel, rows=rows), grid=(count /...  13.7 us
    dynamic_slice x4, local copies, waits for them, and re-layouts, core_halves(): other = lax.dynamic_index_in_dim(weight, 1 - core, axis=2, keepdims=False)  13.2 us
    all_to_all x1, starting transfers between devices, gather_seq(): lax.all_to_all(copies, 'seq', split_axis=0, concat_axis=0, tiled=True)  9.34 us
    ppermute x3, starting transfers between devices, gather_tp(): lax.ppermute(block, 'tp', chip_shift(tp_count, shift))  9.23 us
    dynamic_slice x2, local copies, waits for them, and re-layouts, core_halves(): mine = lax.dynamic_index_in_dim(weight, core, axis=2, keepdims=False)  8.36 us
  transfers between devices with their start and end apart: 15, of which 10 were waited for; matrix products, arithmetic and copies ran while one was open for 23% of the time, Pallas kernels for 0%

profile of v15, /device:TPU:1, one launch (start us, length us, event | category | flops | bytes accessed | tf_op | source)
XLA Modules:
  0.0 191.0 jit_solution(15406523162257228434)
XLA Ops:
  0.7 1.0 reduce-window.9
  1.7 0.7 bitcast_subtract_fusion
  2.4 0.8 select_reduce_fusion
  3.1 0.7 subtract_convert_fusion.1
  3.9 1.5 multiply_reduce_fusion
  5.4 2.0 %fusion.5 = bf16[256,1,1,128]{0,3,2,1:T(8,128)(2,1)S(1)} fusion(bf16[2048,128]{1,0:T(8,128)(2,1)} %param.22, f32[2048]{0:T(1024)} %param.19, f32[256]{0:T(256)S(1)} %add_rsqrt_fusion.3, bf16[256,2048]{1,0:T(8,128)(2,1)} %param.15), kind=kOutput, calls=%fused_computation.18 | convolution fusion | flops 136347648 | bytes 1647616 | tf_op jit(solution)/shard_map/dot_general | solution.py:233
  8.7 2.4 %broadcast_in_dim.24 = bf16[32,272,256]{2,1,0:T(8,128)(2,1)} broadcast(bf16[272,256]{1,0:T(8,128)(2,1)S(1)} %maximum_maximum_fusion), dimensions={1,2} | broadcast | bytes 4595712 | tf_op jit(solution)/shard_map/broadcast_in_dim | solution.py:41
  11.1 9.3 %all-to-all-start = ((bf16[32,272,256]{2,1,0:T(8,128)(2,1)}), bf16[32,272,256]{2,1,0:T(8,128)(2,1)}, u32[]{:S(2)}, u32[]{:S(2)}) async-start(bf16[32,272,256]{2,1,0:T(8,128)(2,1)} %broadcast_in_dim.24), calls=%async_computation | async-start | bytes 8912896 | tf_op jit(solution)/shard_map/all_to_all | solution.py:42
  20.5 1.8 reshape.485
  22.3 3.5 %constant_dynamic-slice_fusion.10 = (bf16[256,4,1,256]{3,2,1,0:T(2,128)(2,1)}, bf16[256,4,1,256]{3,2,1,0:T(2,128)(2,1)}) fusion(bf16[256,4,2,256]{3,2,1,0:T(2,128)(2,1)S(1)} %reshape.485, s32[]{:T(128)S(6)} %select_n.202, s32[]{:T(128)S(6)} %select_n.201), kind=kLoop, calls=%fused_computation.97 | loop fusion | bytes 2097160 | tf_op jit(solution)/shard_map/jit(dynamic_index_in_dim)/dynamic_slice | solution.py:53
  25.8 3.6 %copy.64 = bf16[256,4,1,256]{0,3,1,2:T(8,128)(2,1)} copy(bf16[256,4,1,256]{3,2,1,0:T(2,128)(2,1)} %get-tuple-element.21) | data formatting | bytes 1048576 | tf_op jit(solution)/shard_map/jit(dynamic_index_in_dim)/dynamic_slice | solution.py:52
  29.4 2.0 %copy.65 = bf16[256,4,1,256]{0,3,1,2:T(8,128)(2,1)} copy(bf16[256,4,1,256]{3,2,1,0:T(2,128)(2,1)S(1)} %copy-done.4) | data formatting | bytes 1048576 | tf_op jit(solution)/shard_map/jit(dynamic_index_in_dim)/dynamic_slice | solution.py:53
  31.4 2.9 %reshape.486 = bf16[384,4,2,256]{3,2,1,0:T(2,128)(2,1)S(1)} reshape(bf16[384,2048]{1,0:T(8,128)(2,1)} %param.29) | data formatting | bytes 3145728 | tf_op jit(solution)/shard_map/reshape | solution.py:243
  34.2 4.9 %constant_dynamic-slice_fusion.8 = (bf16[384,4,1,256]{3,2,1,0:T(2,128)(2,1)}, bf16[384,4,1,256]{3,2,1,0:T(2,128)(2,1)}) fusion(bf16[384,4,2,256]{3,2,1,0:T(2,128)(2,1)S(1)} %reshape.486, s32[]{:T(128)S(6)} %select_n.202, s32[]{:T(128)S(6)} %select_n.201), kind=kLoop, calls=%fused_computation.95 | loop fusion | bytes 3145736 | tf_op jit(solution)/shard_map/jit(dynamic_index_in_dim)/dynamic_slice | solution.py:53
  39.1 4.8 %copy.66 = bf16[384,4,1,256]{0,3,1,2:T(8,128)(2,1)} copy(bf16[384,4,1,256]{3,2,1,0:T(2,128)(2,1)} %get-tuple-element.19) | data formatting | bytes 1572864 | tf_op jit(solution)/shard_map/jit(dynamic_index_in_dim)/dynamic_slice | solution.py:52
  43.9 2.8 %copy.67 = bf16[384,4,1,256]{0,3,1,2:T(8,128)(2,1)} copy(bf16[384,4,1,256]{3,2,1,0:T(2,128)(2,1)S(1)} %copy-done.1) | data formatting | bytes 1572864 | tf_op jit(solution)/shard_map/jit(dynamic_index_in_dim)/dynamic_slice | solution.py:53
  46.7 2.2 %multiply_reduce_fusion.1 = (f32[256,2]{0,1:T(2,128)S(1)}, f32[256,256]{0,1:T(8,128)S(1)}) fusion(bf16[2048,256]{1,0:T(8,128)(2,1)} %param.20, f32[2048]{0:T(1024)S(1)} %copy-done.17, f32[256]{0:T(256)S(1)} %add_rsqrt_fusion.3, bf16[256,2048]{1,0:T(8,128)(2,1)} %param.15), kind=kOutput, calls=%fused_computation.37 | convolution fusion | flops 270663168 | bytes 2370560 | tf_op jit(solution)/shard_map/dot_general | solution.py:230
  49.8 0.8 broadcast_in_dim_reshape.9.qtok_ref
  50.7 0.8 broadcast_in_dim_reshape.10.qbeg_ref
  51.5 0.8 pad_maximum_fusion.2.q_ref
  52.3 25.5 %all-to-all-done.kv_ref = bf16[32,272,256]{2,1,0:T(8,128)(2,1)} async-done(((bf16[32,272,256]{2,1,0:T(8,128)(2,1)}), bf16[32,272,256]{2,1,0:T(8,128)(2,1)}, u32[]{:S(2)}, u32[]{:S(2)}) %all-to-all-start) | async-done | bytes 4456480 | tf_op jit(solution)/shard_map/all_to_all | solution.py:42
  77.8 1.7 fusion.41
  79.5 13.7 %shard_map.158 = bf16[512,128]{1,0:T(8,128)(2,1)} custom-call(bf16[512,128]{1,0:T(8,128)(2,1)} %pad_maximum_fusion.2.q_ref, s32[512,1]{1,0:T(8,128)} %broadcast_in_dim_reshape.9.qtok_ref, s32[512,1]{1,0:T(8,128)} %broadcast_in_dim_reshape.10.qbeg_ref, bf16[32,272,256]{2,1,0:T(8,128)(2,1)} %all-to-all-done.kv_ref, s32[1,8192]{1,0:T(1,128)} %bitcast.112), custom_call_target="tpu_custom_call" | custom-call | tf_op jit(solution)/shard_map/pallas_call | solution.py:187
  93.1 1.0 reshape.524
  94.1 1.2 fusion.3
  95.3 1.8 collective-permute-start
  97.1 1.9 collective-permute-done
  99.0 2.3 %fusion.53 = (bf16[4,256,256]{1,2,0:T(8,128)(2,1)S(1)}, f32[4,256,256]{1,2,0:T(8,128)}) fusion(bf16[4,256,256]{1,2,0:T(8,128)(2,1)} %collective-permute-done, bf16[256,4,256]{0,2,1:T(8,128)(2,1)S(1)} %bitcast.104, bf16[256,256,1]{1,0,2:T(8,128)(2,1)S(1)} %reshape.524), kind=kOutput, calls=%fused_computation.133 | convolution fusion | flops 135004160 | bytes 2752512 | tf_op jit(solution)/shard_map/rk,kcp->crp/dot_general | solution.py:65
  101.5 5.2 %collective-permute-start.3 = (bf16[256,256]{1,0:T(8,128)(2,1)S(1)}, bf16[256,256]{1,0:T(8,128)(2,1)S(1)}, u32[]{:S(2)}, u32[]{:S(2)}) collective-permute-start(bf16[256,256]{1,0:T(8,128)(2,1)S(1)} %bitcast.113), channel_id=1, source_target_pairs={{0,6},{1,7},{2,0},{3,1},{4,2},{5,3},{6,4},{7,5},{8,14},{9,15},{10,... | collective-permute-start | bytes 393224 | tf_op jit(solution)/shard_map/ppermute | solution.py:72
  106.8 1.2 collective-permute-start.2
  108.1 2.2 %collective-permute-start.1 = (bf16[256,256]{1,0:T(8,128)(2,1)S(1)}, bf16[256,256]{1,0:T(8,128)(2,1)}, u32[]{:S(2)}, u32[]{:S(2)}) collective-permute-start(bf16[256,256]{1,0:T(8,128)(2,1)S(1)} %bitcast.115), channel_id=1, source_target_pairs={{0,2},{1,3},{2,4},{3,5},{4,6},{5,7},{6,0},{7,1},{8,10},{9,11},{10,... | collective-permute-start | bytes 393224 | tf_op jit(solution)/shard_map/ppermute | solution.py:72
  110.3 1.6 convert_element_type.116
  111.9 1.0 constant_dynamic-slice_fusion.7
  113.0 6.3 %collective-permute-done.2 = bf16[256,256]{1,0:T(8,128)(2,1)S(1)} collective-permute-done((bf16[256,256]{1,0:T(8,128)(2,1)S(1)}, bf16[256,256]{1,0:T(8,128)(2,1)S(1)}, u32[]{:S(2)}, u32[]{:S(2)}) %collective-permute-start.2) | collective-permute-done | bytes 131104 | tf_op jit(solution)/shard_map/ppermute | solution.py:72
  120.2 1.2 constant_dynamic-update-slice_fusion.4
  121.3 2.7 %collective-permute-start.5 = (bf16[256,256]{1,0:T(8,128)(2,1)S(1)}, bf16[256,256]{1,0:T(8,128)(2,1)S(1)}, u32[]{:S(2)}, u32[]{:S(2)}) collective-permute-start(bf16[256,256]{1,0:T(8,128)(2,1)S(1)} %get-tuple-element.15), channel_id=1, source_target_pairs={{0,2},{1,3},{2,4},{3,5},{4,6},{5,7},{6,0},{7,1},{8,10},{9,11},{10,... | collective-permute-start | bytes 393224 | tf_op jit(solution)/shard_map/ppermute | solution.py:82
  124.0 1.5 collective-permute-start.7
  125.5 5.0 %collective-permute-start.6 = (bf16[256,256]{1,0:T(8,128)(2,1)S(1)}, bf16[256,256]{1,0:T(8,128)(2,1)S(1)}, u32[]{:S(2)}, u32[]{:S(2)}) collective-permute-start(bf16[256,256]{1,0:T(8,128)(2,1)S(1)} %get-tuple-element.15), channel_id=1, source_target_pairs={{0,4},{1,5},{2,6},{3,7},{4,0},{5,1},{6,2},{7,3},{8,12},{9,13},{10,... | collective-permute-start | bytes 393224 | tf_op jit(solution)/shard_map/ppermute | solution.py:82
  130.6 1.6 collective-permute-start.4
  132.2 3.7 %collective-permute-done.7 = bf16[256,256]{1,0:T(8,128)(2,1)S(1)} collective-permute-done((bf16[256,256]{1,0:T(8,128)(2,1)S(1)}, bf16[256,256]{1,0:T(8,128)(2,1)S(1)}, u32[]{:S(2)}, u32[]{:S(2)}) %collective-permute-start.7) | collective-permute-done | bytes 131104 | tf_op jit(solution)/shard_map/ppermute | solution.py:82
  135.9 3.0 %collective-permute-done.6 = bf16[256,256]{1,0:T(8,128)(2,1)S(1)} collective-permute-done((bf16[256,256]{1,0:T(8,128)(2,1)S(1)}, bf16[256,256]{1,0:T(8,128)(2,1)S(1)}, u32[]{:S(2)}, u32[]{:S(2)}) %collective-permute-start.6) | collective-permute-done | bytes 131104 | tf_op jit(solution)/shard_map/ppermute | solution.py:82
  139.0 1.8 collective-permute-start.8
  141.3 0.7 mul.284
  142.1 0.9 constant_dynamic-update-slice_fusion.3
  143.0 0.9 fusion.25
  144.0 0.9 fusion.24
  144.9 0.9 fusion.23
  146.2 0.8 fusion.8
  147.6 0.8 fusion.12
  150.1 1.3 collective-permute-done.9
  151.4 1.6 fusion.51
  153.1 0.8 copy.79
  153.9 0.8 copy.78
  154.6 5.7 %collective-permute-start.11 = (bf16[256,256]{1,0:T(8,128)(2,1)}, bf16[256,256]{1,0:T(8,128)(2,1)}, u32[]{:S(2)}, u32[]{:S(2)}) collective-permute-start(bf16[256,256]{1,0:T(8,128)(2,1)} %bitcast.35), channel_id=1, source_target_pairs={{0,4},{1,5},{2,6},{3,7},{4,0},{5,1},{6,2},{7,3},{8,12},{9,13},{10,... | collective-permute-start | bytes 393224 | tf_op jit(solution)/shard_map/ppermute | solution.py:72
  160.4 0.8 copy.77
  161.1 0.9 copy.80
  162.7 1.4 collective-permute-done.11
  164.2 6.2 %collective-permute-done.10 = bf16[256,256]{1,0:T(8,128)(2,1)} collective-permute-done((bf16[256,256]{1,0:T(8,128)(2,1)}, bf16[256,256]{1,0:T(8,128)(2,1)}, u32[]{:S(2)}, u32[]{:S(2)}) %collective-permute-start.10) | collective-permute-done | bytes 131104 | tf_op jit(solution)/shard_map/ppermute | solution.py:72
  170.4 1.0 fusion.18
  171.5 1.8 gather_fusion.1
  173.3 8.1 %all-to-all-start.1 = ((bf16[32,8,256]{2,1,0:T(8,128)(2,1)}), bf16[32,8,256]{2,1,0:T(8,128)(2,1)S(1)}, u32[]{:S(2)}, u32[]{:S(2)}) async-start(bf16[32,8,256]{2,1,0:T(8,128)(2,1)} %bitcast.38), calls=%async_computation.1 | async-start | bytes 262144 | tf_op jit(solution)/shard_map/all_to_all | solution.py:273
  181.5 2.4 %scatter_custom_fusion.1 = bf16[256,256]{1,0:T(8,128)(2,1)} fusion(s32[256]{0:T(256)S(1)} %bitcast.119, bf16[32,272,256]{2,1,0:T(8,128)(2,1)} %all-to-all-done.kv_ref, s32[]{:T(128)} %constant.201.clone.1, s32[]{:T(128)S(6)} %select_n.228, bf16[]{:T(256)} %constant.196.clone.1), kind=kCustom, calls=%fused_computation.47 | custom fusion | bytes 263172 | tf_op jit(solution)/shard_map/scatter | solution.py:120
  184.0 5.0 %all-to-all-done.1 = bf16[32,8,256]{2,1,0:T(8,128)(2,1)S(1)} async-done(((bf16[32,8,256]{2,1,0:T(8,128)(2,1)}), bf16[32,8,256]{2,1,0:T(8,128)(2,1)S(1)}, u32[]{:S(2)}, u32[]{:S(2)}) %all-to-all-start.1) | async-done | bytes 131104 | tf_op jit(solution)/shard_map/all_to_all | solution.py:273
  188.9 2.1 %scatter_custom_fusion = bf16[256,256]{1,0:T(8,128)(2,1)} fusion(s32[256]{0:T(256)S(1)} %bitcast.118, bf16[32,8,256]{2,1,0:T(8,128)(2,1)S(1)} %all-to-all-done.1, bf16[]{:T(256)} %constant.196.clone.1), kind=kCustom, calls=%fused_computation.49 | custom fusion | bytes 262146 | tf_op jit(solution)/shard_map/scatter | solution.py:278
  (101 shorter events, 7.6 us)
Async XLA Ops:
  0.6 145.5 %copy-start = (bf16[2048,384]{1,0:T(8,128)(2,1)S(1)}, bf16[2048,384]{1,0:T(8,128)(2,1)}, u32[]{:S(2)}) copy-start(bf16[2048,384]{1,0:T(8,128)(2,1)} %param.27) | copy-start | bytes 4718596
  0.6 6.7 %copy-start.2 = (bf16[256,2048]{1,0:T(8,128)(2,1)S(1)}, bf16[256,2048]{1,0:T(8,128)(2,1)}, u32[]{:S(2)}) copy-start(bf16[256,2048]{1,0:T(8,128)(2,1)} %param.15) | copy-start | bytes 3145732
  0.7 6.7 %copy-start.17 = (f32[2048]{0:T(1024)S(1)}, f32[2048]{0:T(1024)}, u32[]{:S(2)}) copy-start(f32[2048]{0:T(1024)} %param.19) | copy-start | bytes 24580
  1.7 5.7 %copy-start.16 = (bf16[2048,128]{1,0:T(8,128)(2,1)S(1)}, bf16[2048,128]{1,0:T(8,128)(2,1)}, u32[]{:S(2)}) copy-start(bf16[2048,128]{1,0:T(8,128)(2,1)} %param.21) | copy-start | bytes 1572868
  5.4 2.6 %copy-start.13 = (f32[128]{0:T(128)S(1)}, f32[128]{0:T(128)}, u32[]{:S(2)}) copy-start(f32[128]{0:T(128)} %param.24) | copy-start | bytes 1540
  11.1 66.7 %all-to-all-start = ((bf16[32,272,256]{2,1,0:T(8,128)(2,1)}), bf16[32,272,256]{2,1,0:T(8,128)(2,1)}, u32[]{:S(2)}, u32[]{:S(2)}) async-start(bf16[32,272,256]{2,1,0:T(8,128)(2,1)} %broadcast_in_dim.24), calls=%async_computation | async-start | bytes 8912896 | tf_op jit(solution)/shard_map/all_to_all | solution.py:42
  25.8 3.6 %copy-start.4 = (bf16[256,4,1,256]{3,2,1,0:T(2,128)(2,1)S(1)}, bf16[256,4,1,256]{3,2,1,0:T(2,128)(2,1)}, u32[]{:S(2)}) copy-start(bf16[256,4,1,256]{3,2,1,0:T(2,128)(2,1)} %get-tuple-element.20) | copy-start | bytes 1572868
  39.1 4.8 %copy-start.1 = (bf16[384,4,1,256]{3,2,1,0:T(2,128)(2,1)S(1)}, bf16[384,4,1,256]{3,2,1,0:T(2,128)(2,1)}, u32[]{:S(2)}) copy-start(bf16[384,4,1,256]{3,2,1,0:T(2,128)(2,1)} %get-tuple-element.18) | copy-start | bytes 2359300
  46.7 2.6 %copy-start.14 = (f32[128]{0:T(128)S(1)}, f32[128]{0:T(128)}, u32[]{:S(2)}) copy-start(f32[128]{0:T(128)} %param.23) | copy-start | bytes 1540
  46.7 3.0 %copy-start.12 = (s32[256]{0:T(256)S(1)}, s32[256]{0:T(256)}, u32[]{:S(2)}) copy-start(s32[256]{0:T(256)} %param.16) | copy-start | bytes 3076
  79.5 14.6 %copy-start.7 = (bf16[256,4,1,256]{0,3,1,2:T(8,128)(2,1)S(1)}, bf16[256,4,1,256]{0,3,1,2:T(8,128)(2,1)}, u32[]{:S(2)}) copy-start(bf16[256,4,1,256]{0,3,1,2:T(8,128)(2,1)} %copy.65) | copy-start | bytes 1572868
  79.5 19.5 %copy-start.8 = (bf16[256,4,1,256]{0,3,1,2:T(8,128)(2,1)S(1)}, bf16[256,4,1,256]{0,3,1,2:T(8,128)(2,1)}, u32[]{:S(2)}) copy-start(bf16[256,4,1,256]{0,3,1,2:T(8,128)(2,1)} %copy.64) | copy-start | bytes 1572868
  95.3 3.7 %collective-permute-start = (bf16[4,256,256]{1,2,0:T(8,128)(2,1)}, bf16[4,256,256]{1,2,0:T(8,128)(2,1)}, u32[]{:S(2)}, u32[]{:S(2)}) collective-permute-start(bf16[4,256,256]{1,2,0:T(8,128)(2,1)} %fusion.3), channel_id=1, source_target_pairs={{0,1},{1,0},{2,3},{3,2},{4,5},{5,4},{6,7},{7,6},{8,9},{9,8},{10,11... | collective-permute-start | bytes 1572872 | tf_op jit(solution)/shard_map/ppermute | solution.py:66
  97.1 13.2 %copy-start.3 = (bf16[256,2048]{1,0:T(8,128)(2,1)S(1)}, bf16[256,2048]{1,0:T(8,128)(2,1)}, u32[]{:S(2)}) copy-start(bf16[256,2048]{1,0:T(8,128)(2,1)} %param.15) | copy-start | bytes 3145732
  101.5 11.6 %collective-permute-start.3 = (bf16[256,256]{1,0:T(8,128)(2,1)S(1)}, bf16[256,256]{1,0:T(8,128)(2,1)S(1)}, u32[]{:S(2)}, u32[]{:S(2)}) collective-permute-start(bf16[256,256]{1,0:T(8,128)(2,1)S(1)} %bitcast.113), channel_id=1, source_target_pairs={{0,6},{1,7},{2,0},{3,1},{4,2},{5,3},{6,4},{7,5},{8,14},{9,15},{10,... | collective-permute-start | bytes 393224 | tf_op jit(solution)/shard_map/ppermute | solution.py:72
  106.8 12.6 %collective-permute-start.2 = (bf16[256,256]{1,0:T(8,128)(2,1)S(1)}, bf16[256,256]{1,0:T(8,128)(2,1)S(1)}, u32[]{:S(2)}, u32[]{:S(2)}) collective-permute-start(bf16[256,256]{1,0:T(8,128)(2,1)S(1)} %bitcast.114), channel_id=1, source_target_pairs={{0,4},{1,5},{2,6},{3,7},{4,0},{5,1},{6,2},{7,3},{8,12},{9,13},{10,... | collective-permute-start | bytes 393224 | tf_op jit(solution)/shard_map/ppermute | solution.py:72
  108.1 11.5 %collective-permute-start.1 = (bf16[256,256]{1,0:T(8,128)(2,1)S(1)}, bf16[256,256]{1,0:T(8,128)(2,1)}, u32[]{:S(2)}, u32[]{:S(2)}) collective-permute-start(bf16[256,256]{1,0:T(8,128)(2,1)S(1)} %bitcast.115), channel_id=1, source_target_pairs={{0,2},{1,3},{2,4},{3,5},{4,6},{5,7},{6,0},{7,1},{8,10},{9,11},{10,... | collective-permute-start | bytes 393224 | tf_op jit(solution)/shard_map/ppermute | solution.py:72
  111.9 28.9 %copy-start.19 = (s32[64]{0:T(128)S(1)}, s32[64]{0:T(128)}, u32[]{:S(2)}) copy-start(s32[64]{0:T(128)} %param.18) | copy-start | bytes 772
  119.4 0.7 copy-start.11
  121.3 10.9 %collective-permute-start.5 = (bf16[256,256]{1,0:T(8,128)(2,1)S(1)}, bf16[256,256]{1,0:T(8,128)(2,1)S(1)}, u32[]{:S(2)}, u32[]{:S(2)}) collective-permute-start(bf16[256,256]{1,0:T(8,128)(2,1)S(1)} %get-tuple-element.15), channel_id=1, source_target_pairs={{0,2},{1,3},{2,4},{3,5},{4,6},{5,7},{6,0},{7,1},{8,10},{9,11},{10,... | collective-permute-start | bytes 393224 | tf_op jit(solution)/shard_map/ppermute | solution.py:82
  124.0 11.9 %collective-permute-start.7 = (bf16[256,256]{1,0:T(8,128)(2,1)S(1)}, bf16[256,256]{1,0:T(8,128)(2,1)S(1)}, u32[]{:S(2)}, u32[]{:S(2)}) collective-permute-start(bf16[256,256]{1,0:T(8,128)(2,1)S(1)} %get-tuple-element.15), channel_id=1, source_target_pairs={{0,6},{1,7},{2,0},{3,1},{4,2},{5,3},{6,4},{7,5},{8,14},{9,15},{10,... | collective-permute-start | bytes 393224 | tf_op jit(solution)/shard_map/ppermute | solution.py:82
  125.5 13.4 %collective-permute-start.6 = (bf16[256,256]{1,0:T(8,128)(2,1)S(1)}, bf16[256,256]{1,0:T(8,128)(2,1)S(1)}, u32[]{:S(2)}, u32[]{:S(2)}) collective-permute-start(bf16[256,256]{1,0:T(8,128)(2,1)S(1)} %get-tuple-element.15), channel_id=1, source_target_pairs={{0,4},{1,5},{2,6},{3,7},{4,0},{5,1},{6,2},{7,3},{8,12},{9,13},{10,... | collective-permute-start | bytes 393224 | tf_op jit(solution)/shard_map/ppermute | solution.py:82
  130.6 11.5 %collective-permute-start.4 = (bf16[256,256]{1,0:T(8,128)(2,1)S(1)}, bf16[256,256]{1,0:T(8,128)(2,1)}, u32[]{:S(2)}, u32[]{:S(2)}) collective-permute-start(bf16[256,256]{1,0:T(8,128)(2,1)S(1)} %get-tuple-element.15), channel_id=1, source_target_pairs={{0,1},{1,0},{2,3},{3,2},{4,5},{5,4},{6,7},{7,6},{8,9},{9,8},{10,11... | collective-permute-start | bytes 393224 | tf_op jit(solution)/shard_map/ppermute | solution.py:85
  139.0 4.0 %collective-permute-start.8 = (bf16[3,256,256]{2,1,0:T(8,128)(2,1)S(1)}, bf16[3,256,256]{2,1,0:T(8,128)(2,1)}, u32[]{:S(2)}, u32[]{:S(2)}) collective-permute-start(bf16[3,256,256]{2,1,0:T(8,128)(2,1)S(1)} %pad_maximum_fusion), channel_id=1, source_target_pairs={{0,1},{1,0},{2,3},{3,2},{4,5},{5,4},{6,7},{7,6},{8,9},{9,8},{10,11... | collective-permute-start | bytes 1179656 | tf_op jit(solution)/shard_map/ppermute | solution.py:86
  142.1 4.1 %copy-start.18 = (f32[2048]{0:T(1024)S(1)}, f32[2048]{0:T(1024)}, u32[]{:S(2)}) copy-start(f32[2048]{0:T(1024)} %param.26) | copy-start | bytes 24580
  146.2 1.4 copy-start.15
  147.6 1.1 copy-start.5
  147.6 2.3 %copy-start.10 = (s32[32,1,256]{2,1,0:T(1,128)S(1)}, s32[32,1,256]{2,1,0:T(1,128)}, u32[]{:S(2)}) copy-start(s32[32,1,256]{2,1,0:T(1,128)} %fusion.41) | copy-start | bytes 98308
  148.7 0.7 copy-start.9
  148.7 2.7 %copy-start.6 = (bf16[384,4,1,256]{0,3,1,2:T(8,128)(2,1)S(1)}, bf16[384,4,1,256]{0,3,1,2:T(8,128)(2,1)}, u32[]{:S(2)}) copy-start(bf16[384,4,1,256]{0,3,1,2:T(8,128)(2,1)} %copy.66) | copy-start | bytes 2359300
  149.4 2.0 %collective-permute-start.9 = (bf16[4,256,256]{1,2,0:T(8,128)(2,1)S(1)}, bf16[4,256,256]{1,2,0:T(8,128)(2,1)}, u32[]{:S(2)}, u32[]{:S(2)}) collective-permute-start(bf16[4,256,256]{1,2,0:T(8,128)(2,1)S(1)} %fusion.4), channel_id=1, source_target_pairs={{0,1},{1,0},{2,3},{3,2},{4,5},{5,4},{6,7},{7,6},{8,9},{9,8},{10,11... | collective-permute-start | bytes 1572872 | tf_op jit(solution)/shard_map/ppermute | solution.py:66
  153.9 8.9 %collective-permute-start.12 = (bf16[256,256]{1,0:T(8,128)(2,1)}, bf16[256,256]{1,0:T(8,128)(2,1)S(1)}, u32[]{:S(2)}, u32[]{:S(2)}) collective-permute-start(bf16[256,256]{1,0:T(8,128)(2,1)} %bitcast.36), channel_id=1, source_target_pairs={{0,6},{1,7},{2,0},{3,1},{4,2},{5,3},{6,4},{7,5},{8,14},{9,15},{10,... | collective-permute-start | bytes 393224 | tf_op jit(solution)/shard_map/ppermute | solution.py:72
  154.6 9.5 %collective-permute-start.11 = (bf16[256,256]{1,0:T(8,128)(2,1)}, bf16[256,256]{1,0:T(8,128)(2,1)}, u32[]{:S(2)}, u32[]{:S(2)}) collective-permute-start(bf16[256,256]{1,0:T(8,128)(2,1)} %bitcast.35), channel_id=1, source_target_pairs={{0,4},{1,5},{2,6},{3,7},{4,0},{5,1},{6,2},{7,3},{8,12},{9,13},{10,... | collective-permute-start | bytes 393224 | tf_op jit(solution)/shard_map/ppermute | solution.py:72
  161.1 9.3 %collective-permute-start.10 = (bf16[256,256]{1,0:T(8,128)(2,1)}, bf16[256,256]{1,0:T(8,128)(2,1)}, u32[]{:S(2)}, u32[]{:S(2)}) collective-permute-start(bf16[256,256]{1,0:T(8,128)(2,1)} %bitcast.34), channel_id=1, source_target_pairs={{0,2},{1,3},{2,4},{3,5},{4,6},{5,7},{6,0},{7,1},{8,10},{9,11},{10,... | collective-permute-start | bytes 393224 | tf_op jit(solution)/shard_map/ppermute | solution.py:72
  173.3 15.7 %all-to-all-start.1 = ((bf16[32,8,256]{2,1,0:T(8,128)(2,1)}), bf16[32,8,256]{2,1,0:T(8,128)(2,1)S(1)}, u32[]{:S(2)}, u32[]{:S(2)}) async-start(bf16[32,8,256]{2,1,0:T(8,128)(2,1)} %bitcast.38), calls=%async_computation.1 | async-start | bytes 262144 | tf_op jit(solution)/shard_map/all_to_all | solution.py:273
